TPU v7x, 32 devices: a whole 2x2x4 slice. The times are simulated.
32 devices in a mesh: groups: 2 (over y), expert: 8 (over z, x), context: 2 (over core).
Axes of the slice: x: 2, y: 2, z: 4, core: 2. Of those that a mesh axis runs over, the one named last changes fastest.
Arguments:
- tokens: bfloat16 [2048, 3584], P(('groups', 'expert', 'context')), parts along dimension 0, may hold values from -6 to 6
- routes: int32 [2048, 8], P(('groups', 'expert', 'context')), parts along dimension 0, may hold values from 0 to 15, all different within a row; in each aligned block of 128 rows (0 to 127, 128 to 255, ...) at most 80 rows name the same one
- route_weight: float32 [2048, 8], P(('groups', 'expert', 'context')), parts along dimension 0, may hold values from 0.5 to 1.5
- w_gate: bfloat16 [8, 320, 3584], P('expert', 'context'), may hold values from -0.09375 to 0.09375
- w_up: bfloat16 [8, 320, 3584], P('expert', 'context'), may hold values from -0.09375 to 0.09375
- w_down: bfloat16 [8, 320, 3584], P('expert', 'context'), may hold values from -0.15625 to 0.15625
Outputs:
- mixed: bfloat16 [2048, 3584], P(('groups', 'expert', 'context')), parts along dimension 0
There are 2 independent parts, one for each index of `groups`. A program takes and returns all parts, laid end to end along the dimension named above; an argument that names none is the same for every part. Nothing has to cross between parts.
Inputs may be any that keep to these rules, and one draw needn't show every extreme that they name: In each aligned block of 128 rows (the tokens of one pair of context devices) no id is named by more than 80 routes, and in some block some id is named by exactly 80. Ids of 2 and above are zero experts.
All inputs are finite; a program needn't handle non-finite values.
Results may differ from a plain program's by a relative error of at most 0.0058.
Values may be sent and summed in bfloat16 or wider, within the bound.
No kernel may reach another device: no remote copies, remote signals or barrier semaphores. Data moves between devices by JAX's collectives and lax.ppermute only.
A program may use at most 64 MiB of HBM per device.

v0:
```python
import jax
import jax.numpy as jnp
from jax import lax
from jax.sharding import PartitionSpec as P

SHARERS = 4


def slab_output(received, w_gate, w_up, w_down):
    rows = received.reshape(-1, received.shape[2])
    dims = (((1,), (1,)), ((), ()))
    gate = lax.dot_general(rows, w_gate[0], dims, preferred_element_type=jnp.float32)
    up = lax.dot_general(rows, w_up[0], dims, preferred_element_type=jnp.float32)
    hidden = (jax.nn.silu(gate) * up).astype(jnp.bfloat16)
    partial_out = jnp.dot(hidden, w_down[0], preferred_element_type=jnp.float32).astype(
        jnp.bfloat16
    )
    return lax.all_to_all(
        partial_out.reshape(received.shape), "expert", split_axis=0, concat_axis=0, tiled=True
    )


def per_device(tokens, routes, route_weight, w_gate, w_up, w_down):
    tok = tokens.shape[0]
    top = routes.shape[1]
    width = tokens.shape[1]
    sharers = SHARERS
    experts = lax.axis_size("expert") // sharers
    route_count = max(5 * experts, 2 * top)
    capacity = max(2, 5 * tok * top // (2 * route_count))
    slots = experts * capacity
    pair_routes = lax.all_gather(routes, "context", axis=0, tiled=True)
    flat = pair_routes.reshape(-1)
    onehot = (flat[:, None] == jnp.arange(experts, dtype=jnp.int32)[None, :]).astype(jnp.int32)
    earlier = jnp.cumsum(onehot, axis=0) - onehot
    slot = jnp.sum(earlier * onehot, axis=1)
    real = flat < experts
    cell = jnp.where(real, flat * capacity + slot, slots)
    match = (
        cell.reshape(2 * tok, top)[None, :, :] == jnp.arange(slots, dtype=jnp.int32)[:, None, None]
    )
    picker = jnp.sum(match.astype(jnp.float32), axis=2).astype(jnp.bfloat16)
    pair_tokens = lax.all_gather(tokens, "context", axis=0, tiled=True)
    packed = jnp.dot(picker, pair_tokens, preferred_element_type=jnp.float32).astype(jnp.bfloat16)
    outgoing = jnp.broadcast_to(
        packed.reshape(experts, 1, capacity, width), (experts, sharers, capacity, width)
    )
    outgoing = outgoing.reshape(experts * sharers, capacity, width)
    returned = slab_output(
        lax.all_to_all(outgoing, "expert", split_axis=0, concat_axis=0, tiled=True),
        w_gate,
        w_up,
        w_down,
    )
    slab_sums = jnp.sum(
        returned.astype(jnp.float32).reshape(experts, sharers, capacity, width), axis=1
    ).reshape(slots, width)
    pair_weight = lax.all_gather(route_weight, "context", axis=0, tiled=True)
    pair_cell = cell.reshape(2 * tok, top)
    pair_match = (
        pair_cell[:, :, None] == jnp.arange(slots, dtype=jnp.int32)[None, None, :]
    ).astype(jnp.float32)
    pair_mixing = jnp.sum(pair_match * pair_weight[:, :, None], axis=1)
    mixed = lax.psum_scatter(
        jnp.dot(
            pair_mixing,
            slab_sums,
            precision=lax.Precision.HIGHEST,
            preferred_element_type=jnp.float32,
        ),
        "context",
        scatter_dimension=0,
        tiled=True,
    )
    return mixed.astype(jnp.bfloat16)


def solution(mesh):
    return jax.shard_map(
        per_device,
        mesh=mesh,
        in_specs=(
            P(("groups", "expert", "context"), None),
            P(("groups", "expert", "context"), None),
            P(("groups", "expert", "context"), None),
            P("expert", "context", None),
            P("expert", "context", None),
            P("expert", "context", None),
        ),
        out_specs=P(("groups", "expert", "context"), None),
        check_vma=False,
    )
```

profile of v0, /device:TPU:0, one launch (start us, length us, event | category | flops | bytes accessed | tf_op | source)
XLA Modules:
  0.0 264.2 jit_solution(15099665242981891155)
XLA Ops:
  6.5 0.0 copy-start
  6.5 2.2 all-gather
  8.7 0.1 copy.27
  8.8 0.1 eq.55
  8.9 0.1 eq.51
  9.1 0.6 reduce-window.6
  9.6 0.2 slice_reduce_fusion
  9.9 0.2 reduce-window.9
  10.0 0.1 add_bitcast_fusion
  10.2 0.1 reduce_sum.39
  10.3 0.1 reshape.73
  10.4 0.1 reshape.71
  10.5 0.2 convert_reduce_fusion.1
  10.7 2.7 %all_gather.11 = bf16[128,3584]{1,0:T(8,128)(2,1)S(1)} all-gather(bf16[64,3584]{1,0:T(8,128)(2,1)} %param.6), channel_id=1, replica_groups=mesh['groups'=2,'expert'=8,'context'=2] {'context'}, dimensions={0}, use_global_device_ids=true | all-gather | bytes 1376256 | tf_op jit(solution)/shard_map/all_gather | solution.py:43
  13.4 0.4 convolution_convert_fusion.1
  13.8 0.4 broadcast_in_dim.17
  14.2 0.0 copy-start.3
  14.2 109.3 %all_to_all.10 = bf16[8,80,3584]{2,1,0:T(8,128)(2,1)S(1)} all-to-all(bf16[8,80,3584]{2,1,0:T(8,128)(2,1)S(1)} %bitcast.51), channel_id=1, replica_groups=mesh['groups'=2,'expert'=8,'context'=2] {'expert'}, dimensions={0} | all-to-all | bytes 9175040 | tf_op jit(solution)/shard_map/all_to_all | solution.py:50
  123.6 2.1 copy-done.1
  125.7 1.6 fusion.4
  127.3 7.9 %convolution_convert_fusion = bf16[640,3584]{1,0:T(8,128)(2,1)} fusion(bf16[640,3584]{1,0:T(8,128)(2,1)} %bitcast.55, bf16[1,160,3584]{2,1,0:T(8,128)(2,1)S(1)} %copy-done, bf16[1,160,3584]{2,1,0:T(8,128)(2,1)S(1)} %copy-done.4, f32[640,160]{0,1:T(8,128)S(1)} %fusion.4), kind=kOutput, calls=%fused_computation.1 | convolution fusion | flops 1470914560 | bytes 11878400 | tf_op jit(solution)/shard_map/dot_general | solution.py:15
  135.2 4.7 %all-to-all-start.1 = ((bf16[8,80,3584]{2,1,0:T(8,128)(2,1)}), bf16[8,80,3584]{2,1,0:T(8,128)(2,1)}, u32[]{:S(2)}, u32[]{:S(2)}) async-start(bf16[8,80,3584]{2,1,0:T(8,128)(2,1)} %bitcast.53), calls=%async_computation.1 | async-start | bytes 9175040 | tf_op jit(solution)/shard_map/all_to_all | solution.py:18
  140.0 0.0 reduce-scatter.2.cloned.1.call-start
  140.0 1.8 all-gather.1
  141.8 0.1 reshape.67
  141.9 0.1 select_reduce_fusion
  142.0 98.4 %all-to-all-done.1 = bf16[8,80,3584]{2,1,0:T(8,128)(2,1)} async-done(((bf16[8,80,3584]{2,1,0:T(8,128)(2,1)}), bf16[8,80,3584]{2,1,0:T(8,128)(2,1)}, u32[]{:S(2)}, u32[]{:S(2)}) %all-to-all-start.1) | async-done | bytes 4587552 | tf_op jit(solution)/shard_map/all_to_all | solution.py:18
  240.4 3.3 %convert_reduce_fusion = f32[2,80,3584]{2,1,0:T(8,128)S(1)} fusion(bf16[8,80,3584]{2,1,0:T(8,128)(2,1)} %all-to-all-done.1), kind=kLoop, calls=%fused_computation | loop fusion | flops 4014080 | bytes 6881280 | tf_op jit(solution)/shard_map/reduce_sum | solution.py:55
  243.7 3.1 %fusion.18 = f32[128,3584]{1,0:T(8,128)} fusion(f32[128,160]{0,1:T(8,128)S(1)} %select_reduce_fusion, f32[160,3584]{1,0:T(8,128)S(1)} %bitcast.52), kind=kOutput, calls=%fused_computation.32 | convolution fusion | flops 880803840 | bytes 4210688 | tf_op jit(solution)/shard_map/dot_general | solution.py:65
  246.8 0.0 reduce-scatter.2.cloned.1.call-update
  246.8 8.6 %reduce-scatter.2.cloned.1.call-done = f32[64,3584]{1,0:T(8,128)} async-done(((f32[128,3584]{1,0:T(8,128)}), f32[64,3584]{1,0:T(8,128)}) %reduce-scatter.2.cloned.1.call-update) | async-done | bytes 917520 | tf_op jit(solution)/shard_map/reduce_scatter | solution.py:64
  255.4 2.0 convert_element_type.34
  (16 shorter events, 0.1 us)
Async XLA Ops:
  6.5 120.8 %copy-start = (bf16[1,160,3584]{2,1,0:T(8,128)(2,1)S(1)}, bf16[1,160,3584]{2,1,0:T(8,128)(2,1)}, u32[]{:S(2)}) copy-start(bf16[1,160,3584]{2,1,0:T(8,128)(2,1)} %param.11) | copy-start | bytes 3440644
  14.2 111.5 %copy-start.3 = (bf16[1,160,3584]{2,1,0:T(8,128)(2,1)S(1)}, bf16[1,160,3584]{2,1,0:T(8,128)(2,1)}, u32[]{:S(2)}) copy-start(bf16[1,160,3584]{2,1,0:T(8,128)(2,1)} %param.9) | copy-start | bytes 3440644
  123.6 2.1 copy-start.1
  125.7 1.6 copy-start.4
  135.2 4.8 %copy-start.2 = (f32[64,8]{0,1:T(8,128)S(1)}, f32[64,8]{0,1:T(8,128)}, u32[]{:S(2)}) copy-start(f32[64,8]{0,1:T(8,128)} %param.8) | copy-start | bytes 6148
  135.2 105.2 %all-to-all-start.1 = ((bf16[8,80,3584]{2,1,0:T(8,128)(2,1)}), bf16[8,80,3584]{2,1,0:T(8,128)(2,1)}, u32[]{:S(2)}, u32[]{:S(2)}) async-start(bf16[8,80,3584]{2,1,0:T(8,128)(2,1)} %bitcast.53), calls=%async_computation.1 | async-start | bytes 9175040 | tf_op jit(solution)/shard_map/all_to_all | solution.py:18
  140.0 115.4 %reduce-scatter.2.cloned.1.call-start = ((), (), s32[]{:S(2)}) async-start(), calls=%async_computation.3 | async-start | bytes 2752512 | tf_op jit(solution)/shard_map/reduce_scatter | solution.py:64
Sparse Core Ops, SparseCore 0:
  246.9 8.4 reduce-scatter.1
where the time goes:
time: 265 us; the launch traced here: 264 us
  blocking collectives  116 us (44%)
  waiting for transfers between devices  107 us (40%)
  between operations  13.5 us (5%)
  matrix products  13 us (5%)
  other arithmetic  6.46 us (2%)
  starting transfers between devices  4.76 us (2%)
  local copies, waits for them, and re-layouts  3.44 us (1%)
    all_to_all x1, blocking collectives, per_device(): lax.all_to_all(outgoing, 'expert', split_axis=0, concat_axis=0, tiled=True)  109 us
    all_to_all x1, waiting for transfers between devices, slab_output(): lax.all_to_all(partial_out.reshape(received.shape), 'expert', split_axis=...  98.4 us
    reduce_scatter x1, waiting for transfers between devices, per_device(): lax.psum_scatter(jnp.dot(pair_mixing, slab_sums, precision=lax.Precision....  8.58 us
    dot_general x1, matrix products, slab_output(): jnp.dot(hidden, w_down[0], preferred_element_type=jnp.float32)  7.9 us
  transfers between devices with their start and end apart: 2, of which 2 were waited for; matrix products, arithmetic and copies ran while one was open for 0% of the time, Pallas kernels for 0%

commit v1 on v0

v1 whole, which is shorter than its diff:
```python
import jax
import jax.numpy as jnp
from jax import lax
from jax.sharding import Mesh
from jax.sharding import PartitionSpec as P

SHARERS = 4
RETURN_DTYPE = jnp.float32


def expert_rows(rows, w_gate, w_up, w_down):
    dims = (((1,), (1,)), ((), ()))
    gate = lax.dot_general(rows, w_gate[0], dims, preferred_element_type=jnp.float32)
    up = lax.dot_general(rows, w_up[0], dims, preferred_element_type=jnp.float32)
    hidden = (jax.nn.silu(gate) * up).astype(jnp.bfloat16)
    return jnp.dot(hidden, w_down[0], preferred_element_type=jnp.float32).astype(jnp.bfloat16)


def per_device(tokens, routes, route_weight, w_gate, w_up, w_down):
    tok = tokens.shape[0]
    top = routes.shape[1]
    width = tokens.shape[1]
    experts = lax.axis_size("ex")
    sharers = lax.axis_size("sh")
    n_ctx = lax.axis_size("context")
    route_count = max(5 * experts, 2 * top)
    capacity = max(2, 5 * tok * top // (2 * route_count))
    half = -(-capacity // n_ctx)
    span = n_ctx * half
    ctx = lax.axis_index("context")

    pair_routes = lax.all_gather(routes, "context", axis=0, tiled=True)
    flat = pair_routes.reshape(-1)
    onehot = (flat[:, None] == jnp.arange(experts, dtype=jnp.int32)[None, :]).astype(jnp.int32)
    earlier = jnp.cumsum(onehot, axis=0) - onehot
    slot = jnp.sum(earlier * onehot, axis=1)
    real = flat < experts
    cell = jnp.where(real, flat * span + slot, experts * span)
    pair_cell = cell.reshape(n_ctx * tok, top)

    own_cells = (
        jnp.arange(experts, dtype=jnp.int32)[:, None] * span
        + ctx * half
        + jnp.arange(half, dtype=jnp.int32)[None, :]
    ).reshape(-1)
    match = pair_cell[None, :, :] == own_cells[:, None, None]
    picker = jnp.sum(match.astype(jnp.float32), axis=2).astype(jnp.bfloat16)
    pair_tokens = lax.all_gather(tokens, "context", axis=0, tiled=True)
    packed = jnp.dot(picker, pair_tokens, preferred_element_type=jnp.float32).astype(jnp.bfloat16)
    packed = packed.reshape(experts, half, width)

    sent = lax.all_to_all(packed, "ex", split_axis=0, concat_axis=0, tiled=True)
    group_rows = lax.all_gather(sent, "sh", axis=0, tiled=False)
    all_rows = lax.all_gather(group_rows, "context", axis=0, tiled=False)
    partial = expert_rows(all_rows.reshape(-1, width), w_gate, w_up, w_down)
    partial = partial.reshape(n_ctx, sharers, experts, half, width)

    chip_parts = lax.all_to_all(partial, "context", split_axis=0, concat_axis=0, tiled=True)
    chip_sum = jnp.sum(chip_parts.astype(jnp.float32), axis=0).astype(jnp.bfloat16)
    group_parts = lax.all_to_all(chip_sum, "sh", split_axis=0, concat_axis=0, tiled=True)
    expert_out = jnp.sum(group_parts.astype(jnp.float32), axis=0).astype(RETURN_DTYPE)
    back = lax.all_to_all(expert_out, "ex", split_axis=0, concat_axis=0, tiled=True)
    slots_out = lax.all_gather(back, "context", axis=0, tiled=False).astype(jnp.float32)
    slots_out = slots_out.reshape(n_ctx * experts * half, width)

    own_cell = lax.dynamic_slice_in_dim(pair_cell, ctx * tok, tok, axis=0)
    expert_of = own_cell // span
    slot_of = own_cell % span
    layout = (slot_of // half) * (experts * half) + expert_of * half + slot_of % half
    layout = jnp.where(own_cell < experts * span, layout, n_ctx * experts * half)
    own_match = (
        layout[:, :, None] == jnp.arange(n_ctx * experts * half, dtype=jnp.int32)[None, None, :]
    ).astype(jnp.float32)
    mixing = jnp.sum(own_match * route_weight[:, :, None], axis=1)
    mixed = jnp.dot(
        mixing, slots_out, precision=lax.Precision.HIGHEST, preferred_element_type=jnp.float32
    )
    return mixed.astype(jnp.bfloat16)


def solution(mesh):
    groups, n_expert, n_ctx = mesh.devices.shape
    split = Mesh(
        mesh.devices.reshape(groups, n_expert // SHARERS, SHARERS, n_ctx),
        ("groups", "ex", "sh", "context"),
    )
    rows = P(("groups", "ex", "sh", "context"), None)
    slabs = P(("ex", "sh"), "context", None)
    return jax.shard_map(
        per_device,
        mesh=split,
        in_specs=(rows, rows, rows, slabs, slabs, slabs),
        out_specs=rows,
        check_vma=False,
    )
```

time: 265 us -> 207 us (0.78)
  waiting for transfers between devices: 107 us -> 70.2 us
  blocking collectives: 116 us -> 100 us
  starting transfers between devices: 4.76 us -> 0.08 us
  matrix products: 13 us -> 16.8 us
    all_to_all x1 -> x0, waiting for transfers between devices: 98.4 us -> none  [slab_output(): lax.all_to_all(partial_out.reshape(received.shape), 'expert', split_axis=...]
    all_gather x0 -> x3, waiting for transfers between devices: none -> 70.2 us  [the longest x1 46.4 us: per_device(): group_rows = lax.all_gather(sent, 'sh', axis=0, tiled=False)]
    all_to_all x1 -> x4, blocking collectives: 109 us -> 95.5 us  [the longest x1 31.7 us: per_device(): lax.all_to_all(chip_sum, 'sh', split_axis=0, concat_axis=0, tiled=True)]
    reduce_scatter x1 -> x0, waiting for transfers between devices: 8.58 us -> none  [per_device(): lax.psum_scatter(jnp.dot(pair_mixing, slab_sums, precision=lax.Precision....]
    all_to_all x1 -> x0, starting transfers between devices: 4.72 us -> none  [slab_output(): lax.all_to_all(partial_out.reshape(received.shape), 'expert', split_axis=...]
    dot_general x3, matrix products: 12.6 us -> 16.5 us  [the longest x1 8.06 us: expert_rows(): jnp.dot(hidden, w_down[0], preferred_element_type=jnp.float32)]
  transfers between devices with their start and end apart: 2 -> 3, of which waited for: 2 -> 3; matrix products, arithmetic and copies ran while one was open for 0% -> 0% of each run, Pallas kernels for 0% -> 0%
where the time goes in v1:
time: 207 us
  blocking collectives  100 us (48%)
  waiting for transfers between devices  70.2 us (34%)
  matrix products  16.8 us (8%)
  between operations  13.2 us (6%)
  other arithmetic  5.14 us (2%)
    all_gather x1, waiting for transfers between devices, per_device(): group_rows = lax.all_gather(sent, 'sh', axis=0, tiled=False)  46.4 us
    all_to_all x1, blocking collectives, per_device(): lax.all_to_all(chip_sum, 'sh', split_axis=0, concat_axis=0, tiled=True)  31.7 us
    all_to_all x1, blocking collectives, per_device(): lax.all_to_all(expert_out, 'ex', split_axis=0, concat_axis=0, tiled=True)  30.2 us
    all_to_all x1, blocking collectives, per_device(): sent = lax.all_to_all(packed, 'ex', split_axis=0, concat_axis=0, tiled=True)  21.1 us
    all_gather x1, waiting for transfers between devices, per_device(): all_rows = lax.all_gather(group_rows, 'context', axis=0, tiled=False)  15.4 us
    all_to_all x1, blocking collectives, per_device(): lax.all_to_all(partial, 'context', split_axis=0, concat_axis=0, tiled=True)  12.6 us
    all_gather x1, waiting for transfers between devices, per_device(): lax.all_gather(back, 'context', axis=0, tiled=False).astype(jnp.float32)  8.36 us
    dot_general x1, matrix products, expert_rows(): jnp.dot(hidden, w_down[0], preferred_element_type=jnp.float32)  8.06 us
  transfers between devices with their start and end apart: 3, of which 3 were waited for; matrix products, arithmetic and copies ran while one was open for 0% of the time, Pallas kernels for 0%

profile of v1, /device:TPU:0, one launch (start us, length us, event | category | flops | bytes accessed | tf_op | source)
XLA Modules:
  0.0 207.0 jit_solution(2873672168269930810)
XLA Ops:
  6.5 2.2 %all-gather.3 = s32[2,64,8]{1,2,0:T(8,128)S(1)} all-gather(s32[1,64,8]{1,2,0:T(8,128)} %bitcast.49), channel_id=1, replica_groups=mesh['groups'=2,'ex'=2,'sh'=4,'context'=2] {'context'}, dimensions={0}, use_global_device_ids=true | all-gather | bytes 6144 | tf_op jit(solution)/shard_map/all_gather | solution.py:32
  8.7 0.1 copy.26
  8.8 0.1 eq.58
  8.9 0.1 eq.54
  9.1 0.6 reduce-window.6
  9.7 0.2 slice_reduce_fusion
  9.9 0.2 reduce-window.9
  10.0 0.1 add_bitcast_fusion
  10.2 0.1 reduce_sum.51
  10.3 0.1 reshape.80
  10.4 0.1 reshape.78
  10.5 0.1 iota_add_fusion
  10.6 0.1 add.73
  10.7 2.7 %all_gather.25 = bf16[128,3584]{1,0:T(8,128)(2,1)S(1)} all-gather(bf16[64,3584]{1,0:T(8,128)(2,1)} %param.6), channel_id=1, replica_groups=mesh['groups'=2,'ex'=2,'sh'=4,'context'=2] {'context'}, dimensions={0}, use_global_device_ids=true | all-gather | bytes 1376256 | tf_op jit(solution)/shard_map/all_gather | solution.py:48
  13.3 0.2 convert_reduce_fusion.1
  13.5 0.3 convolution_convert_fusion.1
  13.8 21.1 %all_to_all.20 = bf16[2,40,3584]{2,1,0:T(8,128)(2,1)} all-to-all(bf16[2,40,3584]{2,1,0:T(8,128)(2,1)S(1)} %bitcast.48), channel_id=1, replica_groups=mesh['groups'=2,'ex'=2,'sh'=4,'context'=2] {'ex'}, dimensions={0} | all-to-all | bytes 1146880 | tf_op jit(solution)/shard_map/all_to_all | solution.py:52
  35.0 46.4 %all-gather.8.cloned.1.call-done = bf16[8,40,3584]{2,1,0:T(8,128)(2,1)} async-done(((bf16[2,40,3584]{2,1,0:T(8,128)(2,1)}), bf16[8,40,3584]{2,1,0:T(8,128)(2,1)}) %all-gather.8.cloned.1.call-update) | async-done | bytes 2293776 | tf_op jit(solution)/shard_map/all_gather | solution.py:53
  81.5 15.4 %all-gather.10.cloned.1.call-done = bf16[8,2,40,3584]{3,2,1,0:T(8,128)(2,1)} async-done(((bf16[4,2,40,3584]{3,2,1,0:T(8,128)(2,1)}), bf16[8,2,40,3584]{3,2,1,0:T(8,128)(2,1)}) %all-gather.10.cloned.1.call-update) | async-done | bytes 4587536 | tf_op jit(solution)/shard_map/all_gather | solution.py:54
  96.9 4.7 %fusion.4 = f32[640,160]{0,1:T(8,128)} fusion(bf16[640,3584]{1,0:T(8,128)(2,1)} %bitcast.51, bf16[1,160,3584]{2,1,0:T(8,128)(2,1)S(1)} %copy-done.2), kind=kOutput, calls=%fused_computation.8 | convolution fusion | flops 734003200 | bytes 6144000 | tf_op jit(solution)/shard_map/dot_general | solution.py:13
  101.7 8.1 %convolution_convert_fusion = bf16[640,3584]{1,0:T(8,128)(2,1)} fusion(bf16[640,3584]{1,0:T(8,128)(2,1)} %bitcast.52, bf16[1,160,3584]{2,1,0:T(8,128)(2,1)S(1)} %copy-done, bf16[1,160,3584]{2,1,0:T(8,128)(2,1)S(1)} %copy-done.3, f32[640,160]{0,1:T(8,128)} %fusion.4), kind=kOutput, calls=%fused_computation | convolution fusion | flops 1470914560 | bytes 11878400 | tf_op jit(solution)/shard_map/dot_general | solution.py:16
  109.7 12.6 %all_to_all.21 = bf16[2,4,2,40,3584]{4,3,2,1,0:T(8,128)(2,1)} all-to-all(bf16[2,4,2,40,3584]{4,3,2,1,0:T(8,128)(2,1)} %bitcast.45), channel_id=1, replica_groups=mesh['groups'=2,'ex'=2,'sh'=4,'context'=2] {'context'}, dimensions={0} | all-to-all | bytes 9175040 | tf_op jit(solution)/shard_map/all_to_all | solution.py:58
  122.3 3.3 %reduce_sum.54 = bf16[4,2,40,3584]{3,2,1,0:T(8,128)(2,1)S(1)} reduce(bf16[2,4,2,40,3584]{4,3,2,1,0:T(8,128)(2,1)} %all_to_all.21, bf16[]{:T(256)} %constant.61.clone.1), dimensions={0}, to_apply=%region_5.6 | reduce | flops 1146880 | bytes 6881282 | tf_op jit(solution)/shard_map/reduce_sum | solution.py:59
  125.6 31.7 %all_to_all.22 = bf16[4,2,40,3584]{3,2,1,0:T(8,128)(2,1)S(1)} all-to-all(bf16[4,2,40,3584]{3,2,1,0:T(8,128)(2,1)S(1)} %reduce_sum.54), channel_id=1, replica_groups=mesh['groups'=2,'ex'=2,'sh'=4,'context'=2] {'sh'}, dimensions={0} | all-to-all | bytes 4587520 | tf_op jit(solution)/shard_map/all_to_all | solution.py:60
  157.3 0.3 convert_reduce_fusion
  157.7 30.2 %all_to_all.23 = f32[2,40,3584]{2,1,0:T(8,128)} all-to-all(f32[2,40,3584]{2,1,0:T(8,128)S(1)} %convert_reduce_fusion), channel_id=1, replica_groups=mesh['groups'=2,'ex'=2,'sh'=4,'context'=2] {'ex'}, dimensions={0} | all-to-all | bytes 2293760 | tf_op jit(solution)/shard_map/all_to_all | solution.py:62
  187.9 0.1 fusion.20
  188.0 0.1 copy.29
  188.1 0.1 copy.30
  188.1 0.2 select_reduce_fusion
  188.4 8.4 %all-gather.12.cloned.1.call-done = f32[4,40,3584]{2,1,0:T(8,128)} async-done(((f32[2,40,3584]{2,1,0:T(8,128)}), f32[4,40,3584]{2,1,0:T(8,128)}) %all-gather.12.cloned.1.call-update) | async-done | bytes 2293776 | tf_op jit(solution)/shard_map/all_gather | solution.py:63
  196.7 3.7 %convolution_convert_fusion.2 = bf16[64,3584]{1,0:T(8,128)(2,1)} fusion(f32[64,160]{1,0:T(8,128)S(1)} %select_reduce_fusion, f32[160,3584]{1,0:T(8,128)} %bitcast.46), kind=kOutput, calls=%fused_computation.2 | convolution fusion | flops 440631296 | bytes 2793472 | tf_op jit(solution)/shard_map/dot_general | solution.py:75
  (23 shorter events, 0.3 us)
Async XLA Ops:
  6.5 95.1 %copy-start = (bf16[1,160,3584]{2,1,0:T(8,128)(2,1)S(1)}, bf16[1,160,3584]{2,1,0:T(8,128)(2,1)}, u32[]{:S(2)}) copy-start(bf16[1,160,3584]{2,1,0:T(8,128)(2,1)} %param.11) | copy-start | bytes 3440644
  6.5 74.9 %all-gather.8.cloned.1.call-start = ((), (), s32[]{:S(2)}) async-start(), calls=%async_computation.4 | async-start | bytes 2867200 | tf_op jit(solution)/shard_map/all_gather | solution.py:53
  13.8 83.1 %copy-start.2 = (bf16[1,160,3584]{2,1,0:T(8,128)(2,1)S(1)}, bf16[1,160,3584]{2,1,0:T(8,128)(2,1)}, u32[]{:S(2)}) copy-start(bf16[1,160,3584]{2,1,0:T(8,128)(2,1)} %param.9) | copy-start | bytes 3440644
  35.0 61.9 %all-gather.10.cloned.1.call-start = ((), (), s32[]{:S(2)}) async-start(), calls=%async_computation.5 | async-start | bytes 6881280 | tf_op jit(solution)/shard_map/all_gather | solution.py:54
  81.4 115.3 %all-gather.12.cloned.1.call-start = ((), (), s32[]{:S(2)}) async-start(), calls=%async_computation.6 | async-start | bytes 3440640 | tf_op jit(solution)/shard_map/all_gather | solution.py:63
  96.9 4.7 %copy-start.3 = (bf16[1,160,3584]{2,1,0:T(8,128)(2,1)S(1)}, bf16[1,160,3584]{2,1,0:T(8,128)(2,1)}, u32[]{:S(2)}) copy-start(bf16[1,160,3584]{2,1,0:T(8,128)(2,1)} %param.10) | copy-start | bytes 3440644
  157.6 30.4 %copy-start.1 = (f32[64,8]{0,1:T(8,128)S(1)}, f32[64,8]{0,1:T(8,128)}, u32[]{:S(2)}) copy-start(f32[64,8]{0,1:T(8,128)} %param.8) | copy-start | bytes 6148
Sparse Core Ops, SparseCore 0:
  35.1 46.2 all-gather.7
  82.9 13.9 all-gather.9
  188.0 8.7 all-gather.11

commit v2 on v1

v2 whole, which is shorter than its diff:
```python
import jax
import jax.numpy as jnp
from jax import lax
from jax.sharding import Mesh
from jax.sharding import PartitionSpec as P

SHARERS = 4
RETURN_DTYPE = jnp.bfloat16


def shift(x, axis, size, k):
    return lax.ppermute(x, axis, [(i, (i + k) % size) for i in range(size)])


def quarter_rows(rows, w_gate, w_up, w_down, n_ctx):
    dims = (((1,), (1,)), ((), ()))
    gate = lax.dot_general(rows, w_gate, dims, preferred_element_type=jnp.float32)
    up = lax.dot_general(rows, w_up, dims, preferred_element_type=jnp.float32)
    hidden = (jax.nn.silu(gate) * up).astype(jnp.bfloat16)
    slab = w_down.shape[0] // n_ctx
    total = None
    for c in range(n_ctx):
        part = jnp.dot(
            hidden[:, c * slab : (c + 1) * slab],
            w_down[c * slab : (c + 1) * slab],
            preferred_element_type=jnp.float32,
        ).astype(jnp.bfloat16)
        total = part.astype(jnp.float32) if total is None else total + part.astype(jnp.float32)
    return total


def per_device(tokens, routes, route_weight, w_gate, w_up, w_down):
    tok = tokens.shape[0]
    top = routes.shape[1]
    width = tokens.shape[1]
    experts = lax.axis_size("ex")
    sharers = lax.axis_size("sh")
    n_ctx = lax.axis_size("context")
    route_count = max(5 * experts, 2 * top)
    capacity = max(2, 5 * tok * top // (2 * route_count))
    half = -(-capacity // n_ctx)
    span = n_ctx * half
    ctx = lax.axis_index("context")
    me = lax.axis_index("ex")
    mine = lax.axis_index("sh")

    wg = lax.all_gather(w_gate[0], "context", axis=0, tiled=True)
    wu = lax.all_gather(w_up[0], "context", axis=0, tiled=True)
    wd = lax.all_gather(w_down[0], "context", axis=0, tiled=True)

    pair_routes = lax.all_gather(routes, "context", axis=0, tiled=True)
    flat = pair_routes.reshape(-1)
    onehot = (flat[:, None] == jnp.arange(experts, dtype=jnp.int32)[None, :]).astype(jnp.int32)
    earlier = jnp.cumsum(onehot, axis=0) - onehot
    slot = jnp.sum(earlier * onehot, axis=1)
    real = flat < experts
    cell = jnp.where(real, flat * span + slot, experts * span)
    pair_cell = cell.reshape(n_ctx * tok, top)

    if experts == 2:
        expert_order = jnp.stack([me, 1 - me])
    else:
        expert_order = jnp.arange(experts, dtype=jnp.int32)
    own_cells = (
        expert_order[:, None] * span + ctx * half + jnp.arange(half, dtype=jnp.int32)[None, :]
    ).reshape(-1)
    match = pair_cell[None, :, :] == own_cells[:, None, None]
    picker = jnp.sum(match.astype(jnp.float32), axis=2).astype(jnp.bfloat16)
    pair_tokens = lax.all_gather(tokens, "context", axis=0, tiled=True)
    packed = jnp.dot(picker, pair_tokens, preferred_element_type=jnp.float32).astype(jnp.bfloat16)
    packed = packed.reshape(experts, half, width)

    if experts == 2:
        sent = jnp.stack([packed[0], shift(packed[1], "ex", 2, 1)])
    else:
        sent = lax.all_to_all(packed, "ex", split_axis=0, concat_axis=0, tiled=True)
    group = [sent] + [shift(sent, "sh", sharers, k) for k in range(1, sharers)]
    rows = jnp.stack(group).reshape(-1, width)
    partial = quarter_rows(rows, wg, wu, wd, n_ctx).astype(jnp.bfloat16)
    partial = partial.reshape(sharers, experts, half, width)

    total = partial[0].astype(jnp.float32)
    for k in range(1, sharers):
        total = total + shift(partial[k], "sh", sharers, -k).astype(jnp.float32)
    expert_out = total.astype(RETURN_DTYPE)
    if experts == 2:
        back = jnp.stack([expert_out[0], shift(expert_out[1], "ex", 2, 1)])
    else:
        back = lax.all_to_all(expert_out, "ex", split_axis=0, concat_axis=0, tiled=True)
    slots_out = lax.all_gather(back, "context", axis=0, tiled=False).astype(jnp.float32)
    slots_out = slots_out.reshape(n_ctx * experts * half, width)

    own_cell = lax.dynamic_slice_in_dim(pair_cell, ctx * tok, tok, axis=0)
    expert_of = own_cell // span
    slot_of = own_cell % span
    if experts == 2:
        position = jnp.where(expert_of == me, 0, 1)
    else:
        position = expert_of
    layout = (slot_of // half) * (experts * half) + position * half + slot_of % half
    layout = jnp.where(own_cell < experts * span, layout, n_ctx * experts * half)
    own_match = (
        layout[:, :, None] == jnp.arange(n_ctx * experts * half, dtype=jnp.int32)[None, None, :]
    ).astype(jnp.float32)
    mixing = jnp.sum(own_match * route_weight[:, :, None], axis=1)
    mixed = jnp.dot(
        mixing, slots_out, precision=lax.Precision.HIGHEST, preferred_element_type=jnp.float32
    )
    return mixed.astype(jnp.bfloat16)


def solution(mesh):
    groups, n_expert, n_ctx = mesh.devices.shape
    split = Mesh(
        mesh.devices.reshape(groups, n_expert // SHARERS, SHARERS, n_ctx),
        ("groups", "ex", "sh", "context"),
    )
    rows = P(("groups", "ex", "sh", "context"), None)
    slabs = P(("ex", "sh"), "context", None)
    return jax.shard_map(
        per_device,
        mesh=split,
        in_specs=(rows, rows, rows, slabs, slabs, slabs),
        out_specs=rows,
        check_vma=False,
    )
```

time: 207 us -> 134 us (0.65)
  blocking collectives: 100 us -> 4.41 us
  waiting for transfers between devices: 70.2 us -> 86.5 us
  starting transfers between devices: 0.08 us -> 13.7 us
  matrix products: 16.8 us -> 11.9 us
    all_to_all x4 -> x0, blocking collectives: 95.5 us -> none  [the longest x1 31.7 us: per_device(): lax.all_to_all(chip_sum, 'sh', split_axis=0, concat_axis=0, tiled=True)]
    ppermute x0 -> x8, waiting for transfers between devices: none -> 74.7 us  [shift(): return lax.ppermute(x, axis, [(i, (i + k) % size) for i in range(size)])]
    all_gather x2 -> x3, waiting for transfers between devices: 61.8 us -> 0.06 us  [the longest x1 0.02 us: per_device(): wu = lax.all_gather(w_up[0], 'context', axis=0, tiled=True)]
    ppermute x0 -> x8, starting transfers between devices: none -> 13.6 us  [shift(): return lax.ppermute(x, axis, [(i, (i + k) % size) for i in range(size)])]
    dot_general x2 -> x4, matrix products: 12.8 us -> 8.99 us  [the longest x1 3.01 us: quarter_rows(): up = lax.dot_general(rows, w_up, dims, preferred_element_type=jnp.float32)]
    reduce_sum x2 -> x0, other arithmetic: 3.66 us -> none  [the longest x1 3.32 us: per_device(): jnp.sum(chip_parts.astype(jnp.float32), axis=0).astype(jnp.bfloat16)]
  transfers between devices with their start and end apart: 3 -> 12, of which waited for: 3 -> 9; matrix products, arithmetic and copies ran while one was open for 0% -> 7% of each run, Pallas kernels for 0% -> 0%
where the time goes in v2:
time: 134 us
  waiting for transfers between devices  86.5 us (65%)
  starting transfers between devices  13.7 us (10%)
  between operations  13.3 us (10%)
  matrix products  11.9 us (9%)
  blocking collectives  4.41 us (3%)
  other arithmetic  3.09 us (2%)
    ppermute x8, waiting for transfers between devices, shift(): return lax.ppermute(x, axis, [(i, (i + k) % size) for i in range(size)])  74.7 us
    ppermute x8, starting transfers between devices, shift(): return lax.ppermute(x, axis, [(i, (i + k) % size) for i in range(size)])  13.6 us
    all_gather x1, waiting for transfers between devices, per_device(): lax.all_gather(back, 'context', axis=0, tiled=False).astype(jnp.float32)  10.3 us
    dot_general x1, matrix products, quarter_rows(): up = lax.dot_general(rows, w_up, dims, preferred_element_type=jnp.float32)  3.01 us
    dot_general x1, matrix products, quarter_rows(): lax.dot_general(rows, w_gate, dims, preferred_element_type=jnp.float32)  3.01 us
    dot_general x2, matrix products, quarter_rows(): jnp.dot(hidden[:, c * slab:(c + 1) * slab], w_down[c * slab:(c + 1) * sla...  2.98 us
  transfers between devices with their start and end apart: 12, of which 9 were waited for; matrix products, arithmetic and copies ran while one was open for 7% of the time, Pallas kernels for 0%

profile of v2, /device:TPU:0, one launch (start us, length us, event | category | flops | bytes accessed | tf_op | source)
XLA Modules:
  0.0 134.3 jit_solution(6308120674154532983)
XLA Ops:
  6.5 0.7 all-gather.10.cloned.1.call-update
  7.3 0.7 all-gather.12.cloned.1.call-update
  8.1 1.9 %all-gather.4 = s32[2,64,8]{1,2,0:T(8,128)S(1)} all-gather(s32[1,64,8]{1,2,0:T(8,128)S(1)} %bitcast.76), channel_id=1, replica_groups=mesh['groups'=2,'ex'=2,'sh'=4,'context'=2] {'context'}, dimensions={0}, use_global_device_ids=true | all-gather | bytes 6144 | tf_op jit(solution)/shard_map/all_gather | solution.py:51
  10.3 0.6 reduce-window.6
  10.9 0.2 slice_reduce_fusion
  12.2 2.5 %all_gather.22 = bf16[128,3584]{1,0:T(8,128)(2,1)S(1)} all-gather(bf16[64,3584]{1,0:T(8,128)(2,1)S(1)} %copy-done.1), channel_id=1, replica_groups=mesh['groups'=2,'ex'=2,'sh'=4,'context'=2] {'context'}, dimensions={0}, use_global_device_ids=true | all-gather | bytes 1376256 | tf_op jit(solution)/shard_map/all_gather | solution.py:69
  14.7 0.3 convolution_convert_fusion.2
  15.0 4.0 %collective-permute-start = (bf16[40,3584]{1,0:T(8,128)(2,1)S(1)}, bf16[40,3584]{1,0:T(8,128)(2,1)S(1)}, u32[]{:S(2)}, u32[]{:S(2)}) collective-permute-start(bf16[40,3584]{1,0:T(8,128)(2,1)S(1)} %get-tuple-element.14), channel_id=1, source_target_pairs={{0,8},{8,0},{1,9},{9,1},{2,10},{10,2},{3,11},{11,3},{4,12},{12,4},... | collective-permute-start | bytes 860168 | tf_op jit(solution)/shard_map/ppermute | solution.py:12
  19.1 13.3 %collective-permute-done = bf16[40,3584]{1,0:T(8,128)(2,1)S(1)} collective-permute-done((bf16[40,3584]{1,0:T(8,128)(2,1)S(1)}, bf16[40,3584]{1,0:T(8,128)(2,1)S(1)}, u32[]{:S(2)}, u32[]{:S(2)}) %collective-permute-start) | collective-permute-done | bytes 286752 | tf_op jit(solution)/shard_map/ppermute | solution.py:12
  32.4 1.6 %collective-permute-start.1 = (bf16[2,40,3584]{2,1,0:T(8,128)(2,1)S(1)}, bf16[2,40,3584]{2,1,0:T(8,128)(2,1)S(1)}, u32[]{:S(2)}, u32[]{:S(2)}) collective-permute-start(bf16[2,40,3584]{2,1,0:T(8,128)(2,1)S(1)} %get-tuple-element.12), channel_id=1, source_target_pairs={{0,2},{2,4},{4,6},{6,0},{1,3},{3,5},{5,7},{7,1},{8,10},{10,12},{12... | collective-permute-start | bytes 1720328 | tf_op jit(solution)/shard_map/ppermute | solution.py:12
  34.0 0.7 collective-permute-start.2
  34.7 1.4 %collective-permute-start.3 = (bf16[2,40,3584]{2,1,0:T(8,128)(2,1)S(1)}, bf16[2,40,3584]{2,1,0:T(8,128)(2,1)S(1)}, u32[]{:S(2)}, u32[]{:S(2)}) collective-permute-start(bf16[2,40,3584]{2,1,0:T(8,128)(2,1)S(1)} %get-tuple-element.12), channel_id=1, source_target_pairs={{0,6},{2,0},{4,2},{6,4},{1,7},{3,1},{5,3},{7,5},{8,14},{10,8},{12,... | collective-permute-start | bytes 1720328 | tf_op jit(solution)/shard_map/ppermute | solution.py:12
  36.1 13.2 %collective-permute-done.1 = bf16[2,40,3584]{2,1,0:T(8,128)(2,1)S(1)} collective-permute-done((bf16[2,40,3584]{2,1,0:T(8,128)(2,1)S(1)}, bf16[2,40,3584]{2,1,0:T(8,128)(2,1)S(1)}, u32[]{:S(2)}, u32[]{:S(2)}) %collective-permute-start.1) | collective-permute-done | bytes 573472 | tf_op jit(solution)/shard_map/ppermute | solution.py:12
  49.3 0.6 collective-permute-done.2
  49.9 10.3 %collective-permute-done.3 = bf16[2,40,3584]{2,1,0:T(8,128)(2,1)S(1)} collective-permute-done((bf16[2,40,3584]{2,1,0:T(8,128)(2,1)S(1)}, bf16[2,40,3584]{2,1,0:T(8,128)(2,1)S(1)}, u32[]{:S(2)}, u32[]{:S(2)}) %collective-permute-start.3) | collective-permute-done | bytes 573472 | tf_op jit(solution)/shard_map/ppermute | solution.py:12
  60.2 0.3 pad_maximum_fusion
  60.6 3.0 %fusion.6 = f32[320,320]{0,1:T(8,128)S(1)} fusion(bf16[320,3584]{1,0:T(8,128)(2,1)S(1)} %bitcast.65, bf16[1,320,3584]{2,1,0:T(8,128)(2,1)} %all-gather.10.cloned.1.call-done), kind=kOutput, calls=%fused_computation.11 | convolution fusion | flops 734003200 | bytes 4997120 | tf_op jit(solution)/shard_map/dot_general | solution.py:17
  63.6 3.0 %multiply_convert_fusion = bf16[320,320]{0,1:T(8,128)(2,1)S(1)} fusion(f32[320,320]{0,1:T(8,128)S(1)} %fusion.6, bf16[320,3584]{1,0:T(8,128)(2,1)S(1)} %bitcast.66, bf16[1,320,3584]{2,1,0:T(8,128)(2,1)} %all-gather.12.cloned.1.call-done), kind=kOutput, calls=%fused_computation.23 | convolution fusion | flops 734617600 | bytes 5201920 | tf_op jit(solution)/shard_map/dot_general | solution.py:18
  66.7 2.2 %fusion.3 = f32[320,3584]{1,0:T(8,128)S(1)} fusion(bf16[1,320,3584]{2,1,0:T(8,128)(2,1)} %all-gather.14.cloned.1.call-done, bf16[320,320]{0,1:T(8,128)(2,1)S(1)} %multiply_convert_fusion), kind=kOutput, calls=%fused_computation.5 | convolution fusion | flops 369295360 | bytes 5857280 | tf_op jit(solution)/shard_map/dot_general | solution.py:23
  68.9 0.8 fusion.2
  69.8 2.3 %collective-permute-start.4 = (bf16[2,40,3584]{2,1,0:T(8,128)(2,1)S(1)}, bf16[2,40,3584]{2,1,0:T(8,128)(2,1)S(1)}, u32[]{:S(2)}, u32[]{:S(2)}) collective-permute-start(bf16[2,40,3584]{2,1,0:T(8,128)(2,1)S(1)} %bitcast.72), channel_id=1, source_target_pairs={{0,6},{2,0},{4,2},{6,4},{1,7},{3,1},{5,3},{7,5},{8,14},{10,8},{12,... | collective-permute-start | bytes 1720328 | tf_op jit(solution)/shard_map/ppermute | solution.py:12
  72.1 0.7 collective-permute-start.5
  73.0 12.7 %collective-permute-done.4 = bf16[2,40,3584]{2,1,0:T(8,128)(2,1)S(1)} collective-permute-done((bf16[2,40,3584]{2,1,0:T(8,128)(2,1)S(1)}, bf16[2,40,3584]{2,1,0:T(8,128)(2,1)S(1)}, u32[]{:S(2)}, u32[]{:S(2)}) %collective-permute-start.4) | collective-permute-done | bytes 573472 | tf_op jit(solution)/shard_map/ppermute | solution.py:12
  85.6 10.8 %collective-permute-done.5 = bf16[2,40,3584]{2,1,0:T(8,128)(2,1)S(1)} collective-permute-done((bf16[2,40,3584]{2,1,0:T(8,128)(2,1)S(1)}, bf16[2,40,3584]{2,1,0:T(8,128)(2,1)S(1)}, u32[]{:S(2)}, u32[]{:S(2)}) %collective-permute-start.5) | collective-permute-done | bytes 573472 | tf_op jit(solution)/shard_map/ppermute | solution.py:12
  96.4 1.8 %collective-permute-done.6 = bf16[2,40,3584]{2,1,0:T(8,128)(2,1)S(1)} collective-permute-done((bf16[2,40,3584]{2,1,0:T(8,128)(2,1)S(1)}, bf16[2,40,3584]{2,1,0:T(8,128)(2,1)S(1)}, u32[]{:S(2)}, u32[]{:S(2)}) %collective-permute-start.6) | collective-permute-done | bytes 573472 | tf_op jit(solution)/shard_map/ppermute | solution.py:12
  98.2 0.3 fusion.10
  98.6 2.8 %collective-permute-start.7 = (bf16[40,3584]{1,0:T(8,128)(2,1)S(1)}, bf16[40,3584]{1,0:T(8,128)(2,1)S(1)}, u32[]{:S(2)}, u32[]{:S(2)}) collective-permute-start(bf16[40,3584]{1,0:T(8,128)(2,1)S(1)} %get-tuple-element.10), channel_id=1, source_target_pairs={{0,8},{8,0},{1,9},{9,1},{2,10},{10,2},{3,11},{11,3},{4,12},{12,4},... | collective-permute-start | bytes 860168 | tf_op jit(solution)/shard_map/ppermute | solution.py:12
  101.4 12.0 %collective-permute-done.7 = bf16[40,3584]{1,0:T(8,128)(2,1)S(1)} collective-permute-done((bf16[40,3584]{1,0:T(8,128)(2,1)S(1)}, bf16[40,3584]{1,0:T(8,128)(2,1)S(1)}, u32[]{:S(2)}, u32[]{:S(2)}) %collective-permute-start.7) | collective-permute-done | bytes 286752 | tf_op jit(solution)/shard_map/ppermute | solution.py:12
  113.4 0.9 pad_maximum_fusion.2
  114.5 0.2 select_reduce_fusion
  114.8 10.3 %all-gather.16.cloned.1.call-done = bf16[4,40,3584]{2,1,0:T(8,128)(2,1)} async-done(((bf16[2,40,3584]{2,1,0:T(8,128)(2,1)}), bf16[4,40,3584]{2,1,0:T(8,128)(2,1)}) %all-gather.16.cloned.1.call-update) | async-done | bytes 1146896 | tf_op jit(solution)/shard_map/all_gather | solution.py:90
  125.1 2.6 %convolution_convert_fusion.3 = bf16[64,3584]{1,0:T(8,128)(2,1)} fusion(f32[64,160]{1,0:T(8,128)S(1)} %select_reduce_fusion, bf16[160,3584]{1,0:T(8,128)(2,1)} %bitcast.67), kind=kOutput, calls=%fused_computation.7 | convolution fusion | flops 440631296 | bytes 1646592 | tf_op jit(solution)/shard_map/dot_general | solution.py:106
  (45 shorter events, 2.3 us)
Async XLA Ops:
  6.5 1.5 %copy-start.2 = (s32[64,8]{0,1:T(8,128)S(1)}, s32[64,8]{0,1:T(8,128)}, u32[]{:S(2)}) copy-start(s32[64,8]{0,1:T(8,128)} %param.7) | copy-start | bytes 6148
  6.5 5.7 %copy-start.1 = (bf16[64,3584]{1,0:T(8,128)(2,1)S(1)}, bf16[64,3584]{1,0:T(8,128)(2,1)}, u32[]{:S(2)}) copy-start(bf16[64,3584]{1,0:T(8,128)(2,1)} %param.6) | copy-start | bytes 1376260
  6.5 54.0 %all-gather.10.cloned.1.call-start = ((), (), s32[]{:S(2)}) async-start(), calls=%async_computation | async-start | bytes 3440640 | tf_op jit(solution)/shard_map/all_gather | solution.py:47
  7.3 56.3 %all-gather.12.cloned.1.call-start = ((), (), s32[]{:S(2)}) async-start(), calls=%async_computation.1 | async-start | bytes 3440640 | tf_op jit(solution)/shard_map/all_gather | solution.py:48
  8.0 58.6 %all-gather.14.cloned.1.call-start = ((), (), s32[]{:S(2)}) async-start(), calls=%async_computation.2 | async-start | bytes 3440640 | tf_op jit(solution)/shard_map/all_gather | solution.py:49
  15.0 17.3 %collective-permute-start = (bf16[40,3584]{1,0:T(8,128)(2,1)S(1)}, bf16[40,3584]{1,0:T(8,128)(2,1)S(1)}, u32[]{:S(2)}, u32[]{:S(2)}) collective-permute-start(bf16[40,3584]{1,0:T(8,128)(2,1)S(1)} %get-tuple-element.14), channel_id=1, source_target_pairs={{0,8},{8,0},{1,9},{9,1},{2,10},{10,2},{3,11},{11,3},{4,12},{12,4},... | collective-permute-start | bytes 860168 | tf_op jit(solution)/shard_map/ppermute | solution.py:12
  19.0 106.1 %all-gather.16.cloned.1.call-start = ((), (), s32[]{:S(2)}) async-start(), calls=%async_computation.3 | async-start | bytes 1720320 | tf_op jit(solution)/shard_map/all_gather | solution.py:90
  32.4 16.9 %collective-permute-start.1 = (bf16[2,40,3584]{2,1,0:T(8,128)(2,1)S(1)}, bf16[2,40,3584]{2,1,0:T(8,128)(2,1)S(1)}, u32[]{:S(2)}, u32[]{:S(2)}) collective-permute-start(bf16[2,40,3584]{2,1,0:T(8,128)(2,1)S(1)} %get-tuple-element.12), channel_id=1, source_target_pairs={{0,2},{2,4},{4,6},{6,0},{1,3},{3,5},{5,7},{7,1},{8,10},{10,12},{12... | collective-permute-start | bytes 1720328 | tf_op jit(solution)/shard_map/ppermute | solution.py:12
  34.0 15.9 %collective-permute-start.2 = (bf16[2,40,3584]{2,1,0:T(8,128)(2,1)S(1)}, bf16[2,40,3584]{2,1,0:T(8,128)(2,1)S(1)}, u32[]{:S(2)}, u32[]{:S(2)}) collective-permute-start(bf16[2,40,3584]{2,1,0:T(8,128)(2,1)S(1)} %get-tuple-element.12), channel_id=1, source_target_pairs={{0,4},{2,6},{4,0},{6,2},{1,5},{3,7},{5,1},{7,3},{8,12},{10,14},{12... | collective-permute-start | bytes 1720328 | tf_op jit(solution)/shard_map/ppermute | solution.py:12
  34.7 25.6 %collective-permute-start.3 = (bf16[2,40,3584]{2,1,0:T(8,128)(2,1)S(1)}, bf16[2,40,3584]{2,1,0:T(8,128)(2,1)S(1)}, u32[]{:S(2)}, u32[]{:S(2)}) collective-permute-start(bf16[2,40,3584]{2,1,0:T(8,128)(2,1)S(1)} %get-tuple-element.12), channel_id=1, source_target_pairs={{0,6},{2,0},{4,2},{6,4},{1,7},{3,1},{5,3},{7,5},{8,14},{10,8},{12,... | collective-permute-start | bytes 1720328 | tf_op jit(solution)/shard_map/ppermute | solution.py:12
  66.7 2.2 %copy-start = (bf16[1,320,3584]{2,1,0:T(8,128)(2,1)S(1)}, bf16[1,320,3584]{2,1,0:T(8,128)(2,1)}, u32[]{:S(2)}) copy-start(bf16[1,320,3584]{2,1,0:T(8,128)(2,1)} %all-gather.14.cloned.1.call-done) | copy-start | bytes 6881284
  69.8 15.8 %collective-permute-start.4 = (bf16[2,40,3584]{2,1,0:T(8,128)(2,1)S(1)}, bf16[2,40,3584]{2,1,0:T(8,128)(2,1)S(1)}, u32[]{:S(2)}, u32[]{:S(2)}) collective-permute-start(bf16[2,40,3584]{2,1,0:T(8,128)(2,1)S(1)} %bitcast.72), channel_id=1, source_target_pairs={{0,6},{2,0},{4,2},{6,4},{1,7},{3,1},{5,3},{7,5},{8,14},{10,8},{12,... | collective-permute-start | bytes 1720328 | tf_op jit(solution)/shard_map/ppermute | solution.py:12
  72.1 24.3 %collective-permute-start.5 = (bf16[2,40,3584]{2,1,0:T(8,128)(2,1)S(1)}, bf16[2,40,3584]{2,1,0:T(8,128)(2,1)S(1)}, u32[]{:S(2)}, u32[]{:S(2)}) collective-permute-start(bf16[2,40,3584]{2,1,0:T(8,128)(2,1)S(1)} %bitcast.70), channel_id=1, source_target_pairs={{0,4},{2,6},{4,0},{6,2},{1,5},{3,7},{5,1},{7,3},{8,12},{10,14},{12... | collective-permute-start | bytes 1720328 | tf_op jit(solution)/shard_map/ppermute | solution.py:12
  72.8 25.4 %collective-permute-start.6 = (bf16[2,40,3584]{2,1,0:T(8,128)(2,1)S(1)}, bf16[2,40,3584]{2,1,0:T(8,128)(2,1)S(1)}, u32[]{:S(2)}, u32[]{:S(2)}) collective-permute-start(bf16[2,40,3584]{2,1,0:T(8,128)(2,1)S(1)} %bitcast.68), channel_id=1, source_target_pairs={{0,2},{2,4},{4,6},{6,0},{1,3},{3,5},{5,7},{7,1},{8,10},{10,12},{12... | collective-permute-start | bytes 1720328 | tf_op jit(solution)/shard_map/ppermute | solution.py:12
  98.2 16.2 %copy-start.3 = (f32[64,8]{0,1:T(8,128)S(1)}, f32[64,8]{0,1:T(8,128)}, u32[]{:S(2)}) copy-start(f32[64,8]{0,1:T(8,128)} %param.8) | copy-start | bytes 6148
  98.6 14.8 %collective-permute-start.7 = (bf16[40,3584]{1,0:T(8,128)(2,1)S(1)}, bf16[40,3584]{1,0:T(8,128)(2,1)S(1)}, u32[]{:S(2)}, u32[]{:S(2)}) collective-permute-start(bf16[40,3584]{1,0:T(8,128)(2,1)S(1)} %get-tuple-element.10), channel_id=1, source_target_pairs={{0,8},{8,0},{1,9},{9,1},{2,10},{10,2},{3,11},{11,3},{4,12},{12,4},... | collective-permute-start | bytes 860168 | tf_op jit(solution)/shard_map/ppermute | solution.py:12
Sparse Core Ops, SparseCore 0:
  8.9 13.5 all-gather.9
  24.0 12.0 all-gather.11
  37.7 12.0 all-gather.13
  114.4 10.6 all-gather.15

commit v3 on v2

--- a/solution.py
+++ b/solution.py
@@ -42,7 +42,6 @@
     span = n_ctx * half
     ctx = lax.axis_index("context")
     me = lax.axis_index("ex")
-    mine = lax.axis_index("sh")
 
     wg = lax.all_gather(w_gate[0], "context", axis=0, tiled=True)
     wu = lax.all_gather(w_up[0], "context", axis=0, tiled=True)
@@ -70,25 +69,28 @@
     packed = jnp.dot(picker, pair_tokens, preferred_element_type=jnp.float32).astype(jnp.bfloat16)
     packed = packed.reshape(experts, half, width)
 
+    def through_group(sent):
+        group = [sent] + [shift(sent, "sh", sharers, k) for k in range(1, sharers)]
+        rows = jnp.stack(group).reshape(-1, width)
+        partial = quarter_rows(rows, wg, wu, wd, n_ctx).astype(jnp.bfloat16)
+        partial = partial.reshape((sharers,) + sent.shape)
+        total = partial[0].astype(jnp.float32)
+        for k in range(1, sharers):
+            total = total + shift(partial[k], "sh", sharers, -k).astype(jnp.float32)
+        return total
+
     if experts == 2:
-        sent = jnp.stack([packed[0], shift(packed[1], "ex", 2, 1)])
+        local_out = through_group(packed[0:1])
+        far_out = through_group(shift(packed[1:2], "ex", 2, 1))
+        back = shift(far_out.astype(RETURN_DTYPE), "ex", 2, 1).astype(jnp.float32)
+        mine = jnp.concatenate([local_out, back], axis=0)
     else:
         sent = lax.all_to_all(packed, "ex", split_axis=0, concat_axis=0, tiled=True)
-    group = [sent] + [shift(sent, "sh", sharers, k) for k in range(1, sharers)]
-    rows = jnp.stack(group).reshape(-1, width)
-    partial = quarter_rows(rows, wg, wu, wd, n_ctx).astype(jnp.bfloat16)
-    partial = partial.reshape(sharers, experts, half, width)
-
-    total = partial[0].astype(jnp.float32)
-    for k in range(1, sharers):
-        total = total + shift(partial[k], "sh", sharers, -k).astype(jnp.float32)
-    expert_out = total.astype(RETURN_DTYPE)
-    if experts == 2:
-        back = jnp.stack([expert_out[0], shift(expert_out[1], "ex", 2, 1)])
-    else:
-        back = lax.all_to_all(expert_out, "ex", split_axis=0, concat_axis=0, tiled=True)
-    slots_out = lax.all_gather(back, "context", axis=0, tiled=False).astype(jnp.float32)
-    slots_out = slots_out.reshape(n_ctx * experts * half, width)
+        expert_out = through_group(sent).astype(RETURN_DTYPE)
+        mine = lax.all_to_all(expert_out, "ex", split_axis=0, concat_axis=0, tiled=True)
+        mine = mine.astype(jnp.float32)
+    theirs = shift(mine, "context", n_ctx, 1)
+    slots_out = jnp.concatenate([mine, theirs], axis=0).reshape(n_ctx * experts * half, width)
 
     own_cell = lax.dynamic_slice_in_dim(pair_cell, ctx * tok, tok, axis=0)
     expert_of = own_cell // span
@@ -97,7 +99,8 @@
         position = jnp.where(expert_of == me, 0, 1)
     else:
         position = expert_of
-    layout = (slot_of // half) * (experts * half) + position * half + slot_of % half
+    block = jnp.where(slot_of // half == ctx, 0, 1)
+    layout = block * (experts * half) + position * half + slot_of % half
     layout = jnp.where(own_cell < experts * span, layout, n_ctx * experts * half)
     own_match = (
         layout[:, :, None] == jnp.arange(n_ctx * experts * half, dtype=jnp.int32)[None, None, :]

time: 134 us -> 107 us (0.80)
  waiting for transfers between devices: 86.5 us -> 52.1 us
  starting transfers between devices: 13.7 us -> 19.2 us
    ppermute x8 -> x15, waiting for transfers between devices: 74.7 us -> 50 us  [shift(): return lax.ppermute(x, axis, [(i, (i + k) % size) for i in range(size)])]
    all_gather x1 -> x0, waiting for transfers between devices: 10.3 us -> none  [per_device(): lax.all_gather(back, 'context', axis=0, tiled=False).astype(jnp.float32)]
    ppermute x8 -> x15, starting transfers between devices: 13.6 us -> 19.2 us  [shift(): return lax.ppermute(x, axis, [(i, (i + k) % size) for i in range(size)])]
    dot_general x1 -> x2, matrix products: 3.01 us -> 3.65 us  [quarter_rows(): up = lax.dot_general(rows, w_up, dims, preferred_element_type=jnp.float32)]
    dot_general x1 -> x2, matrix products: 3.01 us -> 3.65 us  [quarter_rows(): lax.dot_general(rows, w_gate, dims, preferred_element_type=jnp.float32)]
    dot_general x2 -> x4, matrix products: 2.98 us -> 3.32 us  [quarter_rows(): jnp.dot(hidden[:, c * slab:(c + 1) * slab], w_down[c * slab:(c + 1) * sla...]
  transfers between devices with their start and end apart: 12 -> 18, of which waited for: 9 -> 12; matrix products, arithmetic and copies ran while one was open for 7% -> 11% of each run, Pallas kernels for 0% -> 0%
where the time goes in v3:
time: 107 us
  waiting for transfers between devices  52.1 us (49%)
  starting transfers between devices  19.2 us (18%)
  between operations  13.4 us (13%)
  matrix products  13 us (12%)
  blocking collectives  4.42 us (4%)
  local copies, waits for them, and re-layouts  2.51 us (2%)
  other arithmetic  2.42 us (2%)
    ppermute x15, waiting for transfers between devices, shift(): return lax.ppermute(x, axis, [(i, (i + k) % size) for i in range(size)])  50 us
    ppermute x15, starting transfers between devices, shift(): return lax.ppermute(x, axis, [(i, (i + k) % size) for i in range(size)])  19.2 us
    dot_general x2, matrix products, quarter_rows(): up = lax.dot_general(rows, w_up, dims, preferred_element_type=jnp.float32)  3.65 us
    dot_general x2, matrix products, quarter_rows(): lax.dot_general(rows, w_gate, dims, preferred_element_type=jnp.float32)  3.65 us
    dot_general x4, matrix products, quarter_rows(): jnp.dot(hidden[:, c * slab:(c + 1) * slab], w_down[c * slab:(c + 1) * sla...  3.32 us
    all_gather x1, blocking collectives, per_device(): pair_tokens = lax.all_gather(tokens, 'context', axis=0, tiled=True)  2.47 us
  transfers between devices with their start and end apart: 18, of which 12 were waited for; matrix products, arithmetic and copies ran while one was open for 11% of the time, Pallas kernels for 0%

profile of v3, /device:TPU:0, one launch (start us, length us, event | category | flops | bytes accessed | tf_op | source)
XLA Modules:
  0.0 107.1 jit_solution(8054591970851737439)
XLA Ops:
  6.5 0.7 all-gather.8.cloned.1.call-update
  7.3 0.7 all-gather.10.cloned.1.call-update
  8.1 0.7 all-gather.12.cloned.1.call-update
  8.8 1.9 %all-gather.3 = s32[2,64,8]{1,2,0:T(8,128)S(1)} all-gather(s32[1,64,8]{1,2,0:T(8,128)S(1)} %bitcast.110), channel_id=1, replica_groups=mesh['groups'=2,'ex'=2,'sh'=4,'context'=2] {'context'}, dimensions={0}, use_global_device_ids=true | all-gather | bytes 6144 | tf_op jit(solution)/shard_map/all_gather | solution.py:50
  12.7 2.5 %all_gather.16 = bf16[128,3584]{1,0:T(8,128)(2,1)S(1)} all-gather(bf16[64,3584]{1,0:T(8,128)(2,1)S(1)} %copy-done.2), channel_id=1, replica_groups=mesh['groups'=2,'ex'=2,'sh'=4,'context'=2] {'context'}, dimensions={0}, use_global_device_ids=true | all-gather | bytes 1376256 | tf_op jit(solution)/shard_map/all_gather | solution.py:68
  15.7 4.0 %collective-permute-start.6 = (bf16[1,40,3584]{2,1,0:T(8,128)(2,1)S(1)}, bf16[1,40,3584]{2,1,0:T(8,128)(2,1)S(1)}, u32[]{:S(2)}, u32[]{:S(2)}) collective-permute-start(bf16[1,40,3584]{2,1,0:T(8,128)(2,1)S(1)} %get-tuple-element.13), channel_id=1, source_target_pairs={{0,8},{8,0},{1,9},{9,1},{2,10},{10,2},{3,11},{11,3},{4,12},{12,4},... | collective-permute-start | bytes 860168 | tf_op jit(solution)/shard_map/ppermute | solution.py:12
  19.6 2.5 %collective-permute-start.2 = (bf16[1,40,3584]{2,1,0:T(8,128)(2,1)S(1)}, bf16[1,40,3584]{2,1,0:T(8,128)(2,1)S(1)}, u32[]{:S(2)}, u32[]{:S(2)}) collective-permute-start(bf16[1,40,3584]{2,1,0:T(8,128)(2,1)S(1)} %get-tuple-element.12), channel_id=1, source_target_pairs={{0,6},{2,0},{4,2},{6,4},{1,7},{3,1},{5,3},{7,5},{8,14},{10,8},{12,... | collective-permute-start | bytes 860168 | tf_op jit(solution)/shard_map/ppermute | solution.py:12
  23.3 9.8 %collective-permute-done.6 = bf16[1,40,3584]{2,1,0:T(8,128)(2,1)S(1)} collective-permute-done((bf16[1,40,3584]{2,1,0:T(8,128)(2,1)S(1)}, bf16[1,40,3584]{2,1,0:T(8,128)(2,1)S(1)}, u32[]{:S(2)}, u32[]{:S(2)}) %collective-permute-start.6) | collective-permute-done | bytes 286752 | tf_op jit(solution)/shard_map/ppermute | solution.py:12
  33.1 1.6 %collective-permute-start.9 = (bf16[1,40,3584]{2,1,0:T(8,128)(2,1)S(1)}, bf16[1,40,3584]{2,1,0:T(8,128)(2,1)S(1)}, u32[]{:S(2)}, u32[]{:S(2)}) collective-permute-start(bf16[1,40,3584]{2,1,0:T(8,128)(2,1)S(1)} %collective-permute-done.6), channel_id=1, source_target_pairs={{0,6},{2,0},{4,2},{6,4},{1,7},{3,1},{5,3},{7,5},{8,14},{10,8},{12,... | collective-permute-start | bytes 860168 | tf_op jit(solution)/shard_map/ppermute | solution.py:12
  34.7 1.4 %collective-permute-start.8 = (bf16[1,40,3584]{2,1,0:T(8,128)(2,1)S(1)}, bf16[1,40,3584]{2,1,0:T(8,128)(2,1)S(1)}, u32[]{:S(2)}, u32[]{:S(2)}) collective-permute-start(bf16[1,40,3584]{2,1,0:T(8,128)(2,1)S(1)} %collective-permute-done.6), channel_id=1, source_target_pairs={{0,4},{2,6},{4,0},{6,2},{1,5},{3,7},{5,1},{7,3},{8,12},{10,14},{12... | collective-permute-start | bytes 860168 | tf_op jit(solution)/shard_map/ppermute | solution.py:12
  36.1 0.7 collective-permute-start.7
  36.8 4.7 %collective-permute-done.1 = bf16[1,40,3584]{2,1,0:T(8,128)(2,1)S(1)} collective-permute-done((bf16[1,40,3584]{2,1,0:T(8,128)(2,1)S(1)}, bf16[1,40,3584]{2,1,0:T(8,128)(2,1)S(1)}, u32[]{:S(2)}, u32[]{:S(2)}) %collective-permute-start.1) | collective-permute-done | bytes 286752 | tf_op jit(solution)/shard_map/ppermute | solution.py:12
  42.2 5.4 %collective-permute-done.9 = bf16[1,40,3584]{2,1,0:T(8,128)(2,1)S(1)} collective-permute-done((bf16[1,40,3584]{2,1,0:T(8,128)(2,1)S(1)}, bf16[1,40,3584]{2,1,0:T(8,128)(2,1)S(1)}, u32[]{:S(2)}, u32[]{:S(2)}) %collective-permute-start.9) | collective-permute-done | bytes 286752 | tf_op jit(solution)/shard_map/ppermute | solution.py:12
  47.6 5.2 %collective-permute-done.8 = bf16[1,40,3584]{2,1,0:T(8,128)(2,1)S(1)} collective-permute-done((bf16[1,40,3584]{2,1,0:T(8,128)(2,1)S(1)}, bf16[1,40,3584]{2,1,0:T(8,128)(2,1)S(1)}, u32[]{:S(2)}, u32[]{:S(2)}) %collective-permute-start.8) | collective-permute-done | bytes 286752 | tf_op jit(solution)/shard_map/ppermute | solution.py:12
  53.2 2.6 %fusion.12 = f32[160,320]{1,0:T(8,128)S(1)} fusion(bf16[160,3584]{1,0:T(8,128)(2,1)S(1)} %bitcast.101, bf16[1,320,3584]{2,1,0:T(8,128)(2,1)} %all-gather.8.cloned.1.call-done), kind=kOutput, calls=%fused_computation.19 | convolution fusion | flops 367001600 | bytes 3645440 | tf_op jit(solution)/shard_map/dot_general | solution.py:17
  55.9 2.6 %fusion.22 = bf16[160,320]{1,0:T(8,128)(2,1)S(1)} fusion(bf16[160,3584]{1,0:T(8,128)(2,1)S(1)} %bitcast.102, bf16[1,320,3584]{2,1,0:T(8,128)(2,1)} %all-gather.10.cloned.1.call-done, f32[160,320]{1,0:T(8,128)S(1)} %fusion.12), kind=kOutput, calls=%fused_computation.25 | convolution fusion | flops 367308800 | bytes 3747840 | tf_op jit(solution)/shard_map/dot_general | solution.py:18
  58.6 1.9 %fusion.3 = f32[160,3584]{1,0:T(8,128)S(1)} fusion(bf16[1,320,3584]{2,1,0:T(8,128)(2,1)} %all-gather.12.cloned.1.call-done, bf16[160,320]{1,0:T(8,128)(2,1)S(1)} %fusion.22), kind=kOutput, calls=%fused_computation.5 | convolution fusion | flops 184647680 | bytes 3522560 | tf_op jit(solution)/shard_map/dot_general | solution.py:23
  61.2 2.0 %collective-permute-start.12 = (bf16[1,40,3584]{2,1,0:T(8,128)(2,1)S(1)}, bf16[1,40,3584]{2,1,0:T(8,128)(2,1)S(1)}, u32[]{:S(2)}, u32[]{:S(2)}) collective-permute-start(bf16[1,40,3584]{2,1,0:T(8,128)(2,1)S(1)} %get-tuple-element.9), channel_id=1, source_target_pairs={{0,2},{2,4},{4,6},{6,0},{1,3},{3,5},{5,7},{7,1},{8,10},{10,12},{12... | collective-permute-start | bytes 860168 | tf_op jit(solution)/shard_map/ppermute | solution.py:12
  63.2 1.2 %collective-permute-start.11 = (bf16[1,40,3584]{2,1,0:T(8,128)(2,1)S(1)}, bf16[1,40,3584]{2,1,0:T(8,128)(2,1)S(1)}, u32[]{:S(2)}, u32[]{:S(2)}) collective-permute-start(bf16[1,40,3584]{2,1,0:T(8,128)(2,1)S(1)} %get-tuple-element.10), channel_id=1, source_target_pairs={{0,4},{2,6},{4,0},{6,2},{1,5},{3,7},{5,1},{7,3},{8,12},{10,14},{12... | collective-permute-start | bytes 860168 | tf_op jit(solution)/shard_map/ppermute | solution.py:12
  64.4 1.0 fusion.14
  66.0 1.0 fusion.25
  68.1 1.0 collective-permute-start.3
  69.1 1.1 collective-permute-start.5
  70.1 10.3 %collective-permute-done.10 = bf16[1,40,3584]{2,1,0:T(8,128)(2,1)S(1)} collective-permute-done((bf16[1,40,3584]{2,1,0:T(8,128)(2,1)S(1)}, bf16[1,40,3584]{2,1,0:T(8,128)(2,1)S(1)}, u32[]{:S(2)}, u32[]{:S(2)}) %collective-permute-start.10) | collective-permute-done | bytes 286752 | tf_op jit(solution)/shard_map/ppermute | solution.py:12
  80.5 1.9 %collective-permute-start.4 = (bf16[1,40,3584]{2,1,0:T(8,128)(2,1)S(1)}, bf16[1,40,3584]{2,1,0:T(8,128)(2,1)S(1)}, u32[]{:S(2)}, u32[]{:S(2)}) collective-permute-start(bf16[1,40,3584]{2,1,0:T(8,128)(2,1)S(1)} %get-tuple-element.7), channel_id=1, source_target_pairs={{0,4},{2,6},{4,0},{6,2},{1,5},{3,7},{5,1},{7,3},{8,12},{10,14},{12... | collective-permute-start | bytes 860168 | tf_op jit(solution)/shard_map/ppermute | solution.py:12
  82.5 0.7 collective-permute-start.13
  83.2 2.3 %collective-permute-done.3 = bf16[1,40,3584]{2,1,0:T(8,128)(2,1)S(1)} collective-permute-done((bf16[1,40,3584]{2,1,0:T(8,128)(2,1)S(1)}, bf16[1,40,3584]{2,1,0:T(8,128)(2,1)S(1)}, u32[]{:S(2)}, u32[]{:S(2)}) %collective-permute-start.3) | collective-permute-done | bytes 286752 | tf_op jit(solution)/shard_map/ppermute | solution.py:12
  85.4 4.9 %collective-permute-done.5 = bf16[1,40,3584]{2,1,0:T(8,128)(2,1)S(1)} collective-permute-done((bf16[1,40,3584]{2,1,0:T(8,128)(2,1)S(1)}, bf16[1,40,3584]{2,1,0:T(8,128)(2,1)S(1)}, u32[]{:S(2)}, u32[]{:S(2)}) %collective-permute-start.5) | collective-permute-done | bytes 286752 | tf_op jit(solution)/shard_map/ppermute | solution.py:12
  90.4 2.0 %collective-permute-done.4 = bf16[1,40,3584]{2,1,0:T(8,128)(2,1)S(1)} collective-permute-done((bf16[1,40,3584]{2,1,0:T(8,128)(2,1)S(1)}, bf16[1,40,3584]{2,1,0:T(8,128)(2,1)S(1)}, u32[]{:S(2)}, u32[]{:S(2)}) %collective-permute-start.4) | collective-permute-done | bytes 286752 | tf_op jit(solution)/shard_map/ppermute | solution.py:12
  92.6 2.8 %collective-permute-done.13 = bf16[1,40,3584]{2,1,0:T(8,128)(2,1)S(1)} collective-permute-done((bf16[1,40,3584]{2,1,0:T(8,128)(2,1)S(1)}, bf16[1,40,3584]{2,1,0:T(8,128)(2,1)S(1)}, u32[]{:S(2)}, u32[]{:S(2)}) %collective-permute-start.13) | collective-permute-done | bytes 286752 | tf_op jit(solution)/shard_map/ppermute | solution.py:12
  96.5 1.8 %collective-permute-done.14 = f32[2,40,3584]{2,1,0:T(8,128)S(1)} collective-permute-done((f32[2,40,3584]{2,1,0:T(8,128)S(1)}, f32[2,40,3584]{2,1,0:T(8,128)S(1)}, u32[]{:S(2)}, u32[]{:S(2)}) %collective-permute-start.14) | collective-permute-done | bytes 1146912 | tf_op jit(solution)/shard_map/ppermute | solution.py:12
  98.5 2.1 %convolution_convert_fusion.5 = bf16[64,3584]{1,0:T(8,128)(2,1)} fusion(f32[64,160]{1,0:T(8,128)S(1)} %select_reduce_fusion, f32[160,3584]{1,0:T(8,128)S(1)} %bitcast.98), kind=kOutput, calls=%fused_computation.13 | convolution fusion | flops 440631296 | bytes 2793472 | tf_op jit(solution)/shard_map/dot_general | solution.py:109
  (67 shorter events, 8.9 us)
Async XLA Ops:
  6.5 46.6 %all-gather.8.cloned.1.call-start = ((), (), s32[]{:S(2)}) async-start(), calls=%async_computation | async-start | bytes 3440640 | tf_op jit(solution)/shard_map/all_gather | solution.py:46
  7.3 1.5 %copy-start.3 = (s32[64,8]{0,1:T(8,128)S(1)}, s32[64,8]{0,1:T(8,128)}, u32[]{:S(2)}) copy-start(s32[64,8]{0,1:T(8,128)} %param.7) | copy-start | bytes 6148
  7.3 5.4 %copy-start.2 = (bf16[64,3584]{1,0:T(8,128)(2,1)S(1)}, bf16[64,3584]{1,0:T(8,128)(2,1)}, u32[]{:S(2)}) copy-start(bf16[64,3584]{1,0:T(8,128)(2,1)} %param.6) | copy-start | bytes 1376260
  7.3 48.6 %all-gather.10.cloned.1.call-start = ((), (), s32[]{:S(2)}) async-start(), calls=%async_computation.1 | async-start | bytes 3440640 | tf_op jit(solution)/shard_map/all_gather | solution.py:47
  8.0 50.5 %all-gather.12.cloned.1.call-start = ((), (), s32[]{:S(2)}) async-start(), calls=%async_computation.2 | async-start | bytes 3440640 | tf_op jit(solution)/shard_map/all_gather | solution.py:48
  15.7 17.4 %collective-permute-start.6 = (bf16[1,40,3584]{2,1,0:T(8,128)(2,1)S(1)}, bf16[1,40,3584]{2,1,0:T(8,128)(2,1)S(1)}, u32[]{:S(2)}, u32[]{:S(2)}) collective-permute-start(bf16[1,40,3584]{2,1,0:T(8,128)(2,1)S(1)} %get-tuple-element.13), channel_id=1, source_target_pairs={{0,8},{8,0},{1,9},{9,1},{2,10},{10,2},{3,11},{11,3},{4,12},{12,4},... | collective-permute-start | bytes 860168 | tf_op jit(solution)/shard_map/ppermute | solution.py:12
  19.6 16.5 %collective-permute-start.2 = (bf16[1,40,3584]{2,1,0:T(8,128)(2,1)S(1)}, bf16[1,40,3584]{2,1,0:T(8,128)(2,1)S(1)}, u32[]{:S(2)}, u32[]{:S(2)}) collective-permute-start(bf16[1,40,3584]{2,1,0:T(8,128)(2,1)S(1)} %get-tuple-element.12), channel_id=1, source_target_pairs={{0,6},{2,0},{4,2},{6,4},{1,7},{3,1},{5,3},{7,5},{8,14},{10,8},{12,... | collective-permute-start | bytes 860168 | tf_op jit(solution)/shard_map/ppermute | solution.py:12
  22.2 19.3 %collective-permute-start.1 = (bf16[1,40,3584]{2,1,0:T(8,128)(2,1)S(1)}, bf16[1,40,3584]{2,1,0:T(8,128)(2,1)S(1)}, u32[]{:S(2)}, u32[]{:S(2)}) collective-permute-start(bf16[1,40,3584]{2,1,0:T(8,128)(2,1)S(1)} %get-tuple-element.12), channel_id=1, source_target_pairs={{0,4},{2,6},{4,0},{6,2},{1,5},{3,7},{5,1},{7,3},{8,12},{10,14},{12... | collective-permute-start | bytes 860168 | tf_op jit(solution)/shard_map/ppermute | solution.py:12
  22.6 19.5 %collective-permute-start = (bf16[1,40,3584]{2,1,0:T(8,128)(2,1)S(1)}, bf16[1,40,3584]{2,1,0:T(8,128)(2,1)S(1)}, u32[]{:S(2)}, u32[]{:S(2)}) collective-permute-start(bf16[1,40,3584]{2,1,0:T(8,128)(2,1)S(1)} %get-tuple-element.12), channel_id=1, source_target_pairs={{0,2},{2,4},{4,6},{6,0},{1,3},{3,5},{5,7},{7,1},{8,10},{10,12},{12... | collective-permute-start | bytes 860168 | tf_op jit(solution)/shard_map/ppermute | solution.py:12
  33.1 14.5 %collective-permute-start.9 = (bf16[1,40,3584]{2,1,0:T(8,128)(2,1)S(1)}, bf16[1,40,3584]{2,1,0:T(8,128)(2,1)S(1)}, u32[]{:S(2)}, u32[]{:S(2)}) collective-permute-start(bf16[1,40,3584]{2,1,0:T(8,128)(2,1)S(1)} %collective-permute-done.6), channel_id=1, source_target_pairs={{0,6},{2,0},{4,2},{6,4},{1,7},{3,1},{5,3},{7,5},{8,14},{10,8},{12,... | collective-permute-start | bytes 860168 | tf_op jit(solution)/shard_map/ppermute | solution.py:12
  34.7 18.0 %collective-permute-start.8 = (bf16[1,40,3584]{2,1,0:T(8,128)(2,1)S(1)}, bf16[1,40,3584]{2,1,0:T(8,128)(2,1)S(1)}, u32[]{:S(2)}, u32[]{:S(2)}) collective-permute-start(bf16[1,40,3584]{2,1,0:T(8,128)(2,1)S(1)} %collective-permute-done.6), channel_id=1, source_target_pairs={{0,4},{2,6},{4,0},{6,2},{1,5},{3,7},{5,1},{7,3},{8,12},{10,14},{12... | collective-permute-start | bytes 860168 | tf_op jit(solution)/shard_map/ppermute | solution.py:12
  36.1 16.9 %collective-permute-start.7 = (bf16[1,40,3584]{2,1,0:T(8,128)(2,1)S(1)}, bf16[1,40,3584]{2,1,0:T(8,128)(2,1)S(1)}, u32[]{:S(2)}, u32[]{:S(2)}) collective-permute-start(bf16[1,40,3584]{2,1,0:T(8,128)(2,1)S(1)} %collective-permute-done.6), channel_id=1, source_target_pairs={{0,2},{2,4},{4,6},{6,0},{1,3},{3,5},{5,7},{7,1},{8,10},{10,12},{12... | collective-permute-start | bytes 860168 | tf_op jit(solution)/shard_map/ppermute | solution.py:12
  58.6 2.0 %copy-start.1 = (bf16[1,320,3584]{2,1,0:T(8,128)(2,1)S(1)}, bf16[1,320,3584]{2,1,0:T(8,128)(2,1)}, u32[]{:S(2)}) copy-start(bf16[1,320,3584]{2,1,0:T(8,128)(2,1)} %all-gather.12.cloned.1.call-done) | copy-start | bytes 6881284
  60.5 3.8 %copy-start = (bf16[1,320,3584]{2,1,0:T(8,128)(2,1)S(1)}, bf16[1,320,3584]{2,1,0:T(8,128)(2,1)}, u32[]{:S(2)}) copy-start(bf16[1,320,3584]{2,1,0:T(8,128)(2,1)} %all-gather.8.cloned.1.call-done) | copy-start | bytes 6881284
  61.1 19.4 %collective-permute-start.10 = (bf16[1,40,3584]{2,1,0:T(8,128)(2,1)S(1)}, bf16[1,40,3584]{2,1,0:T(8,128)(2,1)S(1)}, u32[]{:S(2)}, u32[]{:S(2)}) collective-permute-start(bf16[1,40,3584]{2,1,0:T(8,128)(2,1)S(1)} %get-tuple-element.8), channel_id=1, source_target_pairs={{0,6},{2,0},{4,2},{6,4},{1,7},{3,1},{5,3},{7,5},{8,14},{10,8},{12,... | collective-permute-start | bytes 860168 | tf_op jit(solution)/shard_map/ppermute | solution.py:12
  61.2 21.2 %collective-permute-start.12 = (bf16[1,40,3584]{2,1,0:T(8,128)(2,1)S(1)}, bf16[1,40,3584]{2,1,0:T(8,128)(2,1)S(1)}, u32[]{:S(2)}, u32[]{:S(2)}) collective-permute-start(bf16[1,40,3584]{2,1,0:T(8,128)(2,1)S(1)} %get-tuple-element.9), channel_id=1, source_target_pairs={{0,2},{2,4},{4,6},{6,0},{1,3},{3,5},{5,7},{7,1},{8,10},{10,12},{12... | collective-permute-start | bytes 860168 | tf_op jit(solution)/shard_map/ppermute | solution.py:12
  63.2 19.2 %collective-permute-start.11 = (bf16[1,40,3584]{2,1,0:T(8,128)(2,1)S(1)}, bf16[1,40,3584]{2,1,0:T(8,128)(2,1)S(1)}, u32[]{:S(2)}, u32[]{:S(2)}) collective-permute-start(bf16[1,40,3584]{2,1,0:T(8,128)(2,1)S(1)} %get-tuple-element.10), channel_id=1, source_target_pairs={{0,4},{2,6},{4,0},{6,2},{1,5},{3,7},{5,1},{7,3},{8,12},{10,14},{12... | collective-permute-start | bytes 860168 | tf_op jit(solution)/shard_map/ppermute | solution.py:12
  64.4 1.6 %copy-start.5 = (bf16[1,320,3584]{2,1,0:T(8,128)(2,1)S(1)}, bf16[1,320,3584]{2,1,0:T(8,128)(2,1)}, u32[]{:S(2)}) copy-start(bf16[1,320,3584]{2,1,0:T(8,128)(2,1)} %all-gather.10.cloned.1.call-done) | copy-start | bytes 6881284
  68.1 17.4 %collective-permute-start.3 = (bf16[1,40,3584]{2,1,0:T(8,128)(2,1)S(1)}, bf16[1,40,3584]{2,1,0:T(8,128)(2,1)S(1)}, u32[]{:S(2)}, u32[]{:S(2)}) collective-permute-start(bf16[1,40,3584]{2,1,0:T(8,128)(2,1)S(1)} %get-tuple-element.5), channel_id=1, source_target_pairs={{0,6},{2,0},{4,2},{6,4},{1,7},{3,1},{5,3},{7,5},{8,14},{10,8},{12,... | collective-permute-start | bytes 860168 | tf_op jit(solution)/shard_map/ppermute | solution.py:12
  69.1 21.3 %collective-permute-start.5 = (bf16[1,40,3584]{2,1,0:T(8,128)(2,1)S(1)}, bf16[1,40,3584]{2,1,0:T(8,128)(2,1)S(1)}, u32[]{:S(2)}, u32[]{:S(2)}) collective-permute-start(bf16[1,40,3584]{2,1,0:T(8,128)(2,1)S(1)} %get-tuple-element.6), channel_id=1, source_target_pairs={{0,2},{2,4},{4,6},{6,0},{1,3},{3,5},{5,7},{7,1},{8,10},{10,12},{12... | collective-permute-start | bytes 860168 | tf_op jit(solution)/shard_map/ppermute | solution.py:12
  80.5 11.9 %collective-permute-start.4 = (bf16[1,40,3584]{2,1,0:T(8,128)(2,1)S(1)}, bf16[1,40,3584]{2,1,0:T(8,128)(2,1)S(1)}, u32[]{:S(2)}, u32[]{:S(2)}) collective-permute-start(bf16[1,40,3584]{2,1,0:T(8,128)(2,1)S(1)} %get-tuple-element.7), channel_id=1, source_target_pairs={{0,4},{2,6},{4,0},{6,2},{1,5},{3,7},{5,1},{7,3},{8,12},{10,14},{12... | collective-permute-start | bytes 860168 | tf_op jit(solution)/shard_map/ppermute | solution.py:12
  82.5 12.8 %collective-permute-start.13 = (bf16[1,40,3584]{2,1,0:T(8,128)(2,1)S(1)}, bf16[1,40,3584]{2,1,0:T(8,128)(2,1)S(1)}, u32[]{:S(2)}, u32[]{:S(2)}) collective-permute-start(bf16[1,40,3584]{2,1,0:T(8,128)(2,1)S(1)} %fusion.30), channel_id=1, source_target_pairs={{0,8},{8,0},{1,9},{9,1},{2,10},{10,2},{3,11},{11,3},{4,12},{12,4},... | collective-permute-start | bytes 860168 | tf_op jit(solution)/shard_map/ppermute | solution.py:12
  95.3 0.7 copy-start.4
  95.4 2.9 %collective-permute-start.14 = (f32[2,40,3584]{2,1,0:T(8,128)S(1)}, f32[2,40,3584]{2,1,0:T(8,128)S(1)}, u32[]{:S(2)}, u32[]{:S(2)}) collective-permute-start(f32[2,40,3584]{2,1,0:T(8,128)S(1)} %pad_maximum_fusion.3), channel_id=1, source_target_pairs={{0,1},{1,0},{2,3},{3,2},{4,5},{5,4},{6,7},{7,6},{8,9},{9,8},{10,11... | collective-permute-start | bytes 3440648 | tf_op jit(solution)/shard_map/ppermute | solution.py:12
Sparse Core Ops, SparseCore 0:
  8.9 13.5 all-gather.7
  24.0 12.0 all-gather.9
  37.7 12.0 all-gather.11

commit v4 on v3

--- a/solution.py
+++ b/solution.py
@@ -43,11 +43,19 @@
     ctx = lax.axis_index("context")
     me = lax.axis_index("ex")
 
-    wg = lax.all_gather(w_gate[0], "context", axis=0, tiled=True)
-    wu = lax.all_gather(w_up[0], "context", axis=0, tiled=True)
-    wd = lax.all_gather(w_down[0], "context", axis=0, tiled=True)
+    def with_sibling(x):
+        return jnp.concatenate([x, shift(x, "context", n_ctx, 1)], axis=0)
 
-    pair_routes = lax.all_gather(routes, "context", axis=0, tiled=True)
+    wg = with_sibling(w_gate[0])
+    wu = with_sibling(w_up[0])
+    wd = with_sibling(w_down[0])
+
+    other_routes = shift(routes, "context", n_ctx, 1)
+    pair_routes = jnp.where(
+        ctx == 0,
+        jnp.concatenate([routes, other_routes], axis=0),
+        jnp.concatenate([other_routes, routes], axis=0),
+    )
     flat = pair_routes.reshape(-1)
     onehot = (flat[:, None] == jnp.arange(experts, dtype=jnp.int32)[None, :]).astype(jnp.int32)
     earlier = jnp.cumsum(onehot, axis=0) - onehot
@@ -55,6 +63,7 @@
     real = flat < experts
     cell = jnp.where(real, flat * span + slot, experts * span)
     pair_cell = cell.reshape(n_ctx * tok, top)
+    local_cell = jnp.where(ctx == 0, pair_cell, jnp.roll(pair_cell, tok, axis=0))
 
     if experts == 2:
         expert_order = jnp.stack([me, 1 - me])
@@ -63,36 +72,40 @@
     own_cells = (
         expert_order[:, None] * span + ctx * half + jnp.arange(half, dtype=jnp.int32)[None, :]
     ).reshape(-1)
-    match = pair_cell[None, :, :] == own_cells[:, None, None]
+    match = local_cell[None, :, :] == own_cells[:, None, None]
     picker = jnp.sum(match.astype(jnp.float32), axis=2).astype(jnp.bfloat16)
-    pair_tokens = lax.all_gather(tokens, "context", axis=0, tiled=True)
+    pair_tokens = with_sibling(tokens)
     packed = jnp.dot(picker, pair_tokens, preferred_element_type=jnp.float32).astype(jnp.bfloat16)
     packed = packed.reshape(experts, half, width)
 
-    def through_group(sent):
+    def group_partial(sent):
         group = [sent] + [shift(sent, "sh", sharers, k) for k in range(1, sharers)]
         rows = jnp.stack(group).reshape(-1, width)
         partial = quarter_rows(rows, wg, wu, wd, n_ctx).astype(jnp.bfloat16)
-        partial = partial.reshape((sharers,) + sent.shape)
+        return partial.reshape((sharers,) + sent.shape)
+
+    def group_sum(partial):
         total = partial[0].astype(jnp.float32)
         for k in range(1, sharers):
             total = total + shift(partial[k], "sh", sharers, -k).astype(jnp.float32)
         return total
 
     if experts == 2:
-        local_out = through_group(packed[0:1])
-        far_out = through_group(shift(packed[1:2], "ex", 2, 1))
+        local_part = group_partial(packed[0:1])
+        far_part = group_partial(shift(packed[1:2], "ex", 2, 1))
+        far_out = group_sum(far_part)
+        local_part, far_out = lax.optimization_barrier((local_part, far_out))
         back = shift(far_out.astype(RETURN_DTYPE), "ex", 2, 1).astype(jnp.float32)
-        mine = jnp.concatenate([local_out, back], axis=0)
+        mine = jnp.concatenate([group_sum(local_part), back], axis=0)
     else:
         sent = lax.all_to_all(packed, "ex", split_axis=0, concat_axis=0, tiled=True)
-        expert_out = through_group(sent).astype(RETURN_DTYPE)
+        expert_out = group_sum(group_partial(sent)).astype(RETURN_DTYPE)
         mine = lax.all_to_all(expert_out, "ex", split_axis=0, concat_axis=0, tiled=True)
         mine = mine.astype(jnp.float32)
     theirs = shift(mine, "context", n_ctx, 1)
     slots_out = jnp.concatenate([mine, theirs], axis=0).reshape(n_ctx * experts * half, width)
 
-    own_cell = lax.dynamic_slice_in_dim(pair_cell, ctx * tok, tok, axis=0)
+    own_cell = local_cell[:tok]
     expert_of = own_cell // span
     slot_of = own_cell % span
     if experts == 2:

time: 107 us -> 92 us (0.86)
  between operations: 13.4 us -> 0.28 us
  waiting for transfers between devices: 52.1 us -> 57.5 us
  matrix products: 13 us -> 8.31 us
  blocking collectives: 4.42 us -> 0 us
  starting transfers between devices: 19.2 us -> 20.5 us
    ppermute x15 -> x20, waiting for transfers between devices: 50 us -> 57.5 us  [shift(): return lax.ppermute(x, axis, [(i, (i + k) % size) for i in range(size)])]
    all_gather x2 -> x0, blocking collectives: 4.42 us -> none  [the longest x1 2.47 us: per_device(): pair_tokens = lax.all_gather(tokens, 'context', axis=0, tiled=True)]
    unnamed x3 -> x0, waiting for transfers between devices: 2.09 us -> none
    dot_general x2, matrix products: 3.65 us -> 2.02 us  [quarter_rows(): up = lax.dot_general(rows, w_up, dims, preferred_element_type=jnp.float32)]
    dot_general x2, matrix products: 3.65 us -> 2.01 us  [quarter_rows(): lax.dot_general(rows, w_gate, dims, preferred_element_type=jnp.float32)]
    dot_general x4, matrix products: 3.32 us -> 1.92 us  [quarter_rows(): jnp.dot(hidden[:, c * slab:(c + 1) * slab], w_down[c * slab:(c + 1) * sla...]
    ppermute x15 -> x20, starting transfers between devices: 19.2 us -> 20.5 us  [shift(): return lax.ppermute(x, axis, [(i, (i + k) % size) for i in range(size)])]
  transfers between devices with their start and end apart: 18 -> 20, of which waited for: 12 -> 13; matrix products, arithmetic and copies ran while one was open for 11% -> 10% of each run, Pallas kernels for 0% -> 0%
where the time goes in v4:
time: 92 us; the launch traced here: 91.8 us
  waiting for transfers between devices  57.5 us (62%)
  starting transfers between devices  20.5 us (22%)
  matrix products  8.31 us (9%)
  other arithmetic  3.37 us (4%)
  local copies, waits for them, and re-layouts  1.84 us (2%)
    ppermute x20, waiting for transfers between devices, shift(): return lax.ppermute(x, axis, [(i, (i + k) % size) for i in range(size)])  57.5 us
    ppermute x20, starting transfers between devices, shift(): return lax.ppermute(x, axis, [(i, (i + k) % size) for i in range(size)])  20.5 us
    dot_general x1, matrix products, per_device(): jnp.dot(mixing, slots_out, precision=lax.Precision.HIGHEST, preferred_ele...  2.07 us
    dot_general x2, matrix products, quarter_rows(): up = lax.dot_general(rows, w_up, dims, preferred_element_type=jnp.float32)  2.02 us
    dot_general x2, matrix products, quarter_rows(): lax.dot_general(rows, w_gate, dims, preferred_element_type=jnp.float32)  2.01 us
    dot_general x4, matrix products, quarter_rows(): jnp.dot(hidden[:, c * slab:(c + 1) * slab], w_down[c * slab:(c + 1) * sla...  1.92 us
  transfers between devices with their start and end apart: 20, of which 13 were waited for; matrix products, arithmetic and copies ran while one was open for 10% of the time, Pallas kernels for 0%

profile of v4, /device:TPU:0, one launch (start us, length us, event | category | flops | bytes accessed | tf_op | source)
XLA Modules:
  0.0 91.8 jit_solution(11519364470831253107)
XLA Ops:
  0.8 0.7 collective-permute-done
  1.5 0.8 pad_add_fusion.1
  2.7 0.6 reduce-window.6
  5.0 4.0 %collective-permute-start.8 = (bf16[1,40,3584]{2,1,0:T(8,128)(2,1)S(1)}, bf16[1,40,3584]{2,1,0:T(8,128)(2,1)S(1)}, u32[]{:S(2)}, u32[]{:S(2)}) collective-permute-start(bf16[1,40,3584]{2,1,0:T(8,128)(2,1)S(1)} %get-tuple-element.15), channel_id=1, source_target_pairs={{0,8},{8,0},{1,9},{9,1},{2,10},{10,2},{3,11},{11,3},{4,12},{12,4},... | collective-permute-start | bytes 860168 | tf_op jit(solution)/shard_map/ppermute | solution.py:12
  8.9 2.5 %collective-permute-start.4 = (bf16[1,40,3584]{2,1,0:T(8,128)(2,1)S(1)}, bf16[1,40,3584]{2,1,0:T(8,128)(2,1)S(1)}, u32[]{:S(2)}, u32[]{:S(2)}) collective-permute-start(bf16[1,40,3584]{2,1,0:T(8,128)(2,1)S(1)} %get-tuple-element.16), channel_id=1, source_target_pairs={{0,6},{2,0},{4,2},{6,4},{1,7},{3,1},{5,3},{7,5},{8,14},{10,8},{12,... | collective-permute-start | bytes 860168 | tf_op jit(solution)/shard_map/ppermute | solution.py:12
  11.9 0.6 collective-permute-start.2
  12.6 9.8 %collective-permute-done.8 = bf16[1,40,3584]{2,1,0:T(8,128)(2,1)S(1)} collective-permute-done((bf16[1,40,3584]{2,1,0:T(8,128)(2,1)S(1)}, bf16[1,40,3584]{2,1,0:T(8,128)(2,1)S(1)}, u32[]{:S(2)}, u32[]{:S(2)}) %collective-permute-start.8) | collective-permute-done | bytes 286752 | tf_op jit(solution)/shard_map/ppermute | solution.py:12
  22.4 3.4 %collective-permute-start.11 = (bf16[1,40,3584]{2,1,0:T(8,128)(2,1)S(1)}, bf16[1,40,3584]{2,1,0:T(8,128)(2,1)S(1)}, u32[]{:S(2)}, u32[]{:S(2)}) collective-permute-start(bf16[1,40,3584]{2,1,0:T(8,128)(2,1)S(1)} %collective-permute-done.8), channel_id=1, source_target_pairs={{0,6},{2,0},{4,2},{6,4},{1,7},{3,1},{5,3},{7,5},{8,14},{10,8},{12,... | collective-permute-start | bytes 860168 | tf_op jit(solution)/shard_map/ppermute | solution.py:12
  25.8 5.0 %collective-permute-done.3 = bf16[1,40,3584]{2,1,0:T(8,128)(2,1)S(1)} collective-permute-done((bf16[1,40,3584]{2,1,0:T(8,128)(2,1)S(1)}, bf16[1,40,3584]{2,1,0:T(8,128)(2,1)S(1)}, u32[]{:S(2)}, u32[]{:S(2)}) %collective-permute-start.3) | collective-permute-done | bytes 286752 | tf_op jit(solution)/shard_map/ppermute | solution.py:12
  31.5 5.9 %collective-permute-done.11 = bf16[1,40,3584]{2,1,0:T(8,128)(2,1)S(1)} collective-permute-done((bf16[1,40,3584]{2,1,0:T(8,128)(2,1)S(1)}, bf16[1,40,3584]{2,1,0:T(8,128)(2,1)S(1)}, u32[]{:S(2)}, u32[]{:S(2)}) %collective-permute-start.11) | collective-permute-done | bytes 286752 | tf_op jit(solution)/shard_map/ppermute | solution.py:12
  37.5 4.6 %collective-permute-done.10 = bf16[1,40,3584]{2,1,0:T(8,128)(2,1)S(1)} collective-permute-done((bf16[1,40,3584]{2,1,0:T(8,128)(2,1)S(1)}, bf16[1,40,3584]{2,1,0:T(8,128)(2,1)S(1)}, u32[]{:S(2)}, u32[]{:S(2)}) %collective-permute-start.10) | collective-permute-done | bytes 286752 | tf_op jit(solution)/shard_map/ppermute | solution.py:12
  42.4 1.0 %fusion.11 = f32[160,320]{1,0:T(8,128)S(1)} fusion(bf16[160,3584]{1,0:T(8,128)(2,1)S(1)} %bitcast.84, bf16[160,3584]{1,0:T(8,128)(2,1)S(1)} %collective-permute-done.5, bf16[160,3584]{1,0:T(8,128)(2,1)S(1)} %bitcast.97), kind=kOutput, calls=%fused_computation.20 | convolution fusion | flops 371589120 | bytes 3645440 | tf_op jit(solution)/shard_map/dot_general | solution.py:17
  43.5 1.0 %multiply_convert_fusion.1 = bf16[160,320]{1,0:T(8,128)(2,1)S(1)} fusion(f32[160,320]{1,0:T(8,128)S(1)} %fusion.11, bf16[160,3584]{1,0:T(8,128)(2,1)S(1)} %bitcast.85, bf16[160,3584]{1,0:T(8,128)(2,1)S(1)} %collective-permute-done.6, bf16[160,3584]{1,0:T(8,128)(2,1)S(1)} %bitcast.100), kind=kOutput, calls=%fused_computation.48 | convolution fusion | flops 371896320 | bytes 3747840 | tf_op jit(solution)/shard_map/dot_general | solution.py:18
  44.5 1.0 %fusion.10 = f32[160,320]{1,0:T(8,128)S(1)} fusion(bf16[160,3584]{1,0:T(8,128)(2,1)S(1)} %bitcast.86, bf16[160,3584]{1,0:T(8,128)(2,1)S(1)} %collective-permute-done.5, bf16[160,3584]{1,0:T(8,128)(2,1)S(1)} %bitcast.98), kind=kOutput, calls=%fused_computation.19 | convolution fusion | flops 371589120 | bytes 3645440 | tf_op jit(solution)/shard_map/dot_general | solution.py:17
  45.9 1.0 %multiply_convert_fusion = bf16[160,320]{1,0:T(8,128)(2,1)S(1)} fusion(f32[160,320]{1,0:T(8,128)S(1)} %fusion.10, bf16[160,3584]{1,0:T(8,128)(2,1)S(1)} %bitcast.87, bf16[160,3584]{1,0:T(8,128)(2,1)S(1)} %collective-permute-done.6, bf16[160,3584]{1,0:T(8,128)(2,1)S(1)} %bitcast.101), kind=kOutput, calls=%fused_computation.47 | convolution fusion | flops 371896320 | bytes 3747840 | tf_op jit(solution)/shard_map/dot_general | solution.py:18
  47.4 0.5 fusion.2
  48.0 1.2 %collective-permute-start.12 = (bf16[1,40,3584]{2,1,0:T(8,128)(2,1)S(1)}, bf16[1,40,3584]{2,1,0:T(8,128)(2,1)S(1)}, u32[]{:S(2)}, u32[]{:S(2)}) collective-permute-start(bf16[1,40,3584]{2,1,0:T(8,128)(2,1)S(1)} %get-tuple-element.12), channel_id=1, source_target_pairs={{0,6},{2,0},{4,2},{6,4},{1,7},{3,1},{5,3},{7,5},{8,14},{10,8},{12,... | collective-permute-start | bytes 860168 | tf_op jit(solution)/shard_map/ppermute | solution.py:12
  49.2 0.9 collective-permute-start.14
  50.1 1.2 %collective-permute-start.13 = (bf16[1,40,3584]{2,1,0:T(8,128)(2,1)S(1)}, bf16[1,40,3584]{2,1,0:T(8,128)(2,1)S(1)}, u32[]{:S(2)}, u32[]{:S(2)}) collective-permute-start(bf16[1,40,3584]{2,1,0:T(8,128)(2,1)S(1)} %get-tuple-element.14), channel_id=1, source_target_pairs={{0,4},{2,6},{4,0},{6,2},{1,5},{3,7},{5,1},{7,3},{8,12},{10,14},{12... | collective-permute-start | bytes 860168 | tf_op jit(solution)/shard_map/ppermute | solution.py:12
  51.3 0.5 fusion.6
  51.8 10.6 %collective-permute-done.12 = bf16[1,40,3584]{2,1,0:T(8,128)(2,1)S(1)} collective-permute-done((bf16[1,40,3584]{2,1,0:T(8,128)(2,1)S(1)}, bf16[1,40,3584]{2,1,0:T(8,128)(2,1)S(1)}, u32[]{:S(2)}, u32[]{:S(2)}) %collective-permute-start.12) | collective-permute-done | bytes 286752 | tf_op jit(solution)/shard_map/ppermute | solution.py:12
  62.3 1.2 %collective-permute-done.13 = bf16[1,40,3584]{2,1,0:T(8,128)(2,1)S(1)} collective-permute-done((bf16[1,40,3584]{2,1,0:T(8,128)(2,1)S(1)}, bf16[1,40,3584]{2,1,0:T(8,128)(2,1)S(1)}, u32[]{:S(2)}, u32[]{:S(2)}) %collective-permute-start.13) | collective-permute-done | bytes 286752 | tf_op jit(solution)/shard_map/ppermute | solution.py:12
  63.7 0.5 collective-permute-start.18
  64.2 2.7 %collective-permute-start.15 = (bf16[1,40,3584]{2,1,0:T(8,128)(2,1)S(1)}, bf16[1,40,3584]{2,1,0:T(8,128)(2,1)S(1)}, u32[]{:S(2)}, u32[]{:S(2)}) collective-permute-start(bf16[1,40,3584]{2,1,0:T(8,128)(2,1)S(1)} %get-tuple-element.9), channel_id=1, source_target_pairs={{0,6},{2,0},{4,2},{6,4},{1,7},{3,1},{5,3},{7,5},{8,14},{10,8},{12,... | collective-permute-start | bytes 860168 | tf_op jit(solution)/shard_map/ppermute | solution.py:12
  66.9 0.8 collective-permute-start.17
  67.8 1.4 %collective-permute-start.16 = (bf16[1,40,3584]{2,1,0:T(8,128)(2,1)S(1)}, bf16[1,40,3584]{2,1,0:T(8,128)(2,1)S(1)}, u32[]{:S(2)}, u32[]{:S(2)}) collective-permute-start(bf16[1,40,3584]{2,1,0:T(8,128)(2,1)S(1)} %get-tuple-element.11), channel_id=1, source_target_pairs={{0,4},{2,6},{4,0},{6,2},{1,5},{3,7},{5,1},{7,3},{8,12},{10,14},{12... | collective-permute-start | bytes 860168 | tf_op jit(solution)/shard_map/ppermute | solution.py:12
  69.2 9.6 %collective-permute-done.18 = bf16[1,40,3584]{2,1,0:T(8,128)(2,1)S(1)} collective-permute-done((bf16[1,40,3584]{2,1,0:T(8,128)(2,1)S(1)}, bf16[1,40,3584]{2,1,0:T(8,128)(2,1)S(1)}, u32[]{:S(2)}, u32[]{:S(2)}) %collective-permute-start.18) | collective-permute-done | bytes 286752 | tf_op jit(solution)/shard_map/ppermute | solution.py:12
  78.8 4.0 %collective-permute-done.17 = bf16[1,40,3584]{2,1,0:T(8,128)(2,1)S(1)} collective-permute-done((bf16[1,40,3584]{2,1,0:T(8,128)(2,1)S(1)}, bf16[1,40,3584]{2,1,0:T(8,128)(2,1)S(1)}, u32[]{:S(2)}, u32[]{:S(2)}) %collective-permute-start.17) | collective-permute-done | bytes 286752 | tf_op jit(solution)/shard_map/ppermute | solution.py:12
  82.8 3.6 %collective-permute-done.16 = bf16[1,40,3584]{2,1,0:T(8,128)(2,1)S(1)} collective-permute-done((bf16[1,40,3584]{2,1,0:T(8,128)(2,1)S(1)}, bf16[1,40,3584]{2,1,0:T(8,128)(2,1)S(1)}, u32[]{:S(2)}, u32[]{:S(2)}) %collective-permute-start.16) | collective-permute-done | bytes 286752 | tf_op jit(solution)/shard_map/ppermute | solution.py:12
  86.8 0.5 copy-done.2
  87.7 1.9 %collective-permute-done.19 = f32[2,40,3584]{2,1,0:T(8,128)S(1)} collective-permute-done((f32[2,40,3584]{2,1,0:T(8,128)S(1)}, f32[2,40,3584]{2,1,0:T(8,128)S(1)}, u32[]{:S(2)}, u32[]{:S(2)}) %collective-permute-start.19) | collective-permute-done | bytes 1146912 | tf_op jit(solution)/shard_map/ppermute | solution.py:12
  89.7 2.1 %convolution_convert_fusion.5 = bf16[64,3584]{1,0:T(8,128)(2,1)} fusion(f32[64,160]{1,0:T(8,128)S(1)} %select_reduce_fusion, f32[160,3584]{1,0:T(8,128)S(1)} %bitcast.80), kind=kOutput, calls=%fused_computation.13 | convolution fusion | flops 440631296 | bytes 2793472 | tf_op jit(solution)/shard_map/dot_general | solution.py:122
  (66 shorter events, 6.4 us)
Async XLA Ops:
  0.0 4.6 %copy-start.1 = (bf16[64,3584]{1,0:T(8,128)(2,1)S(1)}, bf16[64,3584]{1,0:T(8,128)(2,1)}, u32[]{:S(2)}) copy-start(bf16[64,3584]{1,0:T(8,128)(2,1)} %param.6) | copy-start | bytes 1376260
  0.0 1.5 %collective-permute-start = (s32[64,8]{0,1:T(8,128)}, s32[64,8]{0,1:T(8,128)S(1)}, u32[]{:S(2)}, u32[]{:S(2)}) collective-permute-start(s32[64,8]{0,1:T(8,128)} %param.7), channel_id=1, source_target_pairs={{0,1},{1,0},{2,3},{3,2},{4,5},{5,4},{6,7},{7,6},{8,9},{9,8},{10,11... | collective-permute-start | bytes 6152 | tf_op jit(solution)/shard_map/ppermute | solution.py:12
  0.5 4.1 %collective-permute-start.1 = (bf16[64,3584]{1,0:T(8,128)(2,1)}, bf16[64,3584]{1,0:T(8,128)(2,1)S(1)}, u32[]{:S(2)}, u32[]{:S(2)}) collective-permute-start(bf16[64,3584]{1,0:T(8,128)(2,1)} %param.6), channel_id=1, source_target_pairs={{0,1},{1,0},{2,3},{3,2},{4,5},{5,4},{6,7},{7,6},{8,9},{9,8},{10,11... | collective-permute-start | bytes 1376264 | tf_op jit(solution)/shard_map/ppermute | solution.py:12
  4.5 8.0 %copy-start.3 = (bf16[1,160,3584]{2,1,0:T(8,128)(2,1)S(1)}, bf16[1,160,3584]{2,1,0:T(8,128)(2,1)}, u32[]{:S(2)}) copy-start(bf16[1,160,3584]{2,1,0:T(8,128)(2,1)} %param.9) | copy-start | bytes 3440644
  4.6 17.8 %copy-start.4 = (bf16[1,160,3584]{2,1,0:T(8,128)(2,1)S(1)}, bf16[1,160,3584]{2,1,0:T(8,128)(2,1)}, u32[]{:S(2)}) copy-start(bf16[1,160,3584]{2,1,0:T(8,128)(2,1)} %param.10) | copy-start | bytes 3440644
  5.0 17.4 %collective-permute-start.8 = (bf16[1,40,3584]{2,1,0:T(8,128)(2,1)S(1)}, bf16[1,40,3584]{2,1,0:T(8,128)(2,1)S(1)}, u32[]{:S(2)}, u32[]{:S(2)}) collective-permute-start(bf16[1,40,3584]{2,1,0:T(8,128)(2,1)S(1)} %get-tuple-element.15), channel_id=1, source_target_pairs={{0,8},{8,0},{1,9},{9,1},{2,10},{10,2},{3,11},{11,3},{4,12},{12,4},... | collective-permute-start | bytes 860168 | tf_op jit(solution)/shard_map/ppermute | solution.py:12
  8.9 13.4 %collective-permute-start.4 = (bf16[1,40,3584]{2,1,0:T(8,128)(2,1)S(1)}, bf16[1,40,3584]{2,1,0:T(8,128)(2,1)S(1)}, u32[]{:S(2)}, u32[]{:S(2)}) collective-permute-start(bf16[1,40,3584]{2,1,0:T(8,128)(2,1)S(1)} %get-tuple-element.16), channel_id=1, source_target_pairs={{0,6},{2,0},{4,2},{6,4},{1,7},{3,1},{5,3},{7,5},{8,14},{10,8},{12,... | collective-permute-start | bytes 860168 | tf_op jit(solution)/shard_map/ppermute | solution.py:12
  11.5 19.3 %collective-permute-start.3 = (bf16[1,40,3584]{2,1,0:T(8,128)(2,1)S(1)}, bf16[1,40,3584]{2,1,0:T(8,128)(2,1)S(1)}, u32[]{:S(2)}, u32[]{:S(2)}) collective-permute-start(bf16[1,40,3584]{2,1,0:T(8,128)(2,1)S(1)} %get-tuple-element.16), channel_id=1, source_target_pairs={{0,4},{2,6},{4,0},{6,2},{1,5},{3,7},{5,1},{7,3},{8,12},{10,14},{12... | collective-permute-start | bytes 860168 | tf_op jit(solution)/shard_map/ppermute | solution.py:12
  11.9 19.5 %collective-permute-start.2 = (bf16[1,40,3584]{2,1,0:T(8,128)(2,1)S(1)}, bf16[1,40,3584]{2,1,0:T(8,128)(2,1)S(1)}, u32[]{:S(2)}, u32[]{:S(2)}) collective-permute-start(bf16[1,40,3584]{2,1,0:T(8,128)(2,1)S(1)} %get-tuple-element.16), channel_id=1, source_target_pairs={{0,2},{2,4},{4,6},{6,0},{1,3},{3,5},{5,7},{7,1},{8,10},{10,12},{12... | collective-permute-start | bytes 860168 | tf_op jit(solution)/shard_map/ppermute | solution.py:12
  12.6 29.9 %collective-permute-start.5 = (bf16[160,3584]{1,0:T(8,128)(2,1)S(1)}, bf16[160,3584]{1,0:T(8,128)(2,1)S(1)}, u32[]{:S(2)}, u32[]{:S(2)}) collective-permute-start(bf16[160,3584]{1,0:T(8,128)(2,1)S(1)} %bitcast.96), channel_id=1, source_target_pairs={{0,1},{1,0},{2,3},{3,2},{4,5},{5,4},{6,7},{7,6},{8,9},{9,8},{10,11... | collective-permute-start | bytes 3440648 | tf_op jit(solution)/shard_map/ppermute | solution.py:12
  22.4 21.1 %collective-permute-start.6 = (bf16[160,3584]{1,0:T(8,128)(2,1)S(1)}, bf16[160,3584]{1,0:T(8,128)(2,1)S(1)}, u32[]{:S(2)}, u32[]{:S(2)}) collective-permute-start(bf16[160,3584]{1,0:T(8,128)(2,1)S(1)} %bitcast.99), channel_id=1, source_target_pairs={{0,1},{1,0},{2,3},{3,2},{4,5},{5,4},{6,7},{7,6},{8,9},{9,8},{10,11... | collective-permute-start | bytes 3440648 | tf_op jit(solution)/shard_map/ppermute | solution.py:12
  22.4 15.1 %collective-permute-start.11 = (bf16[1,40,3584]{2,1,0:T(8,128)(2,1)S(1)}, bf16[1,40,3584]{2,1,0:T(8,128)(2,1)S(1)}, u32[]{:S(2)}, u32[]{:S(2)}) collective-permute-start(bf16[1,40,3584]{2,1,0:T(8,128)(2,1)S(1)} %collective-permute-done.8), channel_id=1, source_target_pairs={{0,6},{2,0},{4,2},{6,4},{1,7},{3,1},{5,3},{7,5},{8,14},{10,8},{12,... | collective-permute-start | bytes 860168 | tf_op jit(solution)/shard_map/ppermute | solution.py:12
  30.8 11.2 %collective-permute-start.10 = (bf16[1,40,3584]{2,1,0:T(8,128)(2,1)S(1)}, bf16[1,40,3584]{2,1,0:T(8,128)(2,1)S(1)}, u32[]{:S(2)}, u32[]{:S(2)}) collective-permute-start(bf16[1,40,3584]{2,1,0:T(8,128)(2,1)S(1)} %collective-permute-done.8), channel_id=1, source_target_pairs={{0,4},{2,6},{4,0},{6,2},{1,5},{3,7},{5,1},{7,3},{8,12},{10,14},{12... | collective-permute-start | bytes 860168 | tf_op jit(solution)/shard_map/ppermute | solution.py:12
  31.4 10.9 %collective-permute-start.9 = (bf16[1,40,3584]{2,1,0:T(8,128)(2,1)S(1)}, bf16[1,40,3584]{2,1,0:T(8,128)(2,1)S(1)}, u32[]{:S(2)}, u32[]{:S(2)}) collective-permute-start(bf16[1,40,3584]{2,1,0:T(8,128)(2,1)S(1)} %collective-permute-done.8), channel_id=1, source_target_pairs={{0,2},{2,4},{4,6},{6,0},{1,3},{3,5},{5,7},{7,1},{8,10},{10,12},{12... | collective-permute-start | bytes 860168 | tf_op jit(solution)/shard_map/ppermute | solution.py:12
  31.4 6.1 %copy-start = (bf16[1,160,3584]{2,1,0:T(8,128)(2,1)S(1)}, bf16[1,160,3584]{2,1,0:T(8,128)(2,1)}, u32[]{:S(2)}) copy-start(bf16[1,160,3584]{2,1,0:T(8,128)(2,1)} %param.11) | copy-start | bytes 3440644
  37.4 10.0 %collective-permute-start.7 = (bf16[160,3584]{1,0:T(8,128)(2,1)S(1)}, bf16[160,3584]{1,0:T(8,128)(2,1)S(1)}, u32[]{:S(2)}, u32[]{:S(2)}) collective-permute-start(bf16[160,3584]{1,0:T(8,128)(2,1)S(1)} %bitcast.81), channel_id=1, source_target_pairs={{0,1},{1,0},{2,3},{3,2},{4,5},{5,4},{6,7},{7,6},{8,9},{9,8},{10,11... | collective-permute-start | bytes 3440648 | tf_op jit(solution)/shard_map/ppermute | solution.py:12
  48.0 14.3 %collective-permute-start.12 = (bf16[1,40,3584]{2,1,0:T(8,128)(2,1)S(1)}, bf16[1,40,3584]{2,1,0:T(8,128)(2,1)S(1)}, u32[]{:S(2)}, u32[]{:S(2)}) collective-permute-start(bf16[1,40,3584]{2,1,0:T(8,128)(2,1)S(1)} %get-tuple-element.12), channel_id=1, source_target_pairs={{0,6},{2,0},{4,2},{6,4},{1,7},{3,1},{5,3},{7,5},{8,14},{10,8},{12,... | collective-permute-start | bytes 860168 | tf_op jit(solution)/shard_map/ppermute | solution.py:12
  49.2 13.1 %collective-permute-start.14 = (bf16[1,40,3584]{2,1,0:T(8,128)(2,1)S(1)}, bf16[1,40,3584]{2,1,0:T(8,128)(2,1)S(1)}, u32[]{:S(2)}, u32[]{:S(2)}) collective-permute-start(bf16[1,40,3584]{2,1,0:T(8,128)(2,1)S(1)} %get-tuple-element.13), channel_id=1, source_target_pairs={{0,2},{2,4},{4,6},{6,0},{1,3},{3,5},{5,7},{7,1},{8,10},{10,12},{12... | collective-permute-start | bytes 860168 | tf_op jit(solution)/shard_map/ppermute | solution.py:12
  50.1 13.5 %collective-permute-start.13 = (bf16[1,40,3584]{2,1,0:T(8,128)(2,1)S(1)}, bf16[1,40,3584]{2,1,0:T(8,128)(2,1)S(1)}, u32[]{:S(2)}, u32[]{:S(2)}) collective-permute-start(bf16[1,40,3584]{2,1,0:T(8,128)(2,1)S(1)} %get-tuple-element.14), channel_id=1, source_target_pairs={{0,4},{2,6},{4,0},{6,2},{1,5},{3,7},{5,1},{7,3},{8,12},{10,14},{12... | collective-permute-start | bytes 860168 | tf_op jit(solution)/shard_map/ppermute | solution.py:12
  63.7 15.1 %collective-permute-start.18 = (bf16[1,40,3584]{2,1,0:T(8,128)(2,1)S(1)}, bf16[1,40,3584]{2,1,0:T(8,128)(2,1)S(1)}, u32[]{:S(2)}, u32[]{:S(2)}) collective-permute-start(bf16[1,40,3584]{2,1,0:T(8,128)(2,1)S(1)} %fusion.18), channel_id=1, source_target_pairs={{0,8},{8,0},{1,9},{9,1},{2,10},{10,2},{3,11},{11,3},{4,12},{12,4},... | collective-permute-start | bytes 860168 | tf_op jit(solution)/shard_map/ppermute | solution.py:12
  64.2 14.6 %collective-permute-start.15 = (bf16[1,40,3584]{2,1,0:T(8,128)(2,1)S(1)}, bf16[1,40,3584]{2,1,0:T(8,128)(2,1)S(1)}, u32[]{:S(2)}, u32[]{:S(2)}) collective-permute-start(bf16[1,40,3584]{2,1,0:T(8,128)(2,1)S(1)} %get-tuple-element.9), channel_id=1, source_target_pairs={{0,6},{2,0},{4,2},{6,4},{1,7},{3,1},{5,3},{7,5},{8,14},{10,8},{12,... | collective-permute-start | bytes 860168 | tf_op jit(solution)/shard_map/ppermute | solution.py:12
  66.9 15.9 %collective-permute-start.17 = (bf16[1,40,3584]{2,1,0:T(8,128)(2,1)S(1)}, bf16[1,40,3584]{2,1,0:T(8,128)(2,1)S(1)}, u32[]{:S(2)}, u32[]{:S(2)}) collective-permute-start(bf16[1,40,3584]{2,1,0:T(8,128)(2,1)S(1)} %get-tuple-element.10), channel_id=1, source_target_pairs={{0,2},{2,4},{4,6},{6,0},{1,3},{3,5},{5,7},{7,1},{8,10},{10,12},{12... | collective-permute-start | bytes 860168 | tf_op jit(solution)/shard_map/ppermute | solution.py:12
  67.8 18.6 %collective-permute-start.16 = (bf16[1,40,3584]{2,1,0:T(8,128)(2,1)S(1)}, bf16[1,40,3584]{2,1,0:T(8,128)(2,1)S(1)}, u32[]{:S(2)}, u32[]{:S(2)}) collective-permute-start(bf16[1,40,3584]{2,1,0:T(8,128)(2,1)S(1)} %get-tuple-element.11), channel_id=1, source_target_pairs={{0,4},{2,6},{4,0},{6,2},{1,5},{3,7},{5,1},{7,3},{8,12},{10,14},{12... | collective-permute-start | bytes 860168 | tf_op jit(solution)/shard_map/ppermute | solution.py:12
  86.6 0.7 copy-start.2
  86.7 2.9 %collective-permute-start.19 = (f32[2,40,3584]{2,1,0:T(8,128)S(1)}, f32[2,40,3584]{2,1,0:T(8,128)S(1)}, u32[]{:S(2)}, u32[]{:S(2)}) collective-permute-start(f32[2,40,3584]{2,1,0:T(8,128)S(1)} %pad_maximum_fusion.9), channel_id=1, source_target_pairs={{0,1},{1,0},{2,3},{3,2},{4,5},{5,4},{6,7},{7,6},{8,9},{9,8},{10,11... | collective-permute-start | bytes 3440648 | tf_op jit(solution)/shard_map/ppermute | solution.py:12

commit v5 on v4

--- a/solution.py
+++ b/solution.py
@@ -46,9 +46,9 @@
     def with_sibling(x):
         return jnp.concatenate([x, shift(x, "context", n_ctx, 1)], axis=0)
 
-    wg = with_sibling(w_gate[0])
-    wu = with_sibling(w_up[0])
-    wd = with_sibling(w_down[0])
+    slabs = jnp.stack([w_gate[0], w_up[0], w_down[0]])
+    quarter = jnp.concatenate([slabs, shift(slabs, "context", n_ctx, 1)], axis=1)
+    wg, wu, wd = quarter[0], quarter[1], quarter[2]
 
     other_routes = shift(routes, "context", n_ctx, 1)
     pair_routes = jnp.where(
@@ -91,8 +91,10 @@
         return total
 
     if experts == 2:
+        far_sent = shift(packed[1:2], "ex", 2, 1)
         local_part = group_partial(packed[0:1])
-        far_part = group_partial(shift(packed[1:2], "ex", 2, 1))
+        local_part, far_sent = lax.optimization_barrier((local_part, far_sent))
+        far_part = group_partial(far_sent)
         far_out = group_sum(far_part)
         local_part, far_out = lax.optimization_barrier((local_part, far_out))
         back = shift(far_out.astype(RETURN_DTYPE), "ex", 2, 1).astype(jnp.float32)

time: 92 us -> 109 us (1.18)
  local copies, waits for them, and re-layouts: 1.84 us -> 9.15 us
  matrix products: 8.31 us -> 14.6 us
  waiting for transfers between devices: 57.5 us -> 60.1 us
  other arithmetic: 3.37 us -> 5.13 us
    unnamed x13 -> x17, local copies, waits for them, and re-layouts: 0.74 us -> 4.45 us
    dot_general x2, matrix products: 2.02 us -> 4.62 us  [quarter_rows(): up = lax.dot_general(rows, w_up, dims, preferred_element_type=jnp.float32)]
    ppermute x20 -> x18, waiting for transfers between devices: 57.5 us -> 60.1 us  [shift(): return lax.ppermute(x, axis, [(i, (i + k) % size) for i in range(size)])]
    dot_general x2, matrix products: 2.01 us -> 4.52 us  [quarter_rows(): lax.dot_general(rows, w_gate, dims, preferred_element_type=jnp.float32)]
    dot_general x1, matrix products: 0.29 us -> 1.46 us  [per_device(): jnp.dot(picker, pair_tokens, preferred_element_type=jnp.float32)]
    another operation x1 -> x2, local copies, waits for them, and re-layouts: 0.21 us -> 1.3 us  [the longest x1 1.09 us: per_device(): slabs = jnp.stack([w_gate[0], w_up[0], w_down[0]])]
    ppermute x20 -> x18, starting transfers between devices: 20.5 us -> 19.7 us  [shift(): return lax.ppermute(x, axis, [(i, (i + k) % size) for i in range(size)])]
  transfers between devices with their start and end apart: 20 -> 18, of which waited for: 13 -> 12; matrix products, arithmetic and copies ran while one was open for 10% -> 18% of each run, Pallas kernels for 0% -> 0%
where the time goes in v5:
time: 109 us
  waiting for transfers between devices  60.1 us (55%)
  starting transfers between devices  19.7 us (18%)
  matrix products  14.6 us (13%)
  local copies, waits for them, and re-layouts  9.15 us (8%)
  other arithmetic  5.13 us (5%)
    ppermute x18, waiting for transfers between devices, shift(): return lax.ppermute(x, axis, [(i, (i + k) % size) for i in range(size)])  60.1 us
    ppermute x18, starting transfers between devices, shift(): return lax.ppermute(x, axis, [(i, (i + k) % size) for i in range(size)])  19.7 us
    dot_general x2, matrix products, quarter_rows(): up = lax.dot_general(rows, w_up, dims, preferred_element_type=jnp.float32)  4.62 us
    dot_general x2, matrix products, quarter_rows(): lax.dot_general(rows, w_gate, dims, preferred_element_type=jnp.float32)  4.52 us
    unnamed x17, local copies, waits for them, and re-layouts  4.45 us
  transfers between devices with their start and end apart: 18, of which 12 were waited for; matrix products, arithmetic and copies ran while one was open for 18% of the time, Pallas kernels for 0%

profile of v5, /device:TPU:0, one launch (start us, length us, event | category | flops | bytes accessed | tf_op | source)
XLA Modules:
  0.0 109.0 jit_solution(18217491787882764449)
XLA Ops:
  0.5 2.5 %constant_dynamic-update-slice_fusion.2 = bf16[3,160,3584]{2,1,0:T(8,128)(2,1)} fusion(bf16[1,160,3584]{2,1,0:T(8,128)(2,1)} %param.9), kind=kLoop, calls=%fused_computation.78 | loop fusion | bytes 2293760
  3.0 1.1 %constant_dynamic-update-slice_fusion.1 = bf16[3,160,3584]{2,1,0:T(8,128)(2,1)} fusion(bf16[3,160,3584]{2,1,0:T(8,128)(2,1)} %constant_dynamic-update-slice_fusion.2, bf16[1,160,3584]{2,1,0:T(8,128)(2,1)S(1)} %copy-done.2), kind=kLoop, calls=%fused_computation.77 | loop fusion | bytes 2293760
  4.1 1.1 %constant_dynamic-update-slice_fusion = bf16[3,160,3584]{2,1,0:T(8,128)(2,1)} fusion(bf16[3,160,3584]{2,1,0:T(8,128)(2,1)} %constant_dynamic-update-slice_fusion.1, bf16[1,160,3584]{2,1,0:T(8,128)(2,1)S(1)} %copy-done), kind=kLoop, calls=%fused_computation.76 | loop fusion | bytes 2293760 | tf_op jit(solution)/shard_map/stack | solution.py:49
  6.0 0.7 copy.33
  6.7 0.7 copy.32
  7.5 0.9 broadcast_select_fusion.1
  10.3 0.8 add_select_fusion
  12.0 0.7 copy.36
  12.7 0.9 broadcast_select_fusion
  13.9 1.5 %convolution_convert_fusion.4 = bf16[80,3584]{1,0:T(8,128)(2,1)S(1)} fusion(bf16[64,3584]{1,0:T(8,128)(2,1)} %collective-permute-done.1, bf16[64,3584]{1,0:T(8,128)(2,1)} %param.6, bf16[80,128]{1,0:T(8,128)(2,1)S(1)} %convert_reduce_fusion), kind=kOutput, calls=%fused_computation.12 | convolution fusion | flops 75522048 | bytes 1511424 | tf_op jit(solution)/shard_map/dot_general | solution.py:78
  15.4 3.6 %collective-permute-start.4 = (bf16[1,40,3584]{2,1,0:T(8,128)(2,1)S(1)}, bf16[1,40,3584]{2,1,0:T(8,128)(2,1)S(1)}, u32[]{:S(2)}, u32[]{:S(2)}) collective-permute-start(bf16[1,40,3584]{2,1,0:T(8,128)(2,1)S(1)} %get-tuple-element.20), channel_id=1, source_target_pairs={{0,6},{2,0},{4,2},{6,4},{1,7},{3,1},{5,3},{7,5},{8,14},{10,8},{12,... | collective-permute-start | bytes 860168 | tf_op jit(solution)/shard_map/ppermute | solution.py:12
  20.0 2.6 %collective-permute-start.6 = (bf16[1,40,3584]{2,1,0:T(8,128)(2,1)S(1)}, bf16[1,40,3584]{2,1,0:T(8,128)(2,1)S(1)}, u32[]{:S(2)}, u32[]{:S(2)}) collective-permute-start(bf16[1,40,3584]{2,1,0:T(8,128)(2,1)S(1)} %get-tuple-element.19), channel_id=1, source_target_pairs={{0,8},{8,0},{1,9},{9,1},{2,10},{10,2},{3,11},{11,3},{4,12},{12,4},... | collective-permute-start | bytes 860168 | tf_op jit(solution)/shard_map/ppermute | solution.py:12
  22.6 3.5 %collective-permute-done.4 = bf16[1,40,3584]{2,1,0:T(8,128)(2,1)S(1)} collective-permute-done((bf16[1,40,3584]{2,1,0:T(8,128)(2,1)S(1)}, bf16[1,40,3584]{2,1,0:T(8,128)(2,1)S(1)}, u32[]{:S(2)}, u32[]{:S(2)}) %collective-permute-start.4) | collective-permute-done | bytes 286752 | tf_op jit(solution)/shard_map/ppermute | solution.py:12
  26.1 12.8 %collective-permute-done.3 = bf16[1,40,3584]{2,1,0:T(8,128)(2,1)S(1)} collective-permute-done((bf16[1,40,3584]{2,1,0:T(8,128)(2,1)S(1)}, bf16[1,40,3584]{2,1,0:T(8,128)(2,1)S(1)}, u32[]{:S(2)}, u32[]{:S(2)}) %collective-permute-start.3) | collective-permute-done | bytes 286752 | tf_op jit(solution)/shard_map/ppermute | solution.py:12
  39.2 2.3 %fusion.36 = f32[160,320]{1,0:T(8,128)S(1)} fusion(bf16[160,3584]{1,0:T(8,128)(2,1)S(1)} %bitcast.92, bf16[3,160,3584]{2,1,0:T(8,128)(2,1)S(1)} %collective-permute-done.5, bf16[3,160,3584]{2,1,0:T(8,128)(2,1)} %constant_dynamic-update-slice_fusion), kind=kOutput, calls=%fused_computation.90 | convolution fusion | flops 371589120 | bytes 8232960 | tf_op jit(solution)/shard_map/dot_general | solution.py:17
  41.4 2.4 %multiply_convert_fusion.1 = bf16[160,320]{1,0:T(8,128)(2,1)S(1)} fusion(f32[160,320]{1,0:T(8,128)S(1)} %fusion.36, bf16[160,3584]{1,0:T(8,128)(2,1)S(1)} %bitcast.93, bf16[3,160,3584]{2,1,0:T(8,128)(2,1)S(1)} %collective-permute-done.5, bf16[3,160,3584]{2,1,0:T(8,128)(2,1)} %constant_dynamic-update-slice_fusion), kind=kOutput, calls=%fused_computation.48 | convolution fusion | flops 371896320 | bytes 8335360 | tf_op jit(solution)/shard_map/dot_general | solution.py:18
  44.9 1.9 %collective-permute-start.7 = (bf16[1,40,3584]{2,1,0:T(8,128)(2,1)S(1)}, bf16[1,40,3584]{2,1,0:T(8,128)(2,1)S(1)}, u32[]{:S(2)}, u32[]{:S(2)}) collective-permute-start(bf16[1,40,3584]{2,1,0:T(8,128)(2,1)S(1)} %collective-permute-done.6), channel_id=1, source_target_pairs={{0,2},{2,4},{4,6},{6,0},{1,3},{3,5},{5,7},{7,1},{8,10},{10,12},{12... | collective-permute-start | bytes 860168 | tf_op jit(solution)/shard_map/ppermute | solution.py:12
  46.9 6.8 %collective-permute-done.9 = bf16[1,40,3584]{2,1,0:T(8,128)(2,1)S(1)} collective-permute-done((bf16[1,40,3584]{2,1,0:T(8,128)(2,1)S(1)}, bf16[1,40,3584]{2,1,0:T(8,128)(2,1)S(1)}, u32[]{:S(2)}, u32[]{:S(2)}) %collective-permute-start.9) | collective-permute-done | bytes 286752 | tf_op jit(solution)/shard_map/ppermute | solution.py:12
  53.7 3.6 %collective-permute-done.8 = bf16[1,40,3584]{2,1,0:T(8,128)(2,1)S(1)} collective-permute-done((bf16[1,40,3584]{2,1,0:T(8,128)(2,1)S(1)}, bf16[1,40,3584]{2,1,0:T(8,128)(2,1)S(1)}, u32[]{:S(2)}, u32[]{:S(2)}) %collective-permute-start.8) | collective-permute-done | bytes 286752 | tf_op jit(solution)/shard_map/ppermute | solution.py:12
  57.3 3.3 %collective-permute-done.7 = bf16[1,40,3584]{2,1,0:T(8,128)(2,1)S(1)} collective-permute-done((bf16[1,40,3584]{2,1,0:T(8,128)(2,1)S(1)}, bf16[1,40,3584]{2,1,0:T(8,128)(2,1)S(1)}, u32[]{:S(2)}, u32[]{:S(2)}) %collective-permute-start.7) | collective-permute-done | bytes 286752 | tf_op jit(solution)/shard_map/ppermute | solution.py:12
  60.8 2.3 %fusion.35 = f32[160,320]{1,0:T(8,128)S(1)} fusion(bf16[160,3584]{1,0:T(8,128)(2,1)S(1)} %bitcast.94, bf16[3,160,3584]{2,1,0:T(8,128)(2,1)S(1)} %collective-permute-done.5, bf16[3,160,3584]{2,1,0:T(8,128)(2,1)} %constant_dynamic-update-slice_fusion), kind=kOutput, calls=%fused_computation.89 | convolution fusion | flops 371589120 | bytes 8232960 | tf_op jit(solution)/shard_map/dot_general | solution.py:17
  63.0 2.3 %multiply_convert_fusion = bf16[160,320]{1,0:T(8,128)(2,1)S(1)} fusion(f32[160,320]{1,0:T(8,128)S(1)} %fusion.35, bf16[160,3584]{1,0:T(8,128)(2,1)S(1)} %bitcast.95, bf16[3,160,3584]{2,1,0:T(8,128)(2,1)S(1)} %collective-permute-done.5, bf16[3,160,3584]{2,1,0:T(8,128)(2,1)} %constant_dynamic-update-slice_fusion), kind=kOutput, calls=%fused_computation.47 | convolution fusion | flops 371896320 | bytes 8335360 | tf_op jit(solution)/shard_map/dot_general | solution.py:18
  66.4 2.0 %collective-permute-start.12 = (bf16[1,40,3584]{2,1,0:T(8,128)(2,1)S(1)}, bf16[1,40,3584]{2,1,0:T(8,128)(2,1)S(1)}, u32[]{:S(2)}, u32[]{:S(2)}) collective-permute-start(bf16[1,40,3584]{2,1,0:T(8,128)(2,1)S(1)} %get-tuple-element.17), channel_id=1, source_target_pairs={{0,2},{2,4},{4,6},{6,0},{1,3},{3,5},{5,7},{7,1},{8,10},{10,12},{12... | collective-permute-start | bytes 860168 | tf_op jit(solution)/shard_map/ppermute | solution.py:12
  68.7 11.1 %collective-permute-done.10 = bf16[1,40,3584]{2,1,0:T(8,128)(2,1)S(1)} collective-permute-done((bf16[1,40,3584]{2,1,0:T(8,128)(2,1)S(1)}, bf16[1,40,3584]{2,1,0:T(8,128)(2,1)S(1)}, u32[]{:S(2)}, u32[]{:S(2)}) %collective-permute-start.10) | collective-permute-done | bytes 286752 | tf_op jit(solution)/shard_map/ppermute | solution.py:12
  80.0 3.7 %collective-permute-start.16 = (bf16[1,40,3584]{2,1,0:T(8,128)(2,1)S(1)}, bf16[1,40,3584]{2,1,0:T(8,128)(2,1)S(1)}, u32[]{:S(2)}, u32[]{:S(2)}) collective-permute-start(bf16[1,40,3584]{2,1,0:T(8,128)(2,1)S(1)} %fusion.17), channel_id=1, source_target_pairs={{0,8},{8,0},{1,9},{9,1},{2,10},{10,2},{3,11},{11,3},{4,12},{12,4},... | collective-permute-start | bytes 860168 | tf_op jit(solution)/shard_map/ppermute | solution.py:12
  83.7 2.7 %collective-permute-start.13 = (bf16[1,40,3584]{2,1,0:T(8,128)(2,1)S(1)}, bf16[1,40,3584]{2,1,0:T(8,128)(2,1)S(1)}, u32[]{:S(2)}, u32[]{:S(2)}) collective-permute-start(bf16[1,40,3584]{2,1,0:T(8,128)(2,1)S(1)} %get-tuple-element.13), channel_id=1, source_target_pairs={{0,6},{2,0},{4,2},{6,4},{1,7},{3,1},{5,3},{7,5},{8,14},{10,8},{12,... | collective-permute-start | bytes 860168 | tf_op jit(solution)/shard_map/ppermute | solution.py:12
  87.1 9.0 %collective-permute-done.16 = bf16[1,40,3584]{2,1,0:T(8,128)(2,1)S(1)} collective-permute-done((bf16[1,40,3584]{2,1,0:T(8,128)(2,1)S(1)}, bf16[1,40,3584]{2,1,0:T(8,128)(2,1)S(1)}, u32[]{:S(2)}, u32[]{:S(2)}) %collective-permute-start.16) | collective-permute-done | bytes 286752 | tf_op jit(solution)/shard_map/ppermute | solution.py:12
  96.1 1.0 collective-permute-done.13
  97.2 4.5 %collective-permute-done.15 = bf16[1,40,3584]{2,1,0:T(8,128)(2,1)S(1)} collective-permute-done((bf16[1,40,3584]{2,1,0:T(8,128)(2,1)S(1)}, bf16[1,40,3584]{2,1,0:T(8,128)(2,1)S(1)}, u32[]{:S(2)}, u32[]{:S(2)}) %collective-permute-start.15) | collective-permute-done | bytes 286752 | tf_op jit(solution)/shard_map/ppermute | solution.py:12
  101.7 1.9 %collective-permute-done.14 = bf16[1,40,3584]{2,1,0:T(8,128)(2,1)S(1)} collective-permute-done((bf16[1,40,3584]{2,1,0:T(8,128)(2,1)S(1)}, bf16[1,40,3584]{2,1,0:T(8,128)(2,1)S(1)}, u32[]{:S(2)}, u32[]{:S(2)}) %collective-permute-start.14) | collective-permute-done | bytes 286752 | tf_op jit(solution)/shard_map/ppermute | solution.py:12
  104.4 2.4 %collective-permute-done.17 = f32[2,40,3584]{2,1,0:T(8,128)S(1)} collective-permute-done((f32[2,40,3584]{2,1,0:T(8,128)S(1)}, f32[2,40,3584]{2,1,0:T(8,128)S(1)}, u32[]{:S(2)}, u32[]{:S(2)}) %collective-permute-start.17) | collective-permute-done | bytes 1146912 | tf_op jit(solution)/shard_map/ppermute | solution.py:12
  106.9 2.1 %convolution_convert_fusion.5 = bf16[64,3584]{1,0:T(8,128)(2,1)} fusion(f32[64,160]{1,0:T(8,128)S(1)} %select_reduce_fusion, f32[160,3584]{1,0:T(8,128)S(1)} %bitcast.96), kind=kOutput, calls=%fused_computation.13 | convolution fusion | flops 440631296 | bytes 2793472 | tf_op jit(solution)/shard_map/dot_general | solution.py:124
  (67 shorter events, 10.1 us)
Async XLA Ops:
  0.0 3.0 %copy-start.2 = (bf16[1,160,3584]{2,1,0:T(8,128)(2,1)S(1)}, bf16[1,160,3584]{2,1,0:T(8,128)(2,1)}, u32[]{:S(2)}) copy-start(bf16[1,160,3584]{2,1,0:T(8,128)(2,1)} %param.10) | copy-start | bytes 3440644
  0.0 4.1 %copy-start = (bf16[1,160,3584]{2,1,0:T(8,128)(2,1)S(1)}, bf16[1,160,3584]{2,1,0:T(8,128)(2,1)}, u32[]{:S(2)}) copy-start(bf16[1,160,3584]{2,1,0:T(8,128)(2,1)} %param.11) | copy-start | bytes 3440644
  0.0 5.9 %collective-permute-start = (s32[64,8]{0,1:T(8,128)}, s32[64,8]{0,1:T(8,128)S(1)}, u32[]{:S(2)}, u32[]{:S(2)}) collective-permute-start(s32[64,8]{0,1:T(8,128)} %param.7), channel_id=1, source_target_pairs={{0,1},{1,0},{2,3},{3,2},{4,5},{5,4},{6,7},{7,6},{8,9},{9,8},{10,11... | collective-permute-start | bytes 6152 | tf_op jit(solution)/shard_map/ppermute | solution.py:12
  0.5 13.4 %collective-permute-start.1 = (bf16[64,3584]{1,0:T(8,128)(2,1)}, bf16[64,3584]{1,0:T(8,128)(2,1)}, u32[]{:S(2)}, u32[]{:S(2)}) collective-permute-start(bf16[64,3584]{1,0:T(8,128)(2,1)} %param.6), channel_id=1, source_target_pairs={{0,1},{1,0},{2,3},{3,2},{4,5},{5,4},{6,7},{7,6},{8,9},{9,8},{10,11... | collective-permute-start | bytes 1376264 | tf_op jit(solution)/shard_map/ppermute | solution.py:12
  3.0 2.9 %copy-start.5 = (s32[64,8]{0,1:T(8,128)S(1)}, s32[64,8]{0,1:T(8,128)}, u32[]{:S(2)}) copy-start(s32[64,8]{0,1:T(8,128)} %param.7) | copy-start | bytes 6148
  5.2 33.9 %collective-permute-start.5 = (bf16[3,160,3584]{2,1,0:T(8,128)(2,1)}, bf16[3,160,3584]{2,1,0:T(8,128)(2,1)S(1)}, u32[]{:S(2)}, u32[]{:S(2)}) collective-permute-start(bf16[3,160,3584]{2,1,0:T(8,128)(2,1)} %constant_dynamic-update-slice_fusion), channel_id=1, source_target_pairs={{0,1},{1,0},{2,3},{3,2},{4,5},{5,4},{6,7},{7,6},{8,9},{9,8},{10,11... | collective-permute-start | bytes 10321928 | tf_op jit(solution)/shard_map/ppermute | solution.py:12
  11.2 0.6 copy-start.3
  15.4 10.7 %collective-permute-start.4 = (bf16[1,40,3584]{2,1,0:T(8,128)(2,1)S(1)}, bf16[1,40,3584]{2,1,0:T(8,128)(2,1)S(1)}, u32[]{:S(2)}, u32[]{:S(2)}) collective-permute-start(bf16[1,40,3584]{2,1,0:T(8,128)(2,1)S(1)} %get-tuple-element.20), channel_id=1, source_target_pairs={{0,6},{2,0},{4,2},{6,4},{1,7},{3,1},{5,3},{7,5},{8,14},{10,8},{12,... | collective-permute-start | bytes 860168 | tf_op jit(solution)/shard_map/ppermute | solution.py:12
  18.9 20.0 %collective-permute-start.3 = (bf16[1,40,3584]{2,1,0:T(8,128)(2,1)S(1)}, bf16[1,40,3584]{2,1,0:T(8,128)(2,1)S(1)}, u32[]{:S(2)}, u32[]{:S(2)}) collective-permute-start(bf16[1,40,3584]{2,1,0:T(8,128)(2,1)S(1)} %get-tuple-element.20), channel_id=1, source_target_pairs={{0,4},{2,6},{4,0},{6,2},{1,5},{3,7},{5,1},{7,3},{8,12},{10,14},{12... | collective-permute-start | bytes 860168 | tf_op jit(solution)/shard_map/ppermute | solution.py:12
  19.4 19.6 %collective-permute-start.2 = (bf16[1,40,3584]{2,1,0:T(8,128)(2,1)S(1)}, bf16[1,40,3584]{2,1,0:T(8,128)(2,1)S(1)}, u32[]{:S(2)}, u32[]{:S(2)}) collective-permute-start(bf16[1,40,3584]{2,1,0:T(8,128)(2,1)S(1)} %get-tuple-element.20), channel_id=1, source_target_pairs={{0,2},{2,4},{4,6},{6,0},{1,3},{3,5},{5,7},{7,1},{8,10},{10,12},{12... | collective-permute-start | bytes 860168 | tf_op jit(solution)/shard_map/ppermute | solution.py:12
  20.0 24.7 %collective-permute-start.6 = (bf16[1,40,3584]{2,1,0:T(8,128)(2,1)S(1)}, bf16[1,40,3584]{2,1,0:T(8,128)(2,1)S(1)}, u32[]{:S(2)}, u32[]{:S(2)}) collective-permute-start(bf16[1,40,3584]{2,1,0:T(8,128)(2,1)S(1)} %get-tuple-element.19), channel_id=1, source_target_pairs={{0,8},{8,0},{1,9},{9,1},{2,10},{10,2},{3,11},{11,3},{4,12},{12,4},... | collective-permute-start | bytes 860168 | tf_op jit(solution)/shard_map/ppermute | solution.py:12
  41.4 2.4 %copy-start.1 = (bf16[1,160,3584]{2,1,0:T(8,128)(2,1)S(1)}, bf16[1,160,3584]{2,1,0:T(8,128)(2,1)}, u32[]{:S(2)}) copy-start(bf16[1,160,3584]{2,1,0:T(8,128)(2,1)} %param.11) | copy-start | bytes 3440644
  44.8 8.9 %collective-permute-start.9 = (bf16[1,40,3584]{2,1,0:T(8,128)(2,1)S(1)}, bf16[1,40,3584]{2,1,0:T(8,128)(2,1)S(1)}, u32[]{:S(2)}, u32[]{:S(2)}) collective-permute-start(bf16[1,40,3584]{2,1,0:T(8,128)(2,1)S(1)} %collective-permute-done.6), channel_id=1, source_target_pairs={{0,6},{2,0},{4,2},{6,4},{1,7},{3,1},{5,3},{7,5},{8,14},{10,8},{12,... | collective-permute-start | bytes 860168 | tf_op jit(solution)/shard_map/ppermute | solution.py:12
  44.9 12.4 %collective-permute-start.8 = (bf16[1,40,3584]{2,1,0:T(8,128)(2,1)S(1)}, bf16[1,40,3584]{2,1,0:T(8,128)(2,1)S(1)}, u32[]{:S(2)}, u32[]{:S(2)}) collective-permute-start(bf16[1,40,3584]{2,1,0:T(8,128)(2,1)S(1)} %collective-permute-done.6), channel_id=1, source_target_pairs={{0,4},{2,6},{4,0},{6,2},{1,5},{3,7},{5,1},{7,3},{8,12},{10,14},{12... | collective-permute-start | bytes 860168 | tf_op jit(solution)/shard_map/ppermute | solution.py:12
  44.9 15.7 %collective-permute-start.7 = (bf16[1,40,3584]{2,1,0:T(8,128)(2,1)S(1)}, bf16[1,40,3584]{2,1,0:T(8,128)(2,1)S(1)}, u32[]{:S(2)}, u32[]{:S(2)}) collective-permute-start(bf16[1,40,3584]{2,1,0:T(8,128)(2,1)S(1)} %collective-permute-done.6), channel_id=1, source_target_pairs={{0,2},{2,4},{4,6},{6,0},{1,3},{3,5},{5,7},{7,1},{8,10},{10,12},{12... | collective-permute-start | bytes 860168 | tf_op jit(solution)/shard_map/ppermute | solution.py:12
  66.3 13.5 %collective-permute-start.10 = (bf16[1,40,3584]{2,1,0:T(8,128)(2,1)S(1)}, bf16[1,40,3584]{2,1,0:T(8,128)(2,1)S(1)}, u32[]{:S(2)}, u32[]{:S(2)}) collective-permute-start(bf16[1,40,3584]{2,1,0:T(8,128)(2,1)S(1)} %get-tuple-element.16), channel_id=1, source_target_pairs={{0,6},{2,0},{4,2},{6,4},{1,7},{3,1},{5,3},{7,5},{8,14},{10,8},{12,... | collective-permute-start | bytes 860168 | tf_op jit(solution)/shard_map/ppermute | solution.py:12
  66.4 13.4 %collective-permute-start.12 = (bf16[1,40,3584]{2,1,0:T(8,128)(2,1)S(1)}, bf16[1,40,3584]{2,1,0:T(8,128)(2,1)S(1)}, u32[]{:S(2)}, u32[]{:S(2)}) collective-permute-start(bf16[1,40,3584]{2,1,0:T(8,128)(2,1)S(1)} %get-tuple-element.17), channel_id=1, source_target_pairs={{0,2},{2,4},{4,6},{6,0},{1,3},{3,5},{5,7},{7,1},{8,10},{10,12},{12... | collective-permute-start | bytes 860168 | tf_op jit(solution)/shard_map/ppermute | solution.py:12
  68.4 11.4 %collective-permute-start.11 = (bf16[1,40,3584]{2,1,0:T(8,128)(2,1)S(1)}, bf16[1,40,3584]{2,1,0:T(8,128)(2,1)S(1)}, u32[]{:S(2)}, u32[]{:S(2)}) collective-permute-start(bf16[1,40,3584]{2,1,0:T(8,128)(2,1)S(1)} %get-tuple-element.18), channel_id=1, source_target_pairs={{0,4},{2,6},{4,0},{6,2},{1,5},{3,7},{5,1},{7,3},{8,12},{10,14},{12... | collective-permute-start | bytes 860168 | tf_op jit(solution)/shard_map/ppermute | solution.py:12
  80.0 16.1 %collective-permute-start.16 = (bf16[1,40,3584]{2,1,0:T(8,128)(2,1)S(1)}, bf16[1,40,3584]{2,1,0:T(8,128)(2,1)S(1)}, u32[]{:S(2)}, u32[]{:S(2)}) collective-permute-start(bf16[1,40,3584]{2,1,0:T(8,128)(2,1)S(1)} %fusion.17), channel_id=1, source_target_pairs={{0,8},{8,0},{1,9},{9,1},{2,10},{10,2},{3,11},{11,3},{4,12},{12,4},... | collective-permute-start | bytes 860168 | tf_op jit(solution)/shard_map/ppermute | solution.py:12
  83.7 13.4 %collective-permute-start.13 = (bf16[1,40,3584]{2,1,0:T(8,128)(2,1)S(1)}, bf16[1,40,3584]{2,1,0:T(8,128)(2,1)S(1)}, u32[]{:S(2)}, u32[]{:S(2)}) collective-permute-start(bf16[1,40,3584]{2,1,0:T(8,128)(2,1)S(1)} %get-tuple-element.13), channel_id=1, source_target_pairs={{0,6},{2,0},{4,2},{6,4},{1,7},{3,1},{5,3},{7,5},{8,14},{10,8},{12,... | collective-permute-start | bytes 860168 | tf_op jit(solution)/shard_map/ppermute | solution.py:12
  86.4 15.3 %collective-permute-start.15 = (bf16[1,40,3584]{2,1,0:T(8,128)(2,1)S(1)}, bf16[1,40,3584]{2,1,0:T(8,128)(2,1)S(1)}, u32[]{:S(2)}, u32[]{:S(2)}) collective-permute-start(bf16[1,40,3584]{2,1,0:T(8,128)(2,1)S(1)} %get-tuple-element.14), channel_id=1, source_target_pairs={{0,2},{2,4},{4,6},{6,0},{1,3},{3,5},{5,7},{7,1},{8,10},{10,12},{12... | collective-permute-start | bytes 860168 | tf_op jit(solution)/shard_map/ppermute | solution.py:12
  86.4 17.5 %copy-start.4 = (f32[64,8]{0,1:T(8,128)S(1)}, f32[64,8]{0,1:T(8,128)}, u32[]{:S(2)}) copy-start(f32[64,8]{0,1:T(8,128)} %param.8) | copy-start | bytes 6148
  86.4 17.2 %collective-permute-start.14 = (bf16[1,40,3584]{2,1,0:T(8,128)(2,1)S(1)}, bf16[1,40,3584]{2,1,0:T(8,128)(2,1)S(1)}, u32[]{:S(2)}, u32[]{:S(2)}) collective-permute-start(bf16[1,40,3584]{2,1,0:T(8,128)(2,1)S(1)} %get-tuple-element.15), channel_id=1, source_target_pairs={{0,4},{2,6},{4,0},{6,2},{1,5},{3,7},{5,1},{7,3},{8,12},{10,14},{12... | collective-permute-start | bytes 860168 | tf_op jit(solution)/shard_map/ppermute | solution.py:12
  103.9 2.9 %collective-permute-start.17 = (f32[2,40,3584]{2,1,0:T(8,128)S(1)}, f32[2,40,3584]{2,1,0:T(8,128)S(1)}, u32[]{:S(2)}, u32[]{:S(2)}) collective-permute-start(f32[2,40,3584]{2,1,0:T(8,128)S(1)} %pad_maximum_fusion.4), channel_id=1, source_target_pairs={{0,1},{1,0},{2,3},{3,2},{4,5},{5,4},{6,7},{7,6},{8,9},{9,8},{10,11... | collective-permute-start | bytes 3440648 | tf_op jit(solution)/shard_map/ppermute | solution.py:12

commit v6 on v4

--- a/solution.py
+++ b/solution.py
@@ -10,6 +10,10 @@
 
 def shift(x, axis, size, k):
     return lax.ppermute(x, axis, [(i, (i + k) % size) for i in range(size)])
+
+
+def swap(x, axis, size, k):
+    return lax.ppermute(x, axis, [(i, i ^ k) for i in range(size)])
 
 
 def quarter_rows(rows, w_gate, w_up, w_down, n_ctx):
@@ -78,8 +82,18 @@
     packed = jnp.dot(picker, pair_tokens, preferred_element_type=jnp.float32).astype(jnp.bfloat16)
     packed = packed.reshape(experts, half, width)
 
+    def exchange(x, k):
+        if sharers & (sharers - 1) == 0:
+            return swap(x, "sh", sharers, k)
+        return shift(x, "sh", sharers, k)
+
+    def back_exchange(x, k):
+        if sharers & (sharers - 1) == 0:
+            return swap(x, "sh", sharers, k)
+        return shift(x, "sh", sharers, -k)
+
     def group_partial(sent):
-        group = [sent] + [shift(sent, "sh", sharers, k) for k in range(1, sharers)]
+        group = [sent] + [exchange(sent, k) for k in range(1, sharers)]
         rows = jnp.stack(group).reshape(-1, width)
         partial = quarter_rows(rows, wg, wu, wd, n_ctx).astype(jnp.bfloat16)
         return partial.reshape((sharers,) + sent.shape)
@@ -87,7 +101,7 @@
     def group_sum(partial):
         total = partial[0].astype(jnp.float32)
         for k in range(1, sharers):
-            total = total + shift(partial[k], "sh", sharers, -k).astype(jnp.float32)
+            total = total + back_exchange(partial[k], k).astype(jnp.float32)
         return total
 
     if experts == 2:

time: 92 us -> 91 us (0.989)
  starting transfers between devices: 20.5 us -> 19.4 us
    ppermute x0 -> x12, waiting for transfers between devices: none -> 35.2 us  [swap(): return lax.ppermute(x, axis, [(i, i ^ k) for i in range(size)])]
    ppermute x20 -> x8, waiting for transfers between devices: 57.5 us -> 22.4 us  [shift(): return lax.ppermute(x, axis, [(i, (i + k) % size) for i in range(size)])]
    ppermute x20 -> x8, starting transfers between devices: 20.5 us -> 5.94 us  [shift(): return lax.ppermute(x, axis, [(i, (i + k) % size) for i in range(size)])]
    ppermute x0 -> x12, starting transfers between devices: none -> 13.4 us  [swap(): return lax.ppermute(x, axis, [(i, i ^ k) for i in range(size)])]
  transfers between devices with their start and end apart: 20 -> 20, of which waited for: 13 -> 12; matrix products, arithmetic and copies ran while one was open for 10% -> 10% of each run, Pallas kernels for 0% -> 0%
where the time goes in v6:
time: 91 us; the launch traced here: 90.8 us
  waiting for transfers between devices  57.6 us (63%)
  starting transfers between devices  19.4 us (21%)
  matrix products  8.32 us (9%)
  other arithmetic  3.37 us (4%)
  local copies, waits for them, and re-layouts  1.84 us (2%)
    ppermute x12, waiting for transfers between devices, swap(): return lax.ppermute(x, axis, [(i, i ^ k) for i in range(size)])  35.2 us
    ppermute x8, waiting for transfers between devices, shift(): return lax.ppermute(x, axis, [(i, (i + k) % size) for i in range(size)])  22.4 us
    ppermute x12, starting transfers between devices, swap(): return lax.ppermute(x, axis, [(i, i ^ k) for i in range(size)])  13.4 us
    ppermute x8, starting transfers between devices, shift(): return lax.ppermute(x, axis, [(i, (i + k) % size) for i in range(size)])  5.94 us
    dot_general x1, matrix products, per_device(): jnp.dot(mixing, slots_out, precision=lax.Precision.HIGHEST, preferred_ele...  2.08 us
    dot_general x2, matrix products, quarter_rows(): up = lax.dot_general(rows, w_up, dims, preferred_element_type=jnp.float32)  2.02 us
    dot_general x2, matrix products, quarter_rows(): lax.dot_general(rows, w_gate, dims, preferred_element_type=jnp.float32)  2.01 us
    dot_general x4, matrix products, quarter_rows(): jnp.dot(hidden[:, c * slab:(c + 1) * slab], w_down[c * slab:(c + 1) * sla...  1.92 us
  transfers between devices with their start and end apart: 20, of which 12 were waited for; matrix products, arithmetic and copies ran while one was open for 10% of the time, Pallas kernels for 0%

profile of v6, /device:TPU:0, one launch (start us, length us, event | category | flops | bytes accessed | tf_op | source)
XLA Modules:
  0.0 90.8 jit_solution(15108848987378140078)
XLA Ops:
  0.8 0.7 collective-permute-done
  1.5 0.8 pad_add_fusion.1
  2.7 0.6 reduce-window.6
  5.0 4.0 %collective-permute-start.8 = (bf16[1,40,3584]{2,1,0:T(8,128)(2,1)S(1)}, bf16[1,40,3584]{2,1,0:T(8,128)(2,1)S(1)}, u32[]{:S(2)}, u32[]{:S(2)}) collective-permute-start(bf16[1,40,3584]{2,1,0:T(8,128)(2,1)S(1)} %get-tuple-element.15), channel_id=1, source_target_pairs={{0,8},{8,0},{1,9},{9,1},{2,10},{10,2},{3,11},{11,3},{4,12},{12,4},... | collective-permute-start | bytes 860168 | tf_op jit(solution)/shard_map/ppermute | solution.py:12
  8.9 2.5 %collective-permute-start.4 = (bf16[1,40,3584]{2,1,0:T(8,128)(2,1)S(1)}, bf16[1,40,3584]{2,1,0:T(8,128)(2,1)S(1)}, u32[]{:S(2)}, u32[]{:S(2)}) collective-permute-start(bf16[1,40,3584]{2,1,0:T(8,128)(2,1)S(1)} %get-tuple-element.16), channel_id=1, source_target_pairs={{0,6},{2,4},{4,2},{6,0},{1,7},{3,5},{5,3},{7,1},{8,14},{10,12},{12... | collective-permute-start | bytes 860168 | tf_op jit(solution)/shard_map/ppermute | solution.py:16
  11.9 0.5 collective-permute-start.2
  12.4 9.9 %collective-permute-done.8 = bf16[1,40,3584]{2,1,0:T(8,128)(2,1)S(1)} collective-permute-done((bf16[1,40,3584]{2,1,0:T(8,128)(2,1)S(1)}, bf16[1,40,3584]{2,1,0:T(8,128)(2,1)S(1)}, u32[]{:S(2)}, u32[]{:S(2)}) %collective-permute-start.8) | collective-permute-done | bytes 286752 | tf_op jit(solution)/shard_map/ppermute | solution.py:12
  22.4 2.3 %collective-permute-done.4 = bf16[1,40,3584]{2,1,0:T(8,128)(2,1)S(1)} collective-permute-done((bf16[1,40,3584]{2,1,0:T(8,128)(2,1)S(1)}, bf16[1,40,3584]{2,1,0:T(8,128)(2,1)S(1)}, u32[]{:S(2)}, u32[]{:S(2)}) %collective-permute-start.4) | collective-permute-done | bytes 286752 | tf_op jit(solution)/shard_map/ppermute | solution.py:16
  24.6 1.1 %collective-permute-start.11 = (bf16[1,40,3584]{2,1,0:T(8,128)(2,1)S(1)}, bf16[1,40,3584]{2,1,0:T(8,128)(2,1)S(1)}, u32[]{:S(2)}, u32[]{:S(2)}) collective-permute-start(bf16[1,40,3584]{2,1,0:T(8,128)(2,1)S(1)} %collective-permute-done.8), channel_id=1, source_target_pairs={{0,6},{2,4},{4,2},{6,0},{1,7},{3,5},{5,3},{7,1},{8,14},{10,12},{12... | collective-permute-start | bytes 860168 | tf_op jit(solution)/shard_map/ppermute | solution.py:16
  25.8 5.0 %collective-permute-done.3 = bf16[1,40,3584]{2,1,0:T(8,128)(2,1)S(1)} collective-permute-done((bf16[1,40,3584]{2,1,0:T(8,128)(2,1)S(1)}, bf16[1,40,3584]{2,1,0:T(8,128)(2,1)S(1)}, u32[]{:S(2)}, u32[]{:S(2)}) %collective-permute-start.3) | collective-permute-done | bytes 286752 | tf_op jit(solution)/shard_map/ppermute | solution.py:16
  31.0 1.5 %collective-permute-start.9 = (bf16[1,40,3584]{2,1,0:T(8,128)(2,1)S(1)}, bf16[1,40,3584]{2,1,0:T(8,128)(2,1)S(1)}, u32[]{:S(2)}, u32[]{:S(2)}) collective-permute-start(bf16[1,40,3584]{2,1,0:T(8,128)(2,1)S(1)} %collective-permute-done.8), channel_id=1, source_target_pairs={{0,2},{2,0},{4,6},{6,4},{1,3},{3,1},{5,7},{7,5},{8,10},{10,8},{12,... | collective-permute-start | bytes 860168 | tf_op jit(solution)/shard_map/ppermute | solution.py:16
  32.7 4.3 %collective-permute-done.11 = bf16[1,40,3584]{2,1,0:T(8,128)(2,1)S(1)} collective-permute-done((bf16[1,40,3584]{2,1,0:T(8,128)(2,1)S(1)}, bf16[1,40,3584]{2,1,0:T(8,128)(2,1)S(1)}, u32[]{:S(2)}, u32[]{:S(2)}) %collective-permute-start.11) | collective-permute-done | bytes 286752 | tf_op jit(solution)/shard_map/ppermute | solution.py:16
  37.0 5.0 %collective-permute-done.10 = bf16[1,40,3584]{2,1,0:T(8,128)(2,1)S(1)} collective-permute-done((bf16[1,40,3584]{2,1,0:T(8,128)(2,1)S(1)}, bf16[1,40,3584]{2,1,0:T(8,128)(2,1)S(1)}, u32[]{:S(2)}, u32[]{:S(2)}) %collective-permute-start.10) | collective-permute-done | bytes 286752 | tf_op jit(solution)/shard_map/ppermute | solution.py:16
  42.2 1.0 %fusion.11 = f32[160,320]{1,0:T(8,128)S(1)} fusion(bf16[160,3584]{1,0:T(8,128)(2,1)S(1)} %bitcast.84, bf16[160,3584]{1,0:T(8,128)(2,1)S(1)} %collective-permute-done.5, bf16[160,3584]{1,0:T(8,128)(2,1)S(1)} %bitcast.97), kind=kOutput, calls=%fused_computation.20 | convolution fusion | flops 371589120 | bytes 3645440 | tf_op jit(solution)/shard_map/dot_general | solution.py:21
  43.2 1.0 %multiply_convert_fusion.1 = bf16[160,320]{1,0:T(8,128)(2,1)S(1)} fusion(f32[160,320]{1,0:T(8,128)S(1)} %fusion.11, bf16[160,3584]{1,0:T(8,128)(2,1)S(1)} %bitcast.85, bf16[160,3584]{1,0:T(8,128)(2,1)S(1)} %collective-permute-done.6, bf16[160,3584]{1,0:T(8,128)(2,1)S(1)} %bitcast.100), kind=kOutput, calls=%fused_computation.48 | convolution fusion | flops 371896320 | bytes 3747840 | tf_op jit(solution)/shard_map/dot_general | solution.py:22
  44.2 1.0 %fusion.10 = f32[160,320]{1,0:T(8,128)S(1)} fusion(bf16[160,3584]{1,0:T(8,128)(2,1)S(1)} %bitcast.86, bf16[160,3584]{1,0:T(8,128)(2,1)S(1)} %collective-permute-done.5, bf16[160,3584]{1,0:T(8,128)(2,1)S(1)} %bitcast.98), kind=kOutput, calls=%fused_computation.19 | convolution fusion | flops 371589120 | bytes 3645440 | tf_op jit(solution)/shard_map/dot_general | solution.py:21
  45.7 1.0 %multiply_convert_fusion = bf16[160,320]{1,0:T(8,128)(2,1)S(1)} fusion(f32[160,320]{1,0:T(8,128)S(1)} %fusion.10, bf16[160,3584]{1,0:T(8,128)(2,1)S(1)} %bitcast.87, bf16[160,3584]{1,0:T(8,128)(2,1)S(1)} %collective-permute-done.6, bf16[160,3584]{1,0:T(8,128)(2,1)S(1)} %bitcast.101), kind=kOutput, calls=%fused_computation.47 | convolution fusion | flops 371896320 | bytes 3747840 | tf_op jit(solution)/shard_map/dot_general | solution.py:22
  47.2 0.5 fusion.2
  47.8 1.5 %collective-permute-start.12 = (bf16[1,40,3584]{2,1,0:T(8,128)(2,1)S(1)}, bf16[1,40,3584]{2,1,0:T(8,128)(2,1)S(1)}, u32[]{:S(2)}, u32[]{:S(2)}) collective-permute-start(bf16[1,40,3584]{2,1,0:T(8,128)(2,1)S(1)} %get-tuple-element.12), channel_id=1, source_target_pairs={{0,2},{2,0},{4,6},{6,4},{1,3},{3,1},{5,7},{7,5},{8,10},{10,8},{12,... | collective-permute-start | bytes 860168 | tf_op jit(solution)/shard_map/ppermute | solution.py:16
  49.2 1.5 %collective-permute-start.14 = (bf16[1,40,3584]{2,1,0:T(8,128)(2,1)S(1)}, bf16[1,40,3584]{2,1,0:T(8,128)(2,1)S(1)}, u32[]{:S(2)}, u32[]{:S(2)}) collective-permute-start(bf16[1,40,3584]{2,1,0:T(8,128)(2,1)S(1)} %get-tuple-element.13), channel_id=1, source_target_pairs={{0,6},{2,4},{4,2},{6,0},{1,7},{3,5},{5,3},{7,1},{8,14},{10,12},{12... | collective-permute-start | bytes 860168 | tf_op jit(solution)/shard_map/ppermute | solution.py:16
  50.7 0.6 collective-permute-start.13
  51.8 10.9 %collective-permute-done.12 = bf16[1,40,3584]{2,1,0:T(8,128)(2,1)S(1)} collective-permute-done((bf16[1,40,3584]{2,1,0:T(8,128)(2,1)S(1)}, bf16[1,40,3584]{2,1,0:T(8,128)(2,1)S(1)}, u32[]{:S(2)}, u32[]{:S(2)}) %collective-permute-start.12) | collective-permute-done | bytes 286752 | tf_op jit(solution)/shard_map/ppermute | solution.py:16
  62.7 1.2 %collective-permute-done.13 = bf16[1,40,3584]{2,1,0:T(8,128)(2,1)S(1)} collective-permute-done((bf16[1,40,3584]{2,1,0:T(8,128)(2,1)S(1)}, bf16[1,40,3584]{2,1,0:T(8,128)(2,1)S(1)}, u32[]{:S(2)}, u32[]{:S(2)}) %collective-permute-start.13) | collective-permute-done | bytes 286752 | tf_op jit(solution)/shard_map/ppermute | solution.py:16
  64.1 1.4 %collective-permute-start.18 = (bf16[1,40,3584]{2,1,0:T(8,128)(2,1)S(1)}, bf16[1,40,3584]{2,1,0:T(8,128)(2,1)S(1)}, u32[]{:S(2)}, u32[]{:S(2)}) collective-permute-start(bf16[1,40,3584]{2,1,0:T(8,128)(2,1)S(1)} %fusion.18), channel_id=1, source_target_pairs={{0,8},{8,0},{1,9},{9,1},{2,10},{10,2},{3,11},{11,3},{4,12},{12,4},... | collective-permute-start | bytes 860168 | tf_op jit(solution)/shard_map/ppermute | solution.py:12
  65.5 0.8 collective-permute-start.15
  66.3 2.5 %collective-permute-start.17 = (bf16[1,40,3584]{2,1,0:T(8,128)(2,1)S(1)}, bf16[1,40,3584]{2,1,0:T(8,128)(2,1)S(1)}, u32[]{:S(2)}, u32[]{:S(2)}) collective-permute-start(bf16[1,40,3584]{2,1,0:T(8,128)(2,1)S(1)} %get-tuple-element.10), channel_id=1, source_target_pairs={{0,6},{2,4},{4,2},{6,0},{1,7},{3,5},{5,3},{7,1},{8,14},{10,12},{12... | collective-permute-start | bytes 860168 | tf_op jit(solution)/shard_map/ppermute | solution.py:16
  69.0 9.8 %collective-permute-done.18 = bf16[1,40,3584]{2,1,0:T(8,128)(2,1)S(1)} collective-permute-done((bf16[1,40,3584]{2,1,0:T(8,128)(2,1)S(1)}, bf16[1,40,3584]{2,1,0:T(8,128)(2,1)S(1)}, u32[]{:S(2)}, u32[]{:S(2)}) %collective-permute-start.18) | collective-permute-done | bytes 286752 | tf_op jit(solution)/shard_map/ppermute | solution.py:12
  78.9 4.1 %collective-permute-done.17 = bf16[1,40,3584]{2,1,0:T(8,128)(2,1)S(1)} collective-permute-done((bf16[1,40,3584]{2,1,0:T(8,128)(2,1)S(1)}, bf16[1,40,3584]{2,1,0:T(8,128)(2,1)S(1)}, u32[]{:S(2)}, u32[]{:S(2)}) %collective-permute-start.17) | collective-permute-done | bytes 286752 | tf_op jit(solution)/shard_map/ppermute | solution.py:16
  83.0 2.4 %collective-permute-done.16 = bf16[1,40,3584]{2,1,0:T(8,128)(2,1)S(1)} collective-permute-done((bf16[1,40,3584]{2,1,0:T(8,128)(2,1)S(1)}, bf16[1,40,3584]{2,1,0:T(8,128)(2,1)S(1)}, u32[]{:S(2)}, u32[]{:S(2)}) %collective-permute-start.16) | collective-permute-done | bytes 286752 | tf_op jit(solution)/shard_map/ppermute | solution.py:16
  85.7 0.5 copy-done.2
  86.7 1.9 %collective-permute-done.19 = f32[2,40,3584]{2,1,0:T(8,128)S(1)} collective-permute-done((f32[2,40,3584]{2,1,0:T(8,128)S(1)}, f32[2,40,3584]{2,1,0:T(8,128)S(1)}, u32[]{:S(2)}, u32[]{:S(2)}) %collective-permute-start.19) | collective-permute-done | bytes 1146912 | tf_op jit(solution)/shard_map/ppermute | solution.py:12
  88.7 2.1 %convolution_convert_fusion.5 = bf16[64,3584]{1,0:T(8,128)(2,1)} fusion(f32[64,160]{1,0:T(8,128)S(1)} %select_reduce_fusion, f32[160,3584]{1,0:T(8,128)S(1)} %bitcast.80), kind=kOutput, calls=%fused_computation.13 | convolution fusion | flops 440631296 | bytes 2793472 | tf_op jit(solution)/shard_map/dot_general | solution.py:136
  (66 shorter events, 6.6 us)
Async XLA Ops:
  0.0 4.6 %copy-start.1 = (bf16[64,3584]{1,0:T(8,128)(2,1)S(1)}, bf16[64,3584]{1,0:T(8,128)(2,1)}, u32[]{:S(2)}) copy-start(bf16[64,3584]{1,0:T(8,128)(2,1)} %param.6) | copy-start | bytes 1376260
  0.0 1.5 %collective-permute-start = (s32[64,8]{0,1:T(8,128)}, s32[64,8]{0,1:T(8,128)S(1)}, u32[]{:S(2)}, u32[]{:S(2)}) collective-permute-start(s32[64,8]{0,1:T(8,128)} %param.7), channel_id=1, source_target_pairs={{0,1},{1,0},{2,3},{3,2},{4,5},{5,4},{6,7},{7,6},{8,9},{9,8},{10,11... | collective-permute-start | bytes 6152 | tf_op jit(solution)/shard_map/ppermute | solution.py:12
  0.5 4.1 %collective-permute-start.1 = (bf16[64,3584]{1,0:T(8,128)(2,1)}, bf16[64,3584]{1,0:T(8,128)(2,1)S(1)}, u32[]{:S(2)}, u32[]{:S(2)}) collective-permute-start(bf16[64,3584]{1,0:T(8,128)(2,1)} %param.6), channel_id=1, source_target_pairs={{0,1},{1,0},{2,3},{3,2},{4,5},{5,4},{6,7},{7,6},{8,9},{9,8},{10,11... | collective-permute-start | bytes 1376264 | tf_op jit(solution)/shard_map/ppermute | solution.py:12
  4.5 7.9 %copy-start.3 = (bf16[1,160,3584]{2,1,0:T(8,128)(2,1)S(1)}, bf16[1,160,3584]{2,1,0:T(8,128)(2,1)}, u32[]{:S(2)}) copy-start(bf16[1,160,3584]{2,1,0:T(8,128)(2,1)} %param.9) | copy-start | bytes 3440644
  4.6 17.8 %copy-start.4 = (bf16[1,160,3584]{2,1,0:T(8,128)(2,1)S(1)}, bf16[1,160,3584]{2,1,0:T(8,128)(2,1)}, u32[]{:S(2)}) copy-start(bf16[1,160,3584]{2,1,0:T(8,128)(2,1)} %param.10) | copy-start | bytes 3440644
  5.0 17.4 %collective-permute-start.8 = (bf16[1,40,3584]{2,1,0:T(8,128)(2,1)S(1)}, bf16[1,40,3584]{2,1,0:T(8,128)(2,1)S(1)}, u32[]{:S(2)}, u32[]{:S(2)}) collective-permute-start(bf16[1,40,3584]{2,1,0:T(8,128)(2,1)S(1)} %get-tuple-element.15), channel_id=1, source_target_pairs={{0,8},{8,0},{1,9},{9,1},{2,10},{10,2},{3,11},{11,3},{4,12},{12,4},... | collective-permute-start | bytes 860168 | tf_op jit(solution)/shard_map/ppermute | solution.py:12
  8.9 15.7 %collective-permute-start.4 = (bf16[1,40,3584]{2,1,0:T(8,128)(2,1)S(1)}, bf16[1,40,3584]{2,1,0:T(8,128)(2,1)S(1)}, u32[]{:S(2)}, u32[]{:S(2)}) collective-permute-start(bf16[1,40,3584]{2,1,0:T(8,128)(2,1)S(1)} %get-tuple-element.16), channel_id=1, source_target_pairs={{0,6},{2,4},{4,2},{6,0},{1,7},{3,5},{5,3},{7,1},{8,14},{10,12},{12... | collective-permute-start | bytes 860168 | tf_op jit(solution)/shard_map/ppermute | solution.py:16
  11.5 19.3 %collective-permute-start.3 = (bf16[1,40,3584]{2,1,0:T(8,128)(2,1)S(1)}, bf16[1,40,3584]{2,1,0:T(8,128)(2,1)S(1)}, u32[]{:S(2)}, u32[]{:S(2)}) collective-permute-start(bf16[1,40,3584]{2,1,0:T(8,128)(2,1)S(1)} %get-tuple-element.16), channel_id=1, source_target_pairs={{0,4},{2,6},{4,0},{6,2},{1,5},{3,7},{5,1},{7,3},{8,12},{10,14},{12... | collective-permute-start | bytes 860168 | tf_op jit(solution)/shard_map/ppermute | solution.py:16
  11.9 19.1 %collective-permute-start.2 = (bf16[1,40,3584]{2,1,0:T(8,128)(2,1)S(1)}, bf16[1,40,3584]{2,1,0:T(8,128)(2,1)S(1)}, u32[]{:S(2)}, u32[]{:S(2)}) collective-permute-start(bf16[1,40,3584]{2,1,0:T(8,128)(2,1)S(1)} %get-tuple-element.16), channel_id=1, source_target_pairs={{0,2},{2,0},{4,6},{6,4},{1,3},{3,1},{5,7},{7,5},{8,10},{10,8},{12,... | collective-permute-start | bytes 860168 | tf_op jit(solution)/shard_map/ppermute | solution.py:16
  12.4 29.7 %collective-permute-start.5 = (bf16[160,3584]{1,0:T(8,128)(2,1)S(1)}, bf16[160,3584]{1,0:T(8,128)(2,1)S(1)}, u32[]{:S(2)}, u32[]{:S(2)}) collective-permute-start(bf16[160,3584]{1,0:T(8,128)(2,1)S(1)} %bitcast.96), channel_id=1, source_target_pairs={{0,1},{1,0},{2,3},{3,2},{4,5},{5,4},{6,7},{7,6},{8,9},{9,8},{10,11... | collective-permute-start | bytes 3440648 | tf_op jit(solution)/shard_map/ppermute | solution.py:12
  22.4 20.8 %collective-permute-start.6 = (bf16[160,3584]{1,0:T(8,128)(2,1)S(1)}, bf16[160,3584]{1,0:T(8,128)(2,1)S(1)}, u32[]{:S(2)}, u32[]{:S(2)}) collective-permute-start(bf16[160,3584]{1,0:T(8,128)(2,1)S(1)} %bitcast.99), channel_id=1, source_target_pairs={{0,1},{1,0},{2,3},{3,2},{4,5},{5,4},{6,7},{7,6},{8,9},{9,8},{10,11... | collective-permute-start | bytes 3440648 | tf_op jit(solution)/shard_map/ppermute | solution.py:12
  24.6 12.3 %collective-permute-start.11 = (bf16[1,40,3584]{2,1,0:T(8,128)(2,1)S(1)}, bf16[1,40,3584]{2,1,0:T(8,128)(2,1)S(1)}, u32[]{:S(2)}, u32[]{:S(2)}) collective-permute-start(bf16[1,40,3584]{2,1,0:T(8,128)(2,1)S(1)} %collective-permute-done.8), channel_id=1, source_target_pairs={{0,6},{2,4},{4,2},{6,0},{1,7},{3,5},{5,3},{7,1},{8,14},{10,12},{12... | collective-permute-start | bytes 860168 | tf_op jit(solution)/shard_map/ppermute | solution.py:16
  30.8 11.2 %collective-permute-start.10 = (bf16[1,40,3584]{2,1,0:T(8,128)(2,1)S(1)}, bf16[1,40,3584]{2,1,0:T(8,128)(2,1)S(1)}, u32[]{:S(2)}, u32[]{:S(2)}) collective-permute-start(bf16[1,40,3584]{2,1,0:T(8,128)(2,1)S(1)} %collective-permute-done.8), channel_id=1, source_target_pairs={{0,4},{2,6},{4,0},{6,2},{1,5},{3,7},{5,1},{7,3},{8,12},{10,14},{12... | collective-permute-start | bytes 860168 | tf_op jit(solution)/shard_map/ppermute | solution.py:16
  31.0 11.0 %collective-permute-start.9 = (bf16[1,40,3584]{2,1,0:T(8,128)(2,1)S(1)}, bf16[1,40,3584]{2,1,0:T(8,128)(2,1)S(1)}, u32[]{:S(2)}, u32[]{:S(2)}) collective-permute-start(bf16[1,40,3584]{2,1,0:T(8,128)(2,1)S(1)} %collective-permute-done.8), channel_id=1, source_target_pairs={{0,2},{2,0},{4,6},{6,4},{1,3},{3,1},{5,7},{7,5},{8,10},{10,8},{12,... | collective-permute-start | bytes 860168 | tf_op jit(solution)/shard_map/ppermute | solution.py:16
  32.5 4.5 %copy-start = (bf16[1,160,3584]{2,1,0:T(8,128)(2,1)S(1)}, bf16[1,160,3584]{2,1,0:T(8,128)(2,1)}, u32[]{:S(2)}) copy-start(bf16[1,160,3584]{2,1,0:T(8,128)(2,1)} %param.11) | copy-start | bytes 3440644
  37.0 10.2 %collective-permute-start.7 = (bf16[160,3584]{1,0:T(8,128)(2,1)S(1)}, bf16[160,3584]{1,0:T(8,128)(2,1)S(1)}, u32[]{:S(2)}, u32[]{:S(2)}) collective-permute-start(bf16[160,3584]{1,0:T(8,128)(2,1)S(1)} %bitcast.81), channel_id=1, source_target_pairs={{0,1},{1,0},{2,3},{3,2},{4,5},{5,4},{6,7},{7,6},{8,9},{9,8},{10,11... | collective-permute-start | bytes 3440648 | tf_op jit(solution)/shard_map/ppermute | solution.py:12
  47.8 14.9 %collective-permute-start.12 = (bf16[1,40,3584]{2,1,0:T(8,128)(2,1)S(1)}, bf16[1,40,3584]{2,1,0:T(8,128)(2,1)S(1)}, u32[]{:S(2)}, u32[]{:S(2)}) collective-permute-start(bf16[1,40,3584]{2,1,0:T(8,128)(2,1)S(1)} %get-tuple-element.12), channel_id=1, source_target_pairs={{0,2},{2,0},{4,6},{6,4},{1,3},{3,1},{5,7},{7,5},{8,10},{10,8},{12,... | collective-permute-start | bytes 860168 | tf_op jit(solution)/shard_map/ppermute | solution.py:16
  49.2 13.5 %collective-permute-start.14 = (bf16[1,40,3584]{2,1,0:T(8,128)(2,1)S(1)}, bf16[1,40,3584]{2,1,0:T(8,128)(2,1)S(1)}, u32[]{:S(2)}, u32[]{:S(2)}) collective-permute-start(bf16[1,40,3584]{2,1,0:T(8,128)(2,1)S(1)} %get-tuple-element.13), channel_id=1, source_target_pairs={{0,6},{2,4},{4,2},{6,0},{1,7},{3,5},{5,3},{7,1},{8,14},{10,12},{12... | collective-permute-start | bytes 860168 | tf_op jit(solution)/shard_map/ppermute | solution.py:16
  50.7 13.2 %collective-permute-start.13 = (bf16[1,40,3584]{2,1,0:T(8,128)(2,1)S(1)}, bf16[1,40,3584]{2,1,0:T(8,128)(2,1)S(1)}, u32[]{:S(2)}, u32[]{:S(2)}) collective-permute-start(bf16[1,40,3584]{2,1,0:T(8,128)(2,1)S(1)} %get-tuple-element.14), channel_id=1, source_target_pairs={{0,4},{2,6},{4,0},{6,2},{1,5},{3,7},{5,1},{7,3},{8,12},{10,14},{12... | collective-permute-start | bytes 860168 | tf_op jit(solution)/shard_map/ppermute | solution.py:16
  64.1 14.8 %collective-permute-start.18 = (bf16[1,40,3584]{2,1,0:T(8,128)(2,1)S(1)}, bf16[1,40,3584]{2,1,0:T(8,128)(2,1)S(1)}, u32[]{:S(2)}, u32[]{:S(2)}) collective-permute-start(bf16[1,40,3584]{2,1,0:T(8,128)(2,1)S(1)} %fusion.18), channel_id=1, source_target_pairs={{0,8},{8,0},{1,9},{9,1},{2,10},{10,2},{3,11},{11,3},{4,12},{12,4},... | collective-permute-start | bytes 860168 | tf_op jit(solution)/shard_map/ppermute | solution.py:12
  65.5 13.4 %collective-permute-start.15 = (bf16[1,40,3584]{2,1,0:T(8,128)(2,1)S(1)}, bf16[1,40,3584]{2,1,0:T(8,128)(2,1)S(1)}, u32[]{:S(2)}, u32[]{:S(2)}) collective-permute-start(bf16[1,40,3584]{2,1,0:T(8,128)(2,1)S(1)} %get-tuple-element.9), channel_id=1, source_target_pairs={{0,2},{2,0},{4,6},{6,4},{1,3},{3,1},{5,7},{7,5},{8,10},{10,8},{12,... | collective-permute-start | bytes 860168 | tf_op jit(solution)/shard_map/ppermute | solution.py:16
  66.3 16.7 %collective-permute-start.17 = (bf16[1,40,3584]{2,1,0:T(8,128)(2,1)S(1)}, bf16[1,40,3584]{2,1,0:T(8,128)(2,1)S(1)}, u32[]{:S(2)}, u32[]{:S(2)}) collective-permute-start(bf16[1,40,3584]{2,1,0:T(8,128)(2,1)S(1)} %get-tuple-element.10), channel_id=1, source_target_pairs={{0,6},{2,4},{4,2},{6,0},{1,7},{3,5},{5,3},{7,1},{8,14},{10,12},{12... | collective-permute-start | bytes 860168 | tf_op jit(solution)/shard_map/ppermute | solution.py:16
  68.7 16.7 %collective-permute-start.16 = (bf16[1,40,3584]{2,1,0:T(8,128)(2,1)S(1)}, bf16[1,40,3584]{2,1,0:T(8,128)(2,1)S(1)}, u32[]{:S(2)}, u32[]{:S(2)}) collective-permute-start(bf16[1,40,3584]{2,1,0:T(8,128)(2,1)S(1)} %get-tuple-element.11), channel_id=1, source_target_pairs={{0,4},{2,6},{4,0},{6,2},{1,5},{3,7},{5,1},{7,3},{8,12},{10,14},{12... | collective-permute-start | bytes 860168 | tf_op jit(solution)/shard_map/ppermute | solution.py:16
  85.5 0.7 copy-start.2
  85.6 2.9 %collective-permute-start.19 = (f32[2,40,3584]{2,1,0:T(8,128)S(1)}, f32[2,40,3584]{2,1,0:T(8,128)S(1)}, u32[]{:S(2)}, u32[]{:S(2)}) collective-permute-start(f32[2,40,3584]{2,1,0:T(8,128)S(1)} %pad_maximum_fusion.9), channel_id=1, source_target_pairs={{0,1},{1,0},{2,3},{3,2},{4,5},{5,4},{6,7},{7,6},{8,9},{9,8},{10,11... | collective-permute-start | bytes 3440648 | tf_op jit(solution)/shard_map/ppermute | solution.py:12

commit v7 on v6

--- a/solution.py
+++ b/solution.py
@@ -105,12 +105,15 @@
         return total
 
     if experts == 2:
+        cut = half // 2 + (half // 2) % 8 if half >= 16 else half
+        pieces = [(0, cut)] + ([(cut, half)] if cut < half else [])
         local_part = group_partial(packed[0:1])
-        far_part = group_partial(shift(packed[1:2], "ex", 2, 1))
-        far_out = group_sum(far_part)
+        far_out = [
+            group_sum(group_partial(shift(packed[1:2, lo:hi], "ex", 2, 1))) for lo, hi in pieces
+        ]
         local_part, far_out = lax.optimization_barrier((local_part, far_out))
-        back = shift(far_out.astype(RETURN_DTYPE), "ex", 2, 1).astype(jnp.float32)
-        mine = jnp.concatenate([group_sum(local_part), back], axis=0)
+        back = [shift(o.astype(RETURN_DTYPE), "ex", 2, 1).astype(jnp.float32) for o in far_out]
+        mine = jnp.concatenate([group_sum(local_part), jnp.concatenate(back, axis=1)], axis=0)
     else:
         sent = lax.all_to_all(packed, "ex", split_axis=0, concat_axis=0, tiled=True)
         expert_out = group_sum(group_partial(sent)).astype(RETURN_DTYPE)

time: 91 us -> 97.7 us (1.074)
  starting transfers between devices: 19.4 us -> 29.4 us
  waiting for transfers between devices: 57.6 us -> 52.4 us
  matrix products: 8.32 us -> 10.1 us
    ppermute x12 -> x18, starting transfers between devices: 13.4 us -> 21.8 us  [swap(): return lax.ppermute(x, axis, [(i, i ^ k) for i in range(size)])]
    ppermute x12 -> x18, waiting for transfers between devices: 35.2 us -> 27.1 us  [swap(): return lax.ppermute(x, axis, [(i, i ^ k) for i in range(size)])]
    ppermute x8 -> x10, waiting for transfers between devices: 22.4 us -> 25.3 us  [shift(): return lax.ppermute(x, axis, [(i, (i + k) % size) for i in range(size)])]
    ppermute x8 -> x10, starting transfers between devices: 5.94 us -> 7.58 us  [shift(): return lax.ppermute(x, axis, [(i, (i + k) % size) for i in range(size)])]
    dot_general x2 -> x3, matrix products: 2.02 us -> 2.68 us  [quarter_rows(): up = lax.dot_general(rows, w_up, dims, preferred_element_type=jnp.float32)]
    dot_general x2 -> x3, matrix products: 2.01 us -> 2.67 us  [quarter_rows(): lax.dot_general(rows, w_gate, dims, preferred_element_type=jnp.float32)]
    dot_general x4 -> x6, matrix products: 1.92 us -> 2.38 us  [quarter_rows(): jnp.dot(hidden[:, c * slab:(c + 1) * slab], w_down[c * slab:(c + 1) * sla...]
  transfers between devices with their start and end apart: 20 -> 28, of which waited for: 12 -> 16; matrix products, arithmetic and copies ran while one was open for 10% -> 12% of each run, Pallas kernels for 0% -> 0%
where the time goes in v7:
time: 97.7 us; the launch traced here: 97.5 us
  waiting for transfers between devices  52.4 us (54%)
  starting transfers between devices  29.4 us (30%)
  matrix products  10.1 us (10%)
  other arithmetic  3.38 us (3%)
  local copies, waits for them, and re-layouts  1.84 us (2%)
    ppermute x18, waiting for transfers between devices, swap(): return lax.ppermute(x, axis, [(i, i ^ k) for i in range(size)])  27.1 us
    ppermute x10, waiting for transfers between devices, shift(): return lax.ppermute(x, axis, [(i, (i + k) % size) for i in range(size)])  25.3 us
    ppermute x18, starting transfers between devices, swap(): return lax.ppermute(x, axis, [(i, i ^ k) for i in range(size)])  21.8 us
    ppermute x10, starting transfers between devices, shift(): return lax.ppermute(x, axis, [(i, (i + k) % size) for i in range(size)])  7.58 us
    dot_general x3, matrix products, quarter_rows(): up = lax.dot_general(rows, w_up, dims, preferred_element_type=jnp.float32)  2.68 us
    dot_general x3, matrix products, quarter_rows(): lax.dot_general(rows, w_gate, dims, preferred_element_type=jnp.float32)  2.67 us
    dot_general x6, matrix products, quarter_rows(): jnp.dot(hidden[:, c * slab:(c + 1) * slab], w_down[c * slab:(c + 1) * sla...  2.38 us
    dot_general x1, matrix products, per_device(): jnp.dot(mixing, slots_out, precision=lax.Precision.HIGHEST, preferred_ele...  2.08 us
  transfers between devices with their start and end apart: 28, of which 16 were waited for; matrix products, arithmetic and copies ran while one was open for 12% of the time, Pallas kernels for 0%

profile of v7, /device:TPU:0, one launch (start us, length us, event | category | flops | bytes accessed | tf_op | source)
XLA Modules:
  0.0 97.5 jit_solution(5377919956997813478)
XLA Ops:
  1.5 0.8 pad_add_fusion.1
  4.9 4.0 %collective-permute-start.15 = (bf16[1,16,3584]{2,1,0:T(8,128)(2,1)S(1)}, bf16[1,16,3584]{2,1,0:T(8,128)(2,1)S(1)}, u32[]{:S(2)}, u32[]{:S(2)}) collective-permute-start(bf16[1,16,3584]{2,1,0:T(8,128)(2,1)S(1)} %slice.136), channel_id=1, source_target_pairs={{0,8},{8,0},{1,9},{9,1},{2,10},{10,2},{3,11},{11,3},{4,12},{12,4},... | collective-permute-start | bytes 344072 | tf_op jit(solution)/shard_map/ppermute | solution.py:12
  8.9 5.9 %collective-permute-done.15 = bf16[1,16,3584]{2,1,0:T(8,128)(2,1)S(1)} collective-permute-done((bf16[1,16,3584]{2,1,0:T(8,128)(2,1)S(1)}, bf16[1,16,3584]{2,1,0:T(8,128)(2,1)S(1)}, u32[]{:S(2)}, u32[]{:S(2)}) %collective-permute-start.15) | collective-permute-done | bytes 114720 | tf_op jit(solution)/shard_map/ppermute | solution.py:12
  14.8 1.7 %collective-permute-start.18 = (bf16[1,16,3584]{2,1,0:T(8,128)(2,1)S(1)}, bf16[1,16,3584]{2,1,0:T(8,128)(2,1)S(1)}, u32[]{:S(2)}, u32[]{:S(2)}) collective-permute-start(bf16[1,16,3584]{2,1,0:T(8,128)(2,1)S(1)} %collective-permute-done.15), channel_id=1, source_target_pairs={{0,6},{2,4},{4,2},{6,0},{1,7},{3,5},{5,3},{7,1},{8,14},{10,12},{12... | collective-permute-start | bytes 344072 | tf_op jit(solution)/shard_map/ppermute | solution.py:16
  16.5 1.3 %collective-permute-start.17 = (bf16[1,16,3584]{2,1,0:T(8,128)(2,1)S(1)}, bf16[1,16,3584]{2,1,0:T(8,128)(2,1)S(1)}, u32[]{:S(2)}, u32[]{:S(2)}) collective-permute-start(bf16[1,16,3584]{2,1,0:T(8,128)(2,1)S(1)} %collective-permute-done.15), channel_id=1, source_target_pairs={{0,4},{2,6},{4,0},{6,2},{1,5},{3,7},{5,1},{7,3},{8,12},{10,14},{12... | collective-permute-start | bytes 344072 | tf_op jit(solution)/shard_map/ppermute | solution.py:16
  18.4 1.7 %collective-permute-start.4 = (bf16[1,40,3584]{2,1,0:T(8,128)(2,1)S(1)}, bf16[1,40,3584]{2,1,0:T(8,128)(2,1)S(1)}, u32[]{:S(2)}, u32[]{:S(2)}) collective-permute-start(bf16[1,40,3584]{2,1,0:T(8,128)(2,1)S(1)} %get-tuple-element.18), channel_id=1, source_target_pairs={{0,6},{2,4},{4,2},{6,0},{1,7},{3,5},{5,3},{7,1},{8,14},{10,12},{12... | collective-permute-start | bytes 860168 | tf_op jit(solution)/shard_map/ppermute | solution.py:16
  20.1 1.8 %collective-permute-done.18 = bf16[1,16,3584]{2,1,0:T(8,128)(2,1)S(1)} collective-permute-done((bf16[1,16,3584]{2,1,0:T(8,128)(2,1)S(1)}, bf16[1,16,3584]{2,1,0:T(8,128)(2,1)S(1)}, u32[]{:S(2)}, u32[]{:S(2)}) %collective-permute-start.18) | collective-permute-done | bytes 114720 | tf_op jit(solution)/shard_map/ppermute | solution.py:16
  22.5 1.9 %collective-permute-done.17 = bf16[1,16,3584]{2,1,0:T(8,128)(2,1)S(1)} collective-permute-done((bf16[1,16,3584]{2,1,0:T(8,128)(2,1)S(1)}, bf16[1,16,3584]{2,1,0:T(8,128)(2,1)S(1)}, u32[]{:S(2)}, u32[]{:S(2)}) %collective-permute-start.17) | collective-permute-done | bytes 114720 | tf_op jit(solution)/shard_map/ppermute | solution.py:16
  24.8 2.8 %collective-permute-done.16 = bf16[1,16,3584]{2,1,0:T(8,128)(2,1)S(1)} collective-permute-done((bf16[1,16,3584]{2,1,0:T(8,128)(2,1)S(1)}, bf16[1,16,3584]{2,1,0:T(8,128)(2,1)S(1)}, u32[]{:S(2)}, u32[]{:S(2)}) %collective-permute-start.16) | collective-permute-done | bytes 114720 | tf_op jit(solution)/shard_map/ppermute | solution.py:16
  27.7 9.9 %collective-permute-done.8 = bf16[1,24,3584]{2,1,0:T(8,128)(2,1)S(1)} collective-permute-done((bf16[1,24,3584]{2,1,0:T(8,128)(2,1)S(1)}, bf16[1,24,3584]{2,1,0:T(8,128)(2,1)S(1)}, u32[]{:S(2)}, u32[]{:S(2)}) %collective-permute-start.8) | collective-permute-done | bytes 172064 | tf_op jit(solution)/shard_map/ppermute | solution.py:12
  37.6 4.2 %collective-permute-start.11 = (bf16[1,24,3584]{2,1,0:T(8,128)(2,1)S(1)}, bf16[1,24,3584]{2,1,0:T(8,128)(2,1)S(1)}, u32[]{:S(2)}, u32[]{:S(2)}) collective-permute-start(bf16[1,24,3584]{2,1,0:T(8,128)(2,1)S(1)} %collective-permute-done.8), channel_id=1, source_target_pairs={{0,6},{2,4},{4,2},{6,0},{1,7},{3,5},{5,3},{7,1},{8,14},{10,12},{12... | collective-permute-start | bytes 516104 | tf_op jit(solution)/shard_map/ppermute | solution.py:16
  42.6 4.5 %collective-permute-done.11 = bf16[1,24,3584]{2,1,0:T(8,128)(2,1)S(1)} collective-permute-done((bf16[1,24,3584]{2,1,0:T(8,128)(2,1)S(1)}, bf16[1,24,3584]{2,1,0:T(8,128)(2,1)S(1)}, u32[]{:S(2)}, u32[]{:S(2)}) %collective-permute-start.11) | collective-permute-done | bytes 172064 | tf_op jit(solution)/shard_map/ppermute | solution.py:16
  47.0 2.7 %collective-permute-done.10 = bf16[1,24,3584]{2,1,0:T(8,128)(2,1)S(1)} collective-permute-done((bf16[1,24,3584]{2,1,0:T(8,128)(2,1)S(1)}, bf16[1,24,3584]{2,1,0:T(8,128)(2,1)S(1)}, u32[]{:S(2)}, u32[]{:S(2)}) %collective-permute-start.10) | collective-permute-done | bytes 172064 | tf_op jit(solution)/shard_map/ppermute | solution.py:16
  51.4 0.8 multiply_convert_fusion.2
  53.6 2.6 %collective-permute-start.21 = (bf16[1,16,3584]{2,1,0:T(8,128)(2,1)S(1)}, bf16[1,16,3584]{2,1,0:T(8,128)(2,1)S(1)}, u32[]{:S(2)}, u32[]{:S(2)}) collective-permute-start(bf16[1,16,3584]{2,1,0:T(8,128)(2,1)S(1)} %get-tuple-element.20), channel_id=1, source_target_pairs={{0,6},{2,4},{4,2},{6,0},{1,7},{3,5},{5,3},{7,1},{8,14},{10,12},{12... | collective-permute-start | bytes 344072 | tf_op jit(solution)/shard_map/ppermute | solution.py:16
  56.4 0.9 fusion.19
  57.3 0.9 multiply_convert_fusion.1
  59.0 1.2 %collective-permute-start.12 = (bf16[1,24,3584]{2,1,0:T(8,128)(2,1)S(1)}, bf16[1,24,3584]{2,1,0:T(8,128)(2,1)S(1)}, u32[]{:S(2)}, u32[]{:S(2)}) collective-permute-start(bf16[1,24,3584]{2,1,0:T(8,128)(2,1)S(1)} %get-tuple-element.14), channel_id=1, source_target_pairs={{0,2},{2,0},{4,6},{6,4},{1,3},{3,1},{5,7},{7,5},{8,10},{10,8},{12,... | collective-permute-start | bytes 516104 | tf_op jit(solution)/shard_map/ppermute | solution.py:16
  60.2 2.1 %collective-permute-start.14 = (bf16[1,24,3584]{2,1,0:T(8,128)(2,1)S(1)}, bf16[1,24,3584]{2,1,0:T(8,128)(2,1)S(1)}, u32[]{:S(2)}, u32[]{:S(2)}) collective-permute-start(bf16[1,24,3584]{2,1,0:T(8,128)(2,1)S(1)} %get-tuple-element.15), channel_id=1, source_target_pairs={{0,6},{2,4},{4,2},{6,0},{1,7},{3,5},{5,3},{7,1},{8,14},{10,12},{12... | collective-permute-start | bytes 516104 | tf_op jit(solution)/shard_map/ppermute | solution.py:16
  62.3 1.0 %fusion.20 = f32[160,320]{1,0:T(8,128)S(1)} fusion(bf16[160,3584]{1,0:T(8,128)(2,1)S(1)} %bitcast.106, bf16[160,3584]{1,0:T(8,128)(2,1)S(1)} %collective-permute-done.5, bf16[160,3584]{1,0:T(8,128)(2,1)S(1)} %bitcast.127), kind=kOutput, calls=%fused_computation.34 | convolution fusion | flops 371589120 | bytes 3645440 | tf_op jit(solution)/shard_map/dot_general | solution.py:21
  63.3 1.0 %multiply_convert_fusion = bf16[160,320]{1,0:T(8,128)(2,1)S(1)} fusion(f32[160,320]{1,0:T(8,128)S(1)} %fusion.20, bf16[160,3584]{1,0:T(8,128)(2,1)S(1)} %bitcast.107, bf16[160,3584]{1,0:T(8,128)(2,1)S(1)} %collective-permute-done.6, bf16[160,3584]{1,0:T(8,128)(2,1)S(1)} %bitcast.131), kind=kOutput, calls=%fused_computation.52 | convolution fusion | flops 371896320 | bytes 3747840 | tf_op jit(solution)/shard_map/dot_general | solution.py:22
  65.7 2.5 %collective-permute-done.12 = bf16[1,24,3584]{2,1,0:T(8,128)(2,1)S(1)} collective-permute-done((bf16[1,24,3584]{2,1,0:T(8,128)(2,1)S(1)}, bf16[1,24,3584]{2,1,0:T(8,128)(2,1)S(1)}, u32[]{:S(2)}, u32[]{:S(2)}) %collective-permute-start.12) | collective-permute-done | bytes 172064 | tf_op jit(solution)/shard_map/ppermute | solution.py:16
  68.2 2.6 %collective-permute-done.13 = bf16[1,24,3584]{2,1,0:T(8,128)(2,1)S(1)} collective-permute-done((bf16[1,24,3584]{2,1,0:T(8,128)(2,1)S(1)}, bf16[1,24,3584]{2,1,0:T(8,128)(2,1)S(1)}, u32[]{:S(2)}, u32[]{:S(2)}) %collective-permute-start.13) | collective-permute-done | bytes 172064 | tf_op jit(solution)/shard_map/ppermute | solution.py:16
  71.7 2.2 %collective-permute-start.25 = (bf16[1,24,3584]{2,1,0:T(8,128)(2,1)S(1)}, bf16[1,24,3584]{2,1,0:T(8,128)(2,1)S(1)}, u32[]{:S(2)}, u32[]{:S(2)}) collective-permute-start(bf16[1,24,3584]{2,1,0:T(8,128)(2,1)S(1)} %fusion.24), channel_id=1, source_target_pairs={{0,8},{8,0},{1,9},{9,1},{2,10},{10,2},{3,11},{11,3},{4,12},{12,4},... | collective-permute-start | bytes 516104 | tf_op jit(solution)/shard_map/ppermute | solution.py:12
  73.9 1.5 %collective-permute-start.22 = (bf16[1,40,3584]{2,1,0:T(8,128)(2,1)S(1)}, bf16[1,40,3584]{2,1,0:T(8,128)(2,1)S(1)}, u32[]{:S(2)}, u32[]{:S(2)}) collective-permute-start(bf16[1,40,3584]{2,1,0:T(8,128)(2,1)S(1)} %get-tuple-element.11), channel_id=1, source_target_pairs={{0,2},{2,0},{4,6},{6,4},{1,3},{3,1},{5,7},{7,5},{8,10},{10,8},{12,... | collective-permute-start | bytes 860168 | tf_op jit(solution)/shard_map/ppermute | solution.py:16
  76.1 1.4 %collective-permute-start.23 = (bf16[1,40,3584]{2,1,0:T(8,128)(2,1)S(1)}, bf16[1,40,3584]{2,1,0:T(8,128)(2,1)S(1)}, u32[]{:S(2)}, u32[]{:S(2)}) collective-permute-start(bf16[1,40,3584]{2,1,0:T(8,128)(2,1)S(1)} %get-tuple-element.13), channel_id=1, source_target_pairs={{0,4},{2,6},{4,0},{6,2},{1,5},{3,7},{5,1},{7,3},{8,12},{10,14},{12... | collective-permute-start | bytes 860168 | tf_op jit(solution)/shard_map/ppermute | solution.py:16
  77.5 4.4 %collective-permute-done.26 = bf16[1,16,3584]{2,1,0:T(8,128)(2,1)S(1)} collective-permute-done((bf16[1,16,3584]{2,1,0:T(8,128)(2,1)S(1)}, bf16[1,16,3584]{2,1,0:T(8,128)(2,1)S(1)}, u32[]{:S(2)}, u32[]{:S(2)}) %collective-permute-start.26) | collective-permute-done | bytes 114720 | tf_op jit(solution)/shard_map/ppermute | solution.py:12
  81.9 2.4 %collective-permute-done.25 = bf16[1,24,3584]{2,1,0:T(8,128)(2,1)S(1)} collective-permute-done((bf16[1,24,3584]{2,1,0:T(8,128)(2,1)S(1)}, bf16[1,24,3584]{2,1,0:T(8,128)(2,1)S(1)}, u32[]{:S(2)}, u32[]{:S(2)}) %collective-permute-start.25) | collective-permute-done | bytes 172064 | tf_op jit(solution)/shard_map/ppermute | solution.py:12
  84.4 5.2 %collective-permute-done.24 = bf16[1,40,3584]{2,1,0:T(8,128)(2,1)S(1)} collective-permute-done((bf16[1,40,3584]{2,1,0:T(8,128)(2,1)S(1)}, bf16[1,40,3584]{2,1,0:T(8,128)(2,1)S(1)}, u32[]{:S(2)}, u32[]{:S(2)}) %collective-permute-start.24) | collective-permute-done | bytes 286752 | tf_op jit(solution)/shard_map/ppermute | solution.py:16
  89.7 2.5 %collective-permute-done.23 = bf16[1,40,3584]{2,1,0:T(8,128)(2,1)S(1)} collective-permute-done((bf16[1,40,3584]{2,1,0:T(8,128)(2,1)S(1)}, bf16[1,40,3584]{2,1,0:T(8,128)(2,1)S(1)}, u32[]{:S(2)}, u32[]{:S(2)}) %collective-permute-start.23) | collective-permute-done | bytes 286752 | tf_op jit(solution)/shard_map/ppermute | solution.py:16
  93.4 1.9 %collective-permute-done.27 = f32[2,40,3584]{2,1,0:T(8,128)S(1)} collective-permute-done((f32[2,40,3584]{2,1,0:T(8,128)S(1)}, f32[2,40,3584]{2,1,0:T(8,128)S(1)}, u32[]{:S(2)}, u32[]{:S(2)}) %collective-permute-start.27) | collective-permute-done | bytes 1146912 | tf_op jit(solution)/shard_map/ppermute | solution.py:12
  95.4 2.1 %convolution_convert_fusion.5 = bf16[64,3584]{1,0:T(8,128)(2,1)} fusion(f32[64,160]{1,0:T(8,128)S(1)} %select_reduce_fusion, f32[160,3584]{1,0:T(8,128)S(1)} %bitcast.101), kind=kOutput, calls=%fused_computation.13 | convolution fusion | flops 440631296 | bytes 2793472 | tf_op jit(solution)/shard_map/dot_general | solution.py:139
  (91 shorter events, 14.8 us)
Async XLA Ops:
  0.0 4.6 %copy-start.1 = (bf16[64,3584]{1,0:T(8,128)(2,1)S(1)}, bf16[64,3584]{1,0:T(8,128)(2,1)}, u32[]{:S(2)}) copy-start(bf16[64,3584]{1,0:T(8,128)(2,1)} %param.6) | copy-start | bytes 1376260
  0.0 1.5 %collective-permute-start = (s32[64,8]{0,1:T(8,128)}, s32[64,8]{0,1:T(8,128)S(1)}, u32[]{:S(2)}, u32[]{:S(2)}) collective-permute-start(s32[64,8]{0,1:T(8,128)} %param.7), channel_id=1, source_target_pairs={{0,1},{1,0},{2,3},{3,2},{4,5},{5,4},{6,7},{7,6},{8,9},{9,8},{10,11... | collective-permute-start | bytes 6152 | tf_op jit(solution)/shard_map/ppermute | solution.py:12
  0.5 4.1 %collective-permute-start.1 = (bf16[64,3584]{1,0:T(8,128)(2,1)}, bf16[64,3584]{1,0:T(8,128)(2,1)S(1)}, u32[]{:S(2)}, u32[]{:S(2)}) collective-permute-start(bf16[64,3584]{1,0:T(8,128)(2,1)} %param.6), channel_id=1, source_target_pairs={{0,1},{1,0},{2,3},{3,2},{4,5},{5,4},{6,7},{7,6},{8,9},{9,8},{10,11... | collective-permute-start | bytes 1376264 | tf_op jit(solution)/shard_map/ppermute | solution.py:12
  3.9 5.0 %copy-start.3 = (bf16[1,160,3584]{2,1,0:T(8,128)(2,1)S(1)}, bf16[1,160,3584]{2,1,0:T(8,128)(2,1)}, u32[]{:S(2)}) copy-start(bf16[1,160,3584]{2,1,0:T(8,128)(2,1)} %param.9) | copy-start | bytes 3440644
  4.9 32.7 %copy-start.4 = (bf16[1,160,3584]{2,1,0:T(8,128)(2,1)S(1)}, bf16[1,160,3584]{2,1,0:T(8,128)(2,1)}, u32[]{:S(2)}) copy-start(bf16[1,160,3584]{2,1,0:T(8,128)(2,1)} %param.10) | copy-start | bytes 3440644
  4.9 9.9 %collective-permute-start.15 = (bf16[1,16,3584]{2,1,0:T(8,128)(2,1)S(1)}, bf16[1,16,3584]{2,1,0:T(8,128)(2,1)S(1)}, u32[]{:S(2)}, u32[]{:S(2)}) collective-permute-start(bf16[1,16,3584]{2,1,0:T(8,128)(2,1)S(1)} %slice.136), channel_id=1, source_target_pairs={{0,8},{8,0},{1,9},{9,1},{2,10},{10,2},{3,11},{11,3},{4,12},{12,4},... | collective-permute-start | bytes 344072 | tf_op jit(solution)/shard_map/ppermute | solution.py:12
  8.9 41.6 %collective-permute-start.5 = (bf16[160,3584]{1,0:T(8,128)(2,1)S(1)}, bf16[160,3584]{1,0:T(8,128)(2,1)S(1)}, u32[]{:S(2)}, u32[]{:S(2)}) collective-permute-start(bf16[160,3584]{1,0:T(8,128)(2,1)S(1)} %bitcast.124), channel_id=1, source_target_pairs={{0,1},{1,0},{2,3},{3,2},{4,5},{5,4},{6,7},{7,6},{8,9},{9,8},{10,11... | collective-permute-start | bytes 3440648 | tf_op jit(solution)/shard_map/ppermute | solution.py:12
  14.8 7.1 %collective-permute-start.18 = (bf16[1,16,3584]{2,1,0:T(8,128)(2,1)S(1)}, bf16[1,16,3584]{2,1,0:T(8,128)(2,1)S(1)}, u32[]{:S(2)}, u32[]{:S(2)}) collective-permute-start(bf16[1,16,3584]{2,1,0:T(8,128)(2,1)S(1)} %collective-permute-done.15), channel_id=1, source_target_pairs={{0,6},{2,4},{4,2},{6,0},{1,7},{3,5},{5,3},{7,1},{8,14},{10,12},{12... | collective-permute-start | bytes 344072 | tf_op jit(solution)/shard_map/ppermute | solution.py:16
  16.5 7.9 %collective-permute-start.17 = (bf16[1,16,3584]{2,1,0:T(8,128)(2,1)S(1)}, bf16[1,16,3584]{2,1,0:T(8,128)(2,1)S(1)}, u32[]{:S(2)}, u32[]{:S(2)}) collective-permute-start(bf16[1,16,3584]{2,1,0:T(8,128)(2,1)S(1)} %collective-permute-done.15), channel_id=1, source_target_pairs={{0,4},{2,6},{4,0},{6,2},{1,5},{3,7},{5,1},{7,3},{8,12},{10,14},{12... | collective-permute-start | bytes 344072 | tf_op jit(solution)/shard_map/ppermute | solution.py:16
  17.8 9.8 %collective-permute-start.16 = (bf16[1,16,3584]{2,1,0:T(8,128)(2,1)S(1)}, bf16[1,16,3584]{2,1,0:T(8,128)(2,1)S(1)}, u32[]{:S(2)}, u32[]{:S(2)}) collective-permute-start(bf16[1,16,3584]{2,1,0:T(8,128)(2,1)S(1)} %collective-permute-done.15), channel_id=1, source_target_pairs={{0,2},{2,0},{4,6},{6,4},{1,3},{3,1},{5,7},{7,5},{8,10},{10,8},{12,... | collective-permute-start | bytes 344072 | tf_op jit(solution)/shard_map/ppermute | solution.py:16
  18.4 19.2 %collective-permute-start.4 = (bf16[1,40,3584]{2,1,0:T(8,128)(2,1)S(1)}, bf16[1,40,3584]{2,1,0:T(8,128)(2,1)S(1)}, u32[]{:S(2)}, u32[]{:S(2)}) collective-permute-start(bf16[1,40,3584]{2,1,0:T(8,128)(2,1)S(1)} %get-tuple-element.18), channel_id=1, source_target_pairs={{0,6},{2,4},{4,2},{6,0},{1,7},{3,5},{5,3},{7,1},{8,14},{10,12},{12... | collective-permute-start | bytes 860168 | tf_op jit(solution)/shard_map/ppermute | solution.py:16
  21.9 19.9 %collective-permute-start.3 = (bf16[1,40,3584]{2,1,0:T(8,128)(2,1)S(1)}, bf16[1,40,3584]{2,1,0:T(8,128)(2,1)S(1)}, u32[]{:S(2)}, u32[]{:S(2)}) collective-permute-start(bf16[1,40,3584]{2,1,0:T(8,128)(2,1)S(1)} %get-tuple-element.18), channel_id=1, source_target_pairs={{0,4},{2,6},{4,0},{6,2},{1,5},{3,7},{5,1},{7,3},{8,12},{10,14},{12... | collective-permute-start | bytes 860168 | tf_op jit(solution)/shard_map/ppermute | solution.py:16
  24.4 17.4 %collective-permute-start.2 = (bf16[1,40,3584]{2,1,0:T(8,128)(2,1)S(1)}, bf16[1,40,3584]{2,1,0:T(8,128)(2,1)S(1)}, u32[]{:S(2)}, u32[]{:S(2)}) collective-permute-start(bf16[1,40,3584]{2,1,0:T(8,128)(2,1)S(1)} %get-tuple-element.18), channel_id=1, source_target_pairs={{0,2},{2,0},{4,6},{6,4},{1,3},{3,1},{5,7},{7,5},{8,10},{10,8},{12,... | collective-permute-start | bytes 860168 | tf_op jit(solution)/shard_map/ppermute | solution.py:16
  27.6 10.0 %collective-permute-start.8 = (bf16[1,24,3584]{2,1,0:T(8,128)(2,1)S(1)}, bf16[1,24,3584]{2,1,0:T(8,128)(2,1)S(1)}, u32[]{:S(2)}, u32[]{:S(2)}) collective-permute-start(bf16[1,24,3584]{2,1,0:T(8,128)(2,1)S(1)} %slice.129), channel_id=1, source_target_pairs={{0,8},{8,0},{1,9},{9,1},{2,10},{10,2},{3,11},{11,3},{4,12},{12,4},... | collective-permute-start | bytes 516104 | tf_op jit(solution)/shard_map/ppermute | solution.py:12
  37.6 13.8 %collective-permute-start.6 = (bf16[160,3584]{1,0:T(8,128)(2,1)S(1)}, bf16[160,3584]{1,0:T(8,128)(2,1)S(1)}, u32[]{:S(2)}, u32[]{:S(2)}) collective-permute-start(bf16[160,3584]{1,0:T(8,128)(2,1)S(1)} %bitcast.128), channel_id=1, source_target_pairs={{0,1},{1,0},{2,3},{3,2},{4,5},{5,4},{6,7},{7,6},{8,9},{9,8},{10,11... | collective-permute-start | bytes 3440648 | tf_op jit(solution)/shard_map/ppermute | solution.py:12
  37.6 9.5 %collective-permute-start.11 = (bf16[1,24,3584]{2,1,0:T(8,128)(2,1)S(1)}, bf16[1,24,3584]{2,1,0:T(8,128)(2,1)S(1)}, u32[]{:S(2)}, u32[]{:S(2)}) collective-permute-start(bf16[1,24,3584]{2,1,0:T(8,128)(2,1)S(1)} %collective-permute-done.8), channel_id=1, source_target_pairs={{0,6},{2,4},{4,2},{6,0},{1,7},{3,5},{5,3},{7,1},{8,14},{10,12},{12... | collective-permute-start | bytes 516104 | tf_op jit(solution)/shard_map/ppermute | solution.py:16
  41.8 8.0 %collective-permute-start.10 = (bf16[1,24,3584]{2,1,0:T(8,128)(2,1)S(1)}, bf16[1,24,3584]{2,1,0:T(8,128)(2,1)S(1)}, u32[]{:S(2)}, u32[]{:S(2)}) collective-permute-start(bf16[1,24,3584]{2,1,0:T(8,128)(2,1)S(1)} %collective-permute-done.8), channel_id=1, source_target_pairs={{0,4},{2,6},{4,0},{6,2},{1,5},{3,7},{5,1},{7,3},{8,12},{10,14},{12... | collective-permute-start | bytes 516104 | tf_op jit(solution)/shard_map/ppermute | solution.py:16
  41.8 8.7 %collective-permute-start.9 = (bf16[1,24,3584]{2,1,0:T(8,128)(2,1)S(1)}, bf16[1,24,3584]{2,1,0:T(8,128)(2,1)S(1)}, u32[]{:S(2)}, u32[]{:S(2)}) collective-permute-start(bf16[1,24,3584]{2,1,0:T(8,128)(2,1)S(1)} %collective-permute-done.8), channel_id=1, source_target_pairs={{0,2},{2,0},{4,6},{6,4},{1,3},{3,1},{5,7},{7,5},{8,10},{10,8},{12,... | collective-permute-start | bytes 516104 | tf_op jit(solution)/shard_map/ppermute | solution.py:16
  42.4 4.6 %copy-start = (bf16[1,160,3584]{2,1,0:T(8,128)(2,1)S(1)}, bf16[1,160,3584]{2,1,0:T(8,128)(2,1)}, u32[]{:S(2)}) copy-start(bf16[1,160,3584]{2,1,0:T(8,128)(2,1)} %param.11) | copy-start | bytes 3440644
  47.0 5.4 %collective-permute-start.7 = (bf16[160,3584]{1,0:T(8,128)(2,1)S(1)}, bf16[160,3584]{1,0:T(8,128)(2,1)S(1)}, u32[]{:S(2)}, u32[]{:S(2)}) collective-permute-start(bf16[160,3584]{1,0:T(8,128)(2,1)S(1)} %bitcast.100), channel_id=1, source_target_pairs={{0,1},{1,0},{2,3},{3,2},{4,5},{5,4},{6,7},{7,6},{8,9},{9,8},{10,11... | collective-permute-start | bytes 3440648 | tf_op jit(solution)/shard_map/ppermute | solution.py:12
  52.9 12.4 %collective-permute-start.19 = (bf16[1,16,3584]{2,1,0:T(8,128)(2,1)S(1)}, bf16[1,16,3584]{2,1,0:T(8,128)(2,1)S(1)}, u32[]{:S(2)}, u32[]{:S(2)}) collective-permute-start(bf16[1,16,3584]{2,1,0:T(8,128)(2,1)S(1)} %get-tuple-element.19), channel_id=1, source_target_pairs={{0,2},{2,0},{4,6},{6,4},{1,3},{3,1},{5,7},{7,5},{8,10},{10,8},{12,... | collective-permute-start | bytes 344072 | tf_op jit(solution)/shard_map/ppermute | solution.py:16
  53.6 12.1 %collective-permute-start.21 = (bf16[1,16,3584]{2,1,0:T(8,128)(2,1)S(1)}, bf16[1,16,3584]{2,1,0:T(8,128)(2,1)S(1)}, u32[]{:S(2)}, u32[]{:S(2)}) collective-permute-start(bf16[1,16,3584]{2,1,0:T(8,128)(2,1)S(1)} %get-tuple-element.20), channel_id=1, source_target_pairs={{0,6},{2,4},{4,2},{6,0},{1,7},{3,5},{5,3},{7,1},{8,14},{10,12},{12... | collective-permute-start | bytes 344072 | tf_op jit(solution)/shard_map/ppermute | solution.py:16
  56.2 9.4 %collective-permute-start.20 = (bf16[1,16,3584]{2,1,0:T(8,128)(2,1)S(1)}, bf16[1,16,3584]{2,1,0:T(8,128)(2,1)S(1)}, u32[]{:S(2)}, u32[]{:S(2)}) collective-permute-start(bf16[1,16,3584]{2,1,0:T(8,128)(2,1)S(1)} %get-tuple-element.21), channel_id=1, source_target_pairs={{0,4},{2,6},{4,0},{6,2},{1,5},{3,7},{5,1},{7,3},{8,12},{10,14},{12... | collective-permute-start | bytes 344072 | tf_op jit(solution)/shard_map/ppermute | solution.py:16
  59.0 9.2 %collective-permute-start.12 = (bf16[1,24,3584]{2,1,0:T(8,128)(2,1)S(1)}, bf16[1,24,3584]{2,1,0:T(8,128)(2,1)S(1)}, u32[]{:S(2)}, u32[]{:S(2)}) collective-permute-start(bf16[1,24,3584]{2,1,0:T(8,128)(2,1)S(1)} %get-tuple-element.14), channel_id=1, source_target_pairs={{0,2},{2,0},{4,6},{6,4},{1,3},{3,1},{5,7},{7,5},{8,10},{10,8},{12,... | collective-permute-start | bytes 516104 | tf_op jit(solution)/shard_map/ppermute | solution.py:16
  60.2 8.0 %collective-permute-start.14 = (bf16[1,24,3584]{2,1,0:T(8,128)(2,1)S(1)}, bf16[1,24,3584]{2,1,0:T(8,128)(2,1)S(1)}, u32[]{:S(2)}, u32[]{:S(2)}) collective-permute-start(bf16[1,24,3584]{2,1,0:T(8,128)(2,1)S(1)} %get-tuple-element.15), channel_id=1, source_target_pairs={{0,6},{2,4},{4,2},{6,0},{1,7},{3,5},{5,3},{7,1},{8,14},{10,12},{12... | collective-permute-start | bytes 516104 | tf_op jit(solution)/shard_map/ppermute | solution.py:16
  65.3 5.5 %collective-permute-start.13 = (bf16[1,24,3584]{2,1,0:T(8,128)(2,1)S(1)}, bf16[1,24,3584]{2,1,0:T(8,128)(2,1)S(1)}, u32[]{:S(2)}, u32[]{:S(2)}) collective-permute-start(bf16[1,24,3584]{2,1,0:T(8,128)(2,1)S(1)} %get-tuple-element.16), channel_id=1, source_target_pairs={{0,4},{2,6},{4,0},{6,2},{1,5},{3,7},{5,1},{7,3},{8,12},{10,14},{12... | collective-permute-start | bytes 516104 | tf_op jit(solution)/shard_map/ppermute | solution.py:16
  70.9 11.1 %collective-permute-start.26 = (bf16[1,16,3584]{2,1,0:T(8,128)(2,1)S(1)}, bf16[1,16,3584]{2,1,0:T(8,128)(2,1)S(1)}, u32[]{:S(2)}, u32[]{:S(2)}) collective-permute-start(bf16[1,16,3584]{2,1,0:T(8,128)(2,1)S(1)} %fusion.26), channel_id=1, source_target_pairs={{0,8},{8,0},{1,9},{9,1},{2,10},{10,2},{3,11},{11,3},{4,12},{12,4},... | collective-permute-start | bytes 344072 | tf_op jit(solution)/shard_map/ppermute | solution.py:12
  71.7 12.7 %collective-permute-start.25 = (bf16[1,24,3584]{2,1,0:T(8,128)(2,1)S(1)}, bf16[1,24,3584]{2,1,0:T(8,128)(2,1)S(1)}, u32[]{:S(2)}, u32[]{:S(2)}) collective-permute-start(bf16[1,24,3584]{2,1,0:T(8,128)(2,1)S(1)} %fusion.24), channel_id=1, source_target_pairs={{0,8},{8,0},{1,9},{9,1},{2,10},{10,2},{3,11},{11,3},{4,12},{12,4},... | collective-permute-start | bytes 516104 | tf_op jit(solution)/shard_map/ppermute | solution.py:12
  73.9 10.5 %collective-permute-start.22 = (bf16[1,40,3584]{2,1,0:T(8,128)(2,1)S(1)}, bf16[1,40,3584]{2,1,0:T(8,128)(2,1)S(1)}, u32[]{:S(2)}, u32[]{:S(2)}) collective-permute-start(bf16[1,40,3584]{2,1,0:T(8,128)(2,1)S(1)} %get-tuple-element.11), channel_id=1, source_target_pairs={{0,2},{2,0},{4,6},{6,4},{1,3},{3,1},{5,7},{7,5},{8,10},{10,8},{12,... | collective-permute-start | bytes 860168 | tf_op jit(solution)/shard_map/ppermute | solution.py:16
  75.4 14.2 %collective-permute-start.24 = (bf16[1,40,3584]{2,1,0:T(8,128)(2,1)S(1)}, bf16[1,40,3584]{2,1,0:T(8,128)(2,1)S(1)}, u32[]{:S(2)}, u32[]{:S(2)}) collective-permute-start(bf16[1,40,3584]{2,1,0:T(8,128)(2,1)S(1)} %get-tuple-element.12), channel_id=1, source_target_pairs={{0,6},{2,4},{4,2},{6,0},{1,7},{3,5},{5,3},{7,1},{8,14},{10,12},{12... | collective-permute-start | bytes 860168 | tf_op jit(solution)/shard_map/ppermute | solution.py:16
  76.1 16.0 %collective-permute-start.23 = (bf16[1,40,3584]{2,1,0:T(8,128)(2,1)S(1)}, bf16[1,40,3584]{2,1,0:T(8,128)(2,1)S(1)}, u32[]{:S(2)}, u32[]{:S(2)}) collective-permute-start(bf16[1,40,3584]{2,1,0:T(8,128)(2,1)S(1)} %get-tuple-element.13), channel_id=1, source_target_pairs={{0,4},{2,6},{4,0},{6,2},{1,5},{3,7},{5,1},{7,3},{8,12},{10,14},{12... | collective-permute-start | bytes 860168 | tf_op jit(solution)/shard_map/ppermute | solution.py:16
  92.4 2.9 %collective-permute-start.27 = (f32[2,40,3584]{2,1,0:T(8,128)S(1)}, f32[2,40,3584]{2,1,0:T(8,128)S(1)}, u32[]{:S(2)}, u32[]{:S(2)}) collective-permute-start(f32[2,40,3584]{2,1,0:T(8,128)S(1)} %pad_maximum_fusion.4), channel_id=1, source_target_pairs={{0,1},{1,0},{2,3},{3,2},{4,5},{5,4},{6,7},{7,6},{8,9},{9,8},{10,11... | collective-permute-start | bytes 3440648 | tf_op jit(solution)/shard_map/ppermute | solution.py:12
  (1 other events, 0.7 us)

commit v8 on v6

--- a/solution.py
+++ b/solution.py
@@ -16,21 +16,13 @@
     return lax.ppermute(x, axis, [(i, i ^ k) for i in range(size)])
 
 
-def quarter_rows(rows, w_gate, w_up, w_down, n_ctx):
+def slab_rows(rows, w_gate, w_up, w_down):
     dims = (((1,), (1,)), ((), ()))
     gate = lax.dot_general(rows, w_gate, dims, preferred_element_type=jnp.float32)
     up = lax.dot_general(rows, w_up, dims, preferred_element_type=jnp.float32)
     hidden = (jax.nn.silu(gate) * up).astype(jnp.bfloat16)
-    slab = w_down.shape[0] // n_ctx
-    total = None
-    for c in range(n_ctx):
-        part = jnp.dot(
-            hidden[:, c * slab : (c + 1) * slab],
-            w_down[c * slab : (c + 1) * slab],
-            preferred_element_type=jnp.float32,
-        ).astype(jnp.bfloat16)
-        total = part.astype(jnp.float32) if total is None else total + part.astype(jnp.float32)
-    return total
+    part = jnp.dot(hidden, w_down, preferred_element_type=jnp.float32).astype(jnp.bfloat16)
+    return part.astype(jnp.float32)
 
 
 def per_device(tokens, routes, route_weight, w_gate, w_up, w_down):
@@ -47,12 +39,11 @@
     ctx = lax.axis_index("context")
     me = lax.axis_index("ex")
 
+    own_slab = (w_gate[0], w_up[0], w_down[0])
+    other_slab = tuple(shift(w, "context", n_ctx, 1) for w in own_slab)
+
     def with_sibling(x):
         return jnp.concatenate([x, shift(x, "context", n_ctx, 1)], axis=0)
-
-    wg = with_sibling(w_gate[0])
-    wu = with_sibling(w_up[0])
-    wd = with_sibling(w_down[0])
 
     other_routes = shift(routes, "context", n_ctx, 1)
     pair_routes = jnp.where(
@@ -95,7 +86,7 @@
     def group_partial(sent):
         group = [sent] + [exchange(sent, k) for k in range(1, sharers)]
         rows = jnp.stack(group).reshape(-1, width)
-        partial = quarter_rows(rows, wg, wu, wd, n_ctx).astype(jnp.bfloat16)
+        partial = (slab_rows(rows, *own_slab) + slab_rows(rows, *other_slab)).astype(jnp.bfloat16)
         return partial.reshape((sharers,) + sent.shape)
 
     def group_sum(partial):

time: 91 us -> 108 us (1.19)
  matrix products: 8.32 us -> 29.3 us
  waiting for transfers between devices: 57.6 us -> 46 us
  starting transfers between devices: 19.4 us -> 22.7 us
  other arithmetic: 3.37 us -> 5.78 us
  local copies, waits for them, and re-layouts: 1.84 us -> 3.82 us
    dot_general x8, matrix products: 5.95 us -> 26.9 us  [the longest x4 18 us: slab_rows(): jnp.dot(hidden, w_down, preferred_element_type=jnp.float32)]
    ppermute x8, waiting for transfers between devices: 22.4 us -> 14.3 us  [shift(): return lax.ppermute(x, axis, [(i, (i + k) % size) for i in range(size)])]
    ppermute x12, waiting for transfers between devices: 35.2 us -> 31.8 us  [swap(): return lax.ppermute(x, axis, [(i, i ^ k) for i in range(size)])]
    squeeze x2, local copies, waits for them, and re-layouts: 0.11 us -> 2.09 us  [group_sum(): total = total + back_exchange(partial[k], k).astype(jnp.float32)]
    ppermute x12, starting transfers between devices: 13.4 us -> 15.2 us  [swap(): return lax.ppermute(x, axis, [(i, i ^ k) for i in range(size)])]
    ppermute x8, starting transfers between devices: 5.94 us -> 7.58 us  [shift(): return lax.ppermute(x, axis, [(i, (i + k) % size) for i in range(size)])]
    another operation x2, other arithmetic: 0.29 us -> 1.51 us  [group_partial(): rows = jnp.stack(group).reshape(-1, width)]
    add x2, other arithmetic: 0.32 us -> 1.51 us  [group_sum(): total = total + back_exchange(partial[k], k).astype(jnp.float32)]
  transfers between devices with their start and end apart: 20 -> 20, of which waited for: 12 -> 14; matrix products, arithmetic and copies ran while one was open for 10% -> 25% of each run, Pallas kernels for 0% -> 0%
where the time goes in v8:
time: 108 us
  waiting for transfers between devices  46 us (43%)
  matrix products  29.3 us (27%)
  starting transfers between devices  22.7 us (21%)
  other arithmetic  5.78 us (5%)
  local copies, waits for them, and re-layouts  3.82 us (4%)
    ppermute x12, waiting for transfers between devices, swap(): return lax.ppermute(x, axis, [(i, i ^ k) for i in range(size)])  31.8 us
    dot_general x4, matrix products, slab_rows(): jnp.dot(hidden, w_down, preferred_element_type=jnp.float32)  18 us
    ppermute x12, starting transfers between devices, swap(): return lax.ppermute(x, axis, [(i, i ^ k) for i in range(size)])  15.2 us
    ppermute x8, waiting for transfers between devices, shift(): return lax.ppermute(x, axis, [(i, (i + k) % size) for i in range(size)])  14.3 us
    dot_general x4, matrix products, slab_rows(): lax.dot_general(rows, w_gate, dims, preferred_element_type=jnp.float32)  8.92 us
    ppermute x8, starting transfers between devices, shift(): return lax.ppermute(x, axis, [(i, (i + k) % size) for i in range(size)])  7.58 us
  transfers between devices with their start and end apart: 20, of which 14 were waited for; matrix products, arithmetic and copies ran while one was open for 25% of the time, Pallas kernels for 0%

profile of v8, /device:TPU:0, one launch (start us, length us, event | category | flops | bytes accessed | tf_op | source)
XLA Modules:
  0.0 107.9 jit_solution(13205799729497959613)
XLA Ops:
  4.9 3.9 %collective-permute-start.4 = (bf16[1,40,3584]{2,1,0:T(8,128)(2,1)S(1)}, bf16[1,40,3584]{2,1,0:T(8,128)(2,1)S(1)}, u32[]{:S(2)}, u32[]{:S(2)}) collective-permute-start(bf16[1,40,3584]{2,1,0:T(8,128)(2,1)S(1)} %get-tuple-element.16), channel_id=1, source_target_pairs={{0,6},{2,4},{4,2},{6,0},{1,7},{3,5},{5,3},{7,1},{8,14},{10,12},{12... | collective-permute-start | bytes 860168 | tf_op jit(solution)/shard_map/ppermute | solution.py:16
  10.0 6.5 %collective-permute-done.4 = bf16[1,40,3584]{2,1,0:T(8,128)(2,1)S(1)} collective-permute-done((bf16[1,40,3584]{2,1,0:T(8,128)(2,1)S(1)}, bf16[1,40,3584]{2,1,0:T(8,128)(2,1)S(1)}, u32[]{:S(2)}, u32[]{:S(2)}) %collective-permute-start.4) | collective-permute-done | bytes 286752 | tf_op jit(solution)/shard_map/ppermute | solution.py:16
  16.5 3.0 %collective-permute-start.8 = (bf16[1,40,3584]{2,1,0:T(8,128)(2,1)S(1)}, bf16[1,40,3584]{2,1,0:T(8,128)(2,1)S(1)}, u32[]{:S(2)}, u32[]{:S(2)}) collective-permute-start(bf16[1,40,3584]{2,1,0:T(8,128)(2,1)S(1)} %get-tuple-element.15), channel_id=1, source_target_pairs={{0,8},{8,0},{1,9},{9,1},{2,10},{10,2},{3,11},{11,3},{4,12},{12,4},... | collective-permute-start | bytes 860168 | tf_op jit(solution)/shard_map/ppermute | solution.py:12
  19.5 8.1 %collective-permute-done.3 = bf16[1,40,3584]{2,1,0:T(8,128)(2,1)S(1)} collective-permute-done((bf16[1,40,3584]{2,1,0:T(8,128)(2,1)S(1)}, bf16[1,40,3584]{2,1,0:T(8,128)(2,1)S(1)}, u32[]{:S(2)}, u32[]{:S(2)}) %collective-permute-start.3) | collective-permute-done | bytes 286752 | tf_op jit(solution)/shard_map/ppermute | solution.py:16
  27.8 1.7 %fusion.44 = f32[160,160]{1,0:T(8,128)S(1)} fusion(bf16[160,3584]{1,0:T(8,128)(2,1)S(1)} %bitcast.98, bf16[1,160,3584]{2,1,0:T(8,128)(2,1)} %param.9), kind=kOutput, calls=%fused_computation.90 | convolution fusion | flops 183500800 | bytes 2396160 | tf_op jit(solution)/shard_map/dot_general | solution.py:21
  29.5 2.0 %collective-permute-done.8 = bf16[1,40,3584]{2,1,0:T(8,128)(2,1)S(1)} collective-permute-done((bf16[1,40,3584]{2,1,0:T(8,128)(2,1)S(1)}, bf16[1,40,3584]{2,1,0:T(8,128)(2,1)S(1)}, u32[]{:S(2)}, u32[]{:S(2)}) %collective-permute-start.8) | collective-permute-done | bytes 286752 | tf_op jit(solution)/shard_map/ppermute | solution.py:12
  31.5 1.5 %collective-permute-start.11 = (bf16[1,40,3584]{2,1,0:T(8,128)(2,1)S(1)}, bf16[1,40,3584]{2,1,0:T(8,128)(2,1)S(1)}, u32[]{:S(2)}, u32[]{:S(2)}) collective-permute-start(bf16[1,40,3584]{2,1,0:T(8,128)(2,1)S(1)} %collective-permute-done.8), channel_id=1, source_target_pairs={{0,6},{2,4},{4,2},{6,0},{1,7},{3,5},{5,3},{7,1},{8,14},{10,12},{12... | collective-permute-start | bytes 860168 | tf_op jit(solution)/shard_map/ppermute | solution.py:16
  33.1 1.2 %collective-permute-start.10 = (bf16[1,40,3584]{2,1,0:T(8,128)(2,1)S(1)}, bf16[1,40,3584]{2,1,0:T(8,128)(2,1)S(1)}, u32[]{:S(2)}, u32[]{:S(2)}) collective-permute-start(bf16[1,40,3584]{2,1,0:T(8,128)(2,1)S(1)} %collective-permute-done.8), channel_id=1, source_target_pairs={{0,4},{2,6},{4,0},{6,2},{1,5},{3,7},{5,1},{7,3},{8,12},{10,14},{12... | collective-permute-start | bytes 860168 | tf_op jit(solution)/shard_map/ppermute | solution.py:16
  35.0 4.4 %fusion.7 = f32[160,3584]{1,0:T(8,128)} fusion(f32[160,160]{1,0:T(8,128)S(1)} %fusion.44, bf16[160,3584]{1,0:T(8,128)(2,1)S(1)} %bitcast.99, bf16[1,160,3584]{2,1,0:T(8,128)(2,1)} %param.11, bf16[1,160,3584]{2,1,0:T(8,128)(2,1)} %param.10), kind=kOutput, calls=%fused_computation.11 | convolution fusion | flops 368302080 | bytes 5836800 | tf_op jit(solution)/shard_map/dot_general | solution.py:24
  39.4 2.3 %collective-permute-done.11 = bf16[1,40,3584]{2,1,0:T(8,128)(2,1)S(1)} collective-permute-done((bf16[1,40,3584]{2,1,0:T(8,128)(2,1)S(1)}, bf16[1,40,3584]{2,1,0:T(8,128)(2,1)S(1)}, u32[]{:S(2)}, u32[]{:S(2)}) %collective-permute-start.11) | collective-permute-done | bytes 286752 | tf_op jit(solution)/shard_map/ppermute | solution.py:16
  41.8 2.1 %collective-permute-done.10 = bf16[1,40,3584]{2,1,0:T(8,128)(2,1)S(1)} collective-permute-done((bf16[1,40,3584]{2,1,0:T(8,128)(2,1)S(1)}, bf16[1,40,3584]{2,1,0:T(8,128)(2,1)S(1)}, u32[]{:S(2)}, u32[]{:S(2)}) %collective-permute-start.10) | collective-permute-done | bytes 286752 | tf_op jit(solution)/shard_map/ppermute | solution.py:16
  43.9 0.9 collective-permute-done.9
  44.8 1.4 %pad_maximum_fusion.2 = bf16[4,1,40,3584]{3,2,1,0:T(8,128)(2,1)S(1)} fusion(bf16[1,1,40,3584]{3,2,1,0:T(8,128)(2,1)} %bitcast.113, bf16[1,1,40,3584]{3,2,1,0:T(8,128)(2,1)} %bitcast.114, bf16[1,1,40,3584]{3,2,1,0:T(8,128)(2,1)} %bitcast.15, bf16[1,1,40,3584]{3,2,1,0:T(8,128)(2,1)} %bitcast.109), kind=kLoop, calls=%fused_computation.16 | loop fusion | flops 1720320 | bytes 2293760 | tf_op jit(solution)/shard_map/stack | solution.py:88
  46.2 2.4 %fusion.42 = f32[160,160]{1,0:T(8,128)} fusion(bf16[160,3584]{1,0:T(8,128)(2,1)S(1)} %bitcast.102, bf16[1,160,3584]{2,1,0:T(8,128)(2,1)} %param.9), kind=kOutput, calls=%fused_computation.88 | convolution fusion | flops 183500800 | bytes 2396160 | tf_op jit(solution)/shard_map/dot_general | solution.py:21
  48.6 4.5 %fusion.3 = f32[160,3584]{1,0:T(8,128)} fusion(f32[160,160]{1,0:T(8,128)} %fusion.42, bf16[160,3584]{1,0:T(8,128)(2,1)S(1)} %bitcast.103, bf16[1,160,3584]{2,1,0:T(8,128)(2,1)} %param.11, bf16[1,160,3584]{2,1,0:T(8,128)(2,1)} %param.10), kind=kOutput, calls=%fused_computation.5 | convolution fusion | flops 368302080 | bytes 5836800 | tf_op jit(solution)/shard_map/dot_general | solution.py:24
  53.1 2.4 %fusion.56 = f32[160,160]{1,0:T(8,128)} fusion(bf16[160,3584]{1,0:T(8,128)(2,1)S(1)} %bitcast.104, bf16[160,3584]{1,0:T(8,128)(2,1)} %collective-permute-done.5), kind=kOutput, calls=%fused_computation.100 | convolution fusion | flops 183500800 | bytes 2396160 | tf_op jit(solution)/shard_map/dot_general | solution.py:21
  55.5 4.9 %fusion.2 = bf16[160,3584]{1,0:T(8,128)(2,1)} fusion(f32[160,3584]{1,0:T(8,128)} %fusion.3, bf16[160,3584]{1,0:T(8,128)(2,1)S(1)} %collective-permute-done.7, f32[160,160]{1,0:T(8,128)} %fusion.56, bf16[160,3584]{1,0:T(8,128)(2,1)S(1)} %bitcast.105, bf16[160,3584]{1,0:T(8,128)(2,1)} %collective-permute-done.6), kind=kOutput, calls=%fused_computation.3 | convolution fusion | flops 369448960 | bytes 6983680 | tf_op jit(solution)/shard_map/dot_general | solution.py:24
  60.4 2.0 %slice_bitcast_fusion.6 = (bf16[1,40,3584]{2,1,0:T(8,128)(2,1)}, bf16[1,40,3584]{2,1,0:T(8,128)(2,1)}, bf16[1,40,3584]{2,1,0:T(8,128)(2,1)}) fusion(bf16[160,3584]{1,0:T(8,128)(2,1)} %fusion.2), kind=kLoop, calls=%fused_computation.36 | loop fusion | bytes 1720320 | tf_op jit(solution)/shard_map/squeeze | solution.py:95
  62.4 2.4 %collective-permute-start.14 = (bf16[1,40,3584]{2,1,0:T(8,128)(2,1)}, bf16[1,40,3584]{2,1,0:T(8,128)(2,1)}, u32[]{:S(2)}, u32[]{:S(2)}) collective-permute-start(bf16[1,40,3584]{2,1,0:T(8,128)(2,1)} %get-tuple-element.13), channel_id=1, source_target_pairs={{0,6},{2,4},{4,2},{6,0},{1,7},{3,5},{5,3},{7,1},{8,14},{10,12},{12... | collective-permute-start | bytes 860168 | tf_op jit(solution)/shard_map/ppermute | solution.py:16
  65.1 0.9 collective-permute-start.12
  66.0 2.4 %fusion.55 = f32[160,160]{1,0:T(8,128)} fusion(bf16[160,3584]{1,0:T(8,128)(2,1)S(1)} %bitcast.100, bf16[160,3584]{1,0:T(8,128)(2,1)} %collective-permute-done.5), kind=kOutput, calls=%fused_computation.99 | convolution fusion | flops 183500800 | bytes 2396160 | tf_op jit(solution)/shard_map/dot_general | solution.py:21
  68.4 4.1 %fusion.6 = bf16[160,3584]{1,0:T(8,128)(2,1)} fusion(f32[160,3584]{1,0:T(8,128)S(1)} %copy-done, bf16[160,3584]{1,0:T(8,128)(2,1)} %copy-done.1, f32[160,160]{1,0:T(8,128)} %fusion.55, bf16[160,3584]{1,0:T(8,128)(2,1)S(1)} %bitcast.101, bf16[160,3584]{1,0:T(8,128)(2,1)} %collective-permute-done.6), kind=kOutput, calls=%fused_computation.9 | convolution fusion | flops 369448960 | bytes 6983680 | tf_op jit(solution)/shard_map/dot_general | solution.py:24
  72.6 0.9 collective-permute-done.14
  73.5 3.9 %collective-permute-done.13 = bf16[1,40,3584]{2,1,0:T(8,128)(2,1)} collective-permute-done((bf16[1,40,3584]{2,1,0:T(8,128)(2,1)}, bf16[1,40,3584]{2,1,0:T(8,128)(2,1)}, u32[]{:S(2)}, u32[]{:S(2)}) %collective-permute-start.13) | collective-permute-done | bytes 286752 | tf_op jit(solution)/shard_map/ppermute | solution.py:16
  78.1 1.4 %fusion.14 = bf16[1,40,3584]{2,1,0:T(8,128)(2,1)S(1)} fusion(bf16[1,40,3584]{2,1,0:T(8,128)(2,1)} %collective-permute-done.14, bf16[1,40,3584]{2,1,0:T(8,128)(2,1)} %collective-permute-done.13, bf16[1,40,3584]{2,1,0:T(8,128)(2,1)} %collective-permute-done.12, bf16[160,3584]{1,0:T(8,128)(2,1)} %fusion.2), kind=kLoop, calls=%fused_computation.26 | loop fusion | flops 1146880 | bytes 1433600 | tf_op jit(solution)/shard_map/add | solution.py:95
  79.4 3.4 %collective-permute-start.18 = (bf16[1,40,3584]{2,1,0:T(8,128)(2,1)S(1)}, bf16[1,40,3584]{2,1,0:T(8,128)(2,1)S(1)}, u32[]{:S(2)}, u32[]{:S(2)}) collective-permute-start(bf16[1,40,3584]{2,1,0:T(8,128)(2,1)S(1)} %fusion.14), channel_id=1, source_target_pairs={{0,8},{8,0},{1,9},{9,1},{2,10},{10,2},{3,11},{11,3},{4,12},{12,4},... | collective-permute-start | bytes 860168 | tf_op jit(solution)/shard_map/ppermute | solution.py:12
  82.9 2.7 %collective-permute-start.17 = (bf16[1,40,3584]{2,1,0:T(8,128)(2,1)S(1)}, bf16[1,40,3584]{2,1,0:T(8,128)(2,1)S(1)}, u32[]{:S(2)}, u32[]{:S(2)}) collective-permute-start(bf16[1,40,3584]{2,1,0:T(8,128)(2,1)S(1)} %get-tuple-element.10), channel_id=1, source_target_pairs={{0,6},{2,4},{4,2},{6,0},{1,7},{3,5},{5,3},{7,1},{8,14},{10,12},{12... | collective-permute-start | bytes 860168 | tf_op jit(solution)/shard_map/ppermute | solution.py:16
  85.7 0.8 collective-permute-start.15
  86.5 9.6 %collective-permute-done.18 = bf16[1,40,3584]{2,1,0:T(8,128)(2,1)S(1)} collective-permute-done((bf16[1,40,3584]{2,1,0:T(8,128)(2,1)S(1)}, bf16[1,40,3584]{2,1,0:T(8,128)(2,1)S(1)}, u32[]{:S(2)}, u32[]{:S(2)}) %collective-permute-start.18) | collective-permute-done | bytes 286752 | tf_op jit(solution)/shard_map/ppermute | solution.py:12
  96.6 5.9 %collective-permute-done.16 = bf16[1,40,3584]{2,1,0:T(8,128)(2,1)S(1)} collective-permute-done((bf16[1,40,3584]{2,1,0:T(8,128)(2,1)S(1)}, bf16[1,40,3584]{2,1,0:T(8,128)(2,1)S(1)}, u32[]{:S(2)}, u32[]{:S(2)}) %collective-permute-start.16) | collective-permute-done | bytes 286752 | tf_op jit(solution)/shard_map/ppermute | solution.py:16
  103.8 1.9 %collective-permute-done.19 = f32[2,40,3584]{2,1,0:T(8,128)S(1)} collective-permute-done((f32[2,40,3584]{2,1,0:T(8,128)S(1)}, f32[2,40,3584]{2,1,0:T(8,128)S(1)}, u32[]{:S(2)}, u32[]{:S(2)}) %collective-permute-start.19) | collective-permute-done | bytes 1146912 | tf_op jit(solution)/shard_map/ppermute | solution.py:12
  105.8 2.1 %convolution_convert_fusion.5 = bf16[64,3584]{1,0:T(8,128)(2,1)} fusion(f32[64,160]{1,0:T(8,128)S(1)} %select_reduce_fusion, f32[160,3584]{1,0:T(8,128)S(1)} %bitcast.106), kind=kOutput, calls=%fused_computation.13 | convolution fusion | flops 440631296 | bytes 2793472 | tf_op jit(solution)/shard_map/dot_general | solution.py:127
  (72 shorter events, 9.9 us)
Async XLA Ops:
  0.0 4.6 %copy-start.3 = (bf16[64,3584]{1,0:T(8,128)(2,1)S(1)}, bf16[64,3584]{1,0:T(8,128)(2,1)}, u32[]{:S(2)}) copy-start(bf16[64,3584]{1,0:T(8,128)(2,1)} %param.6) | copy-start | bytes 1376260
  0.0 1.5 %collective-permute-start = (s32[64,8]{0,1:T(8,128)}, s32[64,8]{0,1:T(8,128)S(1)}, u32[]{:S(2)}, u32[]{:S(2)}) collective-permute-start(s32[64,8]{0,1:T(8,128)} %param.7), channel_id=1, source_target_pairs={{0,1},{1,0},{2,3},{3,2},{4,5},{5,4},{6,7},{7,6},{8,9},{9,8},{10,11... | collective-permute-start | bytes 6152 | tf_op jit(solution)/shard_map/ppermute | solution.py:12
  0.5 4.1 %collective-permute-start.1 = (bf16[64,3584]{1,0:T(8,128)(2,1)}, bf16[64,3584]{1,0:T(8,128)(2,1)S(1)}, u32[]{:S(2)}, u32[]{:S(2)}) collective-permute-start(bf16[64,3584]{1,0:T(8,128)(2,1)} %param.6), channel_id=1, source_target_pairs={{0,1},{1,0},{2,3},{3,2},{4,5},{5,4},{6,7},{7,6},{8,9},{9,8},{10,11... | collective-permute-start | bytes 1376264 | tf_op jit(solution)/shard_map/ppermute | solution.py:12
  4.9 11.6 %collective-permute-start.4 = (bf16[1,40,3584]{2,1,0:T(8,128)(2,1)S(1)}, bf16[1,40,3584]{2,1,0:T(8,128)(2,1)S(1)}, u32[]{:S(2)}, u32[]{:S(2)}) collective-permute-start(bf16[1,40,3584]{2,1,0:T(8,128)(2,1)S(1)} %get-tuple-element.16), channel_id=1, source_target_pairs={{0,6},{2,4},{4,2},{6,0},{1,7},{3,5},{5,3},{7,1},{8,14},{10,12},{12... | collective-permute-start | bytes 860168 | tf_op jit(solution)/shard_map/ppermute | solution.py:16
  8.8 18.8 %collective-permute-start.3 = (bf16[1,40,3584]{2,1,0:T(8,128)(2,1)S(1)}, bf16[1,40,3584]{2,1,0:T(8,128)(2,1)S(1)}, u32[]{:S(2)}, u32[]{:S(2)}) collective-permute-start(bf16[1,40,3584]{2,1,0:T(8,128)(2,1)S(1)} %get-tuple-element.16), channel_id=1, source_target_pairs={{0,4},{2,6},{4,0},{6,2},{1,5},{3,7},{5,1},{7,3},{8,12},{10,14},{12... | collective-permute-start | bytes 860168 | tf_op jit(solution)/shard_map/ppermute | solution.py:16
  9.3 18.3 %collective-permute-start.2 = (bf16[1,40,3584]{2,1,0:T(8,128)(2,1)S(1)}, bf16[1,40,3584]{2,1,0:T(8,128)(2,1)S(1)}, u32[]{:S(2)}, u32[]{:S(2)}) collective-permute-start(bf16[1,40,3584]{2,1,0:T(8,128)(2,1)S(1)} %get-tuple-element.16), channel_id=1, source_target_pairs={{0,2},{2,0},{4,6},{6,4},{1,3},{3,1},{5,7},{7,5},{8,10},{10,8},{12,... | collective-permute-start | bytes 860168 | tf_op jit(solution)/shard_map/ppermute | solution.py:16
  9.5 46.0 %collective-permute-start.7 = (bf16[160,3584]{1,0:T(8,128)(2,1)}, bf16[160,3584]{1,0:T(8,128)(2,1)S(1)}, u32[]{:S(2)}, u32[]{:S(2)}) collective-permute-start(bf16[160,3584]{1,0:T(8,128)(2,1)} %bitcast.11), channel_id=1, source_target_pairs={{0,1},{1,0},{2,3},{3,2},{4,5},{5,4},{6,7},{7,6},{8,9},{9,8},{10,11... | collective-permute-start | bytes 3440648 | tf_op jit(solution)/shard_map/ppermute | solution.py:12
  9.5 43.6 %collective-permute-start.5 = (bf16[160,3584]{1,0:T(8,128)(2,1)}, bf16[160,3584]{1,0:T(8,128)(2,1)}, u32[]{:S(2)}, u32[]{:S(2)}) collective-permute-start(bf16[160,3584]{1,0:T(8,128)(2,1)} %bitcast.9), channel_id=1, source_target_pairs={{0,1},{1,0},{2,3},{3,2},{4,5},{5,4},{6,7},{7,6},{8,9},{9,8},{10,11... | collective-permute-start | bytes 3440648 | tf_op jit(solution)/shard_map/ppermute | solution.py:12
  16.5 15.0 %collective-permute-start.8 = (bf16[1,40,3584]{2,1,0:T(8,128)(2,1)S(1)}, bf16[1,40,3584]{2,1,0:T(8,128)(2,1)S(1)}, u32[]{:S(2)}, u32[]{:S(2)}) collective-permute-start(bf16[1,40,3584]{2,1,0:T(8,128)(2,1)S(1)} %get-tuple-element.15), channel_id=1, source_target_pairs={{0,8},{8,0},{1,9},{9,1},{2,10},{10,2},{3,11},{11,3},{4,12},{12,4},... | collective-permute-start | bytes 860168 | tf_op jit(solution)/shard_map/ppermute | solution.py:12
  31.5 7.9 %copy-start.4 = (bf16[1,40,3584]{2,1,0:T(8,128)(2,1)}, bf16[1,40,3584]{2,1,0:T(8,128)(2,1)S(1)}, u32[]{:S(2)}) copy-start(bf16[1,40,3584]{2,1,0:T(8,128)(2,1)S(1)} %collective-permute-done.8) | copy-start | bytes 860164
  31.5 10.2 %collective-permute-start.11 = (bf16[1,40,3584]{2,1,0:T(8,128)(2,1)S(1)}, bf16[1,40,3584]{2,1,0:T(8,128)(2,1)S(1)}, u32[]{:S(2)}, u32[]{:S(2)}) collective-permute-start(bf16[1,40,3584]{2,1,0:T(8,128)(2,1)S(1)} %collective-permute-done.8), channel_id=1, source_target_pairs={{0,6},{2,4},{4,2},{6,0},{1,7},{3,5},{5,3},{7,1},{8,14},{10,12},{12... | collective-permute-start | bytes 860168 | tf_op jit(solution)/shard_map/ppermute | solution.py:16
  33.1 10.8 %collective-permute-start.10 = (bf16[1,40,3584]{2,1,0:T(8,128)(2,1)S(1)}, bf16[1,40,3584]{2,1,0:T(8,128)(2,1)S(1)}, u32[]{:S(2)}, u32[]{:S(2)}) collective-permute-start(bf16[1,40,3584]{2,1,0:T(8,128)(2,1)S(1)} %collective-permute-done.8), channel_id=1, source_target_pairs={{0,4},{2,6},{4,0},{6,2},{1,5},{3,7},{5,1},{7,3},{8,12},{10,14},{12... | collective-permute-start | bytes 860168 | tf_op jit(solution)/shard_map/ppermute | solution.py:16
  34.3 10.5 %collective-permute-start.9 = (bf16[1,40,3584]{2,1,0:T(8,128)(2,1)S(1)}, bf16[1,40,3584]{2,1,0:T(8,128)(2,1)}, u32[]{:S(2)}, u32[]{:S(2)}) collective-permute-start(bf16[1,40,3584]{2,1,0:T(8,128)(2,1)S(1)} %collective-permute-done.8), channel_id=1, source_target_pairs={{0,2},{2,0},{4,6},{6,4},{1,3},{3,1},{5,7},{7,5},{8,10},{10,8},{12,... | collective-permute-start | bytes 860168 | tf_op jit(solution)/shard_map/ppermute | solution.py:16
  41.8 3.0 %copy-start.5 = (bf16[1,40,3584]{2,1,0:T(8,128)(2,1)}, bf16[1,40,3584]{2,1,0:T(8,128)(2,1)S(1)}, u32[]{:S(2)}) copy-start(bf16[1,40,3584]{2,1,0:T(8,128)(2,1)S(1)} %collective-permute-done.11) | copy-start | bytes 860164
  41.8 13.7 %collective-permute-start.6 = (bf16[160,3584]{1,0:T(8,128)(2,1)}, bf16[160,3584]{1,0:T(8,128)(2,1)}, u32[]{:S(2)}, u32[]{:S(2)}) collective-permute-start(bf16[160,3584]{1,0:T(8,128)(2,1)} %bitcast.10), channel_id=1, source_target_pairs={{0,1},{1,0},{2,3},{3,2},{4,5},{5,4},{6,7},{7,6},{8,9},{9,8},{10,11... | collective-permute-start | bytes 3440648 | tf_op jit(solution)/shard_map/ppermute | solution.py:12
  43.9 0.9 copy-start.6
  55.5 4.9 %copy-start.1 = (bf16[160,3584]{1,0:T(8,128)(2,1)}, bf16[160,3584]{1,0:T(8,128)(2,1)S(1)}, u32[]{:S(2)}) copy-start(bf16[160,3584]{1,0:T(8,128)(2,1)S(1)} %collective-permute-done.7) | copy-start | bytes 3440644
  62.4 11.0 %collective-permute-start.14 = (bf16[1,40,3584]{2,1,0:T(8,128)(2,1)}, bf16[1,40,3584]{2,1,0:T(8,128)(2,1)}, u32[]{:S(2)}, u32[]{:S(2)}) collective-permute-start(bf16[1,40,3584]{2,1,0:T(8,128)(2,1)} %get-tuple-element.13), channel_id=1, source_target_pairs={{0,6},{2,4},{4,2},{6,0},{1,7},{3,5},{5,3},{7,1},{8,14},{10,12},{12... | collective-permute-start | bytes 860168 | tf_op jit(solution)/shard_map/ppermute | solution.py:16
  64.8 12.6 %collective-permute-start.13 = (bf16[1,40,3584]{2,1,0:T(8,128)(2,1)}, bf16[1,40,3584]{2,1,0:T(8,128)(2,1)}, u32[]{:S(2)}, u32[]{:S(2)}) collective-permute-start(bf16[1,40,3584]{2,1,0:T(8,128)(2,1)} %get-tuple-element.14), channel_id=1, source_target_pairs={{0,4},{2,6},{4,0},{6,2},{1,5},{3,7},{5,1},{7,3},{8,12},{10,14},{12... | collective-permute-start | bytes 860168 | tf_op jit(solution)/shard_map/ppermute | solution.py:16
  65.1 3.3 %copy-start = (f32[160,3584]{1,0:T(8,128)S(1)}, f32[160,3584]{1,0:T(8,128)}, u32[]{:S(2)}) copy-start(f32[160,3584]{1,0:T(8,128)} %fusion.7) | copy-start | bytes 6881284
  65.1 12.9 %collective-permute-start.12 = (bf16[1,40,3584]{2,1,0:T(8,128)(2,1)}, bf16[1,40,3584]{2,1,0:T(8,128)(2,1)}, u32[]{:S(2)}, u32[]{:S(2)}) collective-permute-start(bf16[1,40,3584]{2,1,0:T(8,128)(2,1)} %get-tuple-element.12), channel_id=1, source_target_pairs={{0,2},{2,0},{4,6},{6,4},{1,3},{3,1},{5,7},{7,5},{8,10},{10,8},{12,... | collective-permute-start | bytes 860168 | tf_op jit(solution)/shard_map/ppermute | solution.py:16
  72.6 10.3 %copy-start.2 = (bf16[160,3584]{1,0:T(8,128)(2,1)S(1)}, bf16[160,3584]{1,0:T(8,128)(2,1)}, u32[]{:S(2)}) copy-start(bf16[160,3584]{1,0:T(8,128)(2,1)} %fusion.6) | copy-start | bytes 3440644
  79.4 16.7 %collective-permute-start.18 = (bf16[1,40,3584]{2,1,0:T(8,128)(2,1)S(1)}, bf16[1,40,3584]{2,1,0:T(8,128)(2,1)S(1)}, u32[]{:S(2)}, u32[]{:S(2)}) collective-permute-start(bf16[1,40,3584]{2,1,0:T(8,128)(2,1)S(1)} %fusion.14), channel_id=1, source_target_pairs={{0,8},{8,0},{1,9},{9,1},{2,10},{10,2},{3,11},{11,3},{4,12},{12,4},... | collective-permute-start | bytes 860168 | tf_op jit(solution)/shard_map/ppermute | solution.py:12
  82.9 13.7 %collective-permute-start.17 = (bf16[1,40,3584]{2,1,0:T(8,128)(2,1)S(1)}, bf16[1,40,3584]{2,1,0:T(8,128)(2,1)S(1)}, u32[]{:S(2)}, u32[]{:S(2)}) collective-permute-start(bf16[1,40,3584]{2,1,0:T(8,128)(2,1)S(1)} %get-tuple-element.10), channel_id=1, source_target_pairs={{0,6},{2,4},{4,2},{6,0},{1,7},{3,5},{5,3},{7,1},{8,14},{10,12},{12... | collective-permute-start | bytes 860168 | tf_op jit(solution)/shard_map/ppermute | solution.py:16
  85.7 16.8 %collective-permute-start.16 = (bf16[1,40,3584]{2,1,0:T(8,128)(2,1)S(1)}, bf16[1,40,3584]{2,1,0:T(8,128)(2,1)S(1)}, u32[]{:S(2)}, u32[]{:S(2)}) collective-permute-start(bf16[1,40,3584]{2,1,0:T(8,128)(2,1)S(1)} %get-tuple-element.11), channel_id=1, source_target_pairs={{0,4},{2,6},{4,0},{6,2},{1,5},{3,7},{5,1},{7,3},{8,12},{10,14},{12... | collective-permute-start | bytes 860168 | tf_op jit(solution)/shard_map/ppermute | solution.py:16
  85.7 16.8 %collective-permute-start.15 = (bf16[1,40,3584]{2,1,0:T(8,128)(2,1)S(1)}, bf16[1,40,3584]{2,1,0:T(8,128)(2,1)S(1)}, u32[]{:S(2)}, u32[]{:S(2)}) collective-permute-start(bf16[1,40,3584]{2,1,0:T(8,128)(2,1)S(1)} %get-tuple-element.9), channel_id=1, source_target_pairs={{0,2},{2,0},{4,6},{6,4},{1,3},{3,1},{5,7},{7,5},{8,10},{10,8},{12,... | collective-permute-start | bytes 860168 | tf_op jit(solution)/shard_map/ppermute | solution.py:16
  102.7 0.7 copy-start.7
  102.8 2.9 %collective-permute-start.19 = (f32[2,40,3584]{2,1,0:T(8,128)S(1)}, f32[2,40,3584]{2,1,0:T(8,128)S(1)}, u32[]{:S(2)}, u32[]{:S(2)}) collective-permute-start(f32[2,40,3584]{2,1,0:T(8,128)S(1)} %pad_maximum_fusion.3), channel_id=1, source_target_pairs={{0,1},{1,0},{2,3},{3,2},{4,5},{5,4},{6,7},{7,6},{8,9},{9,8},{10,11... | collective-permute-start | bytes 3440648 | tf_op jit(solution)/shard_map/ppermute | solution.py:12

commit v9 on v6

--- a/solution.py
+++ b/solution.py
@@ -134,7 +134,7 @@
     ).astype(jnp.float32)
     mixing = jnp.sum(own_match * route_weight[:, :, None], axis=1)
     mixed = jnp.dot(
-        mixing, slots_out, precision=lax.Precision.HIGHEST, preferred_element_type=jnp.float32
+        mixing, slots_out, precision=lax.Precision.HIGH, preferred_element_type=jnp.float32
     )
     return mixed.astype(jnp.bfloat16)
 

time: 91 us -> 90.5 us (level)
  no operation moved by 1% of the time
where the time goes in v9:
time: 90.5 us; the launch traced here: 90.3 us
  waiting for transfers between devices  57.6 us (64%)
  starting transfers between devices  19.4 us (21%)
  matrix products  7.88 us (9%)
  other arithmetic  3.37 us (4%)
  local copies, waits for them, and re-layouts  1.84 us (2%)
    ppermute x12, waiting for transfers between devices, swap(): return lax.ppermute(x, axis, [(i, i ^ k) for i in range(size)])  35.2 us
    ppermute x8, waiting for transfers between devices, shift(): return lax.ppermute(x, axis, [(i, (i + k) % size) for i in range(size)])  22.4 us
    ppermute x12, starting transfers between devices, swap(): return lax.ppermute(x, axis, [(i, i ^ k) for i in range(size)])  13.4 us
    ppermute x8, starting transfers between devices, shift(): return lax.ppermute(x, axis, [(i, (i + k) % size) for i in range(size)])  5.94 us
    dot_general x2, matrix products, quarter_rows(): up = lax.dot_general(rows, w_up, dims, preferred_element_type=jnp.float32)  2.02 us
    dot_general x2, matrix products, quarter_rows(): lax.dot_general(rows, w_gate, dims, preferred_element_type=jnp.float32)  2.01 us
    dot_general x4, matrix products, quarter_rows(): jnp.dot(hidden[:, c * slab:(c + 1) * slab], w_down[c * slab:(c + 1) * sla...  1.92 us
  transfers between devices with their start and end apart: 20, of which 12 were waited for; matrix products, arithmetic and copies ran while one was open for 10% of the time, Pallas kernels for 0%

profile of v9, /device:TPU:0, one launch (start us, length us, event | category | flops | bytes accessed | tf_op | source)
XLA Modules:
  0.0 90.3 jit_solution(126609237579513921)
XLA Ops:
  0.8 0.7 collective-permute-done
  1.5 0.8 pad_add_fusion.1
  2.7 0.6 reduce-window.6
  5.0 4.0 %collective-permute-start.8 = (bf16[1,40,3584]{2,1,0:T(8,128)(2,1)S(1)}, bf16[1,40,3584]{2,1,0:T(8,128)(2,1)S(1)}, u32[]{:S(2)}, u32[]{:S(2)}) collective-permute-start(bf16[1,40,3584]{2,1,0:T(8,128)(2,1)S(1)} %get-tuple-element.15), channel_id=1, source_target_pairs={{0,8},{8,0},{1,9},{9,1},{2,10},{10,2},{3,11},{11,3},{4,12},{12,4},... | collective-permute-start | bytes 860168 | tf_op jit(solution)/shard_map/ppermute | solution.py:12
  8.9 2.5 %collective-permute-start.4 = (bf16[1,40,3584]{2,1,0:T(8,128)(2,1)S(1)}, bf16[1,40,3584]{2,1,0:T(8,128)(2,1)S(1)}, u32[]{:S(2)}, u32[]{:S(2)}) collective-permute-start(bf16[1,40,3584]{2,1,0:T(8,128)(2,1)S(1)} %get-tuple-element.16), channel_id=1, source_target_pairs={{0,6},{2,4},{4,2},{6,0},{1,7},{3,5},{5,3},{7,1},{8,14},{10,12},{12... | collective-permute-start | bytes 860168 | tf_op jit(solution)/shard_map/ppermute | solution.py:16
  11.9 0.5 collective-permute-start.2
  12.4 9.9 %collective-permute-done.8 = bf16[1,40,3584]{2,1,0:T(8,128)(2,1)S(1)} collective-permute-done((bf16[1,40,3584]{2,1,0:T(8,128)(2,1)S(1)}, bf16[1,40,3584]{2,1,0:T(8,128)(2,1)S(1)}, u32[]{:S(2)}, u32[]{:S(2)}) %collective-permute-start.8) | collective-permute-done | bytes 286752 | tf_op jit(solution)/shard_map/ppermute | solution.py:12
  22.4 2.3 %collective-permute-done.4 = bf16[1,40,3584]{2,1,0:T(8,128)(2,1)S(1)} collective-permute-done((bf16[1,40,3584]{2,1,0:T(8,128)(2,1)S(1)}, bf16[1,40,3584]{2,1,0:T(8,128)(2,1)S(1)}, u32[]{:S(2)}, u32[]{:S(2)}) %collective-permute-start.4) | collective-permute-done | bytes 286752 | tf_op jit(solution)/shard_map/ppermute | solution.py:16
  24.6 1.1 %collective-permute-start.11 = (bf16[1,40,3584]{2,1,0:T(8,128)(2,1)S(1)}, bf16[1,40,3584]{2,1,0:T(8,128)(2,1)S(1)}, u32[]{:S(2)}, u32[]{:S(2)}) collective-permute-start(bf16[1,40,3584]{2,1,0:T(8,128)(2,1)S(1)} %collective-permute-done.8), channel_id=1, source_target_pairs={{0,6},{2,4},{4,2},{6,0},{1,7},{3,5},{5,3},{7,1},{8,14},{10,12},{12... | collective-permute-start | bytes 860168 | tf_op jit(solution)/shard_map/ppermute | solution.py:16
  25.8 5.0 %collective-permute-done.3 = bf16[1,40,3584]{2,1,0:T(8,128)(2,1)S(1)} collective-permute-done((bf16[1,40,3584]{2,1,0:T(8,128)(2,1)S(1)}, bf16[1,40,3584]{2,1,0:T(8,128)(2,1)S(1)}, u32[]{:S(2)}, u32[]{:S(2)}) %collective-permute-start.3) | collective-permute-done | bytes 286752 | tf_op jit(solution)/shard_map/ppermute | solution.py:16
  31.0 1.5 %collective-permute-start.9 = (bf16[1,40,3584]{2,1,0:T(8,128)(2,1)S(1)}, bf16[1,40,3584]{2,1,0:T(8,128)(2,1)S(1)}, u32[]{:S(2)}, u32[]{:S(2)}) collective-permute-start(bf16[1,40,3584]{2,1,0:T(8,128)(2,1)S(1)} %collective-permute-done.8), channel_id=1, source_target_pairs={{0,2},{2,0},{4,6},{6,4},{1,3},{3,1},{5,7},{7,5},{8,10},{10,8},{12,... | collective-permute-start | bytes 860168 | tf_op jit(solution)/shard_map/ppermute | solution.py:16
  32.7 4.3 %collective-permute-done.11 = bf16[1,40,3584]{2,1,0:T(8,128)(2,1)S(1)} collective-permute-done((bf16[1,40,3584]{2,1,0:T(8,128)(2,1)S(1)}, bf16[1,40,3584]{2,1,0:T(8,128)(2,1)S(1)}, u32[]{:S(2)}, u32[]{:S(2)}) %collective-permute-start.11) | collective-permute-done | bytes 286752 | tf_op jit(solution)/shard_map/ppermute | solution.py:16
  37.0 5.0 %collective-permute-done.10 = bf16[1,40,3584]{2,1,0:T(8,128)(2,1)S(1)} collective-permute-done((bf16[1,40,3584]{2,1,0:T(8,128)(2,1)S(1)}, bf16[1,40,3584]{2,1,0:T(8,128)(2,1)S(1)}, u32[]{:S(2)}, u32[]{:S(2)}) %collective-permute-start.10) | collective-permute-done | bytes 286752 | tf_op jit(solution)/shard_map/ppermute | solution.py:16
  42.2 1.0 %fusion.11 = f32[160,320]{1,0:T(8,128)S(1)} fusion(bf16[160,3584]{1,0:T(8,128)(2,1)S(1)} %bitcast.84, bf16[160,3584]{1,0:T(8,128)(2,1)S(1)} %collective-permute-done.5, bf16[160,3584]{1,0:T(8,128)(2,1)S(1)} %bitcast.97), kind=kOutput, calls=%fused_computation.20 | convolution fusion | flops 371589120 | bytes 3645440 | tf_op jit(solution)/shard_map/dot_general | solution.py:21
  43.2 1.0 %multiply_convert_fusion.1 = bf16[160,320]{1,0:T(8,128)(2,1)S(1)} fusion(f32[160,320]{1,0:T(8,128)S(1)} %fusion.11, bf16[160,3584]{1,0:T(8,128)(2,1)S(1)} %bitcast.85, bf16[160,3584]{1,0:T(8,128)(2,1)S(1)} %collective-permute-done.6, bf16[160,3584]{1,0:T(8,128)(2,1)S(1)} %bitcast.100), kind=kOutput, calls=%fused_computation.48 | convolution fusion | flops 371896320 | bytes 3747840 | tf_op jit(solution)/shard_map/dot_general | solution.py:22
  44.2 1.0 %fusion.10 = f32[160,320]{1,0:T(8,128)S(1)} fusion(bf16[160,3584]{1,0:T(8,128)(2,1)S(1)} %bitcast.86, bf16[160,3584]{1,0:T(8,128)(2,1)S(1)} %collective-permute-done.5, bf16[160,3584]{1,0:T(8,128)(2,1)S(1)} %bitcast.98), kind=kOutput, calls=%fused_computation.19 | convolution fusion | flops 371589120 | bytes 3645440 | tf_op jit(solution)/shard_map/dot_general | solution.py:21
  45.7 1.0 %multiply_convert_fusion = bf16[160,320]{1,0:T(8,128)(2,1)S(1)} fusion(f32[160,320]{1,0:T(8,128)S(1)} %fusion.10, bf16[160,3584]{1,0:T(8,128)(2,1)S(1)} %bitcast.87, bf16[160,3584]{1,0:T(8,128)(2,1)S(1)} %collective-permute-done.6, bf16[160,3584]{1,0:T(8,128)(2,1)S(1)} %bitcast.101), kind=kOutput, calls=%fused_computation.47 | convolution fusion | flops 371896320 | bytes 3747840 | tf_op jit(solution)/shard_map/dot_general | solution.py:22
  47.2 0.5 fusion.2
  47.8 1.5 %collective-permute-start.12 = (bf16[1,40,3584]{2,1,0:T(8,128)(2,1)S(1)}, bf16[1,40,3584]{2,1,0:T(8,128)(2,1)S(1)}, u32[]{:S(2)}, u32[]{:S(2)}) collective-permute-start(bf16[1,40,3584]{2,1,0:T(8,128)(2,1)S(1)} %get-tuple-element.12), channel_id=1, source_target_pairs={{0,2},{2,0},{4,6},{6,4},{1,3},{3,1},{5,7},{7,5},{8,10},{10,8},{12,... | collective-permute-start | bytes 860168 | tf_op jit(solution)/shard_map/ppermute | solution.py:16
  49.2 1.5 %collective-permute-start.14 = (bf16[1,40,3584]{2,1,0:T(8,128)(2,1)S(1)}, bf16[1,40,3584]{2,1,0:T(8,128)(2,1)S(1)}, u32[]{:S(2)}, u32[]{:S(2)}) collective-permute-start(bf16[1,40,3584]{2,1,0:T(8,128)(2,1)S(1)} %get-tuple-element.13), channel_id=1, source_target_pairs={{0,6},{2,4},{4,2},{6,0},{1,7},{3,5},{5,3},{7,1},{8,14},{10,12},{12... | collective-permute-start | bytes 860168 | tf_op jit(solution)/shard_map/ppermute | solution.py:16
  50.7 0.6 collective-permute-start.13
  51.8 10.9 %collective-permute-done.12 = bf16[1,40,3584]{2,1,0:T(8,128)(2,1)S(1)} collective-permute-done((bf16[1,40,3584]{2,1,0:T(8,128)(2,1)S(1)}, bf16[1,40,3584]{2,1,0:T(8,128)(2,1)S(1)}, u32[]{:S(2)}, u32[]{:S(2)}) %collective-permute-start.12) | collective-permute-done | bytes 286752 | tf_op jit(solution)/shard_map/ppermute | solution.py:16
  62.7 1.2 %collective-permute-done.13 = bf16[1,40,3584]{2,1,0:T(8,128)(2,1)S(1)} collective-permute-done((bf16[1,40,3584]{2,1,0:T(8,128)(2,1)S(1)}, bf16[1,40,3584]{2,1,0:T(8,128)(2,1)S(1)}, u32[]{:S(2)}, u32[]{:S(2)}) %collective-permute-start.13) | collective-permute-done | bytes 286752 | tf_op jit(solution)/shard_map/ppermute | solution.py:16
  64.1 1.4 %collective-permute-start.18 = (bf16[1,40,3584]{2,1,0:T(8,128)(2,1)S(1)}, bf16[1,40,3584]{2,1,0:T(8,128)(2,1)S(1)}, u32[]{:S(2)}, u32[]{:S(2)}) collective-permute-start(bf16[1,40,3584]{2,1,0:T(8,128)(2,1)S(1)} %fusion.18), channel_id=1, source_target_pairs={{0,8},{8,0},{1,9},{9,1},{2,10},{10,2},{3,11},{11,3},{4,12},{12,4},... | collective-permute-start | bytes 860168 | tf_op jit(solution)/shard_map/ppermute | solution.py:12
  65.5 0.8 collective-permute-start.15
  66.3 2.5 %collective-permute-start.17 = (bf16[1,40,3584]{2,1,0:T(8,128)(2,1)S(1)}, bf16[1,40,3584]{2,1,0:T(8,128)(2,1)S(1)}, u32[]{:S(2)}, u32[]{:S(2)}) collective-permute-start(bf16[1,40,3584]{2,1,0:T(8,128)(2,1)S(1)} %get-tuple-element.10), channel_id=1, source_target_pairs={{0,6},{2,4},{4,2},{6,0},{1,7},{3,5},{5,3},{7,1},{8,14},{10,12},{12... | collective-permute-start | bytes 860168 | tf_op jit(solution)/shard_map/ppermute | solution.py:16
  69.0 9.8 %collective-permute-done.18 = bf16[1,40,3584]{2,1,0:T(8,128)(2,1)S(1)} collective-permute-done((bf16[1,40,3584]{2,1,0:T(8,128)(2,1)S(1)}, bf16[1,40,3584]{2,1,0:T(8,128)(2,1)S(1)}, u32[]{:S(2)}, u32[]{:S(2)}) %collective-permute-start.18) | collective-permute-done | bytes 286752 | tf_op jit(solution)/shard_map/ppermute | solution.py:12
  78.9 4.1 %collective-permute-done.17 = bf16[1,40,3584]{2,1,0:T(8,128)(2,1)S(1)} collective-permute-done((bf16[1,40,3584]{2,1,0:T(8,128)(2,1)S(1)}, bf16[1,40,3584]{2,1,0:T(8,128)(2,1)S(1)}, u32[]{:S(2)}, u32[]{:S(2)}) %collective-permute-start.17) | collective-permute-done | bytes 286752 | tf_op jit(solution)/shard_map/ppermute | solution.py:16
  83.0 2.4 %collective-permute-done.16 = bf16[1,40,3584]{2,1,0:T(8,128)(2,1)S(1)} collective-permute-done((bf16[1,40,3584]{2,1,0:T(8,128)(2,1)S(1)}, bf16[1,40,3584]{2,1,0:T(8,128)(2,1)S(1)}, u32[]{:S(2)}, u32[]{:S(2)}) %collective-permute-start.16) | collective-permute-done | bytes 286752 | tf_op jit(solution)/shard_map/ppermute | solution.py:16
  85.7 0.5 copy-done.2
  86.7 1.9 %collective-permute-done.19 = f32[2,40,3584]{2,1,0:T(8,128)S(1)} collective-permute-done((f32[2,40,3584]{2,1,0:T(8,128)S(1)}, f32[2,40,3584]{2,1,0:T(8,128)S(1)}, u32[]{:S(2)}, u32[]{:S(2)}) %collective-permute-start.19) | collective-permute-done | bytes 1146912 | tf_op jit(solution)/shard_map/ppermute | solution.py:12
  88.7 1.6 %convolution_convert_fusion.5 = bf16[64,3584]{1,0:T(8,128)(2,1)} fusion(f32[64,160]{1,0:T(8,128)S(1)} %select_reduce_fusion, f32[160,3584]{1,0:T(8,128)S(1)} %bitcast.80), kind=kOutput, calls=%fused_computation.13 | convolution fusion | flops 220430336 | bytes 2793472 | tf_op jit(solution)/shard_map/dot_general | solution.py:136
  (66 shorter events, 6.6 us)
Async XLA Ops:
  0.0 4.6 %copy-start.1 = (bf16[64,3584]{1,0:T(8,128)(2,1)S(1)}, bf16[64,3584]{1,0:T(8,128)(2,1)}, u32[]{:S(2)}) copy-start(bf16[64,3584]{1,0:T(8,128)(2,1)} %param.6) | copy-start | bytes 1376260
  0.0 1.5 %collective-permute-start = (s32[64,8]{0,1:T(8,128)}, s32[64,8]{0,1:T(8,128)S(1)}, u32[]{:S(2)}, u32[]{:S(2)}) collective-permute-start(s32[64,8]{0,1:T(8,128)} %param.7), channel_id=1, source_target_pairs={{0,1},{1,0},{2,3},{3,2},{4,5},{5,4},{6,7},{7,6},{8,9},{9,8},{10,11... | collective-permute-start | bytes 6152 | tf_op jit(solution)/shard_map/ppermute | solution.py:12
  0.5 4.1 %collective-permute-start.1 = (bf16[64,3584]{1,0:T(8,128)(2,1)}, bf16[64,3584]{1,0:T(8,128)(2,1)S(1)}, u32[]{:S(2)}, u32[]{:S(2)}) collective-permute-start(bf16[64,3584]{1,0:T(8,128)(2,1)} %param.6), channel_id=1, source_target_pairs={{0,1},{1,0},{2,3},{3,2},{4,5},{5,4},{6,7},{7,6},{8,9},{9,8},{10,11... | collective-permute-start | bytes 1376264 | tf_op jit(solution)/shard_map/ppermute | solution.py:12
  4.5 7.9 %copy-start.3 = (bf16[1,160,3584]{2,1,0:T(8,128)(2,1)S(1)}, bf16[1,160,3584]{2,1,0:T(8,128)(2,1)}, u32[]{:S(2)}) copy-start(bf16[1,160,3584]{2,1,0:T(8,128)(2,1)} %param.9) | copy-start | bytes 3440644
  4.6 17.8 %copy-start.4 = (bf16[1,160,3584]{2,1,0:T(8,128)(2,1)S(1)}, bf16[1,160,3584]{2,1,0:T(8,128)(2,1)}, u32[]{:S(2)}) copy-start(bf16[1,160,3584]{2,1,0:T(8,128)(2,1)} %param.10) | copy-start | bytes 3440644
  5.0 17.4 %collective-permute-start.8 = (bf16[1,40,3584]{2,1,0:T(8,128)(2,1)S(1)}, bf16[1,40,3584]{2,1,0:T(8,128)(2,1)S(1)}, u32[]{:S(2)}, u32[]{:S(2)}) collective-permute-start(bf16[1,40,3584]{2,1,0:T(8,128)(2,1)S(1)} %get-tuple-element.15), channel_id=1, source_target_pairs={{0,8},{8,0},{1,9},{9,1},{2,10},{10,2},{3,11},{11,3},{4,12},{12,4},... | collective-permute-start | bytes 860168 | tf_op jit(solution)/shard_map/ppermute | solution.py:12
  8.9 15.7 %collective-permute-start.4 = (bf16[1,40,3584]{2,1,0:T(8,128)(2,1)S(1)}, bf16[1,40,3584]{2,1,0:T(8,128)(2,1)S(1)}, u32[]{:S(2)}, u32[]{:S(2)}) collective-permute-start(bf16[1,40,3584]{2,1,0:T(8,128)(2,1)S(1)} %get-tuple-element.16), channel_id=1, source_target_pairs={{0,6},{2,4},{4,2},{6,0},{1,7},{3,5},{5,3},{7,1},{8,14},{10,12},{12... | collective-permute-start | bytes 860168 | tf_op jit(solution)/shard_map/ppermute | solution.py:16
  11.5 19.3 %collective-permute-start.3 = (bf16[1,40,3584]{2,1,0:T(8,128)(2,1)S(1)}, bf16[1,40,3584]{2,1,0:T(8,128)(2,1)S(1)}, u32[]{:S(2)}, u32[]{:S(2)}) collective-permute-start(bf16[1,40,3584]{2,1,0:T(8,128)(2,1)S(1)} %get-tuple-element.16), channel_id=1, source_target_pairs={{0,4},{2,6},{4,0},{6,2},{1,5},{3,7},{5,1},{7,3},{8,12},{10,14},{12... | collective-permute-start | bytes 860168 | tf_op jit(solution)/shard_map/ppermute | solution.py:16
  11.9 19.1 %collective-permute-start.2 = (bf16[1,40,3584]{2,1,0:T(8,128)(2,1)S(1)}, bf16[1,40,3584]{2,1,0:T(8,128)(2,1)S(1)}, u32[]{:S(2)}, u32[]{:S(2)}) collective-permute-start(bf16[1,40,3584]{2,1,0:T(8,128)(2,1)S(1)} %get-tuple-element.16), channel_id=1, source_target_pairs={{0,2},{2,0},{4,6},{6,4},{1,3},{3,1},{5,7},{7,5},{8,10},{10,8},{12,... | collective-permute-start | bytes 860168 | tf_op jit(solution)/shard_map/ppermute | solution.py:16
  12.4 29.7 %collective-permute-start.5 = (bf16[160,3584]{1,0:T(8,128)(2,1)S(1)}, bf16[160,3584]{1,0:T(8,128)(2,1)S(1)}, u32[]{:S(2)}, u32[]{:S(2)}) collective-permute-start(bf16[160,3584]{1,0:T(8,128)(2,1)S(1)} %bitcast.96), channel_id=1, source_target_pairs={{0,1},{1,0},{2,3},{3,2},{4,5},{5,4},{6,7},{7,6},{8,9},{9,8},{10,11... | collective-permute-start | bytes 3440648 | tf_op jit(solution)/shard_map/ppermute | solution.py:12
  22.4 20.8 %collective-permute-start.6 = (bf16[160,3584]{1,0:T(8,128)(2,1)S(1)}, bf16[160,3584]{1,0:T(8,128)(2,1)S(1)}, u32[]{:S(2)}, u32[]{:S(2)}) collective-permute-start(bf16[160,3584]{1,0:T(8,128)(2,1)S(1)} %bitcast.99), channel_id=1, source_target_pairs={{0,1},{1,0},{2,3},{3,2},{4,5},{5,4},{6,7},{7,6},{8,9},{9,8},{10,11... | collective-permute-start | bytes 3440648 | tf_op jit(solution)/shard_map/ppermute | solution.py:12
  24.6 12.3 %collective-permute-start.11 = (bf16[1,40,3584]{2,1,0:T(8,128)(2,1)S(1)}, bf16[1,40,3584]{2,1,0:T(8,128)(2,1)S(1)}, u32[]{:S(2)}, u32[]{:S(2)}) collective-permute-start(bf16[1,40,3584]{2,1,0:T(8,128)(2,1)S(1)} %collective-permute-done.8), channel_id=1, source_target_pairs={{0,6},{2,4},{4,2},{6,0},{1,7},{3,5},{5,3},{7,1},{8,14},{10,12},{12... | collective-permute-start | bytes 860168 | tf_op jit(solution)/shard_map/ppermute | solution.py:16
  30.8 11.2 %collective-permute-start.10 = (bf16[1,40,3584]{2,1,0:T(8,128)(2,1)S(1)}, bf16[1,40,3584]{2,1,0:T(8,128)(2,1)S(1)}, u32[]{:S(2)}, u32[]{:S(2)}) collective-permute-start(bf16[1,40,3584]{2,1,0:T(8,128)(2,1)S(1)} %collective-permute-done.8), channel_id=1, source_target_pairs={{0,4},{2,6},{4,0},{6,2},{1,5},{3,7},{5,1},{7,3},{8,12},{10,14},{12... | collective-permute-start | bytes 860168 | tf_op jit(solution)/shard_map/ppermute | solution.py:16
  31.0 11.0 %collective-permute-start.9 = (bf16[1,40,3584]{2,1,0:T(8,128)(2,1)S(1)}, bf16[1,40,3584]{2,1,0:T(8,128)(2,1)S(1)}, u32[]{:S(2)}, u32[]{:S(2)}) collective-permute-start(bf16[1,40,3584]{2,1,0:T(8,128)(2,1)S(1)} %collective-permute-done.8), channel_id=1, source_target_pairs={{0,2},{2,0},{4,6},{6,4},{1,3},{3,1},{5,7},{7,5},{8,10},{10,8},{12,... | collective-permute-start | bytes 860168 | tf_op jit(solution)/shard_map/ppermute | solution.py:16
  32.5 4.5 %copy-start = (bf16[1,160,3584]{2,1,0:T(8,128)(2,1)S(1)}, bf16[1,160,3584]{2,1,0:T(8,128)(2,1)}, u32[]{:S(2)}) copy-start(bf16[1,160,3584]{2,1,0:T(8,128)(2,1)} %param.11) | copy-start | bytes 3440644
  37.0 10.2 %collective-permute-start.7 = (bf16[160,3584]{1,0:T(8,128)(2,1)S(1)}, bf16[160,3584]{1,0:T(8,128)(2,1)S(1)}, u32[]{:S(2)}, u32[]{:S(2)}) collective-permute-start(bf16[160,3584]{1,0:T(8,128)(2,1)S(1)} %bitcast.81), channel_id=1, source_target_pairs={{0,1},{1,0},{2,3},{3,2},{4,5},{5,4},{6,7},{7,6},{8,9},{9,8},{10,11... | collective-permute-start | bytes 3440648 | tf_op jit(solution)/shard_map/ppermute | solution.py:12
  47.8 14.9 %collective-permute-start.12 = (bf16[1,40,3584]{2,1,0:T(8,128)(2,1)S(1)}, bf16[1,40,3584]{2,1,0:T(8,128)(2,1)S(1)}, u32[]{:S(2)}, u32[]{:S(2)}) collective-permute-start(bf16[1,40,3584]{2,1,0:T(8,128)(2,1)S(1)} %get-tuple-element.12), channel_id=1, source_target_pairs={{0,2},{2,0},{4,6},{6,4},{1,3},{3,1},{5,7},{7,5},{8,10},{10,8},{12,... | collective-permute-start | bytes 860168 | tf_op jit(solution)/shard_map/ppermute | solution.py:16
  49.2 13.5 %collective-permute-start.14 = (bf16[1,40,3584]{2,1,0:T(8,128)(2,1)S(1)}, bf16[1,40,3584]{2,1,0:T(8,128)(2,1)S(1)}, u32[]{:S(2)}, u32[]{:S(2)}) collective-permute-start(bf16[1,40,3584]{2,1,0:T(8,128)(2,1)S(1)} %get-tuple-element.13), channel_id=1, source_target_pairs={{0,6},{2,4},{4,2},{6,0},{1,7},{3,5},{5,3},{7,1},{8,14},{10,12},{12... | collective-permute-start | bytes 860168 | tf_op jit(solution)/shard_map/ppermute | solution.py:16
  50.7 13.2 %collective-permute-start.13 = (bf16[1,40,3584]{2,1,0:T(8,128)(2,1)S(1)}, bf16[1,40,3584]{2,1,0:T(8,128)(2,1)S(1)}, u32[]{:S(2)}, u32[]{:S(2)}) collective-permute-start(bf16[1,40,3584]{2,1,0:T(8,128)(2,1)S(1)} %get-tuple-element.14), channel_id=1, source_target_pairs={{0,4},{2,6},{4,0},{6,2},{1,5},{3,7},{5,1},{7,3},{8,12},{10,14},{12... | collective-permute-start | bytes 860168 | tf_op jit(solution)/shard_map/ppermute | solution.py:16
  64.1 14.8 %collective-permute-start.18 = (bf16[1,40,3584]{2,1,0:T(8,128)(2,1)S(1)}, bf16[1,40,3584]{2,1,0:T(8,128)(2,1)S(1)}, u32[]{:S(2)}, u32[]{:S(2)}) collective-permute-start(bf16[1,40,3584]{2,1,0:T(8,128)(2,1)S(1)} %fusion.18), channel_id=1, source_target_pairs={{0,8},{8,0},{1,9},{9,1},{2,10},{10,2},{3,11},{11,3},{4,12},{12,4},... | collective-permute-start | bytes 860168 | tf_op jit(solution)/shard_map/ppermute | solution.py:12
  65.5 13.4 %collective-permute-start.15 = (bf16[1,40,3584]{2,1,0:T(8,128)(2,1)S(1)}, bf16[1,40,3584]{2,1,0:T(8,128)(2,1)S(1)}, u32[]{:S(2)}, u32[]{:S(2)}) collective-permute-start(bf16[1,40,3584]{2,1,0:T(8,128)(2,1)S(1)} %get-tuple-element.9), channel_id=1, source_target_pairs={{0,2},{2,0},{4,6},{6,4},{1,3},{3,1},{5,7},{7,5},{8,10},{10,8},{12,... | collective-permute-start | bytes 860168 | tf_op jit(solution)/shard_map/ppermute | solution.py:16
  66.3 16.7 %collective-permute-start.17 = (bf16[1,40,3584]{2,1,0:T(8,128)(2,1)S(1)}, bf16[1,40,3584]{2,1,0:T(8,128)(2,1)S(1)}, u32[]{:S(2)}, u32[]{:S(2)}) collective-permute-start(bf16[1,40,3584]{2,1,0:T(8,128)(2,1)S(1)} %get-tuple-element.10), channel_id=1, source_target_pairs={{0,6},{2,4},{4,2},{6,0},{1,7},{3,5},{5,3},{7,1},{8,14},{10,12},{12... | collective-permute-start | bytes 860168 | tf_op jit(solution)/shard_map/ppermute | solution.py:16
  68.7 16.7 %collective-permute-start.16 = (bf16[1,40,3584]{2,1,0:T(8,128)(2,1)S(1)}, bf16[1,40,3584]{2,1,0:T(8,128)(2,1)S(1)}, u32[]{:S(2)}, u32[]{:S(2)}) collective-permute-start(bf16[1,40,3584]{2,1,0:T(8,128)(2,1)S(1)} %get-tuple-element.11), channel_id=1, source_target_pairs={{0,4},{2,6},{4,0},{6,2},{1,5},{3,7},{5,1},{7,3},{8,12},{10,14},{12... | collective-permute-start | bytes 860168 | tf_op jit(solution)/shard_map/ppermute | solution.py:16
  85.5 0.7 copy-start.2
  85.6 2.9 %collective-permute-start.19 = (f32[2,40,3584]{2,1,0:T(8,128)S(1)}, f32[2,40,3584]{2,1,0:T(8,128)S(1)}, u32[]{:S(2)}, u32[]{:S(2)}) collective-permute-start(f32[2,40,3584]{2,1,0:T(8,128)S(1)} %pad_maximum_fusion.9), channel_id=1, source_target_pairs={{0,1},{1,0},{2,3},{3,2},{4,5},{5,4},{6,7},{7,6},{8,9},{9,8},{10,11... | collective-permute-start | bytes 3440648 | tf_op jit(solution)/shard_map/ppermute | solution.py:12

commit v10 on v9

--- a/solution.py
+++ b/solution.py
@@ -92,11 +92,14 @@
             return swap(x, "sh", sharers, k)
         return shift(x, "sh", sharers, -k)
 
-    def group_partial(sent):
-        group = [sent] + [exchange(sent, k) for k in range(1, sharers)]
+    def group_rows(sent):
+        return [sent] + [exchange(sent, k) for k in range(1, sharers)]
+
+    def group_partial(group):
+        shape = (sharers,) + group[0].shape
         rows = jnp.stack(group).reshape(-1, width)
         partial = quarter_rows(rows, wg, wu, wd, n_ctx).astype(jnp.bfloat16)
-        return partial.reshape((sharers,) + sent.shape)
+        return partial.reshape(shape)
 
     def group_sum(partial):
         total = partial[0].astype(jnp.float32)
@@ -105,15 +108,17 @@
         return total
 
     if experts == 2:
-        local_part = group_partial(packed[0:1])
-        far_part = group_partial(shift(packed[1:2], "ex", 2, 1))
+        local_rows = group_rows(packed[0:1])
+        far_rows = group_rows(shift(packed[1:2], "ex", 2, 1))
+        both = group_partial([jnp.concatenate(p, axis=0) for p in zip(local_rows, far_rows)])
+        local_part, far_part = both[:, 0:1], both[:, 1:2]
         far_out = group_sum(far_part)
         local_part, far_out = lax.optimization_barrier((local_part, far_out))
         back = shift(far_out.astype(RETURN_DTYPE), "ex", 2, 1).astype(jnp.float32)
         mine = jnp.concatenate([group_sum(local_part), back], axis=0)
     else:
         sent = lax.all_to_all(packed, "ex", split_axis=0, concat_axis=0, tiled=True)
-        expert_out = group_sum(group_partial(sent)).astype(RETURN_DTYPE)
+        expert_out = group_sum(group_partial(group_rows(sent))).astype(RETURN_DTYPE)
         mine = lax.all_to_all(expert_out, "ex", split_axis=0, concat_axis=0, tiled=True)
         mine = mine.astype(jnp.float32)
     theirs = shift(mine, "context", n_ctx, 1)

time: 90.5 us -> 101 us (1.12)
  waiting for transfers between devices: 57.6 us -> 65.2 us
  matrix products: 7.88 us -> 9.78 us
  starting transfers between devices: 19.4 us -> 21.1 us
    ppermute x12, waiting for transfers between devices: 35.2 us -> 43.6 us  [swap(): return lax.ppermute(x, axis, [(i, i ^ k) for i in range(size)])]
    dot_general x1, matrix products: 0.29 us -> 1.32 us  [per_device(): jnp.dot(picker, pair_tokens, preferred_element_type=jnp.float32)]
    dot_general x2 -> x1, matrix products: 2.02 us -> 2.63 us  [quarter_rows(): up = lax.dot_general(rows, w_up, dims, preferred_element_type=jnp.float32)]
    dot_general x2 -> x1, matrix products: 2.01 us -> 2.62 us  [quarter_rows(): lax.dot_general(rows, w_gate, dims, preferred_element_type=jnp.float32)]
  transfers between devices with their start and end apart: 20 -> 20, of which waited for: 12 -> 14; matrix products, arithmetic and copies ran while one was open for 10% -> 10% of each run, Pallas kernels for 0% -> 0%
where the time goes in v10:
time: 101 us
  waiting for transfers between devices  65.2 us (65%)
  starting transfers between devices  21.1 us (21%)
  matrix products  9.78 us (10%)
  other arithmetic  3.57 us (4%)
  local copies, waits for them, and re-layouts  1.36 us (1%)
    ppermute x12, waiting for transfers between devices, swap(): return lax.ppermute(x, axis, [(i, i ^ k) for i in range(size)])  43.6 us
    ppermute x8, waiting for transfers between devices, shift(): return lax.ppermute(x, axis, [(i, (i + k) % size) for i in range(size)])  21.5 us
    ppermute x12, starting transfers between devices, swap(): return lax.ppermute(x, axis, [(i, i ^ k) for i in range(size)])  14.4 us
    ppermute x8, starting transfers between devices, shift(): return lax.ppermute(x, axis, [(i, (i + k) % size) for i in range(size)])  6.69 us
    dot_general x1, matrix products, quarter_rows(): up = lax.dot_general(rows, w_up, dims, preferred_element_type=jnp.float32)  2.63 us
    dot_general x1, matrix products, quarter_rows(): lax.dot_general(rows, w_gate, dims, preferred_element_type=jnp.float32)  2.62 us
  transfers between devices with their start and end apart: 20, of which 14 were waited for; matrix products, arithmetic and copies ran while one was open for 10% of the time, Pallas kernels for 0%

profile of v10, /device:TPU:0, one launch (start us, length us, event | category | flops | bytes accessed | tf_op | source)
XLA Modules:
  0.0 101.2 jit_solution(11637165916507177714)
XLA Ops:
  0.8 0.7 collective-permute-done
  1.5 0.8 pad_add_fusion.1
  4.6 1.3 %convolution_convert_fusion.2 = bf16[80,3584]{1,0:T(8,128)(2,1)S(1)} fusion(bf16[64,3584]{1,0:T(8,128)(2,1)S(1)} %collective-permute-done.1, bf16[64,3584]{1,0:T(8,128)(2,1)} %param.6, bf16[80,128]{1,0:T(8,128)(2,1)S(1)} %convert_reduce_fusion), kind=kOutput, calls=%fused_computation.6 | convolution fusion | flops 75522048 | bytes 1511424 | tf_op jit(solution)/shard_map/dot_general | solution.py:82
  5.9 4.0 %collective-permute-start.2 = (bf16[1,40,3584]{2,1,0:T(8,128)(2,1)S(1)}, bf16[1,40,3584]{2,1,0:T(8,128)(2,1)S(1)}, u32[]{:S(2)}, u32[]{:S(2)}) collective-permute-start(bf16[1,40,3584]{2,1,0:T(8,128)(2,1)S(1)} %get-tuple-element.16), channel_id=1, source_target_pairs={{0,8},{8,0},{1,9},{9,1},{2,10},{10,2},{3,11},{11,3},{4,12},{12,4},... | collective-permute-start | bytes 860168 | tf_op jit(solution)/shard_map/ppermute | solution.py:12
  10.4 2.5 %collective-permute-start.7 = (bf16[1,40,3584]{2,1,0:T(8,128)(2,1)S(1)}, bf16[1,40,3584]{2,1,0:T(8,128)(2,1)S(1)}, u32[]{:S(2)}, u32[]{:S(2)}) collective-permute-start(bf16[1,40,3584]{2,1,0:T(8,128)(2,1)S(1)} %get-tuple-element.15), channel_id=1, source_target_pairs={{0,6},{2,4},{4,2},{6,0},{1,7},{3,5},{5,3},{7,1},{8,14},{10,12},{12... | collective-permute-start | bytes 860168 | tf_op jit(solution)/shard_map/ppermute | solution.py:16
  12.9 10.4 %collective-permute-done.2 = bf16[1,40,3584]{2,1,0:T(8,128)(2,1)S(1)} collective-permute-done((bf16[1,40,3584]{2,1,0:T(8,128)(2,1)S(1)}, bf16[1,40,3584]{2,1,0:T(8,128)(2,1)S(1)}, u32[]{:S(2)}, u32[]{:S(2)}) %collective-permute-start.2) | collective-permute-done | bytes 286752 | tf_op jit(solution)/shard_map/ppermute | solution.py:12
  23.3 1.6 %collective-permute-start.8 = (bf16[1,40,3584]{2,1,0:T(8,128)(2,1)S(1)}, bf16[1,40,3584]{2,1,0:T(8,128)(2,1)S(1)}, u32[]{:S(2)}, u32[]{:S(2)}) collective-permute-start(bf16[1,40,3584]{2,1,0:T(8,128)(2,1)S(1)} %collective-permute-done.2), channel_id=1, source_target_pairs={{0,6},{2,4},{4,2},{6,0},{1,7},{3,5},{5,3},{7,1},{8,14},{10,12},{12... | collective-permute-start | bytes 860168 | tf_op jit(solution)/shard_map/ppermute | solution.py:16
  25.0 0.6 collective-permute-done.7
  25.6 0.9 collective-permute-start.5
  26.5 7.5 %collective-permute-done.8 = bf16[1,40,3584]{2,1,0:T(8,128)(2,1)S(1)} collective-permute-done((bf16[1,40,3584]{2,1,0:T(8,128)(2,1)S(1)}, bf16[1,40,3584]{2,1,0:T(8,128)(2,1)S(1)}, u32[]{:S(2)}, u32[]{:S(2)}) %collective-permute-start.8) | collective-permute-done | bytes 286752 | tf_op jit(solution)/shard_map/ppermute | solution.py:16
  34.0 0.6 collective-permute-start.6
  34.7 5.6 %collective-permute-done.5 = bf16[1,40,3584]{2,1,0:T(8,128)(2,1)S(1)} collective-permute-done((bf16[1,40,3584]{2,1,0:T(8,128)(2,1)S(1)}, bf16[1,40,3584]{2,1,0:T(8,128)(2,1)S(1)}, u32[]{:S(2)}, u32[]{:S(2)}) %collective-permute-start.5) | collective-permute-done | bytes 286752 | tf_op jit(solution)/shard_map/ppermute | solution.py:16
  40.7 3.9 %collective-permute-done.6 = bf16[1,40,3584]{2,1,0:T(8,128)(2,1)S(1)} collective-permute-done((bf16[1,40,3584]{2,1,0:T(8,128)(2,1)S(1)}, bf16[1,40,3584]{2,1,0:T(8,128)(2,1)S(1)}, u32[]{:S(2)}, u32[]{:S(2)}) %collective-permute-start.6) | collective-permute-done | bytes 286752 | tf_op jit(solution)/shard_map/ppermute | solution.py:16
  44.6 0.8 collective-permute-start.4
  45.5 2.6 %collective-permute-done.3 = bf16[1,40,3584]{2,1,0:T(8,128)(2,1)S(1)} collective-permute-done((bf16[1,40,3584]{2,1,0:T(8,128)(2,1)S(1)}, bf16[1,40,3584]{2,1,0:T(8,128)(2,1)S(1)}, u32[]{:S(2)}, u32[]{:S(2)}) %collective-permute-start.3) | collective-permute-done | bytes 286752 | tf_op jit(solution)/shard_map/ppermute | solution.py:16
  48.1 4.9 %collective-permute-done.4 = bf16[1,40,3584]{2,1,0:T(8,128)(2,1)S(1)} collective-permute-done((bf16[1,40,3584]{2,1,0:T(8,128)(2,1)S(1)}, bf16[1,40,3584]{2,1,0:T(8,128)(2,1)S(1)}, u32[]{:S(2)}, u32[]{:S(2)}) %collective-permute-start.4) | collective-permute-done | bytes 286752 | tf_op jit(solution)/shard_map/ppermute | solution.py:16
  53.4 2.6 %fusion.4 = f32[320,320]{0,1:T(8,128)S(1)} fusion(bf16[320,3584]{1,0:T(8,128)(2,1)S(1)} %bitcast.71, bf16[160,3584]{1,0:T(8,128)(2,1)S(1)} %collective-permute-done.9, bf16[160,3584]{1,0:T(8,128)(2,1)} %bitcast.10), kind=kOutput, calls=%fused_computation.9 | convolution fusion | flops 738590720 | bytes 4997120 | tf_op jit(solution)/shard_map/dot_general | solution.py:21
  56.0 2.6 %multiply_convert_fusion = bf16[320,320]{0,1:T(8,128)(2,1)S(1)} fusion(f32[320,320]{0,1:T(8,128)S(1)} %fusion.4, bf16[320,3584]{1,0:T(8,128)(2,1)S(1)} %bitcast.72, bf16[160,3584]{1,0:T(8,128)(2,1)S(1)} %collective-permute-done.10, bf16[160,3584]{1,0:T(8,128)(2,1)} %bitcast.11), kind=kOutput, calls=%fused_computation.34 | convolution fusion | flops 739205120 | bytes 5201920 | tf_op jit(solution)/shard_map/dot_general | solution.py:22
  58.6 0.8 fusion.3
  59.4 0.8 fusion.2
  60.8 1.9 %collective-permute-start.14 = (bf16[1,40,3584]{2,1,0:T(8,128)(2,1)S(1)}, bf16[1,40,3584]{2,1,0:T(8,128)(2,1)S(1)}, u32[]{:S(2)}, u32[]{:S(2)}) collective-permute-start(bf16[1,40,3584]{2,1,0:T(8,128)(2,1)S(1)} %get-tuple-element.10), channel_id=1, source_target_pairs={{0,6},{2,4},{4,2},{6,0},{1,7},{3,5},{5,3},{7,1},{8,14},{10,12},{12... | collective-permute-start | bytes 860168 | tf_op jit(solution)/shard_map/ppermute | solution.py:16
  62.7 1.1 %collective-permute-start.13 = (bf16[1,40,3584]{2,1,0:T(8,128)(2,1)S(1)}, bf16[1,40,3584]{2,1,0:T(8,128)(2,1)S(1)}, u32[]{:S(2)}, u32[]{:S(2)}) collective-permute-start(bf16[1,40,3584]{2,1,0:T(8,128)(2,1)S(1)} %get-tuple-element.11), channel_id=1, source_target_pairs={{0,4},{2,6},{4,0},{6,2},{1,5},{3,7},{5,1},{7,3},{8,12},{10,14},{12... | collective-permute-start | bytes 860168 | tf_op jit(solution)/shard_map/ppermute | solution.py:16
  63.9 10.0 %collective-permute-done.12 = bf16[1,40,3584]{2,1,0:T(8,128)(2,1)S(1)} collective-permute-done((bf16[1,40,3584]{2,1,0:T(8,128)(2,1)S(1)}, bf16[1,40,3584]{2,1,0:T(8,128)(2,1)S(1)}, u32[]{:S(2)}, u32[]{:S(2)}) %collective-permute-start.12) | collective-permute-done | bytes 286752 | tf_op jit(solution)/shard_map/ppermute | solution.py:16
  74.0 1.2 %collective-permute-done.13 = bf16[1,40,3584]{2,1,0:T(8,128)(2,1)S(1)} collective-permute-done((bf16[1,40,3584]{2,1,0:T(8,128)(2,1)S(1)}, bf16[1,40,3584]{2,1,0:T(8,128)(2,1)S(1)}, u32[]{:S(2)}, u32[]{:S(2)}) %collective-permute-start.13) | collective-permute-done | bytes 286752 | tf_op jit(solution)/shard_map/ppermute | solution.py:16
  75.3 1.6 %collective-permute-start.18 = (bf16[1,40,3584]{2,1,0:T(8,128)(2,1)S(1)}, bf16[1,40,3584]{2,1,0:T(8,128)(2,1)S(1)}, u32[]{:S(2)}, u32[]{:S(2)}) collective-permute-start(bf16[1,40,3584]{2,1,0:T(8,128)(2,1)S(1)} %fusion.18), channel_id=1, source_target_pairs={{0,8},{8,0},{1,9},{9,1},{2,10},{10,2},{3,11},{11,3},{4,12},{12,4},... | collective-permute-start | bytes 860168 | tf_op jit(solution)/shard_map/ppermute | solution.py:12
  77.0 2.5 %collective-permute-start.15 = (bf16[1,40,3584]{2,1,0:T(8,128)(2,1)S(1)}, bf16[1,40,3584]{2,1,0:T(8,128)(2,1)S(1)}, u32[]{:S(2)}, u32[]{:S(2)}) collective-permute-start(bf16[1,40,3584]{2,1,0:T(8,128)(2,1)S(1)} %get-tuple-element.12), channel_id=1, source_target_pairs={{0,2},{2,0},{4,6},{6,4},{1,3},{3,1},{5,7},{7,5},{8,10},{10,8},{12,... | collective-permute-start | bytes 860168 | tf_op jit(solution)/shard_map/ppermute | solution.py:16
  79.5 1.3 %collective-permute-start.17 = (bf16[1,40,3584]{2,1,0:T(8,128)(2,1)S(1)}, bf16[1,40,3584]{2,1,0:T(8,128)(2,1)S(1)}, u32[]{:S(2)}, u32[]{:S(2)}) collective-permute-start(bf16[1,40,3584]{2,1,0:T(8,128)(2,1)S(1)} %get-tuple-element.13), channel_id=1, source_target_pairs={{0,6},{2,4},{4,2},{6,0},{1,7},{3,5},{5,3},{7,1},{8,14},{10,12},{12... | collective-permute-start | bytes 860168 | tf_op jit(solution)/shard_map/ppermute | solution.py:16
  81.0 8.0 %collective-permute-done.18 = bf16[1,40,3584]{2,1,0:T(8,128)(2,1)S(1)} collective-permute-done((bf16[1,40,3584]{2,1,0:T(8,128)(2,1)S(1)}, bf16[1,40,3584]{2,1,0:T(8,128)(2,1)S(1)}, u32[]{:S(2)}, u32[]{:S(2)}) %collective-permute-start.18) | collective-permute-done | bytes 286752 | tf_op jit(solution)/shard_map/ppermute | solution.py:12
  89.1 4.8 %collective-permute-done.17 = bf16[1,40,3584]{2,1,0:T(8,128)(2,1)S(1)} collective-permute-done((bf16[1,40,3584]{2,1,0:T(8,128)(2,1)S(1)}, bf16[1,40,3584]{2,1,0:T(8,128)(2,1)S(1)}, u32[]{:S(2)}, u32[]{:S(2)}) %collective-permute-start.17) | collective-permute-done | bytes 286752 | tf_op jit(solution)/shard_map/ppermute | solution.py:16
  93.9 2.4 %collective-permute-done.16 = bf16[1,40,3584]{2,1,0:T(8,128)(2,1)S(1)} collective-permute-done((bf16[1,40,3584]{2,1,0:T(8,128)(2,1)S(1)}, bf16[1,40,3584]{2,1,0:T(8,128)(2,1)S(1)}, u32[]{:S(2)}, u32[]{:S(2)}) %collective-permute-start.16) | collective-permute-done | bytes 286752 | tf_op jit(solution)/shard_map/ppermute | solution.py:16
  97.1 2.4 %collective-permute-done.19 = f32[2,40,3584]{2,1,0:T(8,128)S(1)} collective-permute-done((f32[2,40,3584]{2,1,0:T(8,128)S(1)}, f32[2,40,3584]{2,1,0:T(8,128)S(1)}, u32[]{:S(2)}, u32[]{:S(2)}) %collective-permute-start.19) | collective-permute-done | bytes 1146912 | tf_op jit(solution)/shard_map/ppermute | solution.py:12
  99.6 1.6 %convolution_convert_fusion.3 = bf16[64,3584]{1,0:T(8,128)(2,1)} fusion(f32[64,160]{1,0:T(8,128)S(1)} %select_reduce_fusion, f32[160,3584]{1,0:T(8,128)S(1)} %bitcast.70), kind=kOutput, calls=%fused_computation.7 | convolution fusion | flops 220430336 | bytes 2793472 | tf_op jit(solution)/shard_map/dot_general | solution.py:141
  (60 shorter events, 6.5 us)
Async XLA Ops:
  0.0 10.4 %copy-start = (bf16[1,160,3584]{2,1,0:T(8,128)(2,1)S(1)}, bf16[1,160,3584]{2,1,0:T(8,128)(2,1)}, u32[]{:S(2)}) copy-start(bf16[1,160,3584]{2,1,0:T(8,128)(2,1)} %param.11) | copy-start | bytes 3440644
  0.0 1.5 %collective-permute-start = (s32[64,8]{0,1:T(8,128)}, s32[64,8]{0,1:T(8,128)S(1)}, u32[]{:S(2)}, u32[]{:S(2)}) collective-permute-start(s32[64,8]{0,1:T(8,128)} %param.7), channel_id=1, source_target_pairs={{0,1},{1,0},{2,3},{3,2},{4,5},{5,4},{6,7},{7,6},{8,9},{9,8},{10,11... | collective-permute-start | bytes 6152 | tf_op jit(solution)/shard_map/ppermute | solution.py:12
  0.5 4.1 %collective-permute-start.1 = (bf16[64,3584]{1,0:T(8,128)(2,1)}, bf16[64,3584]{1,0:T(8,128)(2,1)S(1)}, u32[]{:S(2)}, u32[]{:S(2)}) collective-permute-start(bf16[64,3584]{1,0:T(8,128)(2,1)} %param.6), channel_id=1, source_target_pairs={{0,1},{1,0},{2,3},{3,2},{4,5},{5,4},{6,7},{7,6},{8,9},{9,8},{10,11... | collective-permute-start | bytes 1376264 | tf_op jit(solution)/shard_map/ppermute | solution.py:12
  5.9 17.4 %collective-permute-start.2 = (bf16[1,40,3584]{2,1,0:T(8,128)(2,1)S(1)}, bf16[1,40,3584]{2,1,0:T(8,128)(2,1)S(1)}, u32[]{:S(2)}, u32[]{:S(2)}) collective-permute-start(bf16[1,40,3584]{2,1,0:T(8,128)(2,1)S(1)} %get-tuple-element.16), channel_id=1, source_target_pairs={{0,8},{8,0},{1,9},{9,1},{2,10},{10,2},{3,11},{11,3},{4,12},{12,4},... | collective-permute-start | bytes 860168 | tf_op jit(solution)/shard_map/ppermute | solution.py:12
  9.9 43.4 %collective-permute-start.9 = (bf16[160,3584]{1,0:T(8,128)(2,1)}, bf16[160,3584]{1,0:T(8,128)(2,1)S(1)}, u32[]{:S(2)}, u32[]{:S(2)}) collective-permute-start(bf16[160,3584]{1,0:T(8,128)(2,1)} %bitcast.10), channel_id=1, source_target_pairs={{0,1},{1,0},{2,3},{3,2},{4,5},{5,4},{6,7},{7,6},{8,9},{9,8},{10,11... | collective-permute-start | bytes 3440648 | tf_op jit(solution)/shard_map/ppermute | solution.py:12
  9.9 46.1 %collective-permute-start.10 = (bf16[160,3584]{1,0:T(8,128)(2,1)}, bf16[160,3584]{1,0:T(8,128)(2,1)S(1)}, u32[]{:S(2)}, u32[]{:S(2)}) collective-permute-start(bf16[160,3584]{1,0:T(8,128)(2,1)} %bitcast.11), channel_id=1, source_target_pairs={{0,1},{1,0},{2,3},{3,2},{4,5},{5,4},{6,7},{7,6},{8,9},{9,8},{10,11... | collective-permute-start | bytes 3440648 | tf_op jit(solution)/shard_map/ppermute | solution.py:12
  10.4 49.0 %collective-permute-start.11 = (bf16[160,3584]{1,0:T(8,128)(2,1)S(1)}, bf16[160,3584]{1,0:T(8,128)(2,1)S(1)}, u32[]{:S(2)}, u32[]{:S(2)}) collective-permute-start(bf16[160,3584]{1,0:T(8,128)(2,1)S(1)} %bitcast.73), channel_id=1, source_target_pairs={{0,1},{1,0},{2,3},{3,2},{4,5},{5,4},{6,7},{7,6},{8,9},{9,8},{10,11... | collective-permute-start | bytes 3440648 | tf_op jit(solution)/shard_map/ppermute | solution.py:12
  10.4 15.2 %collective-permute-start.7 = (bf16[1,40,3584]{2,1,0:T(8,128)(2,1)S(1)}, bf16[1,40,3584]{2,1,0:T(8,128)(2,1)S(1)}, u32[]{:S(2)}, u32[]{:S(2)}) collective-permute-start(bf16[1,40,3584]{2,1,0:T(8,128)(2,1)S(1)} %get-tuple-element.15), channel_id=1, source_target_pairs={{0,6},{2,4},{4,2},{6,0},{1,7},{3,5},{5,3},{7,1},{8,14},{10,12},{12... | collective-permute-start | bytes 860168 | tf_op jit(solution)/shard_map/ppermute | solution.py:16
  23.3 10.7 %collective-permute-start.8 = (bf16[1,40,3584]{2,1,0:T(8,128)(2,1)S(1)}, bf16[1,40,3584]{2,1,0:T(8,128)(2,1)S(1)}, u32[]{:S(2)}, u32[]{:S(2)}) collective-permute-start(bf16[1,40,3584]{2,1,0:T(8,128)(2,1)S(1)} %collective-permute-done.2), channel_id=1, source_target_pairs={{0,6},{2,4},{4,2},{6,0},{1,7},{3,5},{5,3},{7,1},{8,14},{10,12},{12... | collective-permute-start | bytes 860168 | tf_op jit(solution)/shard_map/ppermute | solution.py:16
  25.6 14.6 %collective-permute-start.5 = (bf16[1,40,3584]{2,1,0:T(8,128)(2,1)S(1)}, bf16[1,40,3584]{2,1,0:T(8,128)(2,1)S(1)}, u32[]{:S(2)}, u32[]{:S(2)}) collective-permute-start(bf16[1,40,3584]{2,1,0:T(8,128)(2,1)S(1)} %get-tuple-element.15), channel_id=1, source_target_pairs={{0,4},{2,6},{4,0},{6,2},{1,5},{3,7},{5,1},{7,3},{8,12},{10,14},{12... | collective-permute-start | bytes 860168 | tf_op jit(solution)/shard_map/ppermute | solution.py:16
  34.0 10.6 %collective-permute-start.6 = (bf16[1,40,3584]{2,1,0:T(8,128)(2,1)S(1)}, bf16[1,40,3584]{2,1,0:T(8,128)(2,1)S(1)}, u32[]{:S(2)}, u32[]{:S(2)}) collective-permute-start(bf16[1,40,3584]{2,1,0:T(8,128)(2,1)S(1)} %collective-permute-done.2), channel_id=1, source_target_pairs={{0,4},{2,6},{4,0},{6,2},{1,5},{3,7},{5,1},{7,3},{8,12},{10,14},{12... | collective-permute-start | bytes 860168 | tf_op jit(solution)/shard_map/ppermute | solution.py:16
  40.2 7.8 %collective-permute-start.3 = (bf16[1,40,3584]{2,1,0:T(8,128)(2,1)S(1)}, bf16[1,40,3584]{2,1,0:T(8,128)(2,1)S(1)}, u32[]{:S(2)}, u32[]{:S(2)}) collective-permute-start(bf16[1,40,3584]{2,1,0:T(8,128)(2,1)S(1)} %get-tuple-element.15), channel_id=1, source_target_pairs={{0,2},{2,0},{4,6},{6,4},{1,3},{3,1},{5,7},{7,5},{8,10},{10,8},{12,... | collective-permute-start | bytes 860168 | tf_op jit(solution)/shard_map/ppermute | solution.py:16
  44.6 8.4 %collective-permute-start.4 = (bf16[1,40,3584]{2,1,0:T(8,128)(2,1)S(1)}, bf16[1,40,3584]{2,1,0:T(8,128)(2,1)S(1)}, u32[]{:S(2)}, u32[]{:S(2)}) collective-permute-start(bf16[1,40,3584]{2,1,0:T(8,128)(2,1)S(1)} %collective-permute-done.2), channel_id=1, source_target_pairs={{0,2},{2,0},{4,6},{6,4},{1,3},{3,1},{5,7},{7,5},{8,10},{10,8},{12,... | collective-permute-start | bytes 860168 | tf_op jit(solution)/shard_map/ppermute | solution.py:16
  60.3 13.7 %collective-permute-start.12 = (bf16[1,40,3584]{2,1,0:T(8,128)(2,1)S(1)}, bf16[1,40,3584]{2,1,0:T(8,128)(2,1)S(1)}, u32[]{:S(2)}, u32[]{:S(2)}) collective-permute-start(bf16[1,40,3584]{2,1,0:T(8,128)(2,1)S(1)} %get-tuple-element.9), channel_id=1, source_target_pairs={{0,2},{2,0},{4,6},{6,4},{1,3},{3,1},{5,7},{7,5},{8,10},{10,8},{12,... | collective-permute-start | bytes 860168 | tf_op jit(solution)/shard_map/ppermute | solution.py:16
  60.8 13.1 %collective-permute-start.14 = (bf16[1,40,3584]{2,1,0:T(8,128)(2,1)S(1)}, bf16[1,40,3584]{2,1,0:T(8,128)(2,1)S(1)}, u32[]{:S(2)}, u32[]{:S(2)}) collective-permute-start(bf16[1,40,3584]{2,1,0:T(8,128)(2,1)S(1)} %get-tuple-element.10), channel_id=1, source_target_pairs={{0,6},{2,4},{4,2},{6,0},{1,7},{3,5},{5,3},{7,1},{8,14},{10,12},{12... | collective-permute-start | bytes 860168 | tf_op jit(solution)/shard_map/ppermute | solution.py:16
  62.7 12.5 %collective-permute-start.13 = (bf16[1,40,3584]{2,1,0:T(8,128)(2,1)S(1)}, bf16[1,40,3584]{2,1,0:T(8,128)(2,1)S(1)}, u32[]{:S(2)}, u32[]{:S(2)}) collective-permute-start(bf16[1,40,3584]{2,1,0:T(8,128)(2,1)S(1)} %get-tuple-element.11), channel_id=1, source_target_pairs={{0,4},{2,6},{4,0},{6,2},{1,5},{3,7},{5,1},{7,3},{8,12},{10,14},{12... | collective-permute-start | bytes 860168 | tf_op jit(solution)/shard_map/ppermute | solution.py:16
  75.3 13.7 %collective-permute-start.18 = (bf16[1,40,3584]{2,1,0:T(8,128)(2,1)S(1)}, bf16[1,40,3584]{2,1,0:T(8,128)(2,1)S(1)}, u32[]{:S(2)}, u32[]{:S(2)}) collective-permute-start(bf16[1,40,3584]{2,1,0:T(8,128)(2,1)S(1)} %fusion.18), channel_id=1, source_target_pairs={{0,8},{8,0},{1,9},{9,1},{2,10},{10,2},{3,11},{11,3},{4,12},{12,4},... | collective-permute-start | bytes 860168 | tf_op jit(solution)/shard_map/ppermute | solution.py:12
  77.0 12.1 %collective-permute-start.15 = (bf16[1,40,3584]{2,1,0:T(8,128)(2,1)S(1)}, bf16[1,40,3584]{2,1,0:T(8,128)(2,1)S(1)}, u32[]{:S(2)}, u32[]{:S(2)}) collective-permute-start(bf16[1,40,3584]{2,1,0:T(8,128)(2,1)S(1)} %get-tuple-element.12), channel_id=1, source_target_pairs={{0,2},{2,0},{4,6},{6,4},{1,3},{3,1},{5,7},{7,5},{8,10},{10,8},{12,... | collective-permute-start | bytes 860168 | tf_op jit(solution)/shard_map/ppermute | solution.py:16
  79.5 14.4 %collective-permute-start.17 = (bf16[1,40,3584]{2,1,0:T(8,128)(2,1)S(1)}, bf16[1,40,3584]{2,1,0:T(8,128)(2,1)S(1)}, u32[]{:S(2)}, u32[]{:S(2)}) collective-permute-start(bf16[1,40,3584]{2,1,0:T(8,128)(2,1)S(1)} %get-tuple-element.13), channel_id=1, source_target_pairs={{0,6},{2,4},{4,2},{6,0},{1,7},{3,5},{5,3},{7,1},{8,14},{10,12},{12... | collective-permute-start | bytes 860168 | tf_op jit(solution)/shard_map/ppermute | solution.py:16
  80.7 15.9 %copy-start.1 = (f32[64,8]{0,1:T(8,128)S(1)}, f32[64,8]{0,1:T(8,128)}, u32[]{:S(2)}) copy-start(f32[64,8]{0,1:T(8,128)} %param.8) | copy-start | bytes 6148
  80.7 15.6 %collective-permute-start.16 = (bf16[1,40,3584]{2,1,0:T(8,128)(2,1)S(1)}, bf16[1,40,3584]{2,1,0:T(8,128)(2,1)S(1)}, u32[]{:S(2)}, u32[]{:S(2)}) collective-permute-start(bf16[1,40,3584]{2,1,0:T(8,128)(2,1)S(1)} %get-tuple-element.14), channel_id=1, source_target_pairs={{0,4},{2,6},{4,0},{6,2},{1,5},{3,7},{5,1},{7,3},{8,12},{10,14},{12... | collective-permute-start | bytes 860168 | tf_op jit(solution)/shard_map/ppermute | solution.py:16
  96.6 2.9 %collective-permute-start.19 = (f32[2,40,3584]{2,1,0:T(8,128)S(1)}, f32[2,40,3584]{2,1,0:T(8,128)S(1)}, u32[]{:S(2)}, u32[]{:S(2)}) collective-permute-start(f32[2,40,3584]{2,1,0:T(8,128)S(1)} %pad_maximum_fusion.2), channel_id=1, source_target_pairs={{0,1},{1,0},{2,3},{3,2},{4,5},{5,4},{6,7},{7,6},{8,9},{9,8},{10,11... | collective-permute-start | bytes 3440648 | tf_op jit(solution)/shard_map/ppermute | solution.py:12

commit v11 on v9

--- a/solution.py
+++ b/solution.py
@@ -60,24 +60,22 @@
         jnp.concatenate([routes, other_routes], axis=0),
         jnp.concatenate([other_routes, routes], axis=0),
     )
-    flat = pair_routes.reshape(-1)
-    onehot = (flat[:, None] == jnp.arange(experts, dtype=jnp.int32)[None, :]).astype(jnp.int32)
-    earlier = jnp.cumsum(onehot, axis=0) - onehot
-    slot = jnp.sum(earlier * onehot, axis=1)
-    real = flat < experts
-    cell = jnp.where(real, flat * span + slot, experts * span)
-    pair_cell = cell.reshape(n_ctx * tok, top)
-    local_cell = jnp.where(ctx == 0, pair_cell, jnp.roll(pair_cell, tok, axis=0))
+    ids = jnp.arange(experts, dtype=jnp.int32)
+    has = jnp.any(pair_routes[None, :, :] == ids[:, None, None], axis=2).astype(jnp.int32)
+    count = jnp.cumsum(has, axis=1) - has
+    local_has = jnp.where(ctx == 0, has, jnp.roll(has, tok, axis=1))
+    local_slot = jnp.where(ctx == 0, count, jnp.roll(count, tok, axis=1))
 
     if experts == 2:
-        expert_order = jnp.stack([me, 1 - me])
+        position = jnp.where(ids == me, 0, 1)
+        order_has = jnp.where(me == 0, local_has, local_has[::-1])
+        order_slot = jnp.where(me == 0, local_slot, local_slot[::-1])
     else:
-        expert_order = jnp.arange(experts, dtype=jnp.int32)
-    own_cells = (
-        expert_order[:, None] * span + ctx * half + jnp.arange(half, dtype=jnp.int32)[None, :]
-    ).reshape(-1)
-    match = local_cell[None, :, :] == own_cells[:, None, None]
-    picker = jnp.sum(match.astype(jnp.float32), axis=2).astype(jnp.bfloat16)
+        position = ids
+        order_has, order_slot = local_has, local_slot
+    wanted = ctx * half + jnp.arange(half, dtype=jnp.int32)
+    picker = (order_has[:, None, :] > 0) & (order_slot[:, None, :] == wanted[None, :, None])
+    picker = picker.astype(jnp.bfloat16).reshape(experts * half, n_ctx * tok)
     pair_tokens = with_sibling(tokens)
     packed = jnp.dot(picker, pair_tokens, preferred_element_type=jnp.float32).astype(jnp.bfloat16)
     packed = packed.reshape(experts, half, width)
@@ -119,20 +117,19 @@
     theirs = shift(mine, "context", n_ctx, 1)
     slots_out = jnp.concatenate([mine, theirs], axis=0).reshape(n_ctx * experts * half, width)
 
-    own_cell = local_cell[:tok]
-    expert_of = own_cell // span
-    slot_of = own_cell % span
-    if experts == 2:
-        position = jnp.where(expert_of == me, 0, 1)
-    else:
-        position = expert_of
-    block = jnp.where(slot_of // half == ctx, 0, 1)
-    layout = block * (experts * half) + position * half + slot_of % half
-    layout = jnp.where(own_cell < experts * span, layout, n_ctx * experts * half)
-    own_match = (
-        layout[:, :, None] == jnp.arange(n_ctx * experts * half, dtype=jnp.int32)[None, None, :]
-    ).astype(jnp.float32)
-    mixing = jnp.sum(own_match * route_weight[:, :, None], axis=1)
+    n_slots = n_ctx * experts * half
+    own_has = local_has[:, :tok] > 0
+    own_slot = local_slot[:, :tok]
+    weight = jnp.sum(
+        jnp.where(routes[None, :, :] == ids[:, None, None], route_weight[None, :, :], 0.0), axis=2
+    )
+    block = jnp.where(own_slot // half == ctx, 0, 1)
+    layout = block * (experts * half) + position[:, None] * half + own_slot % half
+    layout = jnp.where(own_has, layout, n_slots)
+    own_match = (layout[:, :, None] == jnp.arange(n_slots, dtype=jnp.int32)[None, None, :]).astype(
+        jnp.float32
+    )
+    mixing = jnp.sum(own_match * weight[:, :, None], axis=0)
     mixed = jnp.dot(
         mixing, slots_out, precision=lax.Precision.HIGH, preferred_element_type=jnp.float32
     )

time: 90.5 us -> 90.3 us (level)
  matrix products: 7.88 us -> 9.05 us
    dot_general x1, matrix products: 0.29 us -> 1.48 us  [per_device(): jnp.dot(picker, pair_tokens, preferred_element_type=jnp.float32)]
    concatenate x2 -> x0, other arithmetic: 0.91 us -> none  [the longest x1 0.84 us: per_device(): jnp.concatenate([other_routes, routes], axis=0)]
  transfers between devices with their start and end apart: 20 -> 20, of which waited for: 12 -> 12; matrix products, arithmetic and copies ran while one was open for 10% -> 9% of each run, Pallas kernels for 0% -> 0%
where the time goes in v11:
time: 90.3 us; the launch traced here: 90 us
  waiting for transfers between devices  57.9 us (64%)
  starting transfers between devices  19.4 us (21%)
  matrix products  9.05 us (10%)
  other arithmetic  2.48 us (3%)
  local copies, waits for them, and re-layouts  0.99 us (1%)
    ppermute x12, waiting for transfers between devices, swap(): return lax.ppermute(x, axis, [(i, i ^ k) for i in range(size)])  35.2 us
    ppermute x8, waiting for transfers between devices, shift(): return lax.ppermute(x, axis, [(i, (i + k) % size) for i in range(size)])  22.7 us
    ppermute x12, starting transfers between devices, swap(): return lax.ppermute(x, axis, [(i, i ^ k) for i in range(size)])  13.5 us
    ppermute x8, starting transfers between devices, shift(): return lax.ppermute(x, axis, [(i, (i + k) % size) for i in range(size)])  5.94 us
    dot_general x2, matrix products, quarter_rows(): up = lax.dot_general(rows, w_up, dims, preferred_element_type=jnp.float32)  2.01 us
    dot_general x2, matrix products, quarter_rows(): lax.dot_general(rows, w_gate, dims, preferred_element_type=jnp.float32)  2.01 us
    dot_general x4, matrix products, quarter_rows(): jnp.dot(hidden[:, c * slab:(c + 1) * slab], w_down[c * slab:(c + 1) * sla...  1.91 us
  transfers between devices with their start and end apart: 20, of which 12 were waited for; matrix products, arithmetic and copies ran while one was open for 9% of the time, Pallas kernels for 0%

profile of v11, /device:TPU:0, one launch (start us, length us, event | category | flops | bytes accessed | tf_op | source)
XLA Modules:
  0.0 90.0 jit_solution(10214521360888794337)
XLA Ops:
  0.6 0.9 collective-permute-done
  1.5 0.8 add_select_fusion
  3.2 1.5 %convolution_convert_fusion.4 = bf16[80,3584]{1,0:T(8,128)(2,1)S(1)} fusion(pred[80,128]{1,0:T(8,128)(4,1)S(1)} %fusion.23, bf16[64,3584]{1,0:T(8,128)(2,1)S(1)} %collective-permute-done.1, bf16[64,3584]{1,0:T(8,128)(2,1)} %param.6), kind=kOutput, calls=%fused_computation.12 | convolution fusion | flops 75522048 | bytes 1501184 | tf_op jit(solution)/shard_map/dot_general | solution.py:80
  4.7 4.0 %collective-permute-start.8 = (bf16[1,40,3584]{2,1,0:T(8,128)(2,1)S(1)}, bf16[1,40,3584]{2,1,0:T(8,128)(2,1)S(1)}, u32[]{:S(2)}, u32[]{:S(2)}) collective-permute-start(bf16[1,40,3584]{2,1,0:T(8,128)(2,1)S(1)} %get-tuple-element.15), channel_id=1, source_target_pairs={{0,8},{8,0},{1,9},{9,1},{2,10},{10,2},{3,11},{11,3},{4,12},{12,4},... | collective-permute-start | bytes 860168 | tf_op jit(solution)/shard_map/ppermute | solution.py:12
  8.7 2.5 %collective-permute-start.4 = (bf16[1,40,3584]{2,1,0:T(8,128)(2,1)S(1)}, bf16[1,40,3584]{2,1,0:T(8,128)(2,1)S(1)}, u32[]{:S(2)}, u32[]{:S(2)}) collective-permute-start(bf16[1,40,3584]{2,1,0:T(8,128)(2,1)S(1)} %get-tuple-element.16), channel_id=1, source_target_pairs={{0,6},{2,4},{4,2},{6,0},{1,7},{3,5},{5,3},{7,1},{8,14},{10,12},{12... | collective-permute-start | bytes 860168 | tf_op jit(solution)/shard_map/ppermute | solution.py:16
  11.6 0.5 collective-permute-start.2
  12.2 9.9 %collective-permute-done.8 = bf16[1,40,3584]{2,1,0:T(8,128)(2,1)S(1)} collective-permute-done((bf16[1,40,3584]{2,1,0:T(8,128)(2,1)S(1)}, bf16[1,40,3584]{2,1,0:T(8,128)(2,1)S(1)}, u32[]{:S(2)}, u32[]{:S(2)}) %collective-permute-start.8) | collective-permute-done | bytes 286752 | tf_op jit(solution)/shard_map/ppermute | solution.py:12
  22.1 2.3 %collective-permute-done.4 = bf16[1,40,3584]{2,1,0:T(8,128)(2,1)S(1)} collective-permute-done((bf16[1,40,3584]{2,1,0:T(8,128)(2,1)S(1)}, bf16[1,40,3584]{2,1,0:T(8,128)(2,1)S(1)}, u32[]{:S(2)}, u32[]{:S(2)}) %collective-permute-start.4) | collective-permute-done | bytes 286752 | tf_op jit(solution)/shard_map/ppermute | solution.py:16
  24.4 1.1 %collective-permute-start.11 = (bf16[1,40,3584]{2,1,0:T(8,128)(2,1)S(1)}, bf16[1,40,3584]{2,1,0:T(8,128)(2,1)S(1)}, u32[]{:S(2)}, u32[]{:S(2)}) collective-permute-start(bf16[1,40,3584]{2,1,0:T(8,128)(2,1)S(1)} %collective-permute-done.8), channel_id=1, source_target_pairs={{0,6},{2,4},{4,2},{6,0},{1,7},{3,5},{5,3},{7,1},{8,14},{10,12},{12... | collective-permute-start | bytes 860168 | tf_op jit(solution)/shard_map/ppermute | solution.py:16
  25.5 5.0 %collective-permute-done.3 = bf16[1,40,3584]{2,1,0:T(8,128)(2,1)S(1)} collective-permute-done((bf16[1,40,3584]{2,1,0:T(8,128)(2,1)S(1)}, bf16[1,40,3584]{2,1,0:T(8,128)(2,1)S(1)}, u32[]{:S(2)}, u32[]{:S(2)}) %collective-permute-start.3) | collective-permute-done | bytes 286752 | tf_op jit(solution)/shard_map/ppermute | solution.py:16
  30.8 1.5 %collective-permute-start.9 = (bf16[1,40,3584]{2,1,0:T(8,128)(2,1)S(1)}, bf16[1,40,3584]{2,1,0:T(8,128)(2,1)S(1)}, u32[]{:S(2)}, u32[]{:S(2)}) collective-permute-start(bf16[1,40,3584]{2,1,0:T(8,128)(2,1)S(1)} %collective-permute-done.8), channel_id=1, source_target_pairs={{0,2},{2,0},{4,6},{6,4},{1,3},{3,1},{5,7},{7,5},{8,10},{10,8},{12,... | collective-permute-start | bytes 860168 | tf_op jit(solution)/shard_map/ppermute | solution.py:16
  32.4 4.3 %collective-permute-done.11 = bf16[1,40,3584]{2,1,0:T(8,128)(2,1)S(1)} collective-permute-done((bf16[1,40,3584]{2,1,0:T(8,128)(2,1)S(1)}, bf16[1,40,3584]{2,1,0:T(8,128)(2,1)S(1)}, u32[]{:S(2)}, u32[]{:S(2)}) %collective-permute-start.11) | collective-permute-done | bytes 286752 | tf_op jit(solution)/shard_map/ppermute | solution.py:16
  36.7 5.0 %collective-permute-done.10 = bf16[1,40,3584]{2,1,0:T(8,128)(2,1)S(1)} collective-permute-done((bf16[1,40,3584]{2,1,0:T(8,128)(2,1)S(1)}, bf16[1,40,3584]{2,1,0:T(8,128)(2,1)S(1)}, u32[]{:S(2)}, u32[]{:S(2)}) %collective-permute-start.10) | collective-permute-done | bytes 286752 | tf_op jit(solution)/shard_map/ppermute | solution.py:16
  41.9 1.0 %fusion.11 = f32[160,320]{1,0:T(8,128)S(1)} fusion(bf16[160,3584]{1,0:T(8,128)(2,1)S(1)} %bitcast.69, bf16[160,3584]{1,0:T(8,128)(2,1)S(1)} %collective-permute-done.5, bf16[160,3584]{1,0:T(8,128)(2,1)S(1)} %bitcast.81), kind=kOutput, calls=%fused_computation.20 | convolution fusion | flops 371589120 | bytes 3645440 | tf_op jit(solution)/shard_map/dot_general | solution.py:21
  42.9 1.0 %multiply_convert_fusion.1 = bf16[160,320]{1,0:T(8,128)(2,1)S(1)} fusion(f32[160,320]{1,0:T(8,128)S(1)} %fusion.11, bf16[160,3584]{1,0:T(8,128)(2,1)S(1)} %bitcast.70, bf16[160,3584]{1,0:T(8,128)(2,1)S(1)} %collective-permute-done.6, bf16[160,3584]{1,0:T(8,128)(2,1)S(1)} %bitcast.84), kind=kOutput, calls=%fused_computation.45 | convolution fusion | flops 371896320 | bytes 3747840 | tf_op jit(solution)/shard_map/dot_general | solution.py:22
  43.9 1.0 %fusion.10 = f32[160,320]{1,0:T(8,128)S(1)} fusion(bf16[160,3584]{1,0:T(8,128)(2,1)S(1)} %bitcast.71, bf16[160,3584]{1,0:T(8,128)(2,1)S(1)} %collective-permute-done.5, bf16[160,3584]{1,0:T(8,128)(2,1)S(1)} %bitcast.82), kind=kOutput, calls=%fused_computation.19 | convolution fusion | flops 371589120 | bytes 3645440 | tf_op jit(solution)/shard_map/dot_general | solution.py:21
  45.4 1.0 %multiply_convert_fusion = bf16[160,320]{1,0:T(8,128)(2,1)S(1)} fusion(f32[160,320]{1,0:T(8,128)S(1)} %fusion.10, bf16[160,3584]{1,0:T(8,128)(2,1)S(1)} %bitcast.72, bf16[160,3584]{1,0:T(8,128)(2,1)S(1)} %collective-permute-done.6, bf16[160,3584]{1,0:T(8,128)(2,1)S(1)} %bitcast.85), kind=kOutput, calls=%fused_computation.44 | convolution fusion | flops 371896320 | bytes 3747840 | tf_op jit(solution)/shard_map/dot_general | solution.py:22
  46.9 0.5 fusion.2
  47.5 1.5 %collective-permute-start.12 = (bf16[1,40,3584]{2,1,0:T(8,128)(2,1)S(1)}, bf16[1,40,3584]{2,1,0:T(8,128)(2,1)S(1)}, u32[]{:S(2)}, u32[]{:S(2)}) collective-permute-start(bf16[1,40,3584]{2,1,0:T(8,128)(2,1)S(1)} %get-tuple-element.12), channel_id=1, source_target_pairs={{0,2},{2,0},{4,6},{6,4},{1,3},{3,1},{5,7},{7,5},{8,10},{10,8},{12,... | collective-permute-start | bytes 860168 | tf_op jit(solution)/shard_map/ppermute | solution.py:16
  48.9 1.5 %collective-permute-start.14 = (bf16[1,40,3584]{2,1,0:T(8,128)(2,1)S(1)}, bf16[1,40,3584]{2,1,0:T(8,128)(2,1)S(1)}, u32[]{:S(2)}, u32[]{:S(2)}) collective-permute-start(bf16[1,40,3584]{2,1,0:T(8,128)(2,1)S(1)} %get-tuple-element.13), channel_id=1, source_target_pairs={{0,6},{2,4},{4,2},{6,0},{1,7},{3,5},{5,3},{7,1},{8,14},{10,12},{12... | collective-permute-start | bytes 860168 | tf_op jit(solution)/shard_map/ppermute | solution.py:16
  50.4 0.6 collective-permute-start.13
  51.0 0.5 fusion.6
  51.5 10.9 %collective-permute-done.12 = bf16[1,40,3584]{2,1,0:T(8,128)(2,1)S(1)} collective-permute-done((bf16[1,40,3584]{2,1,0:T(8,128)(2,1)S(1)}, bf16[1,40,3584]{2,1,0:T(8,128)(2,1)S(1)}, u32[]{:S(2)}, u32[]{:S(2)}) %collective-permute-start.12) | collective-permute-done | bytes 286752 | tf_op jit(solution)/shard_map/ppermute | solution.py:16
  62.4 1.2 %collective-permute-done.13 = bf16[1,40,3584]{2,1,0:T(8,128)(2,1)S(1)} collective-permute-done((bf16[1,40,3584]{2,1,0:T(8,128)(2,1)S(1)}, bf16[1,40,3584]{2,1,0:T(8,128)(2,1)S(1)}, u32[]{:S(2)}, u32[]{:S(2)}) %collective-permute-start.13) | collective-permute-done | bytes 286752 | tf_op jit(solution)/shard_map/ppermute | solution.py:16
  63.8 1.4 %collective-permute-start.18 = (bf16[1,40,3584]{2,1,0:T(8,128)(2,1)S(1)}, bf16[1,40,3584]{2,1,0:T(8,128)(2,1)S(1)}, u32[]{:S(2)}, u32[]{:S(2)}) collective-permute-start(bf16[1,40,3584]{2,1,0:T(8,128)(2,1)S(1)} %fusion.18), channel_id=1, source_target_pairs={{0,8},{8,0},{1,9},{9,1},{2,10},{10,2},{3,11},{11,3},{4,12},{12,4},... | collective-permute-start | bytes 860168 | tf_op jit(solution)/shard_map/ppermute | solution.py:12
  65.2 0.8 collective-permute-start.15
  66.0 2.5 %collective-permute-start.17 = (bf16[1,40,3584]{2,1,0:T(8,128)(2,1)S(1)}, bf16[1,40,3584]{2,1,0:T(8,128)(2,1)S(1)}, u32[]{:S(2)}, u32[]{:S(2)}) collective-permute-start(bf16[1,40,3584]{2,1,0:T(8,128)(2,1)S(1)} %get-tuple-element.10), channel_id=1, source_target_pairs={{0,6},{2,4},{4,2},{6,0},{1,7},{3,5},{5,3},{7,1},{8,14},{10,12},{12... | collective-permute-start | bytes 860168 | tf_op jit(solution)/shard_map/ppermute | solution.py:16
  68.8 9.8 %collective-permute-done.18 = bf16[1,40,3584]{2,1,0:T(8,128)(2,1)S(1)} collective-permute-done((bf16[1,40,3584]{2,1,0:T(8,128)(2,1)S(1)}, bf16[1,40,3584]{2,1,0:T(8,128)(2,1)S(1)}, u32[]{:S(2)}, u32[]{:S(2)}) %collective-permute-start.18) | collective-permute-done | bytes 286752 | tf_op jit(solution)/shard_map/ppermute | solution.py:12
  78.7 4.1 %collective-permute-done.17 = bf16[1,40,3584]{2,1,0:T(8,128)(2,1)S(1)} collective-permute-done((bf16[1,40,3584]{2,1,0:T(8,128)(2,1)S(1)}, bf16[1,40,3584]{2,1,0:T(8,128)(2,1)S(1)}, u32[]{:S(2)}, u32[]{:S(2)}) %collective-permute-start.17) | collective-permute-done | bytes 286752 | tf_op jit(solution)/shard_map/ppermute | solution.py:16
  82.7 2.4 %collective-permute-done.16 = bf16[1,40,3584]{2,1,0:T(8,128)(2,1)S(1)} collective-permute-done((bf16[1,40,3584]{2,1,0:T(8,128)(2,1)S(1)}, bf16[1,40,3584]{2,1,0:T(8,128)(2,1)S(1)}, u32[]{:S(2)}, u32[]{:S(2)}) %collective-permute-start.16) | collective-permute-done | bytes 286752 | tf_op jit(solution)/shard_map/ppermute | solution.py:16
  86.2 2.1 %collective-permute-done.19 = f32[2,40,3584]{2,1,0:T(8,128)S(1)} collective-permute-done((f32[2,40,3584]{2,1,0:T(8,128)S(1)}, f32[2,40,3584]{2,1,0:T(8,128)S(1)}, u32[]{:S(2)}, u32[]{:S(2)}) %collective-permute-start.19) | collective-permute-done | bytes 1146912 | tf_op jit(solution)/shard_map/ppermute | solution.py:12
  88.4 1.6 %convolution_convert_fusion.5 = bf16[64,3584]{1,0:T(8,128)(2,1)} fusion(f32[64,160]{1,0:T(8,128)S(1)} %select_reduce_fusion, f32[160,3584]{1,0:T(8,128)S(1)} %bitcast.65), kind=kOutput, calls=%fused_computation.13 | convolution fusion | flops 220430336 | bytes 2793472 | tf_op jit(solution)/shard_map/dot_general | solution.py:133
  (58 shorter events, 5.1 us)
Async XLA Ops:
  0.0 1.5 %collective-permute-start = (s32[64,8]{0,1:T(8,128)}, s32[64,8]{0,1:T(8,128)S(1)}, u32[]{:S(2)}, u32[]{:S(2)}) collective-permute-start(s32[64,8]{0,1:T(8,128)} %param.7), channel_id=1, source_target_pairs={{0,1},{1,0},{2,3},{3,2},{4,5},{5,4},{6,7},{7,6},{8,9},{9,8},{10,11... | collective-permute-start | bytes 6152 | tf_op jit(solution)/shard_map/ppermute | solution.py:12
  0.5 2.7 %collective-permute-start.1 = (bf16[64,3584]{1,0:T(8,128)(2,1)}, bf16[64,3584]{1,0:T(8,128)(2,1)S(1)}, u32[]{:S(2)}, u32[]{:S(2)}) collective-permute-start(bf16[64,3584]{1,0:T(8,128)(2,1)} %param.6), channel_id=1, source_target_pairs={{0,1},{1,0},{2,3},{3,2},{4,5},{5,4},{6,7},{7,6},{8,9},{9,8},{10,11... | collective-permute-start | bytes 1376264 | tf_op jit(solution)/shard_map/ppermute | solution.py:12
  3.1 9.1 %copy-start.3 = (bf16[1,160,3584]{2,1,0:T(8,128)(2,1)S(1)}, bf16[1,160,3584]{2,1,0:T(8,128)(2,1)}, u32[]{:S(2)}) copy-start(bf16[1,160,3584]{2,1,0:T(8,128)(2,1)} %param.9) | copy-start | bytes 3440644
  3.1 19.0 %copy-start.4 = (bf16[1,160,3584]{2,1,0:T(8,128)(2,1)S(1)}, bf16[1,160,3584]{2,1,0:T(8,128)(2,1)}, u32[]{:S(2)}) copy-start(bf16[1,160,3584]{2,1,0:T(8,128)(2,1)} %param.10) | copy-start | bytes 3440644
  4.7 17.4 %collective-permute-start.8 = (bf16[1,40,3584]{2,1,0:T(8,128)(2,1)S(1)}, bf16[1,40,3584]{2,1,0:T(8,128)(2,1)S(1)}, u32[]{:S(2)}, u32[]{:S(2)}) collective-permute-start(bf16[1,40,3584]{2,1,0:T(8,128)(2,1)S(1)} %get-tuple-element.15), channel_id=1, source_target_pairs={{0,8},{8,0},{1,9},{9,1},{2,10},{10,2},{3,11},{11,3},{4,12},{12,4},... | collective-permute-start | bytes 860168 | tf_op jit(solution)/shard_map/ppermute | solution.py:12
  8.7 15.7 %collective-permute-start.4 = (bf16[1,40,3584]{2,1,0:T(8,128)(2,1)S(1)}, bf16[1,40,3584]{2,1,0:T(8,128)(2,1)S(1)}, u32[]{:S(2)}, u32[]{:S(2)}) collective-permute-start(bf16[1,40,3584]{2,1,0:T(8,128)(2,1)S(1)} %get-tuple-element.16), channel_id=1, source_target_pairs={{0,6},{2,4},{4,2},{6,0},{1,7},{3,5},{5,3},{7,1},{8,14},{10,12},{12... | collective-permute-start | bytes 860168 | tf_op jit(solution)/shard_map/ppermute | solution.py:16
  11.2 19.3 %collective-permute-start.3 = (bf16[1,40,3584]{2,1,0:T(8,128)(2,1)S(1)}, bf16[1,40,3584]{2,1,0:T(8,128)(2,1)S(1)}, u32[]{:S(2)}, u32[]{:S(2)}) collective-permute-start(bf16[1,40,3584]{2,1,0:T(8,128)(2,1)S(1)} %get-tuple-element.16), channel_id=1, source_target_pairs={{0,4},{2,6},{4,0},{6,2},{1,5},{3,7},{5,1},{7,3},{8,12},{10,14},{12... | collective-permute-start | bytes 860168 | tf_op jit(solution)/shard_map/ppermute | solution.py:16
  11.6 19.1 %collective-permute-start.2 = (bf16[1,40,3584]{2,1,0:T(8,128)(2,1)S(1)}, bf16[1,40,3584]{2,1,0:T(8,128)(2,1)S(1)}, u32[]{:S(2)}, u32[]{:S(2)}) collective-permute-start(bf16[1,40,3584]{2,1,0:T(8,128)(2,1)S(1)} %get-tuple-element.16), channel_id=1, source_target_pairs={{0,2},{2,0},{4,6},{6,4},{1,3},{3,1},{5,7},{7,5},{8,10},{10,8},{12,... | collective-permute-start | bytes 860168 | tf_op jit(solution)/shard_map/ppermute | solution.py:16
  12.2 29.7 %collective-permute-start.5 = (bf16[160,3584]{1,0:T(8,128)(2,1)S(1)}, bf16[160,3584]{1,0:T(8,128)(2,1)S(1)}, u32[]{:S(2)}, u32[]{:S(2)}) collective-permute-start(bf16[160,3584]{1,0:T(8,128)(2,1)S(1)} %bitcast.80), channel_id=1, source_target_pairs={{0,1},{1,0},{2,3},{3,2},{4,5},{5,4},{6,7},{7,6},{8,9},{9,8},{10,11... | collective-permute-start | bytes 3440648 | tf_op jit(solution)/shard_map/ppermute | solution.py:12
  22.1 20.8 %collective-permute-start.6 = (bf16[160,3584]{1,0:T(8,128)(2,1)S(1)}, bf16[160,3584]{1,0:T(8,128)(2,1)S(1)}, u32[]{:S(2)}, u32[]{:S(2)}) collective-permute-start(bf16[160,3584]{1,0:T(8,128)(2,1)S(1)} %bitcast.83), channel_id=1, source_target_pairs={{0,1},{1,0},{2,3},{3,2},{4,5},{5,4},{6,7},{7,6},{8,9},{9,8},{10,11... | collective-permute-start | bytes 3440648 | tf_op jit(solution)/shard_map/ppermute | solution.py:12
  24.4 12.3 %collective-permute-start.11 = (bf16[1,40,3584]{2,1,0:T(8,128)(2,1)S(1)}, bf16[1,40,3584]{2,1,0:T(8,128)(2,1)S(1)}, u32[]{:S(2)}, u32[]{:S(2)}) collective-permute-start(bf16[1,40,3584]{2,1,0:T(8,128)(2,1)S(1)} %collective-permute-done.8), channel_id=1, source_target_pairs={{0,6},{2,4},{4,2},{6,0},{1,7},{3,5},{5,3},{7,1},{8,14},{10,12},{12... | collective-permute-start | bytes 860168 | tf_op jit(solution)/shard_map/ppermute | solution.py:16
  30.5 11.2 %collective-permute-start.10 = (bf16[1,40,3584]{2,1,0:T(8,128)(2,1)S(1)}, bf16[1,40,3584]{2,1,0:T(8,128)(2,1)S(1)}, u32[]{:S(2)}, u32[]{:S(2)}) collective-permute-start(bf16[1,40,3584]{2,1,0:T(8,128)(2,1)S(1)} %collective-permute-done.8), channel_id=1, source_target_pairs={{0,4},{2,6},{4,0},{6,2},{1,5},{3,7},{5,1},{7,3},{8,12},{10,14},{12... | collective-permute-start | bytes 860168 | tf_op jit(solution)/shard_map/ppermute | solution.py:16
  30.8 11.0 %collective-permute-start.9 = (bf16[1,40,3584]{2,1,0:T(8,128)(2,1)S(1)}, bf16[1,40,3584]{2,1,0:T(8,128)(2,1)S(1)}, u32[]{:S(2)}, u32[]{:S(2)}) collective-permute-start(bf16[1,40,3584]{2,1,0:T(8,128)(2,1)S(1)} %collective-permute-done.8), channel_id=1, source_target_pairs={{0,2},{2,0},{4,6},{6,4},{1,3},{3,1},{5,7},{7,5},{8,10},{10,8},{12,... | collective-permute-start | bytes 860168 | tf_op jit(solution)/shard_map/ppermute | solution.py:16
  32.2 4.5 %copy-start = (bf16[1,160,3584]{2,1,0:T(8,128)(2,1)S(1)}, bf16[1,160,3584]{2,1,0:T(8,128)(2,1)}, u32[]{:S(2)}) copy-start(bf16[1,160,3584]{2,1,0:T(8,128)(2,1)} %param.11) | copy-start | bytes 3440644
  36.7 10.1 %collective-permute-start.7 = (bf16[160,3584]{1,0:T(8,128)(2,1)S(1)}, bf16[160,3584]{1,0:T(8,128)(2,1)S(1)}, u32[]{:S(2)}, u32[]{:S(2)}) collective-permute-start(bf16[160,3584]{1,0:T(8,128)(2,1)S(1)} %bitcast.66), channel_id=1, source_target_pairs={{0,1},{1,0},{2,3},{3,2},{4,5},{5,4},{6,7},{7,6},{8,9},{9,8},{10,11... | collective-permute-start | bytes 3440648 | tf_op jit(solution)/shard_map/ppermute | solution.py:12
  47.5 14.9 %collective-permute-start.12 = (bf16[1,40,3584]{2,1,0:T(8,128)(2,1)S(1)}, bf16[1,40,3584]{2,1,0:T(8,128)(2,1)S(1)}, u32[]{:S(2)}, u32[]{:S(2)}) collective-permute-start(bf16[1,40,3584]{2,1,0:T(8,128)(2,1)S(1)} %get-tuple-element.12), channel_id=1, source_target_pairs={{0,2},{2,0},{4,6},{6,4},{1,3},{3,1},{5,7},{7,5},{8,10},{10,8},{12,... | collective-permute-start | bytes 860168 | tf_op jit(solution)/shard_map/ppermute | solution.py:16
  48.9 13.5 %collective-permute-start.14 = (bf16[1,40,3584]{2,1,0:T(8,128)(2,1)S(1)}, bf16[1,40,3584]{2,1,0:T(8,128)(2,1)S(1)}, u32[]{:S(2)}, u32[]{:S(2)}) collective-permute-start(bf16[1,40,3584]{2,1,0:T(8,128)(2,1)S(1)} %get-tuple-element.13), channel_id=1, source_target_pairs={{0,6},{2,4},{4,2},{6,0},{1,7},{3,5},{5,3},{7,1},{8,14},{10,12},{12... | collective-permute-start | bytes 860168 | tf_op jit(solution)/shard_map/ppermute | solution.py:16
  50.4 13.2 %collective-permute-start.13 = (bf16[1,40,3584]{2,1,0:T(8,128)(2,1)S(1)}, bf16[1,40,3584]{2,1,0:T(8,128)(2,1)S(1)}, u32[]{:S(2)}, u32[]{:S(2)}) collective-permute-start(bf16[1,40,3584]{2,1,0:T(8,128)(2,1)S(1)} %get-tuple-element.14), channel_id=1, source_target_pairs={{0,4},{2,6},{4,0},{6,2},{1,5},{3,7},{5,1},{7,3},{8,12},{10,14},{12... | collective-permute-start | bytes 860168 | tf_op jit(solution)/shard_map/ppermute | solution.py:16
  63.8 14.8 %collective-permute-start.18 = (bf16[1,40,3584]{2,1,0:T(8,128)(2,1)S(1)}, bf16[1,40,3584]{2,1,0:T(8,128)(2,1)S(1)}, u32[]{:S(2)}, u32[]{:S(2)}) collective-permute-start(bf16[1,40,3584]{2,1,0:T(8,128)(2,1)S(1)} %fusion.18), channel_id=1, source_target_pairs={{0,8},{8,0},{1,9},{9,1},{2,10},{10,2},{3,11},{11,3},{4,12},{12,4},... | collective-permute-start | bytes 860168 | tf_op jit(solution)/shard_map/ppermute | solution.py:12
  65.2 13.4 %collective-permute-start.15 = (bf16[1,40,3584]{2,1,0:T(8,128)(2,1)S(1)}, bf16[1,40,3584]{2,1,0:T(8,128)(2,1)S(1)}, u32[]{:S(2)}, u32[]{:S(2)}) collective-permute-start(bf16[1,40,3584]{2,1,0:T(8,128)(2,1)S(1)} %get-tuple-element.9), channel_id=1, source_target_pairs={{0,2},{2,0},{4,6},{6,4},{1,3},{3,1},{5,7},{7,5},{8,10},{10,8},{12,... | collective-permute-start | bytes 860168 | tf_op jit(solution)/shard_map/ppermute | solution.py:16
  66.0 16.7 %collective-permute-start.17 = (bf16[1,40,3584]{2,1,0:T(8,128)(2,1)S(1)}, bf16[1,40,3584]{2,1,0:T(8,128)(2,1)S(1)}, u32[]{:S(2)}, u32[]{:S(2)}) collective-permute-start(bf16[1,40,3584]{2,1,0:T(8,128)(2,1)S(1)} %get-tuple-element.10), channel_id=1, source_target_pairs={{0,6},{2,4},{4,2},{6,0},{1,7},{3,5},{5,3},{7,1},{8,14},{10,12},{12... | collective-permute-start | bytes 860168 | tf_op jit(solution)/shard_map/ppermute | solution.py:16
  68.5 16.7 %collective-permute-start.16 = (bf16[1,40,3584]{2,1,0:T(8,128)(2,1)S(1)}, bf16[1,40,3584]{2,1,0:T(8,128)(2,1)S(1)}, u32[]{:S(2)}, u32[]{:S(2)}) collective-permute-start(bf16[1,40,3584]{2,1,0:T(8,128)(2,1)S(1)} %get-tuple-element.11), channel_id=1, source_target_pairs={{0,4},{2,6},{4,0},{6,2},{1,5},{3,7},{5,1},{7,3},{8,12},{10,14},{12... | collective-permute-start | bytes 860168 | tf_op jit(solution)/shard_map/ppermute | solution.py:16
  85.3 0.7 copy-start.1
  85.3 0.7 copy-start.2
  85.4 2.9 %collective-permute-start.19 = (f32[2,40,3584]{2,1,0:T(8,128)S(1)}, f32[2,40,3584]{2,1,0:T(8,128)S(1)}, u32[]{:S(2)}, u32[]{:S(2)}) collective-permute-start(f32[2,40,3584]{2,1,0:T(8,128)S(1)} %pad_maximum_fusion.9), channel_id=1, source_target_pairs={{0,1},{1,0},{2,3},{3,2},{4,5},{5,4},{6,7},{7,6},{8,9},{9,8},{10,11... | collective-permute-start | bytes 3440648 | tf_op jit(solution)/shard_map/ppermute | solution.py:12

commit v12 on v11

--- a/solution.py
+++ b/solution.py
@@ -75,7 +75,7 @@
         order_has, order_slot = local_has, local_slot
     wanted = ctx * half + jnp.arange(half, dtype=jnp.int32)
     picker = (order_has[:, None, :] > 0) & (order_slot[:, None, :] == wanted[None, :, None])
-    picker = picker.astype(jnp.bfloat16).reshape(experts * half, n_ctx * tok)
+    picker = lax.optimization_barrier(picker.astype(jnp.bfloat16).reshape(experts * half, n_ctx * tok))
     pair_tokens = with_sibling(tokens)
     packed = jnp.dot(picker, pair_tokens, preferred_element_type=jnp.float32).astype(jnp.bfloat16)
     packed = packed.reshape(experts, half, width)
@@ -115,7 +115,6 @@
         mine = lax.all_to_all(expert_out, "ex", split_axis=0, concat_axis=0, tiled=True)
         mine = mine.astype(jnp.float32)
     theirs = shift(mine, "context", n_ctx, 1)
-    slots_out = jnp.concatenate([mine, theirs], axis=0).reshape(n_ctx * experts * half, width)
 
     n_slots = n_ctx * experts * half
     own_has = local_has[:, :tok] > 0
@@ -130,8 +129,20 @@
         jnp.float32
     )
     mixing = jnp.sum(own_match * weight[:, :, None], axis=0)
-    mixed = jnp.dot(
-        mixing, slots_out, precision=lax.Precision.HIGH, preferred_element_type=jnp.float32
+    own_rows = experts * half
+    dims = (((1,), (0,)), ((), ()))
+    mixed = lax.dot_general(
+        mixing[:, :own_rows],
+        mine.reshape(own_rows, width),
+        dims,
+        precision=lax.Precision.HIGH,
+        preferred_element_type=jnp.float32,
+    ) + lax.dot_general(
+        mixing[:, own_rows:],
+        theirs.reshape(own_rows, width),
+        dims,
+        precision=lax.Precision.HIGH,
+        preferred_element_type=jnp.float32,
     )
     return mixed.astype(jnp.bfloat16)
 

time: 90.3 us -> 90.3 us (level)
    dot_general x1 -> x2, matrix products: 1.64 us -> 1.85 us  [the longest x1 1.28 us: per_device(): lax.dot_general(mixing[:, :own_rows], mine.reshape(own_rows, width), dims...]
where the time goes in v12:
time: 90.3 us; the launch traced here: 90.1 us
  waiting for transfers between devices  57.9 us (64%)
  starting transfers between devices  19.4 us (21%)
  matrix products  9.27 us (10%)
  other arithmetic  2.34 us (3%)
  local copies, waits for them, and re-layouts  0.99 us (1%)
    ppermute x12, waiting for transfers between devices, swap(): return lax.ppermute(x, axis, [(i, i ^ k) for i in range(size)])  35.2 us
    ppermute x8, waiting for transfers between devices, shift(): return lax.ppermute(x, axis, [(i, (i + k) % size) for i in range(size)])  22.7 us
    ppermute x12, starting transfers between devices, swap(): return lax.ppermute(x, axis, [(i, i ^ k) for i in range(size)])  13.4 us
    ppermute x8, starting transfers between devices, shift(): return lax.ppermute(x, axis, [(i, (i + k) % size) for i in range(size)])  5.93 us
    dot_general x2, matrix products, quarter_rows(): up = lax.dot_general(rows, w_up, dims, preferred_element_type=jnp.float32)  2.01 us
    dot_general x2, matrix products, quarter_rows(): lax.dot_general(rows, w_gate, dims, preferred_element_type=jnp.float32)  2 us
    dot_general x4, matrix products, quarter_rows(): jnp.dot(hidden[:, c * slab:(c + 1) * slab], w_down[c * slab:(c + 1) * sla...  1.92 us
  transfers between devices with their start and end apart: 20, of which 12 were waited for; matrix products, arithmetic and copies ran while one was open for 9% of the time, Pallas kernels for 0%

profile of v12, /device:TPU:0, one launch (start us, length us, event | category | flops | bytes accessed | tf_op | source)
XLA Modules:
  0.0 90.1 jit_solution(11502632090557010243)
XLA Ops:
  0.6 0.9 collective-permute-done
  1.5 0.8 add_select_fusion
  3.2 1.5 %convolution_convert_fusion.4 = bf16[80,3584]{1,0:T(8,128)(2,1)S(1)} fusion(bf16[80,128]{1,0:T(8,128)(2,1)S(1)} %fusion.25, bf16[64,3584]{1,0:T(8,128)(2,1)S(1)} %collective-permute-done.1, bf16[64,3584]{1,0:T(8,128)(2,1)} %param.6), kind=kOutput, calls=%fused_computation.13 | convolution fusion | flops 75522048 | bytes 1511424 | tf_op jit(solution)/shard_map/dot_general | solution.py:80
  4.7 4.0 %collective-permute-start.8 = (bf16[1,40,3584]{2,1,0:T(8,128)(2,1)S(1)}, bf16[1,40,3584]{2,1,0:T(8,128)(2,1)S(1)}, u32[]{:S(2)}, u32[]{:S(2)}) collective-permute-start(bf16[1,40,3584]{2,1,0:T(8,128)(2,1)S(1)} %get-tuple-element.15), channel_id=1, source_target_pairs={{0,8},{8,0},{1,9},{9,1},{2,10},{10,2},{3,11},{11,3},{4,12},{12,4},... | collective-permute-start | bytes 860168 | tf_op jit(solution)/shard_map/ppermute | solution.py:12
  8.7 2.5 %collective-permute-start.4 = (bf16[1,40,3584]{2,1,0:T(8,128)(2,1)S(1)}, bf16[1,40,3584]{2,1,0:T(8,128)(2,1)S(1)}, u32[]{:S(2)}, u32[]{:S(2)}) collective-permute-start(bf16[1,40,3584]{2,1,0:T(8,128)(2,1)S(1)} %get-tuple-element.16), channel_id=1, source_target_pairs={{0,6},{2,4},{4,2},{6,0},{1,7},{3,5},{5,3},{7,1},{8,14},{10,12},{12... | collective-permute-start | bytes 860168 | tf_op jit(solution)/shard_map/ppermute | solution.py:16
  11.6 0.5 collective-permute-start.2
  12.2 9.9 %collective-permute-done.8 = bf16[1,40,3584]{2,1,0:T(8,128)(2,1)S(1)} collective-permute-done((bf16[1,40,3584]{2,1,0:T(8,128)(2,1)S(1)}, bf16[1,40,3584]{2,1,0:T(8,128)(2,1)S(1)}, u32[]{:S(2)}, u32[]{:S(2)}) %collective-permute-start.8) | collective-permute-done | bytes 286752 | tf_op jit(solution)/shard_map/ppermute | solution.py:12
  22.1 2.3 %collective-permute-done.4 = bf16[1,40,3584]{2,1,0:T(8,128)(2,1)S(1)} collective-permute-done((bf16[1,40,3584]{2,1,0:T(8,128)(2,1)S(1)}, bf16[1,40,3584]{2,1,0:T(8,128)(2,1)S(1)}, u32[]{:S(2)}, u32[]{:S(2)}) %collective-permute-start.4) | collective-permute-done | bytes 286752 | tf_op jit(solution)/shard_map/ppermute | solution.py:16
  24.4 1.1 %collective-permute-start.11 = (bf16[1,40,3584]{2,1,0:T(8,128)(2,1)S(1)}, bf16[1,40,3584]{2,1,0:T(8,128)(2,1)S(1)}, u32[]{:S(2)}, u32[]{:S(2)}) collective-permute-start(bf16[1,40,3584]{2,1,0:T(8,128)(2,1)S(1)} %collective-permute-done.8), channel_id=1, source_target_pairs={{0,6},{2,4},{4,2},{6,0},{1,7},{3,5},{5,3},{7,1},{8,14},{10,12},{12... | collective-permute-start | bytes 860168 | tf_op jit(solution)/shard_map/ppermute | solution.py:16
  25.5 5.0 %collective-permute-done.3 = bf16[1,40,3584]{2,1,0:T(8,128)(2,1)S(1)} collective-permute-done((bf16[1,40,3584]{2,1,0:T(8,128)(2,1)S(1)}, bf16[1,40,3584]{2,1,0:T(8,128)(2,1)S(1)}, u32[]{:S(2)}, u32[]{:S(2)}) %collective-permute-start.3) | collective-permute-done | bytes 286752 | tf_op jit(solution)/shard_map/ppermute | solution.py:16
  30.7 1.5 %collective-permute-start.9 = (bf16[1,40,3584]{2,1,0:T(8,128)(2,1)S(1)}, bf16[1,40,3584]{2,1,0:T(8,128)(2,1)S(1)}, u32[]{:S(2)}, u32[]{:S(2)}) collective-permute-start(bf16[1,40,3584]{2,1,0:T(8,128)(2,1)S(1)} %collective-permute-done.8), channel_id=1, source_target_pairs={{0,2},{2,0},{4,6},{6,4},{1,3},{3,1},{5,7},{7,5},{8,10},{10,8},{12,... | collective-permute-start | bytes 860168 | tf_op jit(solution)/shard_map/ppermute | solution.py:16
  32.4 4.3 %collective-permute-done.11 = bf16[1,40,3584]{2,1,0:T(8,128)(2,1)S(1)} collective-permute-done((bf16[1,40,3584]{2,1,0:T(8,128)(2,1)S(1)}, bf16[1,40,3584]{2,1,0:T(8,128)(2,1)S(1)}, u32[]{:S(2)}, u32[]{:S(2)}) %collective-permute-start.11) | collective-permute-done | bytes 286752 | tf_op jit(solution)/shard_map/ppermute | solution.py:16
  36.7 5.0 %collective-permute-done.10 = bf16[1,40,3584]{2,1,0:T(8,128)(2,1)S(1)} collective-permute-done((bf16[1,40,3584]{2,1,0:T(8,128)(2,1)S(1)}, bf16[1,40,3584]{2,1,0:T(8,128)(2,1)S(1)}, u32[]{:S(2)}, u32[]{:S(2)}) %collective-permute-start.10) | collective-permute-done | bytes 286752 | tf_op jit(solution)/shard_map/ppermute | solution.py:16
  41.9 1.0 %fusion.12 = f32[160,320]{1,0:T(8,128)S(1)} fusion(bf16[160,3584]{1,0:T(8,128)(2,1)S(1)} %bitcast.72, bf16[160,3584]{1,0:T(8,128)(2,1)S(1)} %collective-permute-done.5, bf16[160,3584]{1,0:T(8,128)(2,1)S(1)} %bitcast.85), kind=kOutput, calls=%fused_computation.20 | convolution fusion | flops 371589120 | bytes 3645440 | tf_op jit(solution)/shard_map/dot_general | solution.py:21
  42.9 1.0 %multiply_convert_fusion.1 = bf16[160,320]{1,0:T(8,128)(2,1)S(1)} fusion(f32[160,320]{1,0:T(8,128)S(1)} %fusion.12, bf16[160,3584]{1,0:T(8,128)(2,1)S(1)} %bitcast.73, bf16[160,3584]{1,0:T(8,128)(2,1)S(1)} %collective-permute-done.6, bf16[160,3584]{1,0:T(8,128)(2,1)S(1)} %bitcast.88), kind=kOutput, calls=%fused_computation.45 | convolution fusion | flops 371896320 | bytes 3747840 | tf_op jit(solution)/shard_map/dot_general | solution.py:22
  43.9 1.0 %fusion.11 = f32[160,320]{1,0:T(8,128)S(1)} fusion(bf16[160,3584]{1,0:T(8,128)(2,1)S(1)} %bitcast.74, bf16[160,3584]{1,0:T(8,128)(2,1)S(1)} %collective-permute-done.5, bf16[160,3584]{1,0:T(8,128)(2,1)S(1)} %bitcast.86), kind=kOutput, calls=%fused_computation.19 | convolution fusion | flops 371589120 | bytes 3645440 | tf_op jit(solution)/shard_map/dot_general | solution.py:21
  45.4 1.0 %multiply_convert_fusion = bf16[160,320]{1,0:T(8,128)(2,1)S(1)} fusion(f32[160,320]{1,0:T(8,128)S(1)} %fusion.11, bf16[160,3584]{1,0:T(8,128)(2,1)S(1)} %bitcast.75, bf16[160,3584]{1,0:T(8,128)(2,1)S(1)} %collective-permute-done.6, bf16[160,3584]{1,0:T(8,128)(2,1)S(1)} %bitcast.89), kind=kOutput, calls=%fused_computation.44 | convolution fusion | flops 371896320 | bytes 3747840 | tf_op jit(solution)/shard_map/dot_general | solution.py:22
  46.9 0.5 fusion.2
  47.5 1.5 %collective-permute-start.12 = (bf16[1,40,3584]{2,1,0:T(8,128)(2,1)S(1)}, bf16[1,40,3584]{2,1,0:T(8,128)(2,1)S(1)}, u32[]{:S(2)}, u32[]{:S(2)}) collective-permute-start(bf16[1,40,3584]{2,1,0:T(8,128)(2,1)S(1)} %get-tuple-element.12), channel_id=1, source_target_pairs={{0,2},{2,0},{4,6},{6,4},{1,3},{3,1},{5,7},{7,5},{8,10},{10,8},{12,... | collective-permute-start | bytes 860168 | tf_op jit(solution)/shard_map/ppermute | solution.py:16
  48.9 1.5 %collective-permute-start.14 = (bf16[1,40,3584]{2,1,0:T(8,128)(2,1)S(1)}, bf16[1,40,3584]{2,1,0:T(8,128)(2,1)S(1)}, u32[]{:S(2)}, u32[]{:S(2)}) collective-permute-start(bf16[1,40,3584]{2,1,0:T(8,128)(2,1)S(1)} %get-tuple-element.13), channel_id=1, source_target_pairs={{0,6},{2,4},{4,2},{6,0},{1,7},{3,5},{5,3},{7,1},{8,14},{10,12},{12... | collective-permute-start | bytes 860168 | tf_op jit(solution)/shard_map/ppermute | solution.py:16
  50.4 0.6 collective-permute-start.13
  51.5 10.9 %collective-permute-done.12 = bf16[1,40,3584]{2,1,0:T(8,128)(2,1)S(1)} collective-permute-done((bf16[1,40,3584]{2,1,0:T(8,128)(2,1)S(1)}, bf16[1,40,3584]{2,1,0:T(8,128)(2,1)S(1)}, u32[]{:S(2)}, u32[]{:S(2)}) %collective-permute-start.12) | collective-permute-done | bytes 286752 | tf_op jit(solution)/shard_map/ppermute | solution.py:16
  62.4 1.2 %collective-permute-done.13 = bf16[1,40,3584]{2,1,0:T(8,128)(2,1)S(1)} collective-permute-done((bf16[1,40,3584]{2,1,0:T(8,128)(2,1)S(1)}, bf16[1,40,3584]{2,1,0:T(8,128)(2,1)S(1)}, u32[]{:S(2)}, u32[]{:S(2)}) %collective-permute-start.13) | collective-permute-done | bytes 286752 | tf_op jit(solution)/shard_map/ppermute | solution.py:16
  63.8 1.3 %collective-permute-start.18 = (bf16[1,40,3584]{2,1,0:T(8,128)(2,1)S(1)}, bf16[1,40,3584]{2,1,0:T(8,128)(2,1)S(1)}, u32[]{:S(2)}, u32[]{:S(2)}) collective-permute-start(bf16[1,40,3584]{2,1,0:T(8,128)(2,1)S(1)} %fusion.19), channel_id=1, source_target_pairs={{0,8},{8,0},{1,9},{9,1},{2,10},{10,2},{3,11},{11,3},{4,12},{12,4},... | collective-permute-start | bytes 860168 | tf_op jit(solution)/shard_map/ppermute | solution.py:12
  65.2 0.8 collective-permute-start.15
  66.0 2.5 %collective-permute-start.17 = (bf16[1,40,3584]{2,1,0:T(8,128)(2,1)S(1)}, bf16[1,40,3584]{2,1,0:T(8,128)(2,1)S(1)}, u32[]{:S(2)}, u32[]{:S(2)}) collective-permute-start(bf16[1,40,3584]{2,1,0:T(8,128)(2,1)S(1)} %get-tuple-element.10), channel_id=1, source_target_pairs={{0,6},{2,4},{4,2},{6,0},{1,7},{3,5},{5,3},{7,1},{8,14},{10,12},{12... | collective-permute-start | bytes 860168 | tf_op jit(solution)/shard_map/ppermute | solution.py:16
  68.8 9.9 %collective-permute-done.18 = bf16[1,40,3584]{2,1,0:T(8,128)(2,1)S(1)} collective-permute-done((bf16[1,40,3584]{2,1,0:T(8,128)(2,1)S(1)}, bf16[1,40,3584]{2,1,0:T(8,128)(2,1)S(1)}, u32[]{:S(2)}, u32[]{:S(2)}) %collective-permute-start.18) | collective-permute-done | bytes 286752 | tf_op jit(solution)/shard_map/ppermute | solution.py:12
  78.7 4.0 %collective-permute-done.17 = bf16[1,40,3584]{2,1,0:T(8,128)(2,1)S(1)} collective-permute-done((bf16[1,40,3584]{2,1,0:T(8,128)(2,1)S(1)}, bf16[1,40,3584]{2,1,0:T(8,128)(2,1)S(1)}, u32[]{:S(2)}, u32[]{:S(2)}) %collective-permute-start.17) | collective-permute-done | bytes 286752 | tf_op jit(solution)/shard_map/ppermute | solution.py:16
  82.7 2.4 %collective-permute-done.16 = bf16[1,40,3584]{2,1,0:T(8,128)(2,1)S(1)} collective-permute-done((bf16[1,40,3584]{2,1,0:T(8,128)(2,1)S(1)}, bf16[1,40,3584]{2,1,0:T(8,128)(2,1)S(1)}, u32[]{:S(2)}, u32[]{:S(2)}) %collective-permute-start.16) | collective-permute-done | bytes 286752 | tf_op jit(solution)/shard_map/ppermute | solution.py:16
  86.2 2.1 %collective-permute-done.19 = f32[2,40,3584]{2,1,0:T(8,128)S(1)} collective-permute-done((f32[2,40,3584]{2,1,0:T(8,128)S(1)}, f32[2,40,3584]{2,1,0:T(8,128)S(1)}, u32[]{:S(2)}, u32[]{:S(2)}) %collective-permute-start.19) | collective-permute-done | bytes 1146912 | tf_op jit(solution)/shard_map/ppermute | solution.py:12
  88.2 0.6 fusion.26
  88.8 1.3 %fusion.8 = bf16[64,3584]{1,0:T(8,128)(2,1)} fusion(f32[64,3584]{1,0:T(8,128)S(1)} %fusion.26, f32[80,3584]{1,0:T(8,128)S(1)} %bitcast.71, f32[64,160]{1,0:T(8,128)S(1)} %select_reduce_fusion), kind=kOutput, calls=%fused_computation.14 | convolution fusion | flops 110559232 | bytes 2555904 | tf_op jit(solution)/shard_map/dot_general | solution.py:134
  (58 shorter events, 5.5 us)
Async XLA Ops:
  0.0 1.5 %collective-permute-start = (s32[64,8]{0,1:T(8,128)}, s32[64,8]{0,1:T(8,128)S(1)}, u32[]{:S(2)}, u32[]{:S(2)}) collective-permute-start(s32[64,8]{0,1:T(8,128)} %param.7), channel_id=1, source_target_pairs={{0,1},{1,0},{2,3},{3,2},{4,5},{5,4},{6,7},{7,6},{8,9},{9,8},{10,11... | collective-permute-start | bytes 6152 | tf_op jit(solution)/shard_map/ppermute | solution.py:12
  0.5 2.7 %collective-permute-start.1 = (bf16[64,3584]{1,0:T(8,128)(2,1)}, bf16[64,3584]{1,0:T(8,128)(2,1)S(1)}, u32[]{:S(2)}, u32[]{:S(2)}) collective-permute-start(bf16[64,3584]{1,0:T(8,128)(2,1)} %param.6), channel_id=1, source_target_pairs={{0,1},{1,0},{2,3},{3,2},{4,5},{5,4},{6,7},{7,6},{8,9},{9,8},{10,11... | collective-permute-start | bytes 1376264 | tf_op jit(solution)/shard_map/ppermute | solution.py:12
  3.1 9.1 %copy-start.3 = (bf16[1,160,3584]{2,1,0:T(8,128)(2,1)S(1)}, bf16[1,160,3584]{2,1,0:T(8,128)(2,1)}, u32[]{:S(2)}) copy-start(bf16[1,160,3584]{2,1,0:T(8,128)(2,1)} %param.9) | copy-start | bytes 3440644
  3.1 19.0 %copy-start.4 = (bf16[1,160,3584]{2,1,0:T(8,128)(2,1)S(1)}, bf16[1,160,3584]{2,1,0:T(8,128)(2,1)}, u32[]{:S(2)}) copy-start(bf16[1,160,3584]{2,1,0:T(8,128)(2,1)} %param.10) | copy-start | bytes 3440644
  4.7 17.4 %collective-permute-start.8 = (bf16[1,40,3584]{2,1,0:T(8,128)(2,1)S(1)}, bf16[1,40,3584]{2,1,0:T(8,128)(2,1)S(1)}, u32[]{:S(2)}, u32[]{:S(2)}) collective-permute-start(bf16[1,40,3584]{2,1,0:T(8,128)(2,1)S(1)} %get-tuple-element.15), channel_id=1, source_target_pairs={{0,8},{8,0},{1,9},{9,1},{2,10},{10,2},{3,11},{11,3},{4,12},{12,4},... | collective-permute-start | bytes 860168 | tf_op jit(solution)/shard_map/ppermute | solution.py:12
  8.7 15.7 %collective-permute-start.4 = (bf16[1,40,3584]{2,1,0:T(8,128)(2,1)S(1)}, bf16[1,40,3584]{2,1,0:T(8,128)(2,1)S(1)}, u32[]{:S(2)}, u32[]{:S(2)}) collective-permute-start(bf16[1,40,3584]{2,1,0:T(8,128)(2,1)S(1)} %get-tuple-element.16), channel_id=1, source_target_pairs={{0,6},{2,4},{4,2},{6,0},{1,7},{3,5},{5,3},{7,1},{8,14},{10,12},{12... | collective-permute-start | bytes 860168 | tf_op jit(solution)/shard_map/ppermute | solution.py:16
  11.2 19.3 %collective-permute-start.3 = (bf16[1,40,3584]{2,1,0:T(8,128)(2,1)S(1)}, bf16[1,40,3584]{2,1,0:T(8,128)(2,1)S(1)}, u32[]{:S(2)}, u32[]{:S(2)}) collective-permute-start(bf16[1,40,3584]{2,1,0:T(8,128)(2,1)S(1)} %get-tuple-element.16), channel_id=1, source_target_pairs={{0,4},{2,6},{4,0},{6,2},{1,5},{3,7},{5,1},{7,3},{8,12},{10,14},{12... | collective-permute-start | bytes 860168 | tf_op jit(solution)/shard_map/ppermute | solution.py:16
  11.6 19.1 %collective-permute-start.2 = (bf16[1,40,3584]{2,1,0:T(8,128)(2,1)S(1)}, bf16[1,40,3584]{2,1,0:T(8,128)(2,1)S(1)}, u32[]{:S(2)}, u32[]{:S(2)}) collective-permute-start(bf16[1,40,3584]{2,1,0:T(8,128)(2,1)S(1)} %get-tuple-element.16), channel_id=1, source_target_pairs={{0,2},{2,0},{4,6},{6,4},{1,3},{3,1},{5,7},{7,5},{8,10},{10,8},{12,... | collective-permute-start | bytes 860168 | tf_op jit(solution)/shard_map/ppermute | solution.py:16
  12.2 29.7 %collective-permute-start.5 = (bf16[160,3584]{1,0:T(8,128)(2,1)S(1)}, bf16[160,3584]{1,0:T(8,128)(2,1)S(1)}, u32[]{:S(2)}, u32[]{:S(2)}) collective-permute-start(bf16[160,3584]{1,0:T(8,128)(2,1)S(1)} %bitcast.84), channel_id=1, source_target_pairs={{0,1},{1,0},{2,3},{3,2},{4,5},{5,4},{6,7},{7,6},{8,9},{9,8},{10,11... | collective-permute-start | bytes 3440648 | tf_op jit(solution)/shard_map/ppermute | solution.py:12
  22.1 20.8 %collective-permute-start.6 = (bf16[160,3584]{1,0:T(8,128)(2,1)S(1)}, bf16[160,3584]{1,0:T(8,128)(2,1)S(1)}, u32[]{:S(2)}, u32[]{:S(2)}) collective-permute-start(bf16[160,3584]{1,0:T(8,128)(2,1)S(1)} %bitcast.87), channel_id=1, source_target_pairs={{0,1},{1,0},{2,3},{3,2},{4,5},{5,4},{6,7},{7,6},{8,9},{9,8},{10,11... | collective-permute-start | bytes 3440648 | tf_op jit(solution)/shard_map/ppermute | solution.py:12
  24.4 12.3 %collective-permute-start.11 = (bf16[1,40,3584]{2,1,0:T(8,128)(2,1)S(1)}, bf16[1,40,3584]{2,1,0:T(8,128)(2,1)S(1)}, u32[]{:S(2)}, u32[]{:S(2)}) collective-permute-start(bf16[1,40,3584]{2,1,0:T(8,128)(2,1)S(1)} %collective-permute-done.8), channel_id=1, source_target_pairs={{0,6},{2,4},{4,2},{6,0},{1,7},{3,5},{5,3},{7,1},{8,14},{10,12},{12... | collective-permute-start | bytes 860168 | tf_op jit(solution)/shard_map/ppermute | solution.py:16
  30.5 11.2 %collective-permute-start.10 = (bf16[1,40,3584]{2,1,0:T(8,128)(2,1)S(1)}, bf16[1,40,3584]{2,1,0:T(8,128)(2,1)S(1)}, u32[]{:S(2)}, u32[]{:S(2)}) collective-permute-start(bf16[1,40,3584]{2,1,0:T(8,128)(2,1)S(1)} %collective-permute-done.8), channel_id=1, source_target_pairs={{0,4},{2,6},{4,0},{6,2},{1,5},{3,7},{5,1},{7,3},{8,12},{10,14},{12... | collective-permute-start | bytes 860168 | tf_op jit(solution)/shard_map/ppermute | solution.py:16
  30.7 11.0 %collective-permute-start.9 = (bf16[1,40,3584]{2,1,0:T(8,128)(2,1)S(1)}, bf16[1,40,3584]{2,1,0:T(8,128)(2,1)S(1)}, u32[]{:S(2)}, u32[]{:S(2)}) collective-permute-start(bf16[1,40,3584]{2,1,0:T(8,128)(2,1)S(1)} %collective-permute-done.8), channel_id=1, source_target_pairs={{0,2},{2,0},{4,6},{6,4},{1,3},{3,1},{5,7},{7,5},{8,10},{10,8},{12,... | collective-permute-start | bytes 860168 | tf_op jit(solution)/shard_map/ppermute | solution.py:16
  32.2 4.5 %copy-start = (bf16[1,160,3584]{2,1,0:T(8,128)(2,1)S(1)}, bf16[1,160,3584]{2,1,0:T(8,128)(2,1)}, u32[]{:S(2)}) copy-start(bf16[1,160,3584]{2,1,0:T(8,128)(2,1)} %param.11) | copy-start | bytes 3440644
  36.7 10.1 %collective-permute-start.7 = (bf16[160,3584]{1,0:T(8,128)(2,1)S(1)}, bf16[160,3584]{1,0:T(8,128)(2,1)S(1)}, u32[]{:S(2)}, u32[]{:S(2)}) collective-permute-start(bf16[160,3584]{1,0:T(8,128)(2,1)S(1)} %bitcast.68), channel_id=1, source_target_pairs={{0,1},{1,0},{2,3},{3,2},{4,5},{5,4},{6,7},{7,6},{8,9},{9,8},{10,11... | collective-permute-start | bytes 3440648 | tf_op jit(solution)/shard_map/ppermute | solution.py:12
  47.5 14.9 %collective-permute-start.12 = (bf16[1,40,3584]{2,1,0:T(8,128)(2,1)S(1)}, bf16[1,40,3584]{2,1,0:T(8,128)(2,1)S(1)}, u32[]{:S(2)}, u32[]{:S(2)}) collective-permute-start(bf16[1,40,3584]{2,1,0:T(8,128)(2,1)S(1)} %get-tuple-element.12), channel_id=1, source_target_pairs={{0,2},{2,0},{4,6},{6,4},{1,3},{3,1},{5,7},{7,5},{8,10},{10,8},{12,... | collective-permute-start | bytes 860168 | tf_op jit(solution)/shard_map/ppermute | solution.py:16
  48.9 13.5 %collective-permute-start.14 = (bf16[1,40,3584]{2,1,0:T(8,128)(2,1)S(1)}, bf16[1,40,3584]{2,1,0:T(8,128)(2,1)S(1)}, u32[]{:S(2)}, u32[]{:S(2)}) collective-permute-start(bf16[1,40,3584]{2,1,0:T(8,128)(2,1)S(1)} %get-tuple-element.13), channel_id=1, source_target_pairs={{0,6},{2,4},{4,2},{6,0},{1,7},{3,5},{5,3},{7,1},{8,14},{10,12},{12... | collective-permute-start | bytes 860168 | tf_op jit(solution)/shard_map/ppermute | solution.py:16
  50.4 13.2 %collective-permute-start.13 = (bf16[1,40,3584]{2,1,0:T(8,128)(2,1)S(1)}, bf16[1,40,3584]{2,1,0:T(8,128)(2,1)S(1)}, u32[]{:S(2)}, u32[]{:S(2)}) collective-permute-start(bf16[1,40,3584]{2,1,0:T(8,128)(2,1)S(1)} %get-tuple-element.14), channel_id=1, source_target_pairs={{0,4},{2,6},{4,0},{6,2},{1,5},{3,7},{5,1},{7,3},{8,12},{10,14},{12... | collective-permute-start | bytes 860168 | tf_op jit(solution)/shard_map/ppermute | solution.py:16
  63.8 14.8 %collective-permute-start.18 = (bf16[1,40,3584]{2,1,0:T(8,128)(2,1)S(1)}, bf16[1,40,3584]{2,1,0:T(8,128)(2,1)S(1)}, u32[]{:S(2)}, u32[]{:S(2)}) collective-permute-start(bf16[1,40,3584]{2,1,0:T(8,128)(2,1)S(1)} %fusion.19), channel_id=1, source_target_pairs={{0,8},{8,0},{1,9},{9,1},{2,10},{10,2},{3,11},{11,3},{4,12},{12,4},... | collective-permute-start | bytes 860168 | tf_op jit(solution)/shard_map/ppermute | solution.py:12
  65.2 13.5 %collective-permute-start.15 = (bf16[1,40,3584]{2,1,0:T(8,128)(2,1)S(1)}, bf16[1,40,3584]{2,1,0:T(8,128)(2,1)S(1)}, u32[]{:S(2)}, u32[]{:S(2)}) collective-permute-start(bf16[1,40,3584]{2,1,0:T(8,128)(2,1)S(1)} %get-tuple-element.9), channel_id=1, source_target_pairs={{0,2},{2,0},{4,6},{6,4},{1,3},{3,1},{5,7},{7,5},{8,10},{10,8},{12,... | collective-permute-start | bytes 860168 | tf_op jit(solution)/shard_map/ppermute | solution.py:16
  66.0 16.7 %collective-permute-start.17 = (bf16[1,40,3584]{2,1,0:T(8,128)(2,1)S(1)}, bf16[1,40,3584]{2,1,0:T(8,128)(2,1)S(1)}, u32[]{:S(2)}, u32[]{:S(2)}) collective-permute-start(bf16[1,40,3584]{2,1,0:T(8,128)(2,1)S(1)} %get-tuple-element.10), channel_id=1, source_target_pairs={{0,6},{2,4},{4,2},{6,0},{1,7},{3,5},{5,3},{7,1},{8,14},{10,12},{12... | collective-permute-start | bytes 860168 | tf_op jit(solution)/shard_map/ppermute | solution.py:16
  68.4 16.7 %collective-permute-start.16 = (bf16[1,40,3584]{2,1,0:T(8,128)(2,1)S(1)}, bf16[1,40,3584]{2,1,0:T(8,128)(2,1)S(1)}, u32[]{:S(2)}, u32[]{:S(2)}) collective-permute-start(bf16[1,40,3584]{2,1,0:T(8,128)(2,1)S(1)} %get-tuple-element.11), channel_id=1, source_target_pairs={{0,4},{2,6},{4,0},{6,2},{1,5},{3,7},{5,1},{7,3},{8,12},{10,14},{12... | collective-permute-start | bytes 860168 | tf_op jit(solution)/shard_map/ppermute | solution.py:16
  85.3 0.7 copy-start.1
  85.3 0.7 copy-start.2
  85.4 2.9 %collective-permute-start.19 = (f32[2,40,3584]{2,1,0:T(8,128)S(1)}, f32[2,40,3584]{2,1,0:T(8,128)S(1)}, u32[]{:S(2)}, u32[]{:S(2)}) collective-permute-start(f32[2,40,3584]{2,1,0:T(8,128)S(1)} %pad_maximum_fusion.8), channel_id=1, source_target_pairs={{0,1},{1,0},{2,3},{3,2},{4,5},{5,4},{6,7},{7,6},{8,9},{9,8},{10,11... | collective-permute-start | bytes 3440648 | tf_op jit(solution)/shard_map/ppermute | solution.py:12

commit v13 on v11

--- a/solution.py
+++ b/solution.py
@@ -80,38 +80,47 @@
     packed = jnp.dot(picker, pair_tokens, preferred_element_type=jnp.float32).astype(jnp.bfloat16)
     packed = packed.reshape(experts, half, width)
 
-    def exchange(x, k):
-        if sharers & (sharers - 1) == 0:
-            return swap(x, "sh", sharers, k)
-        return shift(x, "sh", sharers, k)
+    doubling = sharers & (sharers - 1) == 0
 
-    def back_exchange(x, k):
-        if sharers & (sharers - 1) == 0:
-            return swap(x, "sh", sharers, k)
-        return shift(x, "sh", sharers, -k)
+    def group_rows(sent):
+        if not doubling:
+            return [sent] + [shift(sent, "sh", sharers, k) for k in range(1, sharers)], list(range(sharers))
+        blocks, xors = [sent], [0]
+        bit = sharers // 2
+        while bit:
+            recv = swap(jnp.stack(blocks), "sh", sharers, bit)
+            blocks = blocks + [recv[i] for i in range(len(blocks))]
+            xors = xors + [x ^ bit for x in xors]
+            bit //= 2
+        return blocks, xors
 
-    def group_partial(sent):
-        group = [sent] + [exchange(sent, k) for k in range(1, sharers)]
-        rows = jnp.stack(group).reshape(-1, width)
+    def group_partial(gathered):
+        blocks, xors = gathered
+        rows = jnp.stack(blocks).reshape(-1, width)
         partial = quarter_rows(rows, wg, wu, wd, n_ctx).astype(jnp.bfloat16)
-        return partial.reshape((sharers,) + sent.shape)
+        return partial.reshape((sharers,) + blocks[0].shape), xors
 
-    def group_sum(partial):
+    def group_sum(parts):
+        partial, xors = parts
         total = partial[0].astype(jnp.float32)
-        for k in range(1, sharers):
-            total = total + back_exchange(partial[k], k).astype(jnp.float32)
+        for p in range(1, sharers):
+            if doubling:
+                back_part = swap(partial[p], "sh", sharers, xors[p])
+            else:
+                back_part = shift(partial[p], "sh", sharers, -xors[p])
+            total = total + back_part.astype(jnp.float32)
         return total
 
     if experts == 2:
-        local_part = group_partial(packed[0:1])
-        far_part = group_partial(shift(packed[1:2], "ex", 2, 1))
+        local_part = group_partial(group_rows(packed[0:1]))
+        far_part = group_partial(group_rows(shift(packed[1:2], "ex", 2, 1)))
         far_out = group_sum(far_part)
-        local_part, far_out = lax.optimization_barrier((local_part, far_out))
+        local_partial, far_out = lax.optimization_barrier((local_part[0], far_out))
         back = shift(far_out.astype(RETURN_DTYPE), "ex", 2, 1).astype(jnp.float32)
-        mine = jnp.concatenate([group_sum(local_part), back], axis=0)
+        mine = jnp.concatenate([group_sum((local_partial, local_part[1])), back], axis=0)
     else:
         sent = lax.all_to_all(packed, "ex", split_axis=0, concat_axis=0, tiled=True)
-        expert_out = group_sum(group_partial(sent)).astype(RETURN_DTYPE)
+        expert_out = group_sum(group_partial(group_rows(sent))).astype(RETURN_DTYPE)
         mine = lax.all_to_all(expert_out, "ex", split_axis=0, concat_axis=0, tiled=True)
         mine = mine.astype(jnp.float32)
     theirs = shift(mine, "context", n_ctx, 1)

time: 90.3 us -> 94.8 us (1.050)
  waiting for transfers between devices: 57.9 us -> 61.1 us
  starting transfers between devices: 19.4 us -> 20.7 us
    ppermute x12 -> x10, waiting for transfers between devices: 35.2 us -> 40.3 us  [swap(): return lax.ppermute(x, axis, [(i, i ^ k) for i in range(size)])]
    ppermute x8, starting transfers between devices: 5.94 us -> 8.54 us  [shift(): return lax.ppermute(x, axis, [(i, (i + k) % size) for i in range(size)])]
    ppermute x8, waiting for transfers between devices: 22.7 us -> 20.8 us  [shift(): return lax.ppermute(x, axis, [(i, (i + k) % size) for i in range(size)])]
    ppermute x12 -> x10, starting transfers between devices: 13.5 us -> 12.1 us  [swap(): return lax.ppermute(x, axis, [(i, i ^ k) for i in range(size)])]
  transfers between devices with their start and end apart: 20 -> 18, of which waited for: 12 -> 12; matrix products, arithmetic and copies ran while one was open for 9% -> 8% of each run, Pallas kernels for 0% -> 0%
where the time goes in v13:
time: 94.8 us; the launch traced here: 94.5 us
  waiting for transfers between devices  61.1 us (64%)
  starting transfers between devices  20.7 us (22%)
  matrix products  8.99 us (9%)
  other arithmetic  2.53 us (3%)
  local copies, waits for them, and re-layouts  0.97 us (1%)
    ppermute x10, waiting for transfers between devices, swap(): return lax.ppermute(x, axis, [(i, i ^ k) for i in range(size)])  40.3 us
    ppermute x8, waiting for transfers between devices, shift(): return lax.ppermute(x, axis, [(i, (i + k) % size) for i in range(size)])  20.8 us
    ppermute x10, starting transfers between devices, swap(): return lax.ppermute(x, axis, [(i, i ^ k) for i in range(size)])  12.1 us
    ppermute x8, starting transfers between devices, shift(): return lax.ppermute(x, axis, [(i, (i + k) % size) for i in range(size)])  8.54 us
    dot_general x2, matrix products, quarter_rows(): up = lax.dot_general(rows, w_up, dims, preferred_element_type=jnp.float32)  2.01 us
    dot_general x2, matrix products, quarter_rows(): lax.dot_general(rows, w_gate, dims, preferred_element_type=jnp.float32)  2 us
    dot_general x4, matrix products, quarter_rows(): jnp.dot(hidden[:, c * slab:(c + 1) * slab], w_down[c * slab:(c + 1) * sla...  1.92 us
  transfers between devices with their start and end apart: 18, of which 12 were waited for; matrix products, arithmetic and copies ran while one was open for 8% of the time, Pallas kernels for 0%

profile of v13, /device:TPU:0, one launch (start us, length us, event | category | flops | bytes accessed | tf_op | source)
XLA Modules:
  0.0 94.5 jit_solution(14178357178368867253)
XLA Ops:
  0.6 0.9 collective-permute-done
  1.5 0.8 add_select_fusion
  3.1 1.4 %convolution_convert_fusion.4 = bf16[80,3584]{1,0:T(8,128)(2,1)S(1)} fusion(pred[80,128]{1,0:T(8,128)(4,1)S(1)} %fusion.23, bf16[64,3584]{1,0:T(8,128)(2,1)S(1)} %collective-permute-done.1, bf16[64,3584]{1,0:T(8,128)(2,1)} %param.6), kind=kOutput, calls=%fused_computation.12 | convolution fusion | flops 75522048 | bytes 1501184 | tf_op jit(solution)/shard_map/dot_general | solution.py:80
  4.6 4.0 %collective-permute-start.7 = (bf16[1,40,3584]{2,1,0:T(8,128)(2,1)S(1)}, bf16[1,40,3584]{2,1,0:T(8,128)(2,1)S(1)}, u32[]{:S(2)}, u32[]{:S(2)}) collective-permute-start(bf16[1,40,3584]{2,1,0:T(8,128)(2,1)S(1)} %get-tuple-element.15), channel_id=1, source_target_pairs={{0,8},{8,0},{1,9},{9,1},{2,10},{10,2},{3,11},{11,3},{4,12},{12,4},... | collective-permute-start | bytes 860168 | tf_op jit(solution)/shard_map/ppermute | solution.py:12
  8.6 1.6 %collective-permute-start.2 = (bf16[1,1,40,3584]{3,2,1,0:T(8,128)(2,1)S(1)}, bf16[1,1,40,3584]{3,2,1,0:T(8,128)(2,1)S(1)}, u32[]{:S(2)}, u32[]{:S(2)}) collective-permute-start(bf16[1,1,40,3584]{3,2,1,0:T(8,128)(2,1)S(1)} %get-tuple-element.16), channel_id=1, source_target_pairs={{0,4},{2,6},{4,0},{6,2},{1,5},{3,7},{5,1},{7,3},{8,12},{10,14},{12... | collective-permute-start | bytes 860168 | tf_op jit(solution)/shard_map/ppermute | solution.py:16
  10.2 11.8 %collective-permute-done.7 = bf16[1,40,3584]{2,1,0:T(8,128)(2,1)S(1)} collective-permute-done((bf16[1,40,3584]{2,1,0:T(8,128)(2,1)S(1)}, bf16[1,40,3584]{2,1,0:T(8,128)(2,1)S(1)}, u32[]{:S(2)}, u32[]{:S(2)}) %collective-permute-start.7) | collective-permute-done | bytes 286752 | tf_op jit(solution)/shard_map/ppermute | solution.py:12
  22.0 0.6 collective-permute-start.8
  22.7 1.6 %collective-permute-start.3 = (bf16[2,1,40,3584]{3,2,1,0:T(8,128)(2,1)S(1)}, bf16[2,1,40,3584]{3,2,1,0:T(8,128)(2,1)S(1)}, u32[]{:S(2)}, u32[]{:S(2)}) collective-permute-start(bf16[2,1,40,3584]{3,2,1,0:T(8,128)(2,1)S(1)} %pad_maximum_fusion.10), channel_id=1, source_target_pairs={{0,2},{2,0},{4,6},{6,4},{1,3},{3,1},{5,7},{7,5},{8,10},{10,8},{12,... | collective-permute-start | bytes 1720328 | tf_op jit(solution)/shard_map/ppermute | solution.py:16
  24.8 5.6 %collective-permute-done.8 = bf16[1,1,40,3584]{3,2,1,0:T(8,128)(2,1)S(1)} collective-permute-done((bf16[1,1,40,3584]{3,2,1,0:T(8,128)(2,1)S(1)}, bf16[1,1,40,3584]{3,2,1,0:T(8,128)(2,1)S(1)}, u32[]{:S(2)}, u32[]{:S(2)}) %collective-permute-start.8) | collective-permute-done | bytes 286752 | tf_op jit(solution)/shard_map/ppermute | solution.py:16
  30.4 1.3 %collective-permute-start.9 = (bf16[2,1,40,3584]{3,2,1,0:T(8,128)(2,1)S(1)}, bf16[2,1,40,3584]{3,2,1,0:T(8,128)(2,1)S(1)}, u32[]{:S(2)}, u32[]{:S(2)}) collective-permute-start(bf16[2,1,40,3584]{3,2,1,0:T(8,128)(2,1)S(1)} %pad_maximum_fusion.11), channel_id=1, source_target_pairs={{0,2},{2,0},{4,6},{6,4},{1,3},{3,1},{5,7},{7,5},{8,10},{10,8},{12,... | collective-permute-start | bytes 1720328 | tf_op jit(solution)/shard_map/ppermute | solution.py:16
  31.7 7.0 %collective-permute-done.3 = bf16[2,1,40,3584]{3,2,1,0:T(8,128)(2,1)S(1)} collective-permute-done((bf16[2,1,40,3584]{3,2,1,0:T(8,128)(2,1)S(1)}, bf16[2,1,40,3584]{3,2,1,0:T(8,128)(2,1)S(1)}, u32[]{:S(2)}, u32[]{:S(2)}) %collective-permute-start.3) | collective-permute-done | bytes 573472 | tf_op jit(solution)/shard_map/ppermute | solution.py:16
  38.8 1.0 %fusion.11 = f32[160,320]{1,0:T(8,128)S(1)} fusion(bf16[160,3584]{1,0:T(8,128)(2,1)S(1)} %bitcast.64, bf16[160,3584]{1,0:T(8,128)(2,1)S(1)} %collective-permute-done.4, bf16[160,3584]{1,0:T(8,128)(2,1)S(1)} %bitcast.69), kind=kOutput, calls=%fused_computation.20 | convolution fusion | flops 371589120 | bytes 3645440 | tf_op jit(solution)/shard_map/dot_general | solution.py:21
  39.8 1.0 %multiply_convert_fusion.1 = bf16[160,320]{1,0:T(8,128)(2,1)S(1)} fusion(f32[160,320]{1,0:T(8,128)S(1)} %fusion.11, bf16[160,3584]{1,0:T(8,128)(2,1)S(1)} %bitcast.65, bf16[160,3584]{1,0:T(8,128)(2,1)S(1)} %collective-permute-done.5, bf16[160,3584]{1,0:T(8,128)(2,1)S(1)} %bitcast.72), kind=kOutput, calls=%fused_computation.46 | convolution fusion | flops 371896320 | bytes 3747840 | tf_op jit(solution)/shard_map/dot_general | solution.py:22
  41.3 8.4 %collective-permute-done.9 = bf16[2,1,40,3584]{3,2,1,0:T(8,128)(2,1)S(1)} collective-permute-done((bf16[2,1,40,3584]{3,2,1,0:T(8,128)(2,1)S(1)}, bf16[2,1,40,3584]{3,2,1,0:T(8,128)(2,1)S(1)}, u32[]{:S(2)}, u32[]{:S(2)}) %collective-permute-start.9) | collective-permute-done | bytes 573472 | tf_op jit(solution)/shard_map/ppermute | solution.py:16
  49.8 1.0 %fusion.10 = f32[160,320]{1,0:T(8,128)S(1)} fusion(bf16[160,3584]{1,0:T(8,128)(2,1)S(1)} %bitcast.66, bf16[160,3584]{1,0:T(8,128)(2,1)S(1)} %collective-permute-done.4, bf16[160,3584]{1,0:T(8,128)(2,1)S(1)} %bitcast.70), kind=kOutput, calls=%fused_computation.19 | convolution fusion | flops 371589120 | bytes 3645440 | tf_op jit(solution)/shard_map/dot_general | solution.py:21
  50.8 1.0 %multiply_convert_fusion = bf16[160,320]{1,0:T(8,128)(2,1)S(1)} fusion(f32[160,320]{1,0:T(8,128)S(1)} %fusion.10, bf16[160,3584]{1,0:T(8,128)(2,1)S(1)} %bitcast.67, bf16[160,3584]{1,0:T(8,128)(2,1)S(1)} %collective-permute-done.5, bf16[160,3584]{1,0:T(8,128)(2,1)S(1)} %bitcast.73), kind=kOutput, calls=%fused_computation.45 | convolution fusion | flops 371896320 | bytes 3747840 | tf_op jit(solution)/shard_map/dot_general | solution.py:22
  52.3 0.5 fusion.2
  52.9 1.0 %collective-permute-start.10 = (bf16[1,40,3584]{2,1,0:T(8,128)(2,1)S(1)}, bf16[1,40,3584]{2,1,0:T(8,128)(2,1)S(1)}, u32[]{:S(2)}, u32[]{:S(2)}) collective-permute-start(bf16[1,40,3584]{2,1,0:T(8,128)(2,1)S(1)} %get-tuple-element.12), channel_id=1, source_target_pairs={{0,4},{2,6},{4,0},{6,2},{1,5},{3,7},{5,1},{7,3},{8,12},{10,14},{12... | collective-permute-start | bytes 860168 | tf_op jit(solution)/shard_map/ppermute | solution.py:16
  53.9 2.0 %collective-permute-start.12 = (bf16[1,40,3584]{2,1,0:T(8,128)(2,1)S(1)}, bf16[1,40,3584]{2,1,0:T(8,128)(2,1)S(1)}, u32[]{:S(2)}, u32[]{:S(2)}) collective-permute-start(bf16[1,40,3584]{2,1,0:T(8,128)(2,1)S(1)} %get-tuple-element.13), channel_id=1, source_target_pairs={{0,6},{2,4},{4,2},{6,0},{1,7},{3,5},{5,3},{7,1},{8,14},{10,12},{12... | collective-permute-start | bytes 860168 | tf_op jit(solution)/shard_map/ppermute | solution.py:16
  55.9 0.5 collective-permute-start.11
  57.0 5.8 %collective-permute-done.10 = bf16[1,40,3584]{2,1,0:T(8,128)(2,1)S(1)} collective-permute-done((bf16[1,40,3584]{2,1,0:T(8,128)(2,1)S(1)}, bf16[1,40,3584]{2,1,0:T(8,128)(2,1)S(1)}, u32[]{:S(2)}, u32[]{:S(2)}) %collective-permute-start.10) | collective-permute-done | bytes 286752 | tf_op jit(solution)/shard_map/ppermute | solution.py:16
  62.7 5.0 %collective-permute-done.12 = bf16[1,40,3584]{2,1,0:T(8,128)(2,1)S(1)} collective-permute-done((bf16[1,40,3584]{2,1,0:T(8,128)(2,1)S(1)}, bf16[1,40,3584]{2,1,0:T(8,128)(2,1)S(1)}, u32[]{:S(2)}, u32[]{:S(2)}) %collective-permute-start.12) | collective-permute-done | bytes 286752 | tf_op jit(solution)/shard_map/ppermute | solution.py:16
  67.8 1.4 %collective-permute-done.11 = bf16[1,40,3584]{2,1,0:T(8,128)(2,1)S(1)} collective-permute-done((bf16[1,40,3584]{2,1,0:T(8,128)(2,1)S(1)}, bf16[1,40,3584]{2,1,0:T(8,128)(2,1)S(1)}, u32[]{:S(2)}, u32[]{:S(2)}) %collective-permute-start.11) | collective-permute-done | bytes 286752 | tf_op jit(solution)/shard_map/ppermute | solution.py:16
  69.3 3.5 %collective-permute-start.16 = (bf16[1,40,3584]{2,1,0:T(8,128)(2,1)S(1)}, bf16[1,40,3584]{2,1,0:T(8,128)(2,1)S(1)}, u32[]{:S(2)}, u32[]{:S(2)}) collective-permute-start(bf16[1,40,3584]{2,1,0:T(8,128)(2,1)S(1)} %fusion.18), channel_id=1, source_target_pairs={{0,8},{8,0},{1,9},{9,1},{2,10},{10,2},{3,11},{11,3},{4,12},{12,4},... | collective-permute-start | bytes 860168 | tf_op jit(solution)/shard_map/ppermute | solution.py:12
  72.8 0.7 collective-permute-start.13
  73.5 1.4 %collective-permute-start.15 = (bf16[1,40,3584]{2,1,0:T(8,128)(2,1)S(1)}, bf16[1,40,3584]{2,1,0:T(8,128)(2,1)S(1)}, u32[]{:S(2)}, u32[]{:S(2)}) collective-permute-start(bf16[1,40,3584]{2,1,0:T(8,128)(2,1)S(1)} %get-tuple-element.10), channel_id=1, source_target_pairs={{0,6},{2,4},{4,2},{6,0},{1,7},{3,5},{5,3},{7,1},{8,14},{10,12},{12... | collective-permute-start | bytes 860168 | tf_op jit(solution)/shard_map/ppermute | solution.py:16
  74.9 1.5 %collective-permute-start.14 = (bf16[1,40,3584]{2,1,0:T(8,128)(2,1)S(1)}, bf16[1,40,3584]{2,1,0:T(8,128)(2,1)S(1)}, u32[]{:S(2)}, u32[]{:S(2)}) collective-permute-start(bf16[1,40,3584]{2,1,0:T(8,128)(2,1)S(1)} %get-tuple-element.11), channel_id=1, source_target_pairs={{0,2},{2,0},{4,6},{6,4},{1,3},{3,1},{5,7},{7,5},{8,10},{10,8},{12,... | collective-permute-start | bytes 860168 | tf_op jit(solution)/shard_map/ppermute | solution.py:16
  76.3 6.1 %collective-permute-done.16 = bf16[1,40,3584]{2,1,0:T(8,128)(2,1)S(1)} collective-permute-done((bf16[1,40,3584]{2,1,0:T(8,128)(2,1)S(1)}, bf16[1,40,3584]{2,1,0:T(8,128)(2,1)S(1)}, u32[]{:S(2)}, u32[]{:S(2)}) %collective-permute-start.16) | collective-permute-done | bytes 286752 | tf_op jit(solution)/shard_map/ppermute | solution.py:12
  82.4 4.1 %collective-permute-done.13 = bf16[1,40,3584]{2,1,0:T(8,128)(2,1)S(1)} collective-permute-done((bf16[1,40,3584]{2,1,0:T(8,128)(2,1)S(1)}, bf16[1,40,3584]{2,1,0:T(8,128)(2,1)S(1)}, u32[]{:S(2)}, u32[]{:S(2)}) %collective-permute-start.13) | collective-permute-done | bytes 286752 | tf_op jit(solution)/shard_map/ppermute | solution.py:16
  86.6 3.0 %collective-permute-done.15 = bf16[1,40,3584]{2,1,0:T(8,128)(2,1)S(1)} collective-permute-done((bf16[1,40,3584]{2,1,0:T(8,128)(2,1)S(1)}, bf16[1,40,3584]{2,1,0:T(8,128)(2,1)S(1)}, u32[]{:S(2)}, u32[]{:S(2)}) %collective-permute-start.15) | collective-permute-done | bytes 286752 | tf_op jit(solution)/shard_map/ppermute | solution.py:16
  90.6 2.1 %collective-permute-done.17 = f32[2,40,3584]{2,1,0:T(8,128)S(1)} collective-permute-done((f32[2,40,3584]{2,1,0:T(8,128)S(1)}, f32[2,40,3584]{2,1,0:T(8,128)S(1)}, u32[]{:S(2)}, u32[]{:S(2)}) %collective-permute-start.17) | collective-permute-done | bytes 1146912 | tf_op jit(solution)/shard_map/ppermute | solution.py:12
  92.9 1.6 %convolution_convert_fusion.5 = bf16[64,3584]{1,0:T(8,128)(2,1)} fusion(f32[64,160]{1,0:T(8,128)S(1)} %select_reduce_fusion, f32[160,3584]{1,0:T(8,128)S(1)} %bitcast.57), kind=kOutput, calls=%fused_computation.13 | convolution fusion | flops 220430336 | bytes 2793472 | tf_op jit(solution)/shard_map/dot_general | solution.py:142
  (56 shorter events, 5.2 us)
Async XLA Ops:
  0.0 1.5 %collective-permute-start = (s32[64,8]{0,1:T(8,128)}, s32[64,8]{0,1:T(8,128)S(1)}, u32[]{:S(2)}, u32[]{:S(2)}) collective-permute-start(s32[64,8]{0,1:T(8,128)} %param.7), channel_id=1, source_target_pairs={{0,1},{1,0},{2,3},{3,2},{4,5},{5,4},{6,7},{7,6},{8,9},{9,8},{10,11... | collective-permute-start | bytes 6152 | tf_op jit(solution)/shard_map/ppermute | solution.py:12
  0.5 2.7 %collective-permute-start.1 = (bf16[64,3584]{1,0:T(8,128)(2,1)}, bf16[64,3584]{1,0:T(8,128)(2,1)S(1)}, u32[]{:S(2)}, u32[]{:S(2)}) collective-permute-start(bf16[64,3584]{1,0:T(8,128)(2,1)} %param.6), channel_id=1, source_target_pairs={{0,1},{1,0},{2,3},{3,2},{4,5},{5,4},{6,7},{7,6},{8,9},{9,8},{10,11... | collective-permute-start | bytes 1376264 | tf_op jit(solution)/shard_map/ppermute | solution.py:12
  3.1 7.1 %copy-start.3 = (bf16[1,160,3584]{2,1,0:T(8,128)(2,1)S(1)}, bf16[1,160,3584]{2,1,0:T(8,128)(2,1)}, u32[]{:S(2)}) copy-start(bf16[1,160,3584]{2,1,0:T(8,128)(2,1)} %param.9) | copy-start | bytes 3440644
  4.6 19.7 %copy-start.4 = (bf16[1,160,3584]{2,1,0:T(8,128)(2,1)S(1)}, bf16[1,160,3584]{2,1,0:T(8,128)(2,1)}, u32[]{:S(2)}) copy-start(bf16[1,160,3584]{2,1,0:T(8,128)(2,1)} %param.10) | copy-start | bytes 3440644
  4.6 19.7 %copy-start = (bf16[1,160,3584]{2,1,0:T(8,128)(2,1)S(1)}, bf16[1,160,3584]{2,1,0:T(8,128)(2,1)}, u32[]{:S(2)}) copy-start(bf16[1,160,3584]{2,1,0:T(8,128)(2,1)} %param.11) | copy-start | bytes 3440644
  4.6 17.4 %collective-permute-start.7 = (bf16[1,40,3584]{2,1,0:T(8,128)(2,1)S(1)}, bf16[1,40,3584]{2,1,0:T(8,128)(2,1)S(1)}, u32[]{:S(2)}, u32[]{:S(2)}) collective-permute-start(bf16[1,40,3584]{2,1,0:T(8,128)(2,1)S(1)} %get-tuple-element.15), channel_id=1, source_target_pairs={{0,8},{8,0},{1,9},{9,1},{2,10},{10,2},{3,11},{11,3},{4,12},{12,4},... | collective-permute-start | bytes 860168 | tf_op jit(solution)/shard_map/ppermute | solution.py:12
  8.6 14.0 %collective-permute-start.2 = (bf16[1,1,40,3584]{3,2,1,0:T(8,128)(2,1)S(1)}, bf16[1,1,40,3584]{3,2,1,0:T(8,128)(2,1)S(1)}, u32[]{:S(2)}, u32[]{:S(2)}) collective-permute-start(bf16[1,1,40,3584]{3,2,1,0:T(8,128)(2,1)S(1)} %get-tuple-element.16), channel_id=1, source_target_pairs={{0,4},{2,6},{4,0},{6,2},{1,5},{3,7},{5,1},{7,3},{8,12},{10,14},{12... | collective-permute-start | bytes 860168 | tf_op jit(solution)/shard_map/ppermute | solution.py:16
  10.2 28.6 %collective-permute-start.4 = (bf16[160,3584]{1,0:T(8,128)(2,1)S(1)}, bf16[160,3584]{1,0:T(8,128)(2,1)S(1)}, u32[]{:S(2)}, u32[]{:S(2)}) collective-permute-start(bf16[160,3584]{1,0:T(8,128)(2,1)S(1)} %bitcast.68), channel_id=1, source_target_pairs={{0,1},{1,0},{2,3},{3,2},{4,5},{5,4},{6,7},{7,6},{8,9},{9,8},{10,11... | collective-permute-start | bytes 3440648 | tf_op jit(solution)/shard_map/ppermute | solution.py:12
  22.0 8.3 %collective-permute-start.8 = (bf16[1,1,40,3584]{3,2,1,0:T(8,128)(2,1)S(1)}, bf16[1,1,40,3584]{3,2,1,0:T(8,128)(2,1)S(1)}, u32[]{:S(2)}, u32[]{:S(2)}) collective-permute-start(bf16[1,1,40,3584]{3,2,1,0:T(8,128)(2,1)S(1)} %bitcast.61), channel_id=1, source_target_pairs={{0,4},{2,6},{4,0},{6,2},{1,5},{3,7},{5,1},{7,3},{8,12},{10,14},{12... | collective-permute-start | bytes 860168 | tf_op jit(solution)/shard_map/ppermute | solution.py:16
  22.7 15.9 %collective-permute-start.3 = (bf16[2,1,40,3584]{3,2,1,0:T(8,128)(2,1)S(1)}, bf16[2,1,40,3584]{3,2,1,0:T(8,128)(2,1)S(1)}, u32[]{:S(2)}, u32[]{:S(2)}) collective-permute-start(bf16[2,1,40,3584]{3,2,1,0:T(8,128)(2,1)S(1)} %pad_maximum_fusion.10), channel_id=1, source_target_pairs={{0,2},{2,0},{4,6},{6,4},{1,3},{3,1},{5,7},{7,5},{8,10},{10,8},{12,... | collective-permute-start | bytes 1720328 | tf_op jit(solution)/shard_map/ppermute | solution.py:16
  24.3 15.5 %collective-permute-start.5 = (bf16[160,3584]{1,0:T(8,128)(2,1)S(1)}, bf16[160,3584]{1,0:T(8,128)(2,1)S(1)}, u32[]{:S(2)}, u32[]{:S(2)}) collective-permute-start(bf16[160,3584]{1,0:T(8,128)(2,1)S(1)} %bitcast.71), channel_id=1, source_target_pairs={{0,1},{1,0},{2,3},{3,2},{4,5},{5,4},{6,7},{7,6},{8,9},{9,8},{10,11... | collective-permute-start | bytes 3440648 | tf_op jit(solution)/shard_map/ppermute | solution.py:12
  24.3 28.0 %collective-permute-start.6 = (bf16[160,3584]{1,0:T(8,128)(2,1)S(1)}, bf16[160,3584]{1,0:T(8,128)(2,1)S(1)}, u32[]{:S(2)}, u32[]{:S(2)}) collective-permute-start(bf16[160,3584]{1,0:T(8,128)(2,1)S(1)} %bitcast.58), channel_id=1, source_target_pairs={{0,1},{1,0},{2,3},{3,2},{4,5},{5,4},{6,7},{7,6},{8,9},{9,8},{10,11... | collective-permute-start | bytes 3440648 | tf_op jit(solution)/shard_map/ppermute | solution.py:12
  30.4 19.3 %collective-permute-start.9 = (bf16[2,1,40,3584]{3,2,1,0:T(8,128)(2,1)S(1)}, bf16[2,1,40,3584]{3,2,1,0:T(8,128)(2,1)S(1)}, u32[]{:S(2)}, u32[]{:S(2)}) collective-permute-start(bf16[2,1,40,3584]{3,2,1,0:T(8,128)(2,1)S(1)} %pad_maximum_fusion.11), channel_id=1, source_target_pairs={{0,2},{2,0},{4,6},{6,4},{1,3},{3,1},{5,7},{7,5},{8,10},{10,8},{12,... | collective-permute-start | bytes 1720328 | tf_op jit(solution)/shard_map/ppermute | solution.py:16
  52.9 9.8 %collective-permute-start.10 = (bf16[1,40,3584]{2,1,0:T(8,128)(2,1)S(1)}, bf16[1,40,3584]{2,1,0:T(8,128)(2,1)S(1)}, u32[]{:S(2)}, u32[]{:S(2)}) collective-permute-start(bf16[1,40,3584]{2,1,0:T(8,128)(2,1)S(1)} %get-tuple-element.12), channel_id=1, source_target_pairs={{0,4},{2,6},{4,0},{6,2},{1,5},{3,7},{5,1},{7,3},{8,12},{10,14},{12... | collective-permute-start | bytes 860168 | tf_op jit(solution)/shard_map/ppermute | solution.py:16
  53.9 13.8 %collective-permute-start.12 = (bf16[1,40,3584]{2,1,0:T(8,128)(2,1)S(1)}, bf16[1,40,3584]{2,1,0:T(8,128)(2,1)S(1)}, u32[]{:S(2)}, u32[]{:S(2)}) collective-permute-start(bf16[1,40,3584]{2,1,0:T(8,128)(2,1)S(1)} %get-tuple-element.13), channel_id=1, source_target_pairs={{0,6},{2,4},{4,2},{6,0},{1,7},{3,5},{5,3},{7,1},{8,14},{10,12},{12... | collective-permute-start | bytes 860168 | tf_op jit(solution)/shard_map/ppermute | solution.py:16
  55.9 13.2 %collective-permute-start.11 = (bf16[1,40,3584]{2,1,0:T(8,128)(2,1)S(1)}, bf16[1,40,3584]{2,1,0:T(8,128)(2,1)S(1)}, u32[]{:S(2)}, u32[]{:S(2)}) collective-permute-start(bf16[1,40,3584]{2,1,0:T(8,128)(2,1)S(1)} %get-tuple-element.14), channel_id=1, source_target_pairs={{0,2},{2,0},{4,6},{6,4},{1,3},{3,1},{5,7},{7,5},{8,10},{10,8},{12,... | collective-permute-start | bytes 860168 | tf_op jit(solution)/shard_map/ppermute | solution.py:16
  69.3 13.1 %collective-permute-start.16 = (bf16[1,40,3584]{2,1,0:T(8,128)(2,1)S(1)}, bf16[1,40,3584]{2,1,0:T(8,128)(2,1)S(1)}, u32[]{:S(2)}, u32[]{:S(2)}) collective-permute-start(bf16[1,40,3584]{2,1,0:T(8,128)(2,1)S(1)} %fusion.18), channel_id=1, source_target_pairs={{0,8},{8,0},{1,9},{9,1},{2,10},{10,2},{3,11},{11,3},{4,12},{12,4},... | collective-permute-start | bytes 860168 | tf_op jit(solution)/shard_map/ppermute | solution.py:12
  72.8 13.8 %collective-permute-start.13 = (bf16[1,40,3584]{2,1,0:T(8,128)(2,1)S(1)}, bf16[1,40,3584]{2,1,0:T(8,128)(2,1)S(1)}, u32[]{:S(2)}, u32[]{:S(2)}) collective-permute-start(bf16[1,40,3584]{2,1,0:T(8,128)(2,1)S(1)} %get-tuple-element.9), channel_id=1, source_target_pairs={{0,4},{2,6},{4,0},{6,2},{1,5},{3,7},{5,1},{7,3},{8,12},{10,14},{12... | collective-permute-start | bytes 860168 | tf_op jit(solution)/shard_map/ppermute | solution.py:16
  73.5 16.1 %collective-permute-start.15 = (bf16[1,40,3584]{2,1,0:T(8,128)(2,1)S(1)}, bf16[1,40,3584]{2,1,0:T(8,128)(2,1)S(1)}, u32[]{:S(2)}, u32[]{:S(2)}) collective-permute-start(bf16[1,40,3584]{2,1,0:T(8,128)(2,1)S(1)} %get-tuple-element.10), channel_id=1, source_target_pairs={{0,6},{2,4},{4,2},{6,0},{1,7},{3,5},{5,3},{7,1},{8,14},{10,12},{12... | collective-permute-start | bytes 860168 | tf_op jit(solution)/shard_map/ppermute | solution.py:16
  74.9 14.7 %collective-permute-start.14 = (bf16[1,40,3584]{2,1,0:T(8,128)(2,1)S(1)}, bf16[1,40,3584]{2,1,0:T(8,128)(2,1)S(1)}, u32[]{:S(2)}, u32[]{:S(2)}) collective-permute-start(bf16[1,40,3584]{2,1,0:T(8,128)(2,1)S(1)} %get-tuple-element.11), channel_id=1, source_target_pairs={{0,2},{2,0},{4,6},{6,4},{1,3},{3,1},{5,7},{7,5},{8,10},{10,8},{12,... | collective-permute-start | bytes 860168 | tf_op jit(solution)/shard_map/ppermute | solution.py:16
  89.7 0.7 copy-start.1
  89.8 0.7 copy-start.2
  89.8 2.9 %collective-permute-start.17 = (f32[2,40,3584]{2,1,0:T(8,128)S(1)}, f32[2,40,3584]{2,1,0:T(8,128)S(1)}, u32[]{:S(2)}, u32[]{:S(2)}) collective-permute-start(f32[2,40,3584]{2,1,0:T(8,128)S(1)} %pad_maximum_fusion.9), channel_id=1, source_target_pairs={{0,1},{1,0},{2,3},{3,2},{4,5},{5,4},{6,7},{7,6},{8,9},{9,8},{10,11... | collective-permute-start | bytes 3440648 | tf_op jit(solution)/shard_map/ppermute | solution.py:12

commit v14 on v11

--- a/solution.py
+++ b/solution.py
@@ -106,7 +106,6 @@
         local_part = group_partial(packed[0:1])
         far_part = group_partial(shift(packed[1:2], "ex", 2, 1))
         far_out = group_sum(far_part)
-        local_part, far_out = lax.optimization_barrier((local_part, far_out))
         back = shift(far_out.astype(RETURN_DTYPE), "ex", 2, 1).astype(jnp.float32)
         mine = jnp.concatenate([group_sum(local_part), back], axis=0)
     else:

time: 90.3 us -> 87.3 us (0.967)
  waiting for transfers between devices: 57.9 us -> 53.7 us
  starting transfers between devices: 19.4 us -> 20.6 us
    ppermute x8, waiting for transfers between devices: 22.7 us -> 12.9 us  [shift(): return lax.ppermute(x, axis, [(i, (i + k) % size) for i in range(size)])]
    ppermute x12, waiting for transfers between devices: 35.2 us -> 40.9 us  [swap(): return lax.ppermute(x, axis, [(i, i ^ k) for i in range(size)])]
    ppermute x12, starting transfers between devices: 13.5 us -> 15.3 us  [swap(): return lax.ppermute(x, axis, [(i, i ^ k) for i in range(size)])]
  transfers between devices with their start and end apart: 20 -> 20, of which waited for: 12 -> 11; matrix products, arithmetic and copies ran while one was open for 9% -> 9% of each run, Pallas kernels for 0% -> 0%
where the time goes in v14:
time: 87.3 us; the launch traced here: 87.1 us
  waiting for transfers between devices  53.7 us (62%)
  starting transfers between devices  20.6 us (24%)
  matrix products  9.06 us (10%)
  other arithmetic  2.48 us (3%)
  local copies, waits for them, and re-layouts  0.99 us (1%)
    ppermute x12, waiting for transfers between devices, swap(): return lax.ppermute(x, axis, [(i, i ^ k) for i in range(size)])  40.9 us
    ppermute x12, starting transfers between devices, swap(): return lax.ppermute(x, axis, [(i, i ^ k) for i in range(size)])  15.3 us
    ppermute x8, waiting for transfers between devices, shift(): return lax.ppermute(x, axis, [(i, (i + k) % size) for i in range(size)])  12.9 us
    ppermute x8, starting transfers between devices, shift(): return lax.ppermute(x, axis, [(i, (i + k) % size) for i in range(size)])  5.3 us
    dot_general x2, matrix products, quarter_rows(): up = lax.dot_general(rows, w_up, dims, preferred_element_type=jnp.float32)  2.01 us
    dot_general x2, matrix products, quarter_rows(): lax.dot_general(rows, w_gate, dims, preferred_element_type=jnp.float32)  2.01 us
    dot_general x4, matrix products, quarter_rows(): jnp.dot(hidden[:, c * slab:(c + 1) * slab], w_down[c * slab:(c + 1) * sla...  1.91 us
  transfers between devices with their start and end apart: 20, of which 11 were waited for; matrix products, arithmetic and copies ran while one was open for 9% of the time, Pallas kernels for 0%

profile of v14, /device:TPU:0, one launch (start us, length us, event | category | flops | bytes accessed | tf_op | source)
XLA Modules:
  0.0 87.1 jit_solution(15145510169973994098)
XLA Ops:
  0.6 0.9 %collective-permute-done = s32[64,8]{0,1:T(8,128)S(1)} collective-permute-done((s32[64,8]{0,1:T(8,128)}, s32[64,8]{0,1:T(8,128)S(1)}, u32[]{:S(2)}, u32[]{:S(2)}) %collective-permute-start) | collective-permute-done | bytes 2080 | tf_op jit(solution)/shard_map/ppermute | solution.py:12
  1.5 0.8 add_select_fusion
  3.2 1.5 %convolution_convert_fusion.4 = bf16[80,3584]{1,0:T(8,128)(2,1)S(1)} fusion(pred[80,128]{1,0:T(8,128)(4,1)S(1)} %fusion.24, bf16[64,3584]{1,0:T(8,128)(2,1)S(1)} %collective-permute-done.1, bf16[64,3584]{1,0:T(8,128)(2,1)} %param.6), kind=kOutput, calls=%fused_computation.12 | convolution fusion | flops 75522048 | bytes 1501184 | tf_op jit(solution)/shard_map/dot_general | solution.py:80
  4.7 4.0 %collective-permute-start.11 = (bf16[1,40,3584]{2,1,0:T(8,128)(2,1)S(1)}, bf16[1,40,3584]{2,1,0:T(8,128)(2,1)S(1)}, u32[]{:S(2)}, u32[]{:S(2)}) collective-permute-start(bf16[1,40,3584]{2,1,0:T(8,128)(2,1)S(1)} %get-tuple-element.13), channel_id=1, source_target_pairs={{0,8},{8,0},{1,9},{9,1},{2,10},{10,2},{3,11},{11,3},{4,12},{12,4},... | collective-permute-start | bytes 860168 | tf_op jit(solution)/shard_map/ppermute | solution.py:12
  8.7 2.5 %collective-permute-start.4 = (bf16[1,40,3584]{2,1,0:T(8,128)(2,1)S(1)}, bf16[1,40,3584]{2,1,0:T(8,128)(2,1)S(1)}, u32[]{:S(2)}, u32[]{:S(2)}) collective-permute-start(bf16[1,40,3584]{2,1,0:T(8,128)(2,1)S(1)} %get-tuple-element.12), channel_id=1, source_target_pairs={{0,6},{2,4},{4,2},{6,0},{1,7},{3,5},{5,3},{7,1},{8,14},{10,12},{12... | collective-permute-start | bytes 860168 | tf_op jit(solution)/shard_map/ppermute | solution.py:16
  11.6 0.5 collective-permute-start.2
  12.2 9.9 %collective-permute-done.11 = bf16[1,40,3584]{2,1,0:T(8,128)(2,1)S(1)} collective-permute-done((bf16[1,40,3584]{2,1,0:T(8,128)(2,1)S(1)}, bf16[1,40,3584]{2,1,0:T(8,128)(2,1)S(1)}, u32[]{:S(2)}, u32[]{:S(2)}) %collective-permute-start.11) | collective-permute-done | bytes 286752 | tf_op jit(solution)/shard_map/ppermute | solution.py:12
  22.1 2.3 %collective-permute-done.4 = bf16[1,40,3584]{2,1,0:T(8,128)(2,1)S(1)} collective-permute-done((bf16[1,40,3584]{2,1,0:T(8,128)(2,1)S(1)}, bf16[1,40,3584]{2,1,0:T(8,128)(2,1)S(1)}, u32[]{:S(2)}, u32[]{:S(2)}) %collective-permute-start.4) | collective-permute-done | bytes 286752 | tf_op jit(solution)/shard_map/ppermute | solution.py:16
  24.4 1.1 %collective-permute-start.14 = (bf16[1,40,3584]{2,1,0:T(8,128)(2,1)S(1)}, bf16[1,40,3584]{2,1,0:T(8,128)(2,1)S(1)}, u32[]{:S(2)}, u32[]{:S(2)}) collective-permute-start(bf16[1,40,3584]{2,1,0:T(8,128)(2,1)S(1)} %collective-permute-done.11), channel_id=1, source_target_pairs={{0,6},{2,4},{4,2},{6,0},{1,7},{3,5},{5,3},{7,1},{8,14},{10,12},{12... | collective-permute-start | bytes 860168 | tf_op jit(solution)/shard_map/ppermute | solution.py:16
  25.5 5.0 %collective-permute-done.3 = bf16[1,40,3584]{2,1,0:T(8,128)(2,1)S(1)} collective-permute-done((bf16[1,40,3584]{2,1,0:T(8,128)(2,1)S(1)}, bf16[1,40,3584]{2,1,0:T(8,128)(2,1)S(1)}, u32[]{:S(2)}, u32[]{:S(2)}) %collective-permute-start.3) | collective-permute-done | bytes 286752 | tf_op jit(solution)/shard_map/ppermute | solution.py:16
  30.8 1.5 %collective-permute-start.12 = (bf16[1,40,3584]{2,1,0:T(8,128)(2,1)S(1)}, bf16[1,40,3584]{2,1,0:T(8,128)(2,1)S(1)}, u32[]{:S(2)}, u32[]{:S(2)}) collective-permute-start(bf16[1,40,3584]{2,1,0:T(8,128)(2,1)S(1)} %collective-permute-done.11), channel_id=1, source_target_pairs={{0,2},{2,0},{4,6},{6,4},{1,3},{3,1},{5,7},{7,5},{8,10},{10,8},{12,... | collective-permute-start | bytes 860168 | tf_op jit(solution)/shard_map/ppermute | solution.py:16
  32.4 4.3 %collective-permute-done.14 = bf16[1,40,3584]{2,1,0:T(8,128)(2,1)S(1)} collective-permute-done((bf16[1,40,3584]{2,1,0:T(8,128)(2,1)S(1)}, bf16[1,40,3584]{2,1,0:T(8,128)(2,1)S(1)}, u32[]{:S(2)}, u32[]{:S(2)}) %collective-permute-start.14) | collective-permute-done | bytes 286752 | tf_op jit(solution)/shard_map/ppermute | solution.py:16
  36.7 5.0 %collective-permute-done.13 = bf16[1,40,3584]{2,1,0:T(8,128)(2,1)S(1)} collective-permute-done((bf16[1,40,3584]{2,1,0:T(8,128)(2,1)S(1)}, bf16[1,40,3584]{2,1,0:T(8,128)(2,1)S(1)}, u32[]{:S(2)}, u32[]{:S(2)}) %collective-permute-start.13) | collective-permute-done | bytes 286752 | tf_op jit(solution)/shard_map/ppermute | solution.py:16
  41.9 1.0 %fusion.11 = f32[160,320]{1,0:T(8,128)S(1)} fusion(bf16[160,3584]{1,0:T(8,128)(2,1)S(1)} %bitcast.62, bf16[160,3584]{1,0:T(8,128)(2,1)S(1)} %collective-permute-done.5, bf16[160,3584]{1,0:T(8,128)(2,1)S(1)} %bitcast.74), kind=kOutput, calls=%fused_computation.20 | convolution fusion | flops 371589120 | bytes 3645440 | tf_op jit(solution)/shard_map/dot_general | solution.py:21
  42.9 1.0 %multiply_convert_fusion.1 = bf16[160,320]{1,0:T(8,128)(2,1)S(1)} fusion(f32[160,320]{1,0:T(8,128)S(1)} %fusion.11, bf16[160,3584]{1,0:T(8,128)(2,1)S(1)} %bitcast.63, bf16[160,3584]{1,0:T(8,128)(2,1)S(1)} %collective-permute-done.6, bf16[160,3584]{1,0:T(8,128)(2,1)S(1)} %bitcast.77), kind=kOutput, calls=%fused_computation.46 | convolution fusion | flops 371896320 | bytes 3747840 | tf_op jit(solution)/shard_map/dot_general | solution.py:22
  43.9 1.0 %fusion.10 = f32[160,320]{1,0:T(8,128)S(1)} fusion(bf16[160,3584]{1,0:T(8,128)(2,1)S(1)} %bitcast.64, bf16[160,3584]{1,0:T(8,128)(2,1)S(1)} %collective-permute-done.5, bf16[160,3584]{1,0:T(8,128)(2,1)S(1)} %bitcast.75), kind=kOutput, calls=%fused_computation.19 | convolution fusion | flops 371589120 | bytes 3645440 | tf_op jit(solution)/shard_map/dot_general | solution.py:21
  45.4 1.0 %multiply_convert_fusion = bf16[160,320]{1,0:T(8,128)(2,1)S(1)} fusion(f32[160,320]{1,0:T(8,128)S(1)} %fusion.10, bf16[160,3584]{1,0:T(8,128)(2,1)S(1)} %bitcast.65, bf16[160,3584]{1,0:T(8,128)(2,1)S(1)} %collective-permute-done.6, bf16[160,3584]{1,0:T(8,128)(2,1)S(1)} %bitcast.78), kind=kOutput, calls=%fused_computation.45 | convolution fusion | flops 371896320 | bytes 3747840 | tf_op jit(solution)/shard_map/dot_general | solution.py:22
  46.9 0.5 fusion.2
  47.5 1.5 %collective-permute-start.15 = (bf16[1,40,3584]{2,1,0:T(8,128)(2,1)S(1)}, bf16[1,40,3584]{2,1,0:T(8,128)(2,1)S(1)}, u32[]{:S(2)}, u32[]{:S(2)}) collective-permute-start(bf16[1,40,3584]{2,1,0:T(8,128)(2,1)S(1)} %get-tuple-element.8), channel_id=1, source_target_pairs={{0,2},{2,0},{4,6},{6,4},{1,3},{3,1},{5,7},{7,5},{8,10},{10,8},{12,... | collective-permute-start | bytes 860168 | tf_op jit(solution)/shard_map/ppermute | solution.py:16
  48.9 1.5 %collective-permute-start.17 = (bf16[1,40,3584]{2,1,0:T(8,128)(2,1)S(1)}, bf16[1,40,3584]{2,1,0:T(8,128)(2,1)S(1)}, u32[]{:S(2)}, u32[]{:S(2)}) collective-permute-start(bf16[1,40,3584]{2,1,0:T(8,128)(2,1)S(1)} %get-tuple-element.9), channel_id=1, source_target_pairs={{0,6},{2,4},{4,2},{6,0},{1,7},{3,5},{5,3},{7,1},{8,14},{10,12},{12... | collective-permute-start | bytes 860168 | tf_op jit(solution)/shard_map/ppermute | solution.py:16
  50.4 0.6 collective-permute-start.16
  51.0 0.5 fusion.6
  51.6 1.5 %collective-permute-start.8 = (bf16[1,40,3584]{2,1,0:T(8,128)(2,1)S(1)}, bf16[1,40,3584]{2,1,0:T(8,128)(2,1)S(1)}, u32[]{:S(2)}, u32[]{:S(2)}) collective-permute-start(bf16[1,40,3584]{2,1,0:T(8,128)(2,1)S(1)} %get-tuple-element.5), channel_id=1, source_target_pairs={{0,2},{2,0},{4,6},{6,4},{1,3},{3,1},{5,7},{7,5},{8,10},{10,8},{12,... | collective-permute-start | bytes 860168 | tf_op jit(solution)/shard_map/ppermute | solution.py:16
  53.1 1.5 %collective-permute-start.10 = (bf16[1,40,3584]{2,1,0:T(8,128)(2,1)S(1)}, bf16[1,40,3584]{2,1,0:T(8,128)(2,1)S(1)}, u32[]{:S(2)}, u32[]{:S(2)}) collective-permute-start(bf16[1,40,3584]{2,1,0:T(8,128)(2,1)S(1)} %get-tuple-element.6), channel_id=1, source_target_pairs={{0,6},{2,4},{4,2},{6,0},{1,7},{3,5},{5,3},{7,1},{8,14},{10,12},{12... | collective-permute-start | bytes 860168 | tf_op jit(solution)/shard_map/ppermute | solution.py:16
  54.6 8.9 %collective-permute-done.15 = bf16[1,40,3584]{2,1,0:T(8,128)(2,1)S(1)} collective-permute-done((bf16[1,40,3584]{2,1,0:T(8,128)(2,1)S(1)}, bf16[1,40,3584]{2,1,0:T(8,128)(2,1)S(1)}, u32[]{:S(2)}, u32[]{:S(2)}) %collective-permute-start.15) | collective-permute-done | bytes 286752 | tf_op jit(solution)/shard_map/ppermute | solution.py:16
  63.5 2.4 %collective-permute-start.9 = (bf16[1,40,3584]{2,1,0:T(8,128)(2,1)S(1)}, bf16[1,40,3584]{2,1,0:T(8,128)(2,1)S(1)}, u32[]{:S(2)}, u32[]{:S(2)}) collective-permute-start(bf16[1,40,3584]{2,1,0:T(8,128)(2,1)S(1)} %get-tuple-element.7), channel_id=1, source_target_pairs={{0,4},{2,6},{4,0},{6,2},{1,5},{3,7},{5,1},{7,3},{8,12},{10,14},{12... | collective-permute-start | bytes 860168 | tf_op jit(solution)/shard_map/ppermute | solution.py:16
  66.0 0.7 collective-permute-start.18
  66.8 4.7 %collective-permute-done.8 = bf16[1,40,3584]{2,1,0:T(8,128)(2,1)S(1)} collective-permute-done((bf16[1,40,3584]{2,1,0:T(8,128)(2,1)S(1)}, bf16[1,40,3584]{2,1,0:T(8,128)(2,1)S(1)}, u32[]{:S(2)}, u32[]{:S(2)}) %collective-permute-start.8) | collective-permute-done | bytes 286752 | tf_op jit(solution)/shard_map/ppermute | solution.py:16
  71.4 6.6 %collective-permute-done.10 = bf16[1,40,3584]{2,1,0:T(8,128)(2,1)S(1)} collective-permute-done((bf16[1,40,3584]{2,1,0:T(8,128)(2,1)S(1)}, bf16[1,40,3584]{2,1,0:T(8,128)(2,1)S(1)}, u32[]{:S(2)}, u32[]{:S(2)}) %collective-permute-start.10) | collective-permute-done | bytes 286752 | tf_op jit(solution)/shard_map/ppermute | solution.py:16
  78.1 4.0 %collective-permute-done.9 = bf16[1,40,3584]{2,1,0:T(8,128)(2,1)S(1)} collective-permute-done((bf16[1,40,3584]{2,1,0:T(8,128)(2,1)S(1)}, bf16[1,40,3584]{2,1,0:T(8,128)(2,1)S(1)}, u32[]{:S(2)}, u32[]{:S(2)}) %collective-permute-start.9) | collective-permute-done | bytes 286752 | tf_op jit(solution)/shard_map/ppermute | solution.py:16
  83.2 2.1 %collective-permute-done.19 = f32[2,40,3584]{2,1,0:T(8,128)S(1)} collective-permute-done((f32[2,40,3584]{2,1,0:T(8,128)S(1)}, f32[2,40,3584]{2,1,0:T(8,128)S(1)}, u32[]{:S(2)}, u32[]{:S(2)}) %collective-permute-start.19) | collective-permute-done | bytes 1146912 | tf_op jit(solution)/shard_map/ppermute | solution.py:12
  85.4 1.6 %convolution_convert_fusion.5 = bf16[64,3584]{1,0:T(8,128)(2,1)} fusion(f32[64,160]{1,0:T(8,128)S(1)} %select_reduce_fusion, f32[160,3584]{1,0:T(8,128)S(1)} %bitcast.60), kind=kOutput, calls=%fused_computation.13 | convolution fusion | flops 220430336 | bytes 2793472 | tf_op jit(solution)/shard_map/dot_general | solution.py:132
  (58 shorter events, 4.8 us)
Async XLA Ops:
  0.0 1.5 %collective-permute-start = (s32[64,8]{0,1:T(8,128)}, s32[64,8]{0,1:T(8,128)S(1)}, u32[]{:S(2)}, u32[]{:S(2)}) collective-permute-start(s32[64,8]{0,1:T(8,128)} %param.7), channel_id=1, source_target_pairs={{0,1},{1,0},{2,3},{3,2},{4,5},{5,4},{6,7},{7,6},{8,9},{9,8},{10,11... | collective-permute-start | bytes 6152 | tf_op jit(solution)/shard_map/ppermute | solution.py:12
  0.5 2.7 %collective-permute-start.1 = (bf16[64,3584]{1,0:T(8,128)(2,1)}, bf16[64,3584]{1,0:T(8,128)(2,1)S(1)}, u32[]{:S(2)}, u32[]{:S(2)}) collective-permute-start(bf16[64,3584]{1,0:T(8,128)(2,1)} %param.6), channel_id=1, source_target_pairs={{0,1},{1,0},{2,3},{3,2},{4,5},{5,4},{6,7},{7,6},{8,9},{9,8},{10,11... | collective-permute-start | bytes 1376264 | tf_op jit(solution)/shard_map/ppermute | solution.py:12
  3.1 9.1 %copy-start.3 = (bf16[1,160,3584]{2,1,0:T(8,128)(2,1)S(1)}, bf16[1,160,3584]{2,1,0:T(8,128)(2,1)}, u32[]{:S(2)}) copy-start(bf16[1,160,3584]{2,1,0:T(8,128)(2,1)} %param.9) | copy-start | bytes 3440644
  3.1 19.0 %copy-start.4 = (bf16[1,160,3584]{2,1,0:T(8,128)(2,1)S(1)}, bf16[1,160,3584]{2,1,0:T(8,128)(2,1)}, u32[]{:S(2)}) copy-start(bf16[1,160,3584]{2,1,0:T(8,128)(2,1)} %param.10) | copy-start | bytes 3440644
  4.7 17.4 %collective-permute-start.11 = (bf16[1,40,3584]{2,1,0:T(8,128)(2,1)S(1)}, bf16[1,40,3584]{2,1,0:T(8,128)(2,1)S(1)}, u32[]{:S(2)}, u32[]{:S(2)}) collective-permute-start(bf16[1,40,3584]{2,1,0:T(8,128)(2,1)S(1)} %get-tuple-element.13), channel_id=1, source_target_pairs={{0,8},{8,0},{1,9},{9,1},{2,10},{10,2},{3,11},{11,3},{4,12},{12,4},... | collective-permute-start | bytes 860168 | tf_op jit(solution)/shard_map/ppermute | solution.py:12
  8.7 15.7 %collective-permute-start.4 = (bf16[1,40,3584]{2,1,0:T(8,128)(2,1)S(1)}, bf16[1,40,3584]{2,1,0:T(8,128)(2,1)S(1)}, u32[]{:S(2)}, u32[]{:S(2)}) collective-permute-start(bf16[1,40,3584]{2,1,0:T(8,128)(2,1)S(1)} %get-tuple-element.12), channel_id=1, source_target_pairs={{0,6},{2,4},{4,2},{6,0},{1,7},{3,5},{5,3},{7,1},{8,14},{10,12},{12... | collective-permute-start | bytes 860168 | tf_op jit(solution)/shard_map/ppermute | solution.py:16
  11.2 19.3 %collective-permute-start.3 = (bf16[1,40,3584]{2,1,0:T(8,128)(2,1)S(1)}, bf16[1,40,3584]{2,1,0:T(8,128)(2,1)S(1)}, u32[]{:S(2)}, u32[]{:S(2)}) collective-permute-start(bf16[1,40,3584]{2,1,0:T(8,128)(2,1)S(1)} %get-tuple-element.12), channel_id=1, source_target_pairs={{0,4},{2,6},{4,0},{6,2},{1,5},{3,7},{5,1},{7,3},{8,12},{10,14},{12... | collective-permute-start | bytes 860168 | tf_op jit(solution)/shard_map/ppermute | solution.py:16
  11.6 19.1 %collective-permute-start.2 = (bf16[1,40,3584]{2,1,0:T(8,128)(2,1)S(1)}, bf16[1,40,3584]{2,1,0:T(8,128)(2,1)S(1)}, u32[]{:S(2)}, u32[]{:S(2)}) collective-permute-start(bf16[1,40,3584]{2,1,0:T(8,128)(2,1)S(1)} %get-tuple-element.12), channel_id=1, source_target_pairs={{0,2},{2,0},{4,6},{6,4},{1,3},{3,1},{5,7},{7,5},{8,10},{10,8},{12,... | collective-permute-start | bytes 860168 | tf_op jit(solution)/shard_map/ppermute | solution.py:16
  12.2 29.7 %collective-permute-start.5 = (bf16[160,3584]{1,0:T(8,128)(2,1)S(1)}, bf16[160,3584]{1,0:T(8,128)(2,1)S(1)}, u32[]{:S(2)}, u32[]{:S(2)}) collective-permute-start(bf16[160,3584]{1,0:T(8,128)(2,1)S(1)} %bitcast.73), channel_id=1, source_target_pairs={{0,1},{1,0},{2,3},{3,2},{4,5},{5,4},{6,7},{7,6},{8,9},{9,8},{10,11... | collective-permute-start | bytes 3440648 | tf_op jit(solution)/shard_map/ppermute | solution.py:12
  22.1 20.8 %collective-permute-start.6 = (bf16[160,3584]{1,0:T(8,128)(2,1)S(1)}, bf16[160,3584]{1,0:T(8,128)(2,1)S(1)}, u32[]{:S(2)}, u32[]{:S(2)}) collective-permute-start(bf16[160,3584]{1,0:T(8,128)(2,1)S(1)} %bitcast.76), channel_id=1, source_target_pairs={{0,1},{1,0},{2,3},{3,2},{4,5},{5,4},{6,7},{7,6},{8,9},{9,8},{10,11... | collective-permute-start | bytes 3440648 | tf_op jit(solution)/shard_map/ppermute | solution.py:12
  24.4 12.3 %collective-permute-start.14 = (bf16[1,40,3584]{2,1,0:T(8,128)(2,1)S(1)}, bf16[1,40,3584]{2,1,0:T(8,128)(2,1)S(1)}, u32[]{:S(2)}, u32[]{:S(2)}) collective-permute-start(bf16[1,40,3584]{2,1,0:T(8,128)(2,1)S(1)} %collective-permute-done.11), channel_id=1, source_target_pairs={{0,6},{2,4},{4,2},{6,0},{1,7},{3,5},{5,3},{7,1},{8,14},{10,12},{12... | collective-permute-start | bytes 860168 | tf_op jit(solution)/shard_map/ppermute | solution.py:16
  30.5 11.2 %collective-permute-start.13 = (bf16[1,40,3584]{2,1,0:T(8,128)(2,1)S(1)}, bf16[1,40,3584]{2,1,0:T(8,128)(2,1)S(1)}, u32[]{:S(2)}, u32[]{:S(2)}) collective-permute-start(bf16[1,40,3584]{2,1,0:T(8,128)(2,1)S(1)} %collective-permute-done.11), channel_id=1, source_target_pairs={{0,4},{2,6},{4,0},{6,2},{1,5},{3,7},{5,1},{7,3},{8,12},{10,14},{12... | collective-permute-start | bytes 860168 | tf_op jit(solution)/shard_map/ppermute | solution.py:16
  30.8 11.0 %collective-permute-start.12 = (bf16[1,40,3584]{2,1,0:T(8,128)(2,1)S(1)}, bf16[1,40,3584]{2,1,0:T(8,128)(2,1)S(1)}, u32[]{:S(2)}, u32[]{:S(2)}) collective-permute-start(bf16[1,40,3584]{2,1,0:T(8,128)(2,1)S(1)} %collective-permute-done.11), channel_id=1, source_target_pairs={{0,2},{2,0},{4,6},{6,4},{1,3},{3,1},{5,7},{7,5},{8,10},{10,8},{12,... | collective-permute-start | bytes 860168 | tf_op jit(solution)/shard_map/ppermute | solution.py:16
  32.2 4.5 %copy-start = (bf16[1,160,3584]{2,1,0:T(8,128)(2,1)S(1)}, bf16[1,160,3584]{2,1,0:T(8,128)(2,1)}, u32[]{:S(2)}) copy-start(bf16[1,160,3584]{2,1,0:T(8,128)(2,1)} %param.11) | copy-start | bytes 3440644
  36.7 10.1 %collective-permute-start.7 = (bf16[160,3584]{1,0:T(8,128)(2,1)S(1)}, bf16[160,3584]{1,0:T(8,128)(2,1)S(1)}, u32[]{:S(2)}, u32[]{:S(2)}) collective-permute-start(bf16[160,3584]{1,0:T(8,128)(2,1)S(1)} %bitcast.61), channel_id=1, source_target_pairs={{0,1},{1,0},{2,3},{3,2},{4,5},{5,4},{6,7},{7,6},{8,9},{9,8},{10,11... | collective-permute-start | bytes 3440648 | tf_op jit(solution)/shard_map/ppermute | solution.py:12
  47.5 16.0 %collective-permute-start.15 = (bf16[1,40,3584]{2,1,0:T(8,128)(2,1)S(1)}, bf16[1,40,3584]{2,1,0:T(8,128)(2,1)S(1)}, u32[]{:S(2)}, u32[]{:S(2)}) collective-permute-start(bf16[1,40,3584]{2,1,0:T(8,128)(2,1)S(1)} %get-tuple-element.8), channel_id=1, source_target_pairs={{0,2},{2,0},{4,6},{6,4},{1,3},{3,1},{5,7},{7,5},{8,10},{10,8},{12,... | collective-permute-start | bytes 860168 | tf_op jit(solution)/shard_map/ppermute | solution.py:16
  48.9 16.9 %collective-permute-start.17 = (bf16[1,40,3584]{2,1,0:T(8,128)(2,1)S(1)}, bf16[1,40,3584]{2,1,0:T(8,128)(2,1)S(1)}, u32[]{:S(2)}, u32[]{:S(2)}) collective-permute-start(bf16[1,40,3584]{2,1,0:T(8,128)(2,1)S(1)} %get-tuple-element.9), channel_id=1, source_target_pairs={{0,6},{2,4},{4,2},{6,0},{1,7},{3,5},{5,3},{7,1},{8,14},{10,12},{12... | collective-permute-start | bytes 860168 | tf_op jit(solution)/shard_map/ppermute | solution.py:16
  50.4 15.4 %collective-permute-start.16 = (bf16[1,40,3584]{2,1,0:T(8,128)(2,1)S(1)}, bf16[1,40,3584]{2,1,0:T(8,128)(2,1)S(1)}, u32[]{:S(2)}, u32[]{:S(2)}) collective-permute-start(bf16[1,40,3584]{2,1,0:T(8,128)(2,1)S(1)} %get-tuple-element.10), channel_id=1, source_target_pairs={{0,4},{2,6},{4,0},{6,2},{1,5},{3,7},{5,1},{7,3},{8,12},{10,14},{12... | collective-permute-start | bytes 860168 | tf_op jit(solution)/shard_map/ppermute | solution.py:16
  51.6 19.8 %collective-permute-start.8 = (bf16[1,40,3584]{2,1,0:T(8,128)(2,1)S(1)}, bf16[1,40,3584]{2,1,0:T(8,128)(2,1)S(1)}, u32[]{:S(2)}, u32[]{:S(2)}) collective-permute-start(bf16[1,40,3584]{2,1,0:T(8,128)(2,1)S(1)} %get-tuple-element.5), channel_id=1, source_target_pairs={{0,2},{2,0},{4,6},{6,4},{1,3},{3,1},{5,7},{7,5},{8,10},{10,8},{12,... | collective-permute-start | bytes 860168 | tf_op jit(solution)/shard_map/ppermute | solution.py:16
  53.1 25.0 %collective-permute-start.10 = (bf16[1,40,3584]{2,1,0:T(8,128)(2,1)S(1)}, bf16[1,40,3584]{2,1,0:T(8,128)(2,1)S(1)}, u32[]{:S(2)}, u32[]{:S(2)}) collective-permute-start(bf16[1,40,3584]{2,1,0:T(8,128)(2,1)S(1)} %get-tuple-element.6), channel_id=1, source_target_pairs={{0,6},{2,4},{4,2},{6,0},{1,7},{3,5},{5,3},{7,1},{8,14},{10,12},{12... | collective-permute-start | bytes 860168 | tf_op jit(solution)/shard_map/ppermute | solution.py:16
  63.5 18.6 %collective-permute-start.9 = (bf16[1,40,3584]{2,1,0:T(8,128)(2,1)S(1)}, bf16[1,40,3584]{2,1,0:T(8,128)(2,1)S(1)}, u32[]{:S(2)}, u32[]{:S(2)}) collective-permute-start(bf16[1,40,3584]{2,1,0:T(8,128)(2,1)S(1)} %get-tuple-element.7), channel_id=1, source_target_pairs={{0,4},{2,6},{4,0},{6,2},{1,5},{3,7},{5,1},{7,3},{8,12},{10,14},{12... | collective-permute-start | bytes 860168 | tf_op jit(solution)/shard_map/ppermute | solution.py:16
  66.0 16.2 %collective-permute-start.18 = (bf16[1,40,3584]{2,1,0:T(8,128)(2,1)S(1)}, bf16[1,40,3584]{2,1,0:T(8,128)(2,1)S(1)}, u32[]{:S(2)}, u32[]{:S(2)}) collective-permute-start(bf16[1,40,3584]{2,1,0:T(8,128)(2,1)S(1)} %fusion.17), channel_id=1, source_target_pairs={{0,8},{8,0},{1,9},{9,1},{2,10},{10,2},{3,11},{11,3},{4,12},{12,4},... | collective-permute-start | bytes 860168 | tf_op jit(solution)/shard_map/ppermute | solution.py:12
  82.3 0.7 copy-start.1
  82.3 0.7 copy-start.2
  82.4 2.9 %collective-permute-start.19 = (f32[2,40,3584]{2,1,0:T(8,128)S(1)}, f32[2,40,3584]{2,1,0:T(8,128)S(1)}, u32[]{:S(2)}, u32[]{:S(2)}) collective-permute-start(f32[2,40,3584]{2,1,0:T(8,128)S(1)} %pad_maximum_fusion.9), channel_id=1, source_target_pairs={{0,1},{1,0},{2,3},{3,2},{4,5},{5,4},{6,7},{7,6},{8,9},{9,8},{10,11... | collective-permute-start | bytes 3440648 | tf_op jit(solution)/shard_map/ppermute | solution.py:12

commit v15 on v12

--- a/solution.py
+++ b/solution.py
@@ -75,7 +75,7 @@
         order_has, order_slot = local_has, local_slot
     wanted = ctx * half + jnp.arange(half, dtype=jnp.int32)
     picker = (order_has[:, None, :] > 0) & (order_slot[:, None, :] == wanted[None, :, None])
-    picker = lax.optimization_barrier(picker.astype(jnp.bfloat16).reshape(experts * half, n_ctx * tok))
+    picker = picker.astype(jnp.bfloat16).reshape(experts * half, n_ctx * tok)
     pair_tokens = with_sibling(tokens)
     packed = jnp.dot(picker, pair_tokens, preferred_element_type=jnp.float32).astype(jnp.bfloat16)
     packed = packed.reshape(experts, half, width)
@@ -106,15 +106,19 @@
         local_part = group_partial(packed[0:1])
         far_part = group_partial(shift(packed[1:2], "ex", 2, 1))
         far_out = group_sum(far_part)
-        local_part, far_out = lax.optimization_barrier((local_part, far_out))
-        back = shift(far_out.astype(RETURN_DTYPE), "ex", 2, 1).astype(jnp.float32)
-        mine = jnp.concatenate([group_sum(local_part), back], axis=0)
+        back = shift(far_out.astype(RETURN_DTYPE), "ex", 2, 1)
+        local_out = group_sum(local_part)
+        mine = jnp.concatenate([local_out, back.astype(jnp.float32)], axis=0)
+        theirs = jnp.concatenate(
+            [shift(local_out, "context", n_ctx, 1), shift(back, "context", n_ctx, 1).astype(jnp.float32)],
+            axis=0,
+        )
     else:
         sent = lax.all_to_all(packed, "ex", split_axis=0, concat_axis=0, tiled=True)
         expert_out = group_sum(group_partial(sent)).astype(RETURN_DTYPE)
         mine = lax.all_to_all(expert_out, "ex", split_axis=0, concat_axis=0, tiled=True)
         mine = mine.astype(jnp.float32)
-    theirs = shift(mine, "context", n_ctx, 1)
+        theirs = shift(mine, "context", n_ctx, 1)
 
     n_slots = n_ctx * experts * half
     own_has = local_has[:, :tok] > 0

time: 90.3 us -> 91.1 us (level)
  waiting for transfers between devices: 57.9 us -> 51.1 us
  starting transfers between devices: 19.4 us -> 25.5 us
    ppermute x12, starting transfers between devices: 13.4 us -> 20.6 us  [swap(): return lax.ppermute(x, axis, [(i, i ^ k) for i in range(size)])]
    ppermute x8 -> x9, waiting for transfers between devices: 22.7 us -> 17 us  [shift(): return lax.ppermute(x, axis, [(i, (i + k) % size) for i in range(size)])]
    ppermute x12, waiting for transfers between devices: 35.2 us -> 34.1 us  [swap(): return lax.ppermute(x, axis, [(i, i ^ k) for i in range(size)])]
    ppermute x8 -> x9, starting transfers between devices: 5.93 us -> 4.94 us  [shift(): return lax.ppermute(x, axis, [(i, (i + k) % size) for i in range(size)])]
  transfers between devices with their start and end apart: 20 -> 21, of which waited for: 12 -> 8; matrix products, arithmetic and copies ran while one was open for 9% -> 11% of each run, Pallas kernels for 0% -> 0%
where the time goes in v15:
time: 91.1 us; the launch traced here: 90.8 us
  waiting for transfers between devices  51.1 us (56%)
  starting transfers between devices  25.5 us (28%)
  matrix products  9.21 us (10%)
  other arithmetic  3.16 us (3%)
  local copies, waits for them, and re-layouts  1.57 us (2%)
    ppermute x12, waiting for transfers between devices, swap(): return lax.ppermute(x, axis, [(i, i ^ k) for i in range(size)])  34.1 us
    ppermute x12, starting transfers between devices, swap(): return lax.ppermute(x, axis, [(i, i ^ k) for i in range(size)])  20.6 us
    ppermute x9, waiting for transfers between devices, shift(): return lax.ppermute(x, axis, [(i, (i + k) % size) for i in range(size)])  17 us
    ppermute x9, starting transfers between devices, shift(): return lax.ppermute(x, axis, [(i, (i + k) % size) for i in range(size)])  4.94 us
    dot_general x2, matrix products, quarter_rows(): up = lax.dot_general(rows, w_up, dims, preferred_element_type=jnp.float32)  2.01 us
    dot_general x2, matrix products, quarter_rows(): lax.dot_general(rows, w_gate, dims, preferred_element_type=jnp.float32)  2.01 us
    dot_general x4, matrix products, quarter_rows(): jnp.dot(hidden[:, c * slab:(c + 1) * slab], w_down[c * slab:(c + 1) * sla...  1.92 us
  transfers between devices with their start and end apart: 21, of which 8 were waited for; matrix products, arithmetic and copies ran while one was open for 11% of the time, Pallas kernels for 0%

profile of v15, /device:TPU:0, one launch (start us, length us, event | category | flops | bytes accessed | tf_op | source)
XLA Modules:
  0.0 90.8 jit_solution(192011403876465233)
XLA Ops:
  0.0 0.5 collective-permute-start
  0.5 0.5 collective-permute-start.5
  1.0 0.7 select_reduce_fusion.1
  1.8 0.8 add_select_fusion
  3.4 1.4 %convolution_convert_fusion.4 = bf16[80,3584]{1,0:T(8,128)(2,1)S(1)} fusion(pred[80,128]{1,0:T(8,128)(4,1)S(1)} %fusion.25, bf16[64,3584]{1,0:T(8,128)(2,1)S(1)} %collective-permute-done.1, bf16[64,3584]{1,0:T(8,128)(2,1)} %param.6), kind=kOutput, calls=%fused_computation.13 | convolution fusion | flops 75522048 | bytes 1501184 | tf_op jit(solution)/shard_map/dot_general | solution.py:80
  4.9 3.6 %collective-permute-start.4 = (bf16[1,40,3584]{2,1,0:T(8,128)(2,1)S(1)}, bf16[1,40,3584]{2,1,0:T(8,128)(2,1)S(1)}, u32[]{:S(2)}, u32[]{:S(2)}) collective-permute-start(bf16[1,40,3584]{2,1,0:T(8,128)(2,1)S(1)} %get-tuple-element.12), channel_id=1, source_target_pairs={{0,6},{2,4},{4,2},{6,0},{1,7},{3,5},{5,3},{7,1},{8,14},{10,12},{12... | collective-permute-start | bytes 860168 | tf_op jit(solution)/shard_map/ppermute | solution.py:16
  9.2 2.9 %collective-permute-start.11 = (bf16[1,40,3584]{2,1,0:T(8,128)(2,1)S(1)}, bf16[1,40,3584]{2,1,0:T(8,128)(2,1)S(1)}, u32[]{:S(2)}, u32[]{:S(2)}) collective-permute-start(bf16[1,40,3584]{2,1,0:T(8,128)(2,1)S(1)} %get-tuple-element.13), channel_id=1, source_target_pairs={{0,8},{8,0},{1,9},{9,1},{2,10},{10,2},{3,11},{11,3},{4,12},{12,4},... | collective-permute-start | bytes 860168 | tf_op jit(solution)/shard_map/ppermute | solution.py:12
  12.2 15.4 %collective-permute-done.11 = bf16[1,40,3584]{2,1,0:T(8,128)(2,1)S(1)} collective-permute-done((bf16[1,40,3584]{2,1,0:T(8,128)(2,1)S(1)}, bf16[1,40,3584]{2,1,0:T(8,128)(2,1)S(1)}, u32[]{:S(2)}, u32[]{:S(2)}) %collective-permute-start.11) | collective-permute-done | bytes 286752 | tf_op jit(solution)/shard_map/ppermute | solution.py:12
  27.6 3.5 %collective-permute-start.14 = (bf16[1,40,3584]{2,1,0:T(8,128)(2,1)S(1)}, bf16[1,40,3584]{2,1,0:T(8,128)(2,1)S(1)}, u32[]{:S(2)}, u32[]{:S(2)}) collective-permute-start(bf16[1,40,3584]{2,1,0:T(8,128)(2,1)S(1)} %collective-permute-done.11), channel_id=1, source_target_pairs={{0,6},{2,4},{4,2},{6,0},{1,7},{3,5},{5,3},{7,1},{8,14},{10,12},{12... | collective-permute-start | bytes 860168 | tf_op jit(solution)/shard_map/ppermute | solution.py:16
  31.3 1.4 %collective-permute-start.12 = (bf16[1,40,3584]{2,1,0:T(8,128)(2,1)S(1)}, bf16[1,40,3584]{2,1,0:T(8,128)(2,1)S(1)}, u32[]{:S(2)}, u32[]{:S(2)}) collective-permute-start(bf16[1,40,3584]{2,1,0:T(8,128)(2,1)S(1)} %collective-permute-done.11), channel_id=1, source_target_pairs={{0,2},{2,0},{4,6},{6,4},{1,3},{3,1},{5,7},{7,5},{8,10},{10,8},{12,... | collective-permute-start | bytes 860168 | tf_op jit(solution)/shard_map/ppermute | solution.py:16
  32.9 6.0 %collective-permute-done.14 = bf16[1,40,3584]{2,1,0:T(8,128)(2,1)S(1)} collective-permute-done((bf16[1,40,3584]{2,1,0:T(8,128)(2,1)S(1)}, bf16[1,40,3584]{2,1,0:T(8,128)(2,1)S(1)}, u32[]{:S(2)}, u32[]{:S(2)}) %collective-permute-start.14) | collective-permute-done | bytes 286752 | tf_op jit(solution)/shard_map/ppermute | solution.py:16
  38.9 5.9 %collective-permute-done.13 = bf16[1,40,3584]{2,1,0:T(8,128)(2,1)S(1)} collective-permute-done((bf16[1,40,3584]{2,1,0:T(8,128)(2,1)S(1)}, bf16[1,40,3584]{2,1,0:T(8,128)(2,1)S(1)}, u32[]{:S(2)}, u32[]{:S(2)}) %collective-permute-start.13) | collective-permute-done | bytes 286752 | tf_op jit(solution)/shard_map/ppermute | solution.py:16
  45.0 1.1 %copy-done.1 = bf16[1,160,3584]{2,1,0:T(8,128)(2,1)S(1)} copy-done((bf16[1,160,3584]{2,1,0:T(8,128)(2,1)S(1)}, bf16[1,160,3584]{2,1,0:T(8,128)(2,1)}, u32[]{:S(2)}) %copy-start.1) | copy-done | bytes 1146904
  46.1 1.0 %fusion.12 = f32[160,320]{1,0:T(8,128)S(1)} fusion(bf16[160,3584]{1,0:T(8,128)(2,1)S(1)} %bitcast.64, bf16[160,3584]{1,0:T(8,128)(2,1)S(1)} %collective-permute-done.5, bf16[160,3584]{1,0:T(8,128)(2,1)S(1)} %bitcast.76), kind=kOutput, calls=%fused_computation.20 | convolution fusion | flops 371589120 | bytes 3645440 | tf_op jit(solution)/shard_map/dot_general | solution.py:21
  47.1 1.0 %multiply_convert_fusion.1 = bf16[160,320]{1,0:T(8,128)(2,1)S(1)} fusion(f32[160,320]{1,0:T(8,128)S(1)} %fusion.12, bf16[160,3584]{1,0:T(8,128)(2,1)S(1)} %bitcast.65, bf16[160,3584]{1,0:T(8,128)(2,1)S(1)} %collective-permute-done.6, bf16[160,3584]{1,0:T(8,128)(2,1)S(1)} %bitcast.79), kind=kOutput, calls=%fused_computation.47 | convolution fusion | flops 371896320 | bytes 3747840 | tf_op jit(solution)/shard_map/dot_general | solution.py:22
  48.1 1.0 %fusion.11 = f32[160,320]{1,0:T(8,128)S(1)} fusion(bf16[160,3584]{1,0:T(8,128)(2,1)S(1)} %bitcast.66, bf16[160,3584]{1,0:T(8,128)(2,1)S(1)} %collective-permute-done.5, bf16[160,3584]{1,0:T(8,128)(2,1)S(1)} %bitcast.77), kind=kOutput, calls=%fused_computation.19 | convolution fusion | flops 371589120 | bytes 3645440 | tf_op jit(solution)/shard_map/dot_general | solution.py:21
  49.6 1.0 %multiply_convert_fusion = bf16[160,320]{1,0:T(8,128)(2,1)S(1)} fusion(f32[160,320]{1,0:T(8,128)S(1)} %fusion.11, bf16[160,3584]{1,0:T(8,128)(2,1)S(1)} %bitcast.67, bf16[160,3584]{1,0:T(8,128)(2,1)S(1)} %collective-permute-done.6, bf16[160,3584]{1,0:T(8,128)(2,1)S(1)} %bitcast.80), kind=kOutput, calls=%fused_computation.46 | convolution fusion | flops 371896320 | bytes 3747840 | tf_op jit(solution)/shard_map/dot_general | solution.py:22
  51.0 0.5 fusion.2
  51.6 1.5 %collective-permute-start.15 = (bf16[1,40,3584]{2,1,0:T(8,128)(2,1)S(1)}, bf16[1,40,3584]{2,1,0:T(8,128)(2,1)S(1)}, u32[]{:S(2)}, u32[]{:S(2)}) collective-permute-start(bf16[1,40,3584]{2,1,0:T(8,128)(2,1)S(1)} %get-tuple-element.8), channel_id=1, source_target_pairs={{0,2},{2,0},{4,6},{6,4},{1,3},{3,1},{5,7},{7,5},{8,10},{10,8},{12,... | collective-permute-start | bytes 860168 | tf_op jit(solution)/shard_map/ppermute | solution.py:16
  53.1 2.6 %collective-permute-start.17 = (bf16[1,40,3584]{2,1,0:T(8,128)(2,1)S(1)}, bf16[1,40,3584]{2,1,0:T(8,128)(2,1)S(1)}, u32[]{:S(2)}, u32[]{:S(2)}) collective-permute-start(bf16[1,40,3584]{2,1,0:T(8,128)(2,1)S(1)} %get-tuple-element.9), channel_id=1, source_target_pairs={{0,6},{2,4},{4,2},{6,0},{1,7},{3,5},{5,3},{7,1},{8,14},{10,12},{12... | collective-permute-start | bytes 860168 | tf_op jit(solution)/shard_map/ppermute | solution.py:16
  55.7 0.5 fusion.6
  56.3 0.9 collective-permute-start.8
  57.2 2.6 %collective-permute-start.10 = (bf16[1,40,3584]{2,1,0:T(8,128)(2,1)S(1)}, bf16[1,40,3584]{2,1,0:T(8,128)(2,1)S(1)}, u32[]{:S(2)}, u32[]{:S(2)}) collective-permute-start(bf16[1,40,3584]{2,1,0:T(8,128)(2,1)S(1)} %get-tuple-element.6), channel_id=1, source_target_pairs={{0,6},{2,4},{4,2},{6,0},{1,7},{3,5},{5,3},{7,1},{8,14},{10,12},{12... | collective-permute-start | bytes 860168 | tf_op jit(solution)/shard_map/ppermute | solution.py:16
  59.9 7.7 %collective-permute-done.15 = bf16[1,40,3584]{2,1,0:T(8,128)(2,1)S(1)} collective-permute-done((bf16[1,40,3584]{2,1,0:T(8,128)(2,1)S(1)}, bf16[1,40,3584]{2,1,0:T(8,128)(2,1)S(1)}, u32[]{:S(2)}, u32[]{:S(2)}) %collective-permute-start.15) | collective-permute-done | bytes 286752 | tf_op jit(solution)/shard_map/ppermute | solution.py:16
  67.6 3.6 %collective-permute-start.9 = (bf16[1,40,3584]{2,1,0:T(8,128)(2,1)S(1)}, bf16[1,40,3584]{2,1,0:T(8,128)(2,1)S(1)}, u32[]{:S(2)}, u32[]{:S(2)}) collective-permute-start(bf16[1,40,3584]{2,1,0:T(8,128)(2,1)S(1)} %get-tuple-element.7), channel_id=1, source_target_pairs={{0,4},{2,6},{4,0},{6,2},{1,5},{3,7},{5,1},{7,3},{8,12},{10,14},{12... | collective-permute-start | bytes 860168 | tf_op jit(solution)/shard_map/ppermute | solution.py:16
  71.7 4.9 %collective-permute-done.8 = bf16[1,40,3584]{2,1,0:T(8,128)(2,1)S(1)} collective-permute-done((bf16[1,40,3584]{2,1,0:T(8,128)(2,1)S(1)}, bf16[1,40,3584]{2,1,0:T(8,128)(2,1)S(1)}, u32[]{:S(2)}, u32[]{:S(2)}) %collective-permute-start.8) | collective-permute-done | bytes 286752 | tf_op jit(solution)/shard_map/ppermute | solution.py:16
  76.6 5.6 %collective-permute-done.10 = bf16[1,40,3584]{2,1,0:T(8,128)(2,1)S(1)} collective-permute-done((bf16[1,40,3584]{2,1,0:T(8,128)(2,1)S(1)}, bf16[1,40,3584]{2,1,0:T(8,128)(2,1)S(1)}, u32[]{:S(2)}, u32[]{:S(2)}) %collective-permute-start.10) | collective-permute-done | bytes 286752 | tf_op jit(solution)/shard_map/ppermute | solution.py:16
  82.2 4.0 %collective-permute-done.9 = bf16[1,40,3584]{2,1,0:T(8,128)(2,1)S(1)} collective-permute-done((bf16[1,40,3584]{2,1,0:T(8,128)(2,1)S(1)}, bf16[1,40,3584]{2,1,0:T(8,128)(2,1)S(1)}, u32[]{:S(2)}, u32[]{:S(2)}) %collective-permute-start.9) | collective-permute-done | bytes 286752 | tf_op jit(solution)/shard_map/ppermute | solution.py:16
  86.6 0.6 collective-permute-start.20
  87.3 1.6 %collective-permute-done.20 = bf16[1,40,3584]{2,1,0:T(8,128)(2,1)S(1)} collective-permute-done((bf16[1,40,3584]{2,1,0:T(8,128)(2,1)S(1)}, bf16[1,40,3584]{2,1,0:T(8,128)(2,1)S(1)}, u32[]{:S(2)}, u32[]{:S(2)}) %collective-permute-start.20) | collective-permute-done | bytes 286752 | tf_op jit(solution)/shard_map/ppermute | solution.py:12
  89.0 0.6 fusion.26
  89.6 1.3 %fusion.8 = bf16[64,3584]{1,0:T(8,128)(2,1)} fusion(f32[64,3584]{1,0:T(8,128)S(1)} %fusion.26, f32[80,3584]{1,0:T(8,128)S(1)} %bitcast.62, f32[64,160]{1,0:T(8,128)S(1)} %select_reduce_fusion), kind=kOutput, calls=%fused_computation.14 | convolution fusion | flops 110559232 | bytes 2555904 | tf_op jit(solution)/shard_map/dot_general | solution.py:138
  (58 shorter events, 4.3 us)
Async XLA Ops:
  0.0 1.8 %collective-permute-start = (s32[64,8]{0,1:T(8,128)}, s32[64,8]{0,1:T(8,128)S(1)}, u32[]{:S(2)}, u32[]{:S(2)}) collective-permute-start(s32[64,8]{0,1:T(8,128)} %param.7), channel_id=1, source_target_pairs={{0,1},{1,0},{2,3},{3,2},{4,5},{5,4},{6,7},{7,6},{8,9},{9,8},{10,11... | collective-permute-start | bytes 6152 | tf_op jit(solution)/shard_map/ppermute | solution.py:12
  0.5 3.0 %collective-permute-start.1 = (bf16[64,3584]{1,0:T(8,128)(2,1)}, bf16[64,3584]{1,0:T(8,128)(2,1)S(1)}, u32[]{:S(2)}, u32[]{:S(2)}) collective-permute-start(bf16[64,3584]{1,0:T(8,128)(2,1)} %param.6), channel_id=1, source_target_pairs={{0,1},{1,0},{2,3},{3,2},{4,5},{5,4},{6,7},{7,6},{8,9},{9,8},{10,11... | collective-permute-start | bytes 1376264 | tf_op jit(solution)/shard_map/ppermute | solution.py:12
  0.5 44.4 %collective-permute-start.5 = (bf16[160,3584]{1,0:T(8,128)(2,1)}, bf16[160,3584]{1,0:T(8,128)(2,1)S(1)}, u32[]{:S(2)}, u32[]{:S(2)}) collective-permute-start(bf16[160,3584]{1,0:T(8,128)(2,1)} %bitcast.75), channel_id=1, source_target_pairs={{0,1},{1,0},{2,3},{3,2},{4,5},{5,4},{6,7},{7,6},{8,9},{9,8},{10,11... | collective-permute-start | bytes 3440648 | tf_op jit(solution)/shard_map/ppermute | solution.py:12
  3.4 24.2 %copy-start.2 = (bf16[1,160,3584]{2,1,0:T(8,128)(2,1)S(1)}, bf16[1,160,3584]{2,1,0:T(8,128)(2,1)}, u32[]{:S(2)}) copy-start(bf16[1,160,3584]{2,1,0:T(8,128)(2,1)} %param.10) | copy-start | bytes 3440644
  4.9 22.7 %collective-permute-start.4 = (bf16[1,40,3584]{2,1,0:T(8,128)(2,1)S(1)}, bf16[1,40,3584]{2,1,0:T(8,128)(2,1)S(1)}, u32[]{:S(2)}, u32[]{:S(2)}) collective-permute-start(bf16[1,40,3584]{2,1,0:T(8,128)(2,1)S(1)} %get-tuple-element.12), channel_id=1, source_target_pairs={{0,6},{2,4},{4,2},{6,0},{1,7},{3,5},{5,3},{7,1},{8,14},{10,12},{12... | collective-permute-start | bytes 860168 | tf_op jit(solution)/shard_map/ppermute | solution.py:16
  8.5 22.6 %collective-permute-start.3 = (bf16[1,40,3584]{2,1,0:T(8,128)(2,1)S(1)}, bf16[1,40,3584]{2,1,0:T(8,128)(2,1)S(1)}, u32[]{:S(2)}, u32[]{:S(2)}) collective-permute-start(bf16[1,40,3584]{2,1,0:T(8,128)(2,1)S(1)} %get-tuple-element.12), channel_id=1, source_target_pairs={{0,4},{2,6},{4,0},{6,2},{1,5},{3,7},{5,1},{7,3},{8,12},{10,14},{12... | collective-permute-start | bytes 860168 | tf_op jit(solution)/shard_map/ppermute | solution.py:16
  9.0 22.3 %collective-permute-start.2 = (bf16[1,40,3584]{2,1,0:T(8,128)(2,1)S(1)}, bf16[1,40,3584]{2,1,0:T(8,128)(2,1)S(1)}, u32[]{:S(2)}, u32[]{:S(2)}) collective-permute-start(bf16[1,40,3584]{2,1,0:T(8,128)(2,1)S(1)} %get-tuple-element.12), channel_id=1, source_target_pairs={{0,2},{2,0},{4,6},{6,4},{1,3},{3,1},{5,7},{7,5},{8,10},{10,8},{12,... | collective-permute-start | bytes 860168 | tf_op jit(solution)/shard_map/ppermute | solution.py:16
  9.2 18.4 %collective-permute-start.11 = (bf16[1,40,3584]{2,1,0:T(8,128)(2,1)S(1)}, bf16[1,40,3584]{2,1,0:T(8,128)(2,1)S(1)}, u32[]{:S(2)}, u32[]{:S(2)}) collective-permute-start(bf16[1,40,3584]{2,1,0:T(8,128)(2,1)S(1)} %get-tuple-element.13), channel_id=1, source_target_pairs={{0,8},{8,0},{1,9},{9,1},{2,10},{10,2},{3,11},{11,3},{4,12},{12,4},... | collective-permute-start | bytes 860168 | tf_op jit(solution)/shard_map/ppermute | solution.py:12
  27.6 19.5 %collective-permute-start.6 = (bf16[160,3584]{1,0:T(8,128)(2,1)S(1)}, bf16[160,3584]{1,0:T(8,128)(2,1)S(1)}, u32[]{:S(2)}, u32[]{:S(2)}) collective-permute-start(bf16[160,3584]{1,0:T(8,128)(2,1)S(1)} %bitcast.78), channel_id=1, source_target_pairs={{0,1},{1,0},{2,3},{3,2},{4,5},{5,4},{6,7},{7,6},{8,9},{9,8},{10,11... | collective-permute-start | bytes 3440648 | tf_op jit(solution)/shard_map/ppermute | solution.py:12
  27.6 11.3 %collective-permute-start.14 = (bf16[1,40,3584]{2,1,0:T(8,128)(2,1)S(1)}, bf16[1,40,3584]{2,1,0:T(8,128)(2,1)S(1)}, u32[]{:S(2)}, u32[]{:S(2)}) collective-permute-start(bf16[1,40,3584]{2,1,0:T(8,128)(2,1)S(1)} %collective-permute-done.11), channel_id=1, source_target_pairs={{0,6},{2,4},{4,2},{6,0},{1,7},{3,5},{5,3},{7,1},{8,14},{10,12},{12... | collective-permute-start | bytes 860168 | tf_op jit(solution)/shard_map/ppermute | solution.py:16
  31.1 13.6 %collective-permute-start.13 = (bf16[1,40,3584]{2,1,0:T(8,128)(2,1)S(1)}, bf16[1,40,3584]{2,1,0:T(8,128)(2,1)S(1)}, u32[]{:S(2)}, u32[]{:S(2)}) collective-permute-start(bf16[1,40,3584]{2,1,0:T(8,128)(2,1)S(1)} %collective-permute-done.11), channel_id=1, source_target_pairs={{0,4},{2,6},{4,0},{6,2},{1,5},{3,7},{5,1},{7,3},{8,12},{10,14},{12... | collective-permute-start | bytes 860168 | tf_op jit(solution)/shard_map/ppermute | solution.py:16
  31.3 13.5 %collective-permute-start.12 = (bf16[1,40,3584]{2,1,0:T(8,128)(2,1)S(1)}, bf16[1,40,3584]{2,1,0:T(8,128)(2,1)S(1)}, u32[]{:S(2)}, u32[]{:S(2)}) collective-permute-start(bf16[1,40,3584]{2,1,0:T(8,128)(2,1)S(1)} %collective-permute-done.11), channel_id=1, source_target_pairs={{0,2},{2,0},{4,6},{6,4},{1,3},{3,1},{5,7},{7,5},{8,10},{10,8},{12,... | collective-permute-start | bytes 860168 | tf_op jit(solution)/shard_map/ppermute | solution.py:16
  32.7 6.2 %copy-start = (bf16[1,160,3584]{2,1,0:T(8,128)(2,1)S(1)}, bf16[1,160,3584]{2,1,0:T(8,128)(2,1)}, u32[]{:S(2)}) copy-start(bf16[1,160,3584]{2,1,0:T(8,128)(2,1)} %param.11) | copy-start | bytes 3440644
  38.9 12.1 %collective-permute-start.7 = (bf16[160,3584]{1,0:T(8,128)(2,1)S(1)}, bf16[160,3584]{1,0:T(8,128)(2,1)S(1)}, u32[]{:S(2)}, u32[]{:S(2)}) collective-permute-start(bf16[160,3584]{1,0:T(8,128)(2,1)S(1)} %bitcast.61), channel_id=1, source_target_pairs={{0,1},{1,0},{2,3},{3,2},{4,5},{5,4},{6,7},{7,6},{8,9},{9,8},{10,11... | collective-permute-start | bytes 3440648 | tf_op jit(solution)/shard_map/ppermute | solution.py:12
  44.8 1.3 %copy-start.1 = (bf16[1,160,3584]{2,1,0:T(8,128)(2,1)S(1)}, bf16[1,160,3584]{2,1,0:T(8,128)(2,1)}, u32[]{:S(2)}) copy-start(bf16[1,160,3584]{2,1,0:T(8,128)(2,1)} %param.9) | copy-start | bytes 3440644
  51.6 16.0 %collective-permute-start.15 = (bf16[1,40,3584]{2,1,0:T(8,128)(2,1)S(1)}, bf16[1,40,3584]{2,1,0:T(8,128)(2,1)S(1)}, u32[]{:S(2)}, u32[]{:S(2)}) collective-permute-start(bf16[1,40,3584]{2,1,0:T(8,128)(2,1)S(1)} %get-tuple-element.8), channel_id=1, source_target_pairs={{0,2},{2,0},{4,6},{6,4},{1,3},{3,1},{5,7},{7,5},{8,10},{10,8},{12,... | collective-permute-start | bytes 860168 | tf_op jit(solution)/shard_map/ppermute | solution.py:16
  53.1 18.1 %collective-permute-start.17 = (bf16[1,40,3584]{2,1,0:T(8,128)(2,1)S(1)}, bf16[1,40,3584]{2,1,0:T(8,128)(2,1)S(1)}, u32[]{:S(2)}, u32[]{:S(2)}) collective-permute-start(bf16[1,40,3584]{2,1,0:T(8,128)(2,1)S(1)} %get-tuple-element.9), channel_id=1, source_target_pairs={{0,6},{2,4},{4,2},{6,0},{1,7},{3,5},{5,3},{7,1},{8,14},{10,12},{12... | collective-permute-start | bytes 860168 | tf_op jit(solution)/shard_map/ppermute | solution.py:16
  55.7 15.4 %collective-permute-start.16 = (bf16[1,40,3584]{2,1,0:T(8,128)(2,1)S(1)}, bf16[1,40,3584]{2,1,0:T(8,128)(2,1)S(1)}, u32[]{:S(2)}, u32[]{:S(2)}) collective-permute-start(bf16[1,40,3584]{2,1,0:T(8,128)(2,1)S(1)} %get-tuple-element.10), channel_id=1, source_target_pairs={{0,4},{2,6},{4,0},{6,2},{1,5},{3,7},{5,1},{7,3},{8,12},{10,14},{12... | collective-permute-start | bytes 860168 | tf_op jit(solution)/shard_map/ppermute | solution.py:16
  56.3 20.3 %collective-permute-start.8 = (bf16[1,40,3584]{2,1,0:T(8,128)(2,1)S(1)}, bf16[1,40,3584]{2,1,0:T(8,128)(2,1)S(1)}, u32[]{:S(2)}, u32[]{:S(2)}) collective-permute-start(bf16[1,40,3584]{2,1,0:T(8,128)(2,1)S(1)} %get-tuple-element.5), channel_id=1, source_target_pairs={{0,2},{2,0},{4,6},{6,4},{1,3},{3,1},{5,7},{7,5},{8,10},{10,8},{12,... | collective-permute-start | bytes 860168 | tf_op jit(solution)/shard_map/ppermute | solution.py:16
  57.2 25.0 %collective-permute-start.10 = (bf16[1,40,3584]{2,1,0:T(8,128)(2,1)S(1)}, bf16[1,40,3584]{2,1,0:T(8,128)(2,1)S(1)}, u32[]{:S(2)}, u32[]{:S(2)}) collective-permute-start(bf16[1,40,3584]{2,1,0:T(8,128)(2,1)S(1)} %get-tuple-element.6), channel_id=1, source_target_pairs={{0,6},{2,4},{4,2},{6,0},{1,7},{3,5},{5,3},{7,1},{8,14},{10,12},{12... | collective-permute-start | bytes 860168 | tf_op jit(solution)/shard_map/ppermute | solution.py:16
  67.6 18.7 %collective-permute-start.9 = (bf16[1,40,3584]{2,1,0:T(8,128)(2,1)S(1)}, bf16[1,40,3584]{2,1,0:T(8,128)(2,1)S(1)}, u32[]{:S(2)}, u32[]{:S(2)}) collective-permute-start(bf16[1,40,3584]{2,1,0:T(8,128)(2,1)S(1)} %get-tuple-element.7), channel_id=1, source_target_pairs={{0,4},{2,6},{4,0},{6,2},{1,5},{3,7},{5,1},{7,3},{8,12},{10,14},{12... | collective-permute-start | bytes 860168 | tf_op jit(solution)/shard_map/ppermute | solution.py:16
  71.3 15.3 %collective-permute-start.18 = (bf16[1,40,3584]{2,1,0:T(8,128)(2,1)S(1)}, bf16[1,40,3584]{2,1,0:T(8,128)(2,1)S(1)}, u32[]{:S(2)}, u32[]{:S(2)}) collective-permute-start(bf16[1,40,3584]{2,1,0:T(8,128)(2,1)S(1)} %fusion.18), channel_id=1, source_target_pairs={{0,8},{8,0},{1,9},{9,1},{2,10},{10,2},{3,11},{11,3},{4,12},{12,4},... | collective-permute-start | bytes 860168 | tf_op jit(solution)/shard_map/ppermute | solution.py:12
  86.4 2.5 %collective-permute-start.19 = (f32[1,40,3584]{2,1,0:T(8,128)S(1)}, f32[1,40,3584]{2,1,0:T(8,128)S(1)}, u32[]{:S(2)}, u32[]{:S(2)}) collective-permute-start(f32[1,40,3584]{2,1,0:T(8,128)S(1)} %fusion.20), channel_id=1, source_target_pairs={{0,1},{1,0},{2,3},{3,2},{4,5},{5,4},{6,7},{7,6},{8,9},{9,8},{10,11... | collective-permute-start | bytes 1720328 | tf_op jit(solution)/shard_map/ppermute | solution.py:12
  86.6 2.3 %collective-permute-start.20 = (bf16[1,40,3584]{2,1,0:T(8,128)(2,1)S(1)}, bf16[1,40,3584]{2,1,0:T(8,128)(2,1)S(1)}, u32[]{:S(2)}, u32[]{:S(2)}) collective-permute-start(bf16[1,40,3584]{2,1,0:T(8,128)(2,1)S(1)} %collective-permute-done.18), channel_id=1, source_target_pairs={{0,1},{1,0},{2,3},{3,2},{4,5},{5,4},{6,7},{7,6},{8,9},{9,8},{10,11... | collective-permute-start | bytes 860168 | tf_op jit(solution)/shard_map/ppermute | solution.py:12

commit v16 on v14

--- a/solution.py
+++ b/solution.py
@@ -52,7 +52,7 @@
 
     wg = with_sibling(w_gate[0])
     wu = with_sibling(w_up[0])
-    wd = with_sibling(w_down[0])
+    wd_other = shift(w_down[0], "context", n_ctx, 1)
 
     other_routes = shift(routes, "context", n_ctx, 1)
     pair_routes = jnp.where(
@@ -90,7 +90,7 @@
             return swap(x, "sh", sharers, k)
         return shift(x, "sh", sharers, -k)
 
-    def group_partial(sent):
+    def group_partial(sent, wd):
         group = [sent] + [exchange(sent, k) for k in range(1, sharers)]
         rows = jnp.stack(group).reshape(-1, width)
         partial = quarter_rows(rows, wg, wu, wd, n_ctx).astype(jnp.bfloat16)
@@ -103,14 +103,17 @@
         return total
 
     if experts == 2:
-        local_part = group_partial(packed[0:1])
-        far_part = group_partial(shift(packed[1:2], "ex", 2, 1))
+        far_sent, wd_other = lax.optimization_barrier((shift(packed[1:2], "ex", 2, 1), wd_other))
+        wd = jnp.concatenate([w_down[0], wd_other], axis=0)
+        local_part = group_partial(packed[0:1], wd)
+        far_part = group_partial(far_sent, wd)
         far_out = group_sum(far_part)
         back = shift(far_out.astype(RETURN_DTYPE), "ex", 2, 1).astype(jnp.float32)
         mine = jnp.concatenate([group_sum(local_part), back], axis=0)
     else:
         sent = lax.all_to_all(packed, "ex", split_axis=0, concat_axis=0, tiled=True)
-        expert_out = group_sum(group_partial(sent)).astype(RETURN_DTYPE)
+        wd = jnp.concatenate([w_down[0], wd_other], axis=0)
+        expert_out = group_sum(group_partial(sent, wd)).astype(RETURN_DTYPE)
         mine = lax.all_to_all(expert_out, "ex", split_axis=0, concat_axis=0, tiled=True)
         mine = mine.astype(jnp.float32)
     theirs = shift(mine, "context", n_ctx, 1)

time: 87.3 us -> 95 us (1.088)
  starting transfers between devices: 20.6 us -> 26 us
  waiting for transfers between devices: 53.7 us -> 55.8 us
    ppermute x12, starting transfers between devices: 15.3 us -> 18.9 us  [swap(): return lax.ppermute(x, axis, [(i, i ^ k) for i in range(size)])]
    ppermute x8, waiting for transfers between devices: 12.9 us -> 14.8 us  [shift(): return lax.ppermute(x, axis, [(i, (i + k) % size) for i in range(size)])]
    ppermute x8, starting transfers between devices: 5.3 us -> 7.12 us  [shift(): return lax.ppermute(x, axis, [(i, (i + k) % size) for i in range(size)])]
  transfers between devices with their start and end apart: 20 -> 20, of which waited for: 11 -> 12; matrix products, arithmetic and copies ran while one was open for 9% -> 7% of each run, Pallas kernels for 0% -> 0%
where the time goes in v16:
time: 95 us; the launch traced here: 94.7 us
  waiting for transfers between devices  55.8 us (59%)
  starting transfers between devices  26 us (27%)
  matrix products  9.01 us (9%)
  other arithmetic  2.48 us (3%)
  local copies, waits for them, and re-layouts  1.21 us (1%)
    ppermute x12, waiting for transfers between devices, swap(): return lax.ppermute(x, axis, [(i, i ^ k) for i in range(size)])  40.9 us
    ppermute x12, starting transfers between devices, swap(): return lax.ppermute(x, axis, [(i, i ^ k) for i in range(size)])  18.9 us
    ppermute x8, waiting for transfers between devices, shift(): return lax.ppermute(x, axis, [(i, (i + k) % size) for i in range(size)])  14.8 us
    ppermute x8, starting transfers between devices, shift(): return lax.ppermute(x, axis, [(i, (i + k) % size) for i in range(size)])  7.12 us
    dot_general x2, matrix products, quarter_rows(): up = lax.dot_general(rows, w_up, dims, preferred_element_type=jnp.float32)  2.01 us
    dot_general x2, matrix products, quarter_rows(): lax.dot_general(rows, w_gate, dims, preferred_element_type=jnp.float32)  2 us
    dot_general x4, matrix products, quarter_rows(): jnp.dot(hidden[:, c * slab:(c + 1) * slab], w_down[c * slab:(c + 1) * sla...  1.94 us
  transfers between devices with their start and end apart: 20, of which 12 were waited for; matrix products, arithmetic and copies ran while one was open for 7% of the time, Pallas kernels for 0%

profile of v16, /device:TPU:0, one launch (start us, length us, event | category | flops | bytes accessed | tf_op | source)
XLA Modules:
  0.0 94.7 jit_solution(12224292982574624719)
XLA Ops:
  1.5 0.8 add_select_fusion
  3.1 1.4 %convolution_convert_fusion.4 = bf16[80,3584]{1,0:T(8,128)(2,1)S(1)} fusion(pred[80,128]{1,0:T(8,128)(4,1)S(1)} %fusion.24, bf16[64,3584]{1,0:T(8,128)(2,1)S(1)} %collective-permute-done.1, bf16[64,3584]{1,0:T(8,128)(2,1)} %param.6), kind=kOutput, calls=%fused_computation.12 | convolution fusion | flops 75522048 | bytes 1501184 | tf_op jit(solution)/shard_map/dot_general | solution.py:80
  4.6 3.9 %collective-permute-start.4 = (bf16[1,40,3584]{2,1,0:T(8,128)(2,1)S(1)}, bf16[1,40,3584]{2,1,0:T(8,128)(2,1)S(1)}, u32[]{:S(2)}, u32[]{:S(2)}) collective-permute-start(bf16[1,40,3584]{2,1,0:T(8,128)(2,1)S(1)} %get-tuple-element.16), channel_id=1, source_target_pairs={{0,6},{2,4},{4,2},{6,0},{1,7},{3,5},{5,3},{7,1},{8,14},{10,12},{12... | collective-permute-start | bytes 860168 | tf_op jit(solution)/shard_map/ppermute | solution.py:16
  9.0 7.2 %collective-permute-done.4 = bf16[1,40,3584]{2,1,0:T(8,128)(2,1)S(1)} collective-permute-done((bf16[1,40,3584]{2,1,0:T(8,128)(2,1)S(1)}, bf16[1,40,3584]{2,1,0:T(8,128)(2,1)S(1)}, u32[]{:S(2)}, u32[]{:S(2)}) %collective-permute-start.4) | collective-permute-done | bytes 286752 | tf_op jit(solution)/shard_map/ppermute | solution.py:16
  16.2 1.9 %collective-permute-start.2 = (bf16[1,40,3584]{2,1,0:T(8,128)(2,1)S(1)}, bf16[1,40,3584]{2,1,0:T(8,128)(2,1)S(1)}, u32[]{:S(2)}, u32[]{:S(2)}) collective-permute-start(bf16[1,40,3584]{2,1,0:T(8,128)(2,1)S(1)} %get-tuple-element.16), channel_id=1, source_target_pairs={{0,2},{2,0},{4,6},{6,4},{1,3},{3,1},{5,7},{7,5},{8,10},{10,8},{12,... | collective-permute-start | bytes 860168 | tf_op jit(solution)/shard_map/ppermute | solution.py:16
  18.1 3.9 %collective-permute-done.3 = bf16[1,40,3584]{2,1,0:T(8,128)(2,1)S(1)} collective-permute-done((bf16[1,40,3584]{2,1,0:T(8,128)(2,1)S(1)}, bf16[1,40,3584]{2,1,0:T(8,128)(2,1)S(1)}, u32[]{:S(2)}, u32[]{:S(2)}) %collective-permute-start.3) | collective-permute-done | bytes 286752 | tf_op jit(solution)/shard_map/ppermute | solution.py:16
  22.0 2.6 %collective-permute-start.7 = (bf16[1,40,3584]{2,1,0:T(8,128)(2,1)S(1)}, bf16[1,40,3584]{2,1,0:T(8,128)(2,1)S(1)}, u32[]{:S(2)}, u32[]{:S(2)}) collective-permute-start(bf16[1,40,3584]{2,1,0:T(8,128)(2,1)S(1)} %get-tuple-element.17), channel_id=1, source_target_pairs={{0,8},{8,0},{1,9},{9,1},{2,10},{10,2},{3,11},{11,3},{4,12},{12,4},... | collective-permute-start | bytes 860168 | tf_op jit(solution)/shard_map/ppermute | solution.py:12
  24.8 12.4 %collective-permute-done.7 = bf16[1,40,3584]{2,1,0:T(8,128)(2,1)S(1)} collective-permute-done((bf16[1,40,3584]{2,1,0:T(8,128)(2,1)S(1)}, bf16[1,40,3584]{2,1,0:T(8,128)(2,1)S(1)}, u32[]{:S(2)}, u32[]{:S(2)}) %collective-permute-start.7) | collective-permute-done | bytes 286752 | tf_op jit(solution)/shard_map/ppermute | solution.py:12
  37.1 0.6 collective-permute-start.14
  37.8 1.5 %collective-permute-start.13 = (bf16[1,40,3584]{2,1,0:T(8,128)(2,1)S(1)}, bf16[1,40,3584]{2,1,0:T(8,128)(2,1)S(1)}, u32[]{:S(2)}, u32[]{:S(2)}) collective-permute-start(bf16[1,40,3584]{2,1,0:T(8,128)(2,1)S(1)} %collective-permute-done.7), channel_id=1, source_target_pairs={{0,4},{2,6},{4,0},{6,2},{1,5},{3,7},{5,1},{7,3},{8,12},{10,14},{12... | collective-permute-start | bytes 860168 | tf_op jit(solution)/shard_map/ppermute | solution.py:16
  39.3 1.3 %collective-permute-start.12 = (bf16[1,40,3584]{2,1,0:T(8,128)(2,1)S(1)}, bf16[1,40,3584]{2,1,0:T(8,128)(2,1)S(1)}, u32[]{:S(2)}, u32[]{:S(2)}) collective-permute-start(bf16[1,40,3584]{2,1,0:T(8,128)(2,1)S(1)} %collective-permute-done.7), channel_id=1, source_target_pairs={{0,2},{2,0},{4,6},{6,4},{1,3},{3,1},{5,7},{7,5},{8,10},{10,8},{12,... | collective-permute-start | bytes 860168 | tf_op jit(solution)/shard_map/ppermute | solution.py:16
  40.6 1.0 %fusion.11 = f32[160,320]{1,0:T(8,128)S(1)} fusion(bf16[160,3584]{1,0:T(8,128)(2,1)S(1)} %bitcast.62, bf16[160,3584]{1,0:T(8,128)(2,1)S(1)} %collective-permute-done.5, bf16[160,3584]{1,0:T(8,128)(2,1)S(1)} %bitcast.74), kind=kOutput, calls=%fused_computation.20 | convolution fusion | flops 371589120 | bytes 3645440 | tf_op jit(solution)/shard_map/dot_general | solution.py:21
  41.7 1.0 %multiply_convert_fusion.1 = bf16[160,320]{1,0:T(8,128)(2,1)S(1)} fusion(f32[160,320]{1,0:T(8,128)S(1)} %fusion.11, bf16[160,3584]{1,0:T(8,128)(2,1)S(1)} %bitcast.63, bf16[160,3584]{1,0:T(8,128)(2,1)S(1)} %collective-permute-done.6, bf16[160,3584]{1,0:T(8,128)(2,1)S(1)} %bitcast.77), kind=kOutput, calls=%fused_computation.46 | convolution fusion | flops 371896320 | bytes 3747840 | tf_op jit(solution)/shard_map/dot_general | solution.py:22
  43.3 0.5 fusion.6
  43.9 4.0 %collective-permute-done.14 = bf16[1,40,3584]{2,1,0:T(8,128)(2,1)S(1)} collective-permute-done((bf16[1,40,3584]{2,1,0:T(8,128)(2,1)S(1)}, bf16[1,40,3584]{2,1,0:T(8,128)(2,1)S(1)}, u32[]{:S(2)}, u32[]{:S(2)}) %collective-permute-start.14) | collective-permute-done | bytes 286752 | tf_op jit(solution)/shard_map/ppermute | solution.py:16
  47.8 3.5 %collective-permute-done.13 = bf16[1,40,3584]{2,1,0:T(8,128)(2,1)S(1)} collective-permute-done((bf16[1,40,3584]{2,1,0:T(8,128)(2,1)S(1)}, bf16[1,40,3584]{2,1,0:T(8,128)(2,1)S(1)}, u32[]{:S(2)}, u32[]{:S(2)}) %collective-permute-start.13) | collective-permute-done | bytes 286752 | tf_op jit(solution)/shard_map/ppermute | solution.py:16
  52.0 1.0 %fusion.10 = f32[160,320]{1,0:T(8,128)S(1)} fusion(bf16[160,3584]{1,0:T(8,128)(2,1)S(1)} %bitcast.64, bf16[160,3584]{1,0:T(8,128)(2,1)S(1)} %collective-permute-done.5, bf16[160,3584]{1,0:T(8,128)(2,1)S(1)} %bitcast.75), kind=kOutput, calls=%fused_computation.19 | convolution fusion | flops 371589120 | bytes 3645440 | tf_op jit(solution)/shard_map/dot_general | solution.py:21
  53.0 1.0 %multiply_convert_fusion = bf16[160,320]{1,0:T(8,128)(2,1)S(1)} fusion(f32[160,320]{1,0:T(8,128)S(1)} %fusion.10, bf16[160,3584]{1,0:T(8,128)(2,1)S(1)} %bitcast.65, bf16[160,3584]{1,0:T(8,128)(2,1)S(1)} %collective-permute-done.6, bf16[160,3584]{1,0:T(8,128)(2,1)S(1)} %bitcast.78), kind=kOutput, calls=%fused_computation.45 | convolution fusion | flops 371896320 | bytes 3747840 | tf_op jit(solution)/shard_map/dot_general | solution.py:22
  54.5 0.5 fusion.2
  55.1 1.0 %collective-permute-start.15 = (bf16[1,40,3584]{2,1,0:T(8,128)(2,1)S(1)}, bf16[1,40,3584]{2,1,0:T(8,128)(2,1)S(1)}, u32[]{:S(2)}, u32[]{:S(2)}) collective-permute-start(bf16[1,40,3584]{2,1,0:T(8,128)(2,1)S(1)} %get-tuple-element.12), channel_id=1, source_target_pairs={{0,2},{2,0},{4,6},{6,4},{1,3},{3,1},{5,7},{7,5},{8,10},{10,8},{12,... | collective-permute-start | bytes 860168 | tf_op jit(solution)/shard_map/ppermute | solution.py:16
  56.1 2.3 %collective-permute-start.17 = (bf16[1,40,3584]{2,1,0:T(8,128)(2,1)S(1)}, bf16[1,40,3584]{2,1,0:T(8,128)(2,1)S(1)}, u32[]{:S(2)}, u32[]{:S(2)}) collective-permute-start(bf16[1,40,3584]{2,1,0:T(8,128)(2,1)S(1)} %get-tuple-element.13), channel_id=1, source_target_pairs={{0,6},{2,4},{4,2},{6,0},{1,7},{3,5},{5,3},{7,1},{8,14},{10,12},{12... | collective-permute-start | bytes 860168 | tf_op jit(solution)/shard_map/ppermute | solution.py:16
  58.7 1.0 %collective-permute-start.9 = (bf16[1,40,3584]{2,1,0:T(8,128)(2,1)S(1)}, bf16[1,40,3584]{2,1,0:T(8,128)(2,1)S(1)}, u32[]{:S(2)}, u32[]{:S(2)}) collective-permute-start(bf16[1,40,3584]{2,1,0:T(8,128)(2,1)S(1)} %get-tuple-element.9), channel_id=1, source_target_pairs={{0,2},{2,0},{4,6},{6,4},{1,3},{3,1},{5,7},{7,5},{8,10},{10,8},{12,... | collective-permute-start | bytes 860168 | tf_op jit(solution)/shard_map/ppermute | solution.py:16
  59.7 2.3 %collective-permute-start.11 = (bf16[1,40,3584]{2,1,0:T(8,128)(2,1)S(1)}, bf16[1,40,3584]{2,1,0:T(8,128)(2,1)S(1)}, u32[]{:S(2)}, u32[]{:S(2)}) collective-permute-start(bf16[1,40,3584]{2,1,0:T(8,128)(2,1)S(1)} %get-tuple-element.10), channel_id=1, source_target_pairs={{0,6},{2,4},{4,2},{6,0},{1,7},{3,5},{5,3},{7,1},{8,14},{10,12},{12... | collective-permute-start | bytes 860168 | tf_op jit(solution)/shard_map/ppermute | solution.py:16
  62.0 9.5 %collective-permute-done.15 = bf16[1,40,3584]{2,1,0:T(8,128)(2,1)S(1)} collective-permute-done((bf16[1,40,3584]{2,1,0:T(8,128)(2,1)S(1)}, bf16[1,40,3584]{2,1,0:T(8,128)(2,1)S(1)}, u32[]{:S(2)}, u32[]{:S(2)}) %collective-permute-start.15) | collective-permute-done | bytes 286752 | tf_op jit(solution)/shard_map/ppermute | solution.py:16
  71.5 2.3 %collective-permute-start.10 = (bf16[1,40,3584]{2,1,0:T(8,128)(2,1)S(1)}, bf16[1,40,3584]{2,1,0:T(8,128)(2,1)S(1)}, u32[]{:S(2)}, u32[]{:S(2)}) collective-permute-start(bf16[1,40,3584]{2,1,0:T(8,128)(2,1)S(1)} %get-tuple-element.11), channel_id=1, source_target_pairs={{0,4},{2,6},{4,0},{6,2},{1,5},{3,7},{5,1},{7,3},{8,12},{10,14},{12... | collective-permute-start | bytes 860168 | tf_op jit(solution)/shard_map/ppermute | solution.py:16
  73.9 3.4 %collective-permute-start.18 = (bf16[1,40,3584]{2,1,0:T(8,128)(2,1)S(1)}, bf16[1,40,3584]{2,1,0:T(8,128)(2,1)S(1)}, u32[]{:S(2)}, u32[]{:S(2)}) collective-permute-start(bf16[1,40,3584]{2,1,0:T(8,128)(2,1)S(1)} %fusion.17), channel_id=1, source_target_pairs={{0,8},{8,0},{1,9},{9,1},{2,10},{10,2},{3,11},{11,3},{4,12},{12,4},... | collective-permute-start | bytes 860168 | tf_op jit(solution)/shard_map/ppermute | solution.py:12
  77.4 2.2 %collective-permute-done.9 = bf16[1,40,3584]{2,1,0:T(8,128)(2,1)S(1)} collective-permute-done((bf16[1,40,3584]{2,1,0:T(8,128)(2,1)S(1)}, bf16[1,40,3584]{2,1,0:T(8,128)(2,1)S(1)}, u32[]{:S(2)}, u32[]{:S(2)}) %collective-permute-start.9) | collective-permute-done | bytes 286752 | tf_op jit(solution)/shard_map/ppermute | solution.py:16
  79.6 5.6 %collective-permute-done.11 = bf16[1,40,3584]{2,1,0:T(8,128)(2,1)S(1)} collective-permute-done((bf16[1,40,3584]{2,1,0:T(8,128)(2,1)S(1)}, bf16[1,40,3584]{2,1,0:T(8,128)(2,1)S(1)}, u32[]{:S(2)}, u32[]{:S(2)}) %collective-permute-start.11) | collective-permute-done | bytes 286752 | tf_op jit(solution)/shard_map/ppermute | solution.py:16
  85.2 4.5 %collective-permute-done.10 = bf16[1,40,3584]{2,1,0:T(8,128)(2,1)S(1)} collective-permute-done((bf16[1,40,3584]{2,1,0:T(8,128)(2,1)S(1)}, bf16[1,40,3584]{2,1,0:T(8,128)(2,1)S(1)}, u32[]{:S(2)}, u32[]{:S(2)}) %collective-permute-start.10) | collective-permute-done | bytes 286752 | tf_op jit(solution)/shard_map/ppermute | solution.py:16
  90.1 0.5 copy-done.1
  90.8 2.1 %collective-permute-done.19 = f32[2,40,3584]{2,1,0:T(8,128)S(1)} collective-permute-done((f32[2,40,3584]{2,1,0:T(8,128)S(1)}, f32[2,40,3584]{2,1,0:T(8,128)S(1)}, u32[]{:S(2)}, u32[]{:S(2)}) %collective-permute-start.19) | collective-permute-done | bytes 1146912 | tf_op jit(solution)/shard_map/ppermute | solution.py:12
  93.1 1.6 %convolution_convert_fusion.5 = bf16[64,3584]{1,0:T(8,128)(2,1)} fusion(f32[64,160]{1,0:T(8,128)S(1)} %select_reduce_fusion, f32[160,3584]{1,0:T(8,128)S(1)} %bitcast.60), kind=kOutput, calls=%fused_computation.13 | convolution fusion | flops 220430336 | bytes 2793472 | tf_op jit(solution)/shard_map/dot_general | solution.py:135
  (58 shorter events, 5.9 us)
Async XLA Ops:
  0.0 1.5 %collective-permute-start = (s32[64,8]{0,1:T(8,128)}, s32[64,8]{0,1:T(8,128)S(1)}, u32[]{:S(2)}, u32[]{:S(2)}) collective-permute-start(s32[64,8]{0,1:T(8,128)} %param.7), channel_id=1, source_target_pairs={{0,1},{1,0},{2,3},{3,2},{4,5},{5,4},{6,7},{7,6},{8,9},{9,8},{10,11... | collective-permute-start | bytes 6152 | tf_op jit(solution)/shard_map/ppermute | solution.py:12
  0.5 2.7 %collective-permute-start.1 = (bf16[64,3584]{1,0:T(8,128)(2,1)}, bf16[64,3584]{1,0:T(8,128)(2,1)S(1)}, u32[]{:S(2)}, u32[]{:S(2)}) collective-permute-start(bf16[64,3584]{1,0:T(8,128)(2,1)} %param.6), channel_id=1, source_target_pairs={{0,1},{1,0},{2,3},{3,2},{4,5},{5,4},{6,7},{7,6},{8,9},{9,8},{10,11... | collective-permute-start | bytes 1376264 | tf_op jit(solution)/shard_map/ppermute | solution.py:12
  0.5 40.1 %collective-permute-start.5 = (bf16[160,3584]{1,0:T(8,128)(2,1)}, bf16[160,3584]{1,0:T(8,128)(2,1)S(1)}, u32[]{:S(2)}, u32[]{:S(2)}) collective-permute-start(bf16[160,3584]{1,0:T(8,128)(2,1)} %bitcast.73), channel_id=1, source_target_pairs={{0,1},{1,0},{2,3},{3,2},{4,5},{5,4},{6,7},{7,6},{8,9},{9,8},{10,11... | collective-permute-start | bytes 3440648 | tf_op jit(solution)/shard_map/ppermute | solution.py:12
  1.0 36.2 %collective-permute-start.8 = (bf16[160,3584]{1,0:T(8,128)(2,1)}, bf16[160,3584]{1,0:T(8,128)(2,1)S(1)}, u32[]{:S(2)}, u32[]{:S(2)}) collective-permute-start(bf16[160,3584]{1,0:T(8,128)(2,1)} %bitcast.61), channel_id=1, source_target_pairs={{0,1},{1,0},{2,3},{3,2},{4,5},{5,4},{6,7},{7,6},{8,9},{9,8},{10,11... | collective-permute-start | bytes 3440648 | tf_op jit(solution)/shard_map/ppermute | solution.py:12
  3.1 5.4 %copy-start.4 = (bf16[1,160,3584]{2,1,0:T(8,128)(2,1)S(1)}, bf16[1,160,3584]{2,1,0:T(8,128)(2,1)}, u32[]{:S(2)}) copy-start(bf16[1,160,3584]{2,1,0:T(8,128)(2,1)} %param.10) | copy-start | bytes 3440644
  4.6 11.5 %collective-permute-start.4 = (bf16[1,40,3584]{2,1,0:T(8,128)(2,1)S(1)}, bf16[1,40,3584]{2,1,0:T(8,128)(2,1)S(1)}, u32[]{:S(2)}, u32[]{:S(2)}) collective-permute-start(bf16[1,40,3584]{2,1,0:T(8,128)(2,1)S(1)} %get-tuple-element.16), channel_id=1, source_target_pairs={{0,6},{2,4},{4,2},{6,0},{1,7},{3,5},{5,3},{7,1},{8,14},{10,12},{12... | collective-permute-start | bytes 860168 | tf_op jit(solution)/shard_map/ppermute | solution.py:16
  8.5 33.1 %collective-permute-start.6 = (bf16[160,3584]{1,0:T(8,128)(2,1)S(1)}, bf16[160,3584]{1,0:T(8,128)(2,1)S(1)}, u32[]{:S(2)}, u32[]{:S(2)}) collective-permute-start(bf16[160,3584]{1,0:T(8,128)(2,1)S(1)} %bitcast.76), channel_id=1, source_target_pairs={{0,1},{1,0},{2,3},{3,2},{4,5},{5,4},{6,7},{7,6},{8,9},{9,8},{10,11... | collective-permute-start | bytes 3440648 | tf_op jit(solution)/shard_map/ppermute | solution.py:12
  8.5 13.5 %collective-permute-start.3 = (bf16[1,40,3584]{2,1,0:T(8,128)(2,1)S(1)}, bf16[1,40,3584]{2,1,0:T(8,128)(2,1)S(1)}, u32[]{:S(2)}, u32[]{:S(2)}) collective-permute-start(bf16[1,40,3584]{2,1,0:T(8,128)(2,1)S(1)} %get-tuple-element.16), channel_id=1, source_target_pairs={{0,4},{2,6},{4,0},{6,2},{1,5},{3,7},{5,1},{7,3},{8,12},{10,14},{12... | collective-permute-start | bytes 860168 | tf_op jit(solution)/shard_map/ppermute | solution.py:16
  16.2 8.4 %collective-permute-start.2 = (bf16[1,40,3584]{2,1,0:T(8,128)(2,1)S(1)}, bf16[1,40,3584]{2,1,0:T(8,128)(2,1)S(1)}, u32[]{:S(2)}, u32[]{:S(2)}) collective-permute-start(bf16[1,40,3584]{2,1,0:T(8,128)(2,1)S(1)} %get-tuple-element.16), channel_id=1, source_target_pairs={{0,2},{2,0},{4,6},{6,4},{1,3},{3,1},{5,7},{7,5},{8,10},{10,8},{12,... | collective-permute-start | bytes 860168 | tf_op jit(solution)/shard_map/ppermute | solution.py:16
  22.0 15.1 %collective-permute-start.7 = (bf16[1,40,3584]{2,1,0:T(8,128)(2,1)S(1)}, bf16[1,40,3584]{2,1,0:T(8,128)(2,1)S(1)}, u32[]{:S(2)}, u32[]{:S(2)}) collective-permute-start(bf16[1,40,3584]{2,1,0:T(8,128)(2,1)S(1)} %get-tuple-element.17), channel_id=1, source_target_pairs={{0,8},{8,0},{1,9},{9,1},{2,10},{10,2},{3,11},{11,3},{4,12},{12,4},... | collective-permute-start | bytes 860168 | tf_op jit(solution)/shard_map/ppermute | solution.py:12
  24.6 16.0 %copy-start.3 = (bf16[1,160,3584]{2,1,0:T(8,128)(2,1)S(1)}, bf16[1,160,3584]{2,1,0:T(8,128)(2,1)}, u32[]{:S(2)}) copy-start(bf16[1,160,3584]{2,1,0:T(8,128)(2,1)} %param.9) | copy-start | bytes 3440644
  37.1 10.7 %collective-permute-start.14 = (bf16[1,40,3584]{2,1,0:T(8,128)(2,1)S(1)}, bf16[1,40,3584]{2,1,0:T(8,128)(2,1)S(1)}, u32[]{:S(2)}, u32[]{:S(2)}) collective-permute-start(bf16[1,40,3584]{2,1,0:T(8,128)(2,1)S(1)} %collective-permute-done.7), channel_id=1, source_target_pairs={{0,6},{2,4},{4,2},{6,0},{1,7},{3,5},{5,3},{7,1},{8,14},{10,12},{12... | collective-permute-start | bytes 860168 | tf_op jit(solution)/shard_map/ppermute | solution.py:16
  37.8 13.6 %collective-permute-start.13 = (bf16[1,40,3584]{2,1,0:T(8,128)(2,1)S(1)}, bf16[1,40,3584]{2,1,0:T(8,128)(2,1)S(1)}, u32[]{:S(2)}, u32[]{:S(2)}) collective-permute-start(bf16[1,40,3584]{2,1,0:T(8,128)(2,1)S(1)} %collective-permute-done.7), channel_id=1, source_target_pairs={{0,4},{2,6},{4,0},{6,2},{1,5},{3,7},{5,1},{7,3},{8,12},{10,14},{12... | collective-permute-start | bytes 860168 | tf_op jit(solution)/shard_map/ppermute | solution.py:16
  39.3 12.5 %collective-permute-start.12 = (bf16[1,40,3584]{2,1,0:T(8,128)(2,1)S(1)}, bf16[1,40,3584]{2,1,0:T(8,128)(2,1)S(1)}, u32[]{:S(2)}, u32[]{:S(2)}) collective-permute-start(bf16[1,40,3584]{2,1,0:T(8,128)(2,1)S(1)} %collective-permute-done.7), channel_id=1, source_target_pairs={{0,2},{2,0},{4,6},{6,4},{1,3},{3,1},{5,7},{7,5},{8,10},{10,8},{12,... | collective-permute-start | bytes 860168 | tf_op jit(solution)/shard_map/ppermute | solution.py:16
  41.6 1.3 %copy-start = (bf16[1,160,3584]{2,1,0:T(8,128)(2,1)S(1)}, bf16[1,160,3584]{2,1,0:T(8,128)(2,1)}, u32[]{:S(2)}) copy-start(bf16[1,160,3584]{2,1,0:T(8,128)(2,1)} %param.11) | copy-start | bytes 3440644
  55.1 16.4 %collective-permute-start.15 = (bf16[1,40,3584]{2,1,0:T(8,128)(2,1)S(1)}, bf16[1,40,3584]{2,1,0:T(8,128)(2,1)S(1)}, u32[]{:S(2)}, u32[]{:S(2)}) collective-permute-start(bf16[1,40,3584]{2,1,0:T(8,128)(2,1)S(1)} %get-tuple-element.12), channel_id=1, source_target_pairs={{0,2},{2,0},{4,6},{6,4},{1,3},{3,1},{5,7},{7,5},{8,10},{10,8},{12,... | collective-permute-start | bytes 860168 | tf_op jit(solution)/shard_map/ppermute | solution.py:16
  56.1 17.7 %collective-permute-start.17 = (bf16[1,40,3584]{2,1,0:T(8,128)(2,1)S(1)}, bf16[1,40,3584]{2,1,0:T(8,128)(2,1)S(1)}, u32[]{:S(2)}, u32[]{:S(2)}) collective-permute-start(bf16[1,40,3584]{2,1,0:T(8,128)(2,1)S(1)} %get-tuple-element.13), channel_id=1, source_target_pairs={{0,6},{2,4},{4,2},{6,0},{1,7},{3,5},{5,3},{7,1},{8,14},{10,12},{12... | collective-permute-start | bytes 860168 | tf_op jit(solution)/shard_map/ppermute | solution.py:16
  58.3 15.4 %collective-permute-start.16 = (bf16[1,40,3584]{2,1,0:T(8,128)(2,1)S(1)}, bf16[1,40,3584]{2,1,0:T(8,128)(2,1)S(1)}, u32[]{:S(2)}, u32[]{:S(2)}) collective-permute-start(bf16[1,40,3584]{2,1,0:T(8,128)(2,1)S(1)} %get-tuple-element.14), channel_id=1, source_target_pairs={{0,4},{2,6},{4,0},{6,2},{1,5},{3,7},{5,1},{7,3},{8,12},{10,14},{12... | collective-permute-start | bytes 860168 | tf_op jit(solution)/shard_map/ppermute | solution.py:16
  58.7 21.0 %collective-permute-start.9 = (bf16[1,40,3584]{2,1,0:T(8,128)(2,1)S(1)}, bf16[1,40,3584]{2,1,0:T(8,128)(2,1)S(1)}, u32[]{:S(2)}, u32[]{:S(2)}) collective-permute-start(bf16[1,40,3584]{2,1,0:T(8,128)(2,1)S(1)} %get-tuple-element.9), channel_id=1, source_target_pairs={{0,2},{2,0},{4,6},{6,4},{1,3},{3,1},{5,7},{7,5},{8,10},{10,8},{12,... | collective-permute-start | bytes 860168 | tf_op jit(solution)/shard_map/ppermute | solution.py:16
  59.7 25.5 %collective-permute-start.11 = (bf16[1,40,3584]{2,1,0:T(8,128)(2,1)S(1)}, bf16[1,40,3584]{2,1,0:T(8,128)(2,1)S(1)}, u32[]{:S(2)}, u32[]{:S(2)}) collective-permute-start(bf16[1,40,3584]{2,1,0:T(8,128)(2,1)S(1)} %get-tuple-element.10), channel_id=1, source_target_pairs={{0,6},{2,4},{4,2},{6,0},{1,7},{3,5},{5,3},{7,1},{8,14},{10,12},{12... | collective-permute-start | bytes 860168 | tf_op jit(solution)/shard_map/ppermute | solution.py:16
  71.5 18.2 %collective-permute-start.10 = (bf16[1,40,3584]{2,1,0:T(8,128)(2,1)S(1)}, bf16[1,40,3584]{2,1,0:T(8,128)(2,1)S(1)}, u32[]{:S(2)}, u32[]{:S(2)}) collective-permute-start(bf16[1,40,3584]{2,1,0:T(8,128)(2,1)S(1)} %get-tuple-element.11), channel_id=1, source_target_pairs={{0,4},{2,6},{4,0},{6,2},{1,5},{3,7},{5,1},{7,3},{8,12},{10,14},{12... | collective-permute-start | bytes 860168 | tf_op jit(solution)/shard_map/ppermute | solution.py:16
  73.9 15.9 %collective-permute-start.18 = (bf16[1,40,3584]{2,1,0:T(8,128)(2,1)S(1)}, bf16[1,40,3584]{2,1,0:T(8,128)(2,1)S(1)}, u32[]{:S(2)}, u32[]{:S(2)}) collective-permute-start(bf16[1,40,3584]{2,1,0:T(8,128)(2,1)S(1)} %fusion.17), channel_id=1, source_target_pairs={{0,8},{8,0},{1,9},{9,1},{2,10},{10,2},{3,11},{11,3},{4,12},{12,4},... | collective-permute-start | bytes 860168 | tf_op jit(solution)/shard_map/ppermute | solution.py:12
  89.9 0.7 copy-start.1
  89.9 0.7 copy-start.2
  90.0 2.9 %collective-permute-start.19 = (f32[2,40,3584]{2,1,0:T(8,128)S(1)}, f32[2,40,3584]{2,1,0:T(8,128)S(1)}, u32[]{:S(2)}, u32[]{:S(2)}) collective-permute-start(f32[2,40,3584]{2,1,0:T(8,128)S(1)} %pad_maximum_fusion.9), channel_id=1, source_target_pairs={{0,1},{1,0},{2,3},{3,2},{4,5},{5,4},{6,7},{7,6},{8,9},{9,8},{10,11... | collective-permute-start | bytes 3440648 | tf_op jit(solution)/shard_map/ppermute | solution.py:12

commit v17 on v14

--- a/solution.py
+++ b/solution.py
@@ -91,14 +91,16 @@
         return shift(x, "sh", sharers, -k)
 
     def group_partial(sent):
-        group = [sent] + [exchange(sent, k) for k in range(1, sharers)]
+        order = list(range(sharers - 1, 0, -1))
+        received = {k: exchange(sent, k) for k in order}
+        group = [sent] + [received[k] for k in range(1, sharers)]
         rows = jnp.stack(group).reshape(-1, width)
         partial = quarter_rows(rows, wg, wu, wd, n_ctx).astype(jnp.bfloat16)
         return partial.reshape((sharers,) + sent.shape)
 
     def group_sum(partial):
         total = partial[0].astype(jnp.float32)
-        for k in range(1, sharers):
+        for k in range(sharers - 1, 0, -1):
             total = total + back_exchange(partial[k], k).astype(jnp.float32)
         return total
 

time: 87.3 us -> 87 us (level)
    ppermute x12, starting transfers between devices: 15.3 us -> 14.3 us  [swap(): return lax.ppermute(x, axis, [(i, i ^ k) for i in range(size)])]
where the time goes in v17:
time: 87 us; the launch traced here: 86.8 us
  waiting for transfers between devices  53.7 us (62%)
  starting transfers between devices  20.3 us (23%)
  matrix products  9.06 us (10%)
  other arithmetic  2.48 us (3%)
  local copies, waits for them, and re-layouts  0.99 us (1%)
    ppermute x12, waiting for transfers between devices, swap(): return lax.ppermute(x, axis, [(i, i ^ k) for i in range(size)])  40.8 us
    ppermute x12, starting transfers between devices, swap(): return lax.ppermute(x, axis, [(i, i ^ k) for i in range(size)])  14.3 us
    ppermute x8, waiting for transfers between devices, shift(): return lax.ppermute(x, axis, [(i, (i + k) % size) for i in range(size)])  12.9 us
    ppermute x8, starting transfers between devices, shift(): return lax.ppermute(x, axis, [(i, (i + k) % size) for i in range(size)])  5.98 us
    dot_general x2, matrix products, quarter_rows(): up = lax.dot_general(rows, w_up, dims, preferred_element_type=jnp.float32)  2.01 us
    dot_general x2, matrix products, quarter_rows(): lax.dot_general(rows, w_gate, dims, preferred_element_type=jnp.float32)  2.01 us
    dot_general x4, matrix products, quarter_rows(): jnp.dot(hidden[:, c * slab:(c + 1) * slab], w_down[c * slab:(c + 1) * sla...  1.92 us
  transfers between devices with their start and end apart: 20, of which 11 were waited for; matrix products, arithmetic and copies ran while one was open for 9% of the time, Pallas kernels for 0%

profile of v17, /device:TPU:0, one launch (start us, length us, event | category | flops | bytes accessed | tf_op | source)
XLA Modules:
  0.0 86.8 jit_solution(11273958413356042852)
XLA Ops:
  0.6 0.9 %collective-permute-done = s32[64,8]{0,1:T(8,128)S(1)} collective-permute-done((s32[64,8]{0,1:T(8,128)}, s32[64,8]{0,1:T(8,128)S(1)}, u32[]{:S(2)}, u32[]{:S(2)}) %collective-permute-start) | collective-permute-done | bytes 2080 | tf_op jit(solution)/shard_map/ppermute | solution.py:12
  1.5 0.8 add_select_fusion
  3.2 1.5 %convolution_convert_fusion.4 = bf16[80,3584]{1,0:T(8,128)(2,1)S(1)} fusion(pred[80,128]{1,0:T(8,128)(4,1)S(1)} %fusion.24, bf16[64,3584]{1,0:T(8,128)(2,1)S(1)} %collective-permute-done.1, bf16[64,3584]{1,0:T(8,128)(2,1)} %param.6), kind=kOutput, calls=%fused_computation.12 | convolution fusion | flops 75522048 | bytes 1501184 | tf_op jit(solution)/shard_map/dot_general | solution.py:80
  4.7 4.0 %collective-permute-start.11 = (bf16[1,40,3584]{2,1,0:T(8,128)(2,1)S(1)}, bf16[1,40,3584]{2,1,0:T(8,128)(2,1)S(1)}, u32[]{:S(2)}, u32[]{:S(2)}) collective-permute-start(bf16[1,40,3584]{2,1,0:T(8,128)(2,1)S(1)} %get-tuple-element.13), channel_id=1, source_target_pairs={{0,8},{8,0},{1,9},{9,1},{2,10},{10,2},{3,11},{11,3},{4,12},{12,4},... | collective-permute-start | bytes 860168 | tf_op jit(solution)/shard_map/ppermute | solution.py:12
  8.7 2.5 %collective-permute-start.4 = (bf16[1,40,3584]{2,1,0:T(8,128)(2,1)S(1)}, bf16[1,40,3584]{2,1,0:T(8,128)(2,1)S(1)}, u32[]{:S(2)}, u32[]{:S(2)}) collective-permute-start(bf16[1,40,3584]{2,1,0:T(8,128)(2,1)S(1)} %get-tuple-element.12), channel_id=1, source_target_pairs={{0,6},{2,4},{4,2},{6,0},{1,7},{3,5},{5,3},{7,1},{8,14},{10,12},{12... | collective-permute-start | bytes 860168 | tf_op jit(solution)/shard_map/ppermute | solution.py:16
  11.6 0.5 collective-permute-start.2
  12.2 9.9 %collective-permute-done.11 = bf16[1,40,3584]{2,1,0:T(8,128)(2,1)S(1)} collective-permute-done((bf16[1,40,3584]{2,1,0:T(8,128)(2,1)S(1)}, bf16[1,40,3584]{2,1,0:T(8,128)(2,1)S(1)}, u32[]{:S(2)}, u32[]{:S(2)}) %collective-permute-start.11) | collective-permute-done | bytes 286752 | tf_op jit(solution)/shard_map/ppermute | solution.py:12
  22.1 2.3 %collective-permute-done.4 = bf16[1,40,3584]{2,1,0:T(8,128)(2,1)S(1)} collective-permute-done((bf16[1,40,3584]{2,1,0:T(8,128)(2,1)S(1)}, bf16[1,40,3584]{2,1,0:T(8,128)(2,1)S(1)}, u32[]{:S(2)}, u32[]{:S(2)}) %collective-permute-start.4) | collective-permute-done | bytes 286752 | tf_op jit(solution)/shard_map/ppermute | solution.py:16
  24.4 1.1 %collective-permute-start.14 = (bf16[1,40,3584]{2,1,0:T(8,128)(2,1)S(1)}, bf16[1,40,3584]{2,1,0:T(8,128)(2,1)S(1)}, u32[]{:S(2)}, u32[]{:S(2)}) collective-permute-start(bf16[1,40,3584]{2,1,0:T(8,128)(2,1)S(1)} %collective-permute-done.11), channel_id=1, source_target_pairs={{0,6},{2,4},{4,2},{6,0},{1,7},{3,5},{5,3},{7,1},{8,14},{10,12},{12... | collective-permute-start | bytes 860168 | tf_op jit(solution)/shard_map/ppermute | solution.py:16
  25.5 5.0 %collective-permute-done.3 = bf16[1,40,3584]{2,1,0:T(8,128)(2,1)S(1)} collective-permute-done((bf16[1,40,3584]{2,1,0:T(8,128)(2,1)S(1)}, bf16[1,40,3584]{2,1,0:T(8,128)(2,1)S(1)}, u32[]{:S(2)}, u32[]{:S(2)}) %collective-permute-start.3) | collective-permute-done | bytes 286752 | tf_op jit(solution)/shard_map/ppermute | solution.py:16
  30.8 1.5 %collective-permute-start.12 = (bf16[1,40,3584]{2,1,0:T(8,128)(2,1)S(1)}, bf16[1,40,3584]{2,1,0:T(8,128)(2,1)S(1)}, u32[]{:S(2)}, u32[]{:S(2)}) collective-permute-start(bf16[1,40,3584]{2,1,0:T(8,128)(2,1)S(1)} %collective-permute-done.11), channel_id=1, source_target_pairs={{0,2},{2,0},{4,6},{6,4},{1,3},{3,1},{5,7},{7,5},{8,10},{10,8},{12,... | collective-permute-start | bytes 860168 | tf_op jit(solution)/shard_map/ppermute | solution.py:16
  32.4 4.3 %collective-permute-done.14 = bf16[1,40,3584]{2,1,0:T(8,128)(2,1)S(1)} collective-permute-done((bf16[1,40,3584]{2,1,0:T(8,128)(2,1)S(1)}, bf16[1,40,3584]{2,1,0:T(8,128)(2,1)S(1)}, u32[]{:S(2)}, u32[]{:S(2)}) %collective-permute-start.14) | collective-permute-done | bytes 286752 | tf_op jit(solution)/shard_map/ppermute | solution.py:16
  36.7 5.0 %collective-permute-done.13 = bf16[1,40,3584]{2,1,0:T(8,128)(2,1)S(1)} collective-permute-done((bf16[1,40,3584]{2,1,0:T(8,128)(2,1)S(1)}, bf16[1,40,3584]{2,1,0:T(8,128)(2,1)S(1)}, u32[]{:S(2)}, u32[]{:S(2)}) %collective-permute-start.13) | collective-permute-done | bytes 286752 | tf_op jit(solution)/shard_map/ppermute | solution.py:16
  41.9 1.0 %fusion.11 = f32[160,320]{1,0:T(8,128)S(1)} fusion(bf16[160,3584]{1,0:T(8,128)(2,1)S(1)} %bitcast.62, bf16[160,3584]{1,0:T(8,128)(2,1)S(1)} %collective-permute-done.5, bf16[160,3584]{1,0:T(8,128)(2,1)S(1)} %bitcast.74), kind=kOutput, calls=%fused_computation.20 | convolution fusion | flops 371589120 | bytes 3645440 | tf_op jit(solution)/shard_map/dot_general | solution.py:21
  42.9 1.0 %multiply_convert_fusion.1 = bf16[160,320]{1,0:T(8,128)(2,1)S(1)} fusion(f32[160,320]{1,0:T(8,128)S(1)} %fusion.11, bf16[160,3584]{1,0:T(8,128)(2,1)S(1)} %bitcast.63, bf16[160,3584]{1,0:T(8,128)(2,1)S(1)} %collective-permute-done.6, bf16[160,3584]{1,0:T(8,128)(2,1)S(1)} %bitcast.77), kind=kOutput, calls=%fused_computation.46 | convolution fusion | flops 371896320 | bytes 3747840 | tf_op jit(solution)/shard_map/dot_general | solution.py:22
  43.9 1.0 %fusion.10 = f32[160,320]{1,0:T(8,128)S(1)} fusion(bf16[160,3584]{1,0:T(8,128)(2,1)S(1)} %bitcast.64, bf16[160,3584]{1,0:T(8,128)(2,1)S(1)} %collective-permute-done.5, bf16[160,3584]{1,0:T(8,128)(2,1)S(1)} %bitcast.75), kind=kOutput, calls=%fused_computation.19 | convolution fusion | flops 371589120 | bytes 3645440 | tf_op jit(solution)/shard_map/dot_general | solution.py:21
  45.4 1.0 %multiply_convert_fusion = bf16[160,320]{1,0:T(8,128)(2,1)S(1)} fusion(f32[160,320]{1,0:T(8,128)S(1)} %fusion.10, bf16[160,3584]{1,0:T(8,128)(2,1)S(1)} %bitcast.65, bf16[160,3584]{1,0:T(8,128)(2,1)S(1)} %collective-permute-done.6, bf16[160,3584]{1,0:T(8,128)(2,1)S(1)} %bitcast.78), kind=kOutput, calls=%fused_computation.45 | convolution fusion | flops 371896320 | bytes 3747840 | tf_op jit(solution)/shard_map/dot_general | solution.py:22
  46.9 0.5 fusion.2
  47.5 1.6 %collective-permute-start.15 = (bf16[1,40,3584]{2,1,0:T(8,128)(2,1)S(1)}, bf16[1,40,3584]{2,1,0:T(8,128)(2,1)S(1)}, u32[]{:S(2)}, u32[]{:S(2)}) collective-permute-start(bf16[1,40,3584]{2,1,0:T(8,128)(2,1)S(1)} %get-tuple-element.8), channel_id=1, source_target_pairs={{0,6},{2,4},{4,2},{6,0},{1,7},{3,5},{5,3},{7,1},{8,14},{10,12},{12... | collective-permute-start | bytes 860168 | tf_op jit(solution)/shard_map/ppermute | solution.py:16
  49.0 1.4 %collective-permute-start.17 = (bf16[1,40,3584]{2,1,0:T(8,128)(2,1)S(1)}, bf16[1,40,3584]{2,1,0:T(8,128)(2,1)S(1)}, u32[]{:S(2)}, u32[]{:S(2)}) collective-permute-start(bf16[1,40,3584]{2,1,0:T(8,128)(2,1)S(1)} %get-tuple-element.9), channel_id=1, source_target_pairs={{0,2},{2,0},{4,6},{6,4},{1,3},{3,1},{5,7},{7,5},{8,10},{10,8},{12,... | collective-permute-start | bytes 860168 | tf_op jit(solution)/shard_map/ppermute | solution.py:16
  50.4 0.6 collective-permute-start.16
  51.0 0.5 fusion.6
  51.6 1.6 %collective-permute-start.8 = (bf16[1,40,3584]{2,1,0:T(8,128)(2,1)S(1)}, bf16[1,40,3584]{2,1,0:T(8,128)(2,1)S(1)}, u32[]{:S(2)}, u32[]{:S(2)}) collective-permute-start(bf16[1,40,3584]{2,1,0:T(8,128)(2,1)S(1)} %get-tuple-element.5), channel_id=1, source_target_pairs={{0,6},{2,4},{4,2},{6,0},{1,7},{3,5},{5,3},{7,1},{8,14},{10,12},{12... | collective-permute-start | bytes 860168 | tf_op jit(solution)/shard_map/ppermute | solution.py:16
  53.1 1.4 %collective-permute-start.10 = (bf16[1,40,3584]{2,1,0:T(8,128)(2,1)S(1)}, bf16[1,40,3584]{2,1,0:T(8,128)(2,1)S(1)}, u32[]{:S(2)}, u32[]{:S(2)}) collective-permute-start(bf16[1,40,3584]{2,1,0:T(8,128)(2,1)S(1)} %get-tuple-element.6), channel_id=1, source_target_pairs={{0,2},{2,0},{4,6},{6,4},{1,3},{3,1},{5,7},{7,5},{8,10},{10,8},{12,... | collective-permute-start | bytes 860168 | tf_op jit(solution)/shard_map/ppermute | solution.py:16
  54.6 3.6 %collective-permute-done.15 = bf16[1,40,3584]{2,1,0:T(8,128)(2,1)S(1)} collective-permute-done((bf16[1,40,3584]{2,1,0:T(8,128)(2,1)S(1)}, bf16[1,40,3584]{2,1,0:T(8,128)(2,1)S(1)}, u32[]{:S(2)}, u32[]{:S(2)}) %collective-permute-start.15) | collective-permute-done | bytes 286752 | tf_op jit(solution)/shard_map/ppermute | solution.py:16
  58.2 1.4 %collective-permute-start.9 = (bf16[1,40,3584]{2,1,0:T(8,128)(2,1)S(1)}, bf16[1,40,3584]{2,1,0:T(8,128)(2,1)S(1)}, u32[]{:S(2)}, u32[]{:S(2)}) collective-permute-start(bf16[1,40,3584]{2,1,0:T(8,128)(2,1)S(1)} %get-tuple-element.7), channel_id=1, source_target_pairs={{0,4},{2,6},{4,0},{6,2},{1,5},{3,7},{5,1},{7,3},{8,12},{10,14},{12... | collective-permute-start | bytes 860168 | tf_op jit(solution)/shard_map/ppermute | solution.py:16
  59.6 4.8 %collective-permute-done.17 = bf16[1,40,3584]{2,1,0:T(8,128)(2,1)S(1)} collective-permute-done((bf16[1,40,3584]{2,1,0:T(8,128)(2,1)S(1)}, bf16[1,40,3584]{2,1,0:T(8,128)(2,1)S(1)}, u32[]{:S(2)}, u32[]{:S(2)}) %collective-permute-start.17) | collective-permute-done | bytes 286752 | tf_op jit(solution)/shard_map/ppermute | solution.py:16
  64.5 1.4 %collective-permute-start.18 = (bf16[1,40,3584]{2,1,0:T(8,128)(2,1)S(1)}, bf16[1,40,3584]{2,1,0:T(8,128)(2,1)S(1)}, u32[]{:S(2)}, u32[]{:S(2)}) collective-permute-start(bf16[1,40,3584]{2,1,0:T(8,128)(2,1)S(1)} %fusion.17), channel_id=1, source_target_pairs={{0,8},{8,0},{1,9},{9,1},{2,10},{10,2},{3,11},{11,3},{4,12},{12,4},... | collective-permute-start | bytes 860168 | tf_op jit(solution)/shard_map/ppermute | solution.py:12
  65.9 10.7 %collective-permute-done.8 = bf16[1,40,3584]{2,1,0:T(8,128)(2,1)S(1)} collective-permute-done((bf16[1,40,3584]{2,1,0:T(8,128)(2,1)S(1)}, bf16[1,40,3584]{2,1,0:T(8,128)(2,1)S(1)}, u32[]{:S(2)}, u32[]{:S(2)}) %collective-permute-start.8) | collective-permute-done | bytes 286752 | tf_op jit(solution)/shard_map/ppermute | solution.py:16
  76.6 5.1 %collective-permute-done.9 = bf16[1,40,3584]{2,1,0:T(8,128)(2,1)S(1)} collective-permute-done((bf16[1,40,3584]{2,1,0:T(8,128)(2,1)S(1)}, bf16[1,40,3584]{2,1,0:T(8,128)(2,1)S(1)}, u32[]{:S(2)}, u32[]{:S(2)}) %collective-permute-start.9) | collective-permute-done | bytes 286752 | tf_op jit(solution)/shard_map/ppermute | solution.py:16
  82.9 2.1 %collective-permute-done.19 = f32[2,40,3584]{2,1,0:T(8,128)S(1)} collective-permute-done((f32[2,40,3584]{2,1,0:T(8,128)S(1)}, f32[2,40,3584]{2,1,0:T(8,128)S(1)}, u32[]{:S(2)}, u32[]{:S(2)}) %collective-permute-start.19) | collective-permute-done | bytes 1146912 | tf_op jit(solution)/shard_map/ppermute | solution.py:12
  85.1 1.6 %convolution_convert_fusion.5 = bf16[64,3584]{1,0:T(8,128)(2,1)} fusion(f32[64,160]{1,0:T(8,128)S(1)} %select_reduce_fusion, f32[160,3584]{1,0:T(8,128)S(1)} %bitcast.60), kind=kOutput, calls=%fused_computation.13 | convolution fusion | flops 220430336 | bytes 2793472 | tf_op jit(solution)/shard_map/dot_general | solution.py:134
  (58 shorter events, 4.8 us)
Async XLA Ops:
  0.0 1.5 %collective-permute-start = (s32[64,8]{0,1:T(8,128)}, s32[64,8]{0,1:T(8,128)S(1)}, u32[]{:S(2)}, u32[]{:S(2)}) collective-permute-start(s32[64,8]{0,1:T(8,128)} %param.7), channel_id=1, source_target_pairs={{0,1},{1,0},{2,3},{3,2},{4,5},{5,4},{6,7},{7,6},{8,9},{9,8},{10,11... | collective-permute-start | bytes 6152 | tf_op jit(solution)/shard_map/ppermute | solution.py:12
  0.5 2.7 %collective-permute-start.1 = (bf16[64,3584]{1,0:T(8,128)(2,1)}, bf16[64,3584]{1,0:T(8,128)(2,1)S(1)}, u32[]{:S(2)}, u32[]{:S(2)}) collective-permute-start(bf16[64,3584]{1,0:T(8,128)(2,1)} %param.6), channel_id=1, source_target_pairs={{0,1},{1,0},{2,3},{3,2},{4,5},{5,4},{6,7},{7,6},{8,9},{9,8},{10,11... | collective-permute-start | bytes 1376264 | tf_op jit(solution)/shard_map/ppermute | solution.py:12
  3.1 9.1 %copy-start.3 = (bf16[1,160,3584]{2,1,0:T(8,128)(2,1)S(1)}, bf16[1,160,3584]{2,1,0:T(8,128)(2,1)}, u32[]{:S(2)}) copy-start(bf16[1,160,3584]{2,1,0:T(8,128)(2,1)} %param.9) | copy-start | bytes 3440644
  3.1 19.0 %copy-start.4 = (bf16[1,160,3584]{2,1,0:T(8,128)(2,1)S(1)}, bf16[1,160,3584]{2,1,0:T(8,128)(2,1)}, u32[]{:S(2)}) copy-start(bf16[1,160,3584]{2,1,0:T(8,128)(2,1)} %param.10) | copy-start | bytes 3440644
  4.7 17.4 %collective-permute-start.11 = (bf16[1,40,3584]{2,1,0:T(8,128)(2,1)S(1)}, bf16[1,40,3584]{2,1,0:T(8,128)(2,1)S(1)}, u32[]{:S(2)}, u32[]{:S(2)}) collective-permute-start(bf16[1,40,3584]{2,1,0:T(8,128)(2,1)S(1)} %get-tuple-element.13), channel_id=1, source_target_pairs={{0,8},{8,0},{1,9},{9,1},{2,10},{10,2},{3,11},{11,3},{4,12},{12,4},... | collective-permute-start | bytes 860168 | tf_op jit(solution)/shard_map/ppermute | solution.py:12
  8.7 15.7 %collective-permute-start.4 = (bf16[1,40,3584]{2,1,0:T(8,128)(2,1)S(1)}, bf16[1,40,3584]{2,1,0:T(8,128)(2,1)S(1)}, u32[]{:S(2)}, u32[]{:S(2)}) collective-permute-start(bf16[1,40,3584]{2,1,0:T(8,128)(2,1)S(1)} %get-tuple-element.12), channel_id=1, source_target_pairs={{0,6},{2,4},{4,2},{6,0},{1,7},{3,5},{5,3},{7,1},{8,14},{10,12},{12... | collective-permute-start | bytes 860168 | tf_op jit(solution)/shard_map/ppermute | solution.py:16
  11.2 19.3 %collective-permute-start.3 = (bf16[1,40,3584]{2,1,0:T(8,128)(2,1)S(1)}, bf16[1,40,3584]{2,1,0:T(8,128)(2,1)S(1)}, u32[]{:S(2)}, u32[]{:S(2)}) collective-permute-start(bf16[1,40,3584]{2,1,0:T(8,128)(2,1)S(1)} %get-tuple-element.12), channel_id=1, source_target_pairs={{0,4},{2,6},{4,0},{6,2},{1,5},{3,7},{5,1},{7,3},{8,12},{10,14},{12... | collective-permute-start | bytes 860168 | tf_op jit(solution)/shard_map/ppermute | solution.py:16
  11.6 19.1 %collective-permute-start.2 = (bf16[1,40,3584]{2,1,0:T(8,128)(2,1)S(1)}, bf16[1,40,3584]{2,1,0:T(8,128)(2,1)S(1)}, u32[]{:S(2)}, u32[]{:S(2)}) collective-permute-start(bf16[1,40,3584]{2,1,0:T(8,128)(2,1)S(1)} %get-tuple-element.12), channel_id=1, source_target_pairs={{0,2},{2,0},{4,6},{6,4},{1,3},{3,1},{5,7},{7,5},{8,10},{10,8},{12,... | collective-permute-start | bytes 860168 | tf_op jit(solution)/shard_map/ppermute | solution.py:16
  12.2 29.7 %collective-permute-start.5 = (bf16[160,3584]{1,0:T(8,128)(2,1)S(1)}, bf16[160,3584]{1,0:T(8,128)(2,1)S(1)}, u32[]{:S(2)}, u32[]{:S(2)}) collective-permute-start(bf16[160,3584]{1,0:T(8,128)(2,1)S(1)} %bitcast.73), channel_id=1, source_target_pairs={{0,1},{1,0},{2,3},{3,2},{4,5},{5,4},{6,7},{7,6},{8,9},{9,8},{10,11... | collective-permute-start | bytes 3440648 | tf_op jit(solution)/shard_map/ppermute | solution.py:12
  22.1 20.8 %collective-permute-start.6 = (bf16[160,3584]{1,0:T(8,128)(2,1)S(1)}, bf16[160,3584]{1,0:T(8,128)(2,1)S(1)}, u32[]{:S(2)}, u32[]{:S(2)}) collective-permute-start(bf16[160,3584]{1,0:T(8,128)(2,1)S(1)} %bitcast.76), channel_id=1, source_target_pairs={{0,1},{1,0},{2,3},{3,2},{4,5},{5,4},{6,7},{7,6},{8,9},{9,8},{10,11... | collective-permute-start | bytes 3440648 | tf_op jit(solution)/shard_map/ppermute | solution.py:12
  24.4 12.3 %collective-permute-start.14 = (bf16[1,40,3584]{2,1,0:T(8,128)(2,1)S(1)}, bf16[1,40,3584]{2,1,0:T(8,128)(2,1)S(1)}, u32[]{:S(2)}, u32[]{:S(2)}) collective-permute-start(bf16[1,40,3584]{2,1,0:T(8,128)(2,1)S(1)} %collective-permute-done.11), channel_id=1, source_target_pairs={{0,6},{2,4},{4,2},{6,0},{1,7},{3,5},{5,3},{7,1},{8,14},{10,12},{12... | collective-permute-start | bytes 860168 | tf_op jit(solution)/shard_map/ppermute | solution.py:16
  30.5 11.2 %collective-permute-start.13 = (bf16[1,40,3584]{2,1,0:T(8,128)(2,1)S(1)}, bf16[1,40,3584]{2,1,0:T(8,128)(2,1)S(1)}, u32[]{:S(2)}, u32[]{:S(2)}) collective-permute-start(bf16[1,40,3584]{2,1,0:T(8,128)(2,1)S(1)} %collective-permute-done.11), channel_id=1, source_target_pairs={{0,4},{2,6},{4,0},{6,2},{1,5},{3,7},{5,1},{7,3},{8,12},{10,14},{12... | collective-permute-start | bytes 860168 | tf_op jit(solution)/shard_map/ppermute | solution.py:16
  30.8 11.0 %collective-permute-start.12 = (bf16[1,40,3584]{2,1,0:T(8,128)(2,1)S(1)}, bf16[1,40,3584]{2,1,0:T(8,128)(2,1)S(1)}, u32[]{:S(2)}, u32[]{:S(2)}) collective-permute-start(bf16[1,40,3584]{2,1,0:T(8,128)(2,1)S(1)} %collective-permute-done.11), channel_id=1, source_target_pairs={{0,2},{2,0},{4,6},{6,4},{1,3},{3,1},{5,7},{7,5},{8,10},{10,8},{12,... | collective-permute-start | bytes 860168 | tf_op jit(solution)/shard_map/ppermute | solution.py:16
  32.2 4.5 %copy-start = (bf16[1,160,3584]{2,1,0:T(8,128)(2,1)S(1)}, bf16[1,160,3584]{2,1,0:T(8,128)(2,1)}, u32[]{:S(2)}) copy-start(bf16[1,160,3584]{2,1,0:T(8,128)(2,1)} %param.11) | copy-start | bytes 3440644
  36.7 10.1 %collective-permute-start.7 = (bf16[160,3584]{1,0:T(8,128)(2,1)S(1)}, bf16[160,3584]{1,0:T(8,128)(2,1)S(1)}, u32[]{:S(2)}, u32[]{:S(2)}) collective-permute-start(bf16[160,3584]{1,0:T(8,128)(2,1)S(1)} %bitcast.61), channel_id=1, source_target_pairs={{0,1},{1,0},{2,3},{3,2},{4,5},{5,4},{6,7},{7,6},{8,9},{9,8},{10,11... | collective-permute-start | bytes 3440648 | tf_op jit(solution)/shard_map/ppermute | solution.py:12
  47.5 10.7 %collective-permute-start.15 = (bf16[1,40,3584]{2,1,0:T(8,128)(2,1)S(1)}, bf16[1,40,3584]{2,1,0:T(8,128)(2,1)S(1)}, u32[]{:S(2)}, u32[]{:S(2)}) collective-permute-start(bf16[1,40,3584]{2,1,0:T(8,128)(2,1)S(1)} %get-tuple-element.8), channel_id=1, source_target_pairs={{0,6},{2,4},{4,2},{6,0},{1,7},{3,5},{5,3},{7,1},{8,14},{10,12},{12... | collective-permute-start | bytes 860168 | tf_op jit(solution)/shard_map/ppermute | solution.py:16
  49.0 15.4 %collective-permute-start.17 = (bf16[1,40,3584]{2,1,0:T(8,128)(2,1)S(1)}, bf16[1,40,3584]{2,1,0:T(8,128)(2,1)S(1)}, u32[]{:S(2)}, u32[]{:S(2)}) collective-permute-start(bf16[1,40,3584]{2,1,0:T(8,128)(2,1)S(1)} %get-tuple-element.9), channel_id=1, source_target_pairs={{0,2},{2,0},{4,6},{6,4},{1,3},{3,1},{5,7},{7,5},{8,10},{10,8},{12,... | collective-permute-start | bytes 860168 | tf_op jit(solution)/shard_map/ppermute | solution.py:16
  50.4 13.9 %collective-permute-start.16 = (bf16[1,40,3584]{2,1,0:T(8,128)(2,1)S(1)}, bf16[1,40,3584]{2,1,0:T(8,128)(2,1)S(1)}, u32[]{:S(2)}, u32[]{:S(2)}) collective-permute-start(bf16[1,40,3584]{2,1,0:T(8,128)(2,1)S(1)} %get-tuple-element.10), channel_id=1, source_target_pairs={{0,4},{2,6},{4,0},{6,2},{1,5},{3,7},{5,1},{7,3},{8,12},{10,14},{12... | collective-permute-start | bytes 860168 | tf_op jit(solution)/shard_map/ppermute | solution.py:16
  51.6 25.1 %collective-permute-start.8 = (bf16[1,40,3584]{2,1,0:T(8,128)(2,1)S(1)}, bf16[1,40,3584]{2,1,0:T(8,128)(2,1)S(1)}, u32[]{:S(2)}, u32[]{:S(2)}) collective-permute-start(bf16[1,40,3584]{2,1,0:T(8,128)(2,1)S(1)} %get-tuple-element.5), channel_id=1, source_target_pairs={{0,6},{2,4},{4,2},{6,0},{1,7},{3,5},{5,3},{7,1},{8,14},{10,12},{12... | collective-permute-start | bytes 860168 | tf_op jit(solution)/shard_map/ppermute | solution.py:16
  53.1 23.5 %collective-permute-start.10 = (bf16[1,40,3584]{2,1,0:T(8,128)(2,1)S(1)}, bf16[1,40,3584]{2,1,0:T(8,128)(2,1)S(1)}, u32[]{:S(2)}, u32[]{:S(2)}) collective-permute-start(bf16[1,40,3584]{2,1,0:T(8,128)(2,1)S(1)} %get-tuple-element.6), channel_id=1, source_target_pairs={{0,2},{2,0},{4,6},{6,4},{1,3},{3,1},{5,7},{7,5},{8,10},{10,8},{12,... | collective-permute-start | bytes 860168 | tf_op jit(solution)/shard_map/ppermute | solution.py:16
  58.2 23.6 %collective-permute-start.9 = (bf16[1,40,3584]{2,1,0:T(8,128)(2,1)S(1)}, bf16[1,40,3584]{2,1,0:T(8,128)(2,1)S(1)}, u32[]{:S(2)}, u32[]{:S(2)}) collective-permute-start(bf16[1,40,3584]{2,1,0:T(8,128)(2,1)S(1)} %get-tuple-element.7), channel_id=1, source_target_pairs={{0,4},{2,6},{4,0},{6,2},{1,5},{3,7},{5,1},{7,3},{8,12},{10,14},{12... | collective-permute-start | bytes 860168 | tf_op jit(solution)/shard_map/ppermute | solution.py:16
  64.5 17.4 %collective-permute-start.18 = (bf16[1,40,3584]{2,1,0:T(8,128)(2,1)S(1)}, bf16[1,40,3584]{2,1,0:T(8,128)(2,1)S(1)}, u32[]{:S(2)}, u32[]{:S(2)}) collective-permute-start(bf16[1,40,3584]{2,1,0:T(8,128)(2,1)S(1)} %fusion.17), channel_id=1, source_target_pairs={{0,8},{8,0},{1,9},{9,1},{2,10},{10,2},{3,11},{11,3},{4,12},{12,4},... | collective-permute-start | bytes 860168 | tf_op jit(solution)/shard_map/ppermute | solution.py:12
  82.0 0.7 copy-start.1
  82.0 0.7 copy-start.2
  82.1 2.9 %collective-permute-start.19 = (f32[2,40,3584]{2,1,0:T(8,128)S(1)}, f32[2,40,3584]{2,1,0:T(8,128)S(1)}, u32[]{:S(2)}, u32[]{:S(2)}) collective-permute-start(f32[2,40,3584]{2,1,0:T(8,128)S(1)} %pad_maximum_fusion.9), channel_id=1, source_target_pairs={{0,1},{1,0},{2,3},{3,2},{4,5},{5,4},{6,7},{7,6},{8,9},{9,8},{10,11... | collective-permute-start | bytes 3440648 | tf_op jit(solution)/shard_map/ppermute | solution.py:12

commit v18 on v17

--- a/solution.py
+++ b/solution.py
@@ -98,9 +98,9 @@
         partial = quarter_rows(rows, wg, wu, wd, n_ctx).astype(jnp.bfloat16)
         return partial.reshape((sharers,) + sent.shape)
 
-    def group_sum(partial):
+    def group_sum(partial, far_first=True):
         total = partial[0].astype(jnp.float32)
-        for k in range(sharers - 1, 0, -1):
+        for k in range(sharers - 1, 0, -1) if far_first else range(1, sharers):
             total = total + back_exchange(partial[k], k).astype(jnp.float32)
         return total
 
@@ -109,7 +109,7 @@
         far_part = group_partial(shift(packed[1:2], "ex", 2, 1))
         far_out = group_sum(far_part)
         back = shift(far_out.astype(RETURN_DTYPE), "ex", 2, 1).astype(jnp.float32)
-        mine = jnp.concatenate([group_sum(local_part), back], axis=0)
+        mine = jnp.concatenate([group_sum(local_part, far_first=False), back], axis=0)
     else:
         sent = lax.all_to_all(packed, "ex", split_axis=0, concat_axis=0, tiled=True)
         expert_out = group_sum(group_partial(sent)).astype(RETURN_DTYPE)

time: 87 us -> 87 us (level)
  transfers between devices with their start and end apart: 20 -> 20, of which waited for: 11 -> 12; matrix products, arithmetic and copies ran while one was open for 9% -> 9% of each run, Pallas kernels for 0% -> 0%
where the time goes in v18:
time: 87 us; the launch traced here: 86.8 us
  waiting for transfers between devices  53.7 us (62%)
  starting transfers between devices  20.3 us (23%)
  matrix products  9.06 us (10%)
  other arithmetic  2.48 us (3%)
  local copies, waits for them, and re-layouts  0.99 us (1%)
    ppermute x12, waiting for transfers between devices, swap(): return lax.ppermute(x, axis, [(i, i ^ k) for i in range(size)])  40.8 us
    ppermute x12, starting transfers between devices, swap(): return lax.ppermute(x, axis, [(i, i ^ k) for i in range(size)])  14.3 us
    ppermute x8, waiting for transfers between devices, shift(): return lax.ppermute(x, axis, [(i, (i + k) % size) for i in range(size)])  12.9 us
    ppermute x8, starting transfers between devices, shift(): return lax.ppermute(x, axis, [(i, (i + k) % size) for i in range(size)])  5.98 us
    dot_general x2, matrix products, quarter_rows(): up = lax.dot_general(rows, w_up, dims, preferred_element_type=jnp.float32)  2.01 us
    dot_general x2, matrix products, quarter_rows(): lax.dot_general(rows, w_gate, dims, preferred_element_type=jnp.float32)  2.01 us
    dot_general x4, matrix products, quarter_rows(): jnp.dot(hidden[:, c * slab:(c + 1) * slab], w_down[c * slab:(c + 1) * sla...  1.92 us
  transfers between devices with their start and end apart: 20, of which 12 were waited for; matrix products, arithmetic and copies ran while one was open for 9% of the time, Pallas kernels for 0%

profile of v18, /device:TPU:0, one launch (start us, length us, event | category | flops | bytes accessed | tf_op | source)
XLA Modules:
  0.0 86.8 jit_solution(16620551717358899075)
XLA Ops:
  0.6 0.9 %collective-permute-done = s32[64,8]{0,1:T(8,128)S(1)} collective-permute-done((s32[64,8]{0,1:T(8,128)}, s32[64,8]{0,1:T(8,128)S(1)}, u32[]{:S(2)}, u32[]{:S(2)}) %collective-permute-start) | collective-permute-done | bytes 2080 | tf_op jit(solution)/shard_map/ppermute | solution.py:12
  1.5 0.8 add_select_fusion
  3.2 1.5 %convolution_convert_fusion.4 = bf16[80,3584]{1,0:T(8,128)(2,1)S(1)} fusion(pred[80,128]{1,0:T(8,128)(4,1)S(1)} %fusion.24, bf16[64,3584]{1,0:T(8,128)(2,1)S(1)} %collective-permute-done.1, bf16[64,3584]{1,0:T(8,128)(2,1)} %param.6), kind=kOutput, calls=%fused_computation.12 | convolution fusion | flops 75522048 | bytes 1501184 | tf_op jit(solution)/shard_map/dot_general | solution.py:80
  4.7 4.0 %collective-permute-start.11 = (bf16[1,40,3584]{2,1,0:T(8,128)(2,1)S(1)}, bf16[1,40,3584]{2,1,0:T(8,128)(2,1)S(1)}, u32[]{:S(2)}, u32[]{:S(2)}) collective-permute-start(bf16[1,40,3584]{2,1,0:T(8,128)(2,1)S(1)} %get-tuple-element.13), channel_id=1, source_target_pairs={{0,8},{8,0},{1,9},{9,1},{2,10},{10,2},{3,11},{11,3},{4,12},{12,4},... | collective-permute-start | bytes 860168 | tf_op jit(solution)/shard_map/ppermute | solution.py:12
  8.7 2.5 %collective-permute-start.4 = (bf16[1,40,3584]{2,1,0:T(8,128)(2,1)S(1)}, bf16[1,40,3584]{2,1,0:T(8,128)(2,1)S(1)}, u32[]{:S(2)}, u32[]{:S(2)}) collective-permute-start(bf16[1,40,3584]{2,1,0:T(8,128)(2,1)S(1)} %get-tuple-element.12), channel_id=1, source_target_pairs={{0,6},{2,4},{4,2},{6,0},{1,7},{3,5},{5,3},{7,1},{8,14},{10,12},{12... | collective-permute-start | bytes 860168 | tf_op jit(solution)/shard_map/ppermute | solution.py:16
  11.6 0.5 collective-permute-start.2
  12.2 9.9 %collective-permute-done.11 = bf16[1,40,3584]{2,1,0:T(8,128)(2,1)S(1)} collective-permute-done((bf16[1,40,3584]{2,1,0:T(8,128)(2,1)S(1)}, bf16[1,40,3584]{2,1,0:T(8,128)(2,1)S(1)}, u32[]{:S(2)}, u32[]{:S(2)}) %collective-permute-start.11) | collective-permute-done | bytes 286752 | tf_op jit(solution)/shard_map/ppermute | solution.py:12
  22.1 2.3 %collective-permute-done.4 = bf16[1,40,3584]{2,1,0:T(8,128)(2,1)S(1)} collective-permute-done((bf16[1,40,3584]{2,1,0:T(8,128)(2,1)S(1)}, bf16[1,40,3584]{2,1,0:T(8,128)(2,1)S(1)}, u32[]{:S(2)}, u32[]{:S(2)}) %collective-permute-start.4) | collective-permute-done | bytes 286752 | tf_op jit(solution)/shard_map/ppermute | solution.py:16
  24.4 1.1 %collective-permute-start.14 = (bf16[1,40,3584]{2,1,0:T(8,128)(2,1)S(1)}, bf16[1,40,3584]{2,1,0:T(8,128)(2,1)S(1)}, u32[]{:S(2)}, u32[]{:S(2)}) collective-permute-start(bf16[1,40,3584]{2,1,0:T(8,128)(2,1)S(1)} %collective-permute-done.11), channel_id=1, source_target_pairs={{0,6},{2,4},{4,2},{6,0},{1,7},{3,5},{5,3},{7,1},{8,14},{10,12},{12... | collective-permute-start | bytes 860168 | tf_op jit(solution)/shard_map/ppermute | solution.py:16
  25.5 5.0 %collective-permute-done.3 = bf16[1,40,3584]{2,1,0:T(8,128)(2,1)S(1)} collective-permute-done((bf16[1,40,3584]{2,1,0:T(8,128)(2,1)S(1)}, bf16[1,40,3584]{2,1,0:T(8,128)(2,1)S(1)}, u32[]{:S(2)}, u32[]{:S(2)}) %collective-permute-start.3) | collective-permute-done | bytes 286752 | tf_op jit(solution)/shard_map/ppermute | solution.py:16
  30.8 1.5 %collective-permute-start.12 = (bf16[1,40,3584]{2,1,0:T(8,128)(2,1)S(1)}, bf16[1,40,3584]{2,1,0:T(8,128)(2,1)S(1)}, u32[]{:S(2)}, u32[]{:S(2)}) collective-permute-start(bf16[1,40,3584]{2,1,0:T(8,128)(2,1)S(1)} %collective-permute-done.11), channel_id=1, source_target_pairs={{0,2},{2,0},{4,6},{6,4},{1,3},{3,1},{5,7},{7,5},{8,10},{10,8},{12,... | collective-permute-start | bytes 860168 | tf_op jit(solution)/shard_map/ppermute | solution.py:16
  32.4 4.3 %collective-permute-done.14 = bf16[1,40,3584]{2,1,0:T(8,128)(2,1)S(1)} collective-permute-done((bf16[1,40,3584]{2,1,0:T(8,128)(2,1)S(1)}, bf16[1,40,3584]{2,1,0:T(8,128)(2,1)S(1)}, u32[]{:S(2)}, u32[]{:S(2)}) %collective-permute-start.14) | collective-permute-done | bytes 286752 | tf_op jit(solution)/shard_map/ppermute | solution.py:16
  36.7 5.0 %collective-permute-done.13 = bf16[1,40,3584]{2,1,0:T(8,128)(2,1)S(1)} collective-permute-done((bf16[1,40,3584]{2,1,0:T(8,128)(2,1)S(1)}, bf16[1,40,3584]{2,1,0:T(8,128)(2,1)S(1)}, u32[]{:S(2)}, u32[]{:S(2)}) %collective-permute-start.13) | collective-permute-done | bytes 286752 | tf_op jit(solution)/shard_map/ppermute | solution.py:16
  41.9 1.0 %fusion.11 = f32[160,320]{1,0:T(8,128)S(1)} fusion(bf16[160,3584]{1,0:T(8,128)(2,1)S(1)} %bitcast.62, bf16[160,3584]{1,0:T(8,128)(2,1)S(1)} %collective-permute-done.5, bf16[160,3584]{1,0:T(8,128)(2,1)S(1)} %bitcast.74), kind=kOutput, calls=%fused_computation.20 | convolution fusion | flops 371589120 | bytes 3645440 | tf_op jit(solution)/shard_map/dot_general | solution.py:21
  42.9 1.0 %multiply_convert_fusion.1 = bf16[160,320]{1,0:T(8,128)(2,1)S(1)} fusion(f32[160,320]{1,0:T(8,128)S(1)} %fusion.11, bf16[160,3584]{1,0:T(8,128)(2,1)S(1)} %bitcast.63, bf16[160,3584]{1,0:T(8,128)(2,1)S(1)} %collective-permute-done.6, bf16[160,3584]{1,0:T(8,128)(2,1)S(1)} %bitcast.77), kind=kOutput, calls=%fused_computation.46 | convolution fusion | flops 371896320 | bytes 3747840 | tf_op jit(solution)/shard_map/dot_general | solution.py:22
  43.9 1.0 %fusion.10 = f32[160,320]{1,0:T(8,128)S(1)} fusion(bf16[160,3584]{1,0:T(8,128)(2,1)S(1)} %bitcast.64, bf16[160,3584]{1,0:T(8,128)(2,1)S(1)} %collective-permute-done.5, bf16[160,3584]{1,0:T(8,128)(2,1)S(1)} %bitcast.75), kind=kOutput, calls=%fused_computation.19 | convolution fusion | flops 371589120 | bytes 3645440 | tf_op jit(solution)/shard_map/dot_general | solution.py:21
  45.4 1.0 %multiply_convert_fusion = bf16[160,320]{1,0:T(8,128)(2,1)S(1)} fusion(f32[160,320]{1,0:T(8,128)S(1)} %fusion.10, bf16[160,3584]{1,0:T(8,128)(2,1)S(1)} %bitcast.65, bf16[160,3584]{1,0:T(8,128)(2,1)S(1)} %collective-permute-done.6, bf16[160,3584]{1,0:T(8,128)(2,1)S(1)} %bitcast.78), kind=kOutput, calls=%fused_computation.45 | convolution fusion | flops 371896320 | bytes 3747840 | tf_op jit(solution)/shard_map/dot_general | solution.py:22
  46.9 0.5 fusion.2
  47.5 1.6 %collective-permute-start.15 = (bf16[1,40,3584]{2,1,0:T(8,128)(2,1)S(1)}, bf16[1,40,3584]{2,1,0:T(8,128)(2,1)S(1)}, u32[]{:S(2)}, u32[]{:S(2)}) collective-permute-start(bf16[1,40,3584]{2,1,0:T(8,128)(2,1)S(1)} %get-tuple-element.8), channel_id=1, source_target_pairs={{0,6},{2,4},{4,2},{6,0},{1,7},{3,5},{5,3},{7,1},{8,14},{10,12},{12... | collective-permute-start | bytes 860168 | tf_op jit(solution)/shard_map/ppermute | solution.py:16
  49.0 1.4 %collective-permute-start.17 = (bf16[1,40,3584]{2,1,0:T(8,128)(2,1)S(1)}, bf16[1,40,3584]{2,1,0:T(8,128)(2,1)S(1)}, u32[]{:S(2)}, u32[]{:S(2)}) collective-permute-start(bf16[1,40,3584]{2,1,0:T(8,128)(2,1)S(1)} %get-tuple-element.9), channel_id=1, source_target_pairs={{0,2},{2,0},{4,6},{6,4},{1,3},{3,1},{5,7},{7,5},{8,10},{10,8},{12,... | collective-permute-start | bytes 860168 | tf_op jit(solution)/shard_map/ppermute | solution.py:16
  50.4 0.6 collective-permute-start.16
  51.6 1.5 %collective-permute-start.8 = (bf16[1,40,3584]{2,1,0:T(8,128)(2,1)S(1)}, bf16[1,40,3584]{2,1,0:T(8,128)(2,1)S(1)}, u32[]{:S(2)}, u32[]{:S(2)}) collective-permute-start(bf16[1,40,3584]{2,1,0:T(8,128)(2,1)S(1)} %get-tuple-element.5), channel_id=1, source_target_pairs={{0,2},{2,0},{4,6},{6,4},{1,3},{3,1},{5,7},{7,5},{8,10},{10,8},{12,... | collective-permute-start | bytes 860168 | tf_op jit(solution)/shard_map/ppermute | solution.py:16
  53.1 1.5 %collective-permute-start.10 = (bf16[1,40,3584]{2,1,0:T(8,128)(2,1)S(1)}, bf16[1,40,3584]{2,1,0:T(8,128)(2,1)S(1)}, u32[]{:S(2)}, u32[]{:S(2)}) collective-permute-start(bf16[1,40,3584]{2,1,0:T(8,128)(2,1)S(1)} %get-tuple-element.6), channel_id=1, source_target_pairs={{0,6},{2,4},{4,2},{6,0},{1,7},{3,5},{5,3},{7,1},{8,14},{10,12},{12... | collective-permute-start | bytes 860168 | tf_op jit(solution)/shard_map/ppermute | solution.py:16
  54.6 3.6 %collective-permute-done.15 = bf16[1,40,3584]{2,1,0:T(8,128)(2,1)S(1)} collective-permute-done((bf16[1,40,3584]{2,1,0:T(8,128)(2,1)S(1)}, bf16[1,40,3584]{2,1,0:T(8,128)(2,1)S(1)}, u32[]{:S(2)}, u32[]{:S(2)}) %collective-permute-start.15) | collective-permute-done | bytes 286752 | tf_op jit(solution)/shard_map/ppermute | solution.py:16
  58.2 1.4 %collective-permute-start.9 = (bf16[1,40,3584]{2,1,0:T(8,128)(2,1)S(1)}, bf16[1,40,3584]{2,1,0:T(8,128)(2,1)S(1)}, u32[]{:S(2)}, u32[]{:S(2)}) collective-permute-start(bf16[1,40,3584]{2,1,0:T(8,128)(2,1)S(1)} %get-tuple-element.7), channel_id=1, source_target_pairs={{0,4},{2,6},{4,0},{6,2},{1,5},{3,7},{5,1},{7,3},{8,12},{10,14},{12... | collective-permute-start | bytes 860168 | tf_op jit(solution)/shard_map/ppermute | solution.py:16
  59.6 4.8 %collective-permute-done.17 = bf16[1,40,3584]{2,1,0:T(8,128)(2,1)S(1)} collective-permute-done((bf16[1,40,3584]{2,1,0:T(8,128)(2,1)S(1)}, bf16[1,40,3584]{2,1,0:T(8,128)(2,1)S(1)}, u32[]{:S(2)}, u32[]{:S(2)}) %collective-permute-start.17) | collective-permute-done | bytes 286752 | tf_op jit(solution)/shard_map/ppermute | solution.py:16
  64.5 1.4 %collective-permute-start.18 = (bf16[1,40,3584]{2,1,0:T(8,128)(2,1)S(1)}, bf16[1,40,3584]{2,1,0:T(8,128)(2,1)S(1)}, u32[]{:S(2)}, u32[]{:S(2)}) collective-permute-start(bf16[1,40,3584]{2,1,0:T(8,128)(2,1)S(1)} %fusion.17), channel_id=1, source_target_pairs={{0,8},{8,0},{1,9},{9,1},{2,10},{10,2},{3,11},{11,3},{4,12},{12,4},... | collective-permute-start | bytes 860168 | tf_op jit(solution)/shard_map/ppermute | solution.py:12
  65.9 8.8 %collective-permute-done.8 = bf16[1,40,3584]{2,1,0:T(8,128)(2,1)S(1)} collective-permute-done((bf16[1,40,3584]{2,1,0:T(8,128)(2,1)S(1)}, bf16[1,40,3584]{2,1,0:T(8,128)(2,1)S(1)}, u32[]{:S(2)}, u32[]{:S(2)}) %collective-permute-start.8) | collective-permute-done | bytes 286752 | tf_op jit(solution)/shard_map/ppermute | solution.py:16
  74.7 1.9 %collective-permute-done.10 = bf16[1,40,3584]{2,1,0:T(8,128)(2,1)S(1)} collective-permute-done((bf16[1,40,3584]{2,1,0:T(8,128)(2,1)S(1)}, bf16[1,40,3584]{2,1,0:T(8,128)(2,1)S(1)}, u32[]{:S(2)}, u32[]{:S(2)}) %collective-permute-start.10) | collective-permute-done | bytes 286752 | tf_op jit(solution)/shard_map/ppermute | solution.py:16
  76.6 5.1 %collective-permute-done.9 = bf16[1,40,3584]{2,1,0:T(8,128)(2,1)S(1)} collective-permute-done((bf16[1,40,3584]{2,1,0:T(8,128)(2,1)S(1)}, bf16[1,40,3584]{2,1,0:T(8,128)(2,1)S(1)}, u32[]{:S(2)}, u32[]{:S(2)}) %collective-permute-start.9) | collective-permute-done | bytes 286752 | tf_op jit(solution)/shard_map/ppermute | solution.py:16
  82.9 2.1 %collective-permute-done.19 = f32[2,40,3584]{2,1,0:T(8,128)S(1)} collective-permute-done((f32[2,40,3584]{2,1,0:T(8,128)S(1)}, f32[2,40,3584]{2,1,0:T(8,128)S(1)}, u32[]{:S(2)}, u32[]{:S(2)}) %collective-permute-start.19) | collective-permute-done | bytes 1146912 | tf_op jit(solution)/shard_map/ppermute | solution.py:12
  85.1 1.6 %convolution_convert_fusion.5 = bf16[64,3584]{1,0:T(8,128)(2,1)} fusion(f32[64,160]{1,0:T(8,128)S(1)} %select_reduce_fusion, f32[160,3584]{1,0:T(8,128)S(1)} %bitcast.60), kind=kOutput, calls=%fused_computation.13 | convolution fusion | flops 220430336 | bytes 2793472 | tf_op jit(solution)/shard_map/dot_general | solution.py:134
  (58 shorter events, 5.3 us)
Async XLA Ops:
  0.0 1.5 %collective-permute-start = (s32[64,8]{0,1:T(8,128)}, s32[64,8]{0,1:T(8,128)S(1)}, u32[]{:S(2)}, u32[]{:S(2)}) collective-permute-start(s32[64,8]{0,1:T(8,128)} %param.7), channel_id=1, source_target_pairs={{0,1},{1,0},{2,3},{3,2},{4,5},{5,4},{6,7},{7,6},{8,9},{9,8},{10,11... | collective-permute-start | bytes 6152 | tf_op jit(solution)/shard_map/ppermute | solution.py:12
  0.5 2.7 %collective-permute-start.1 = (bf16[64,3584]{1,0:T(8,128)(2,1)}, bf16[64,3584]{1,0:T(8,128)(2,1)S(1)}, u32[]{:S(2)}, u32[]{:S(2)}) collective-permute-start(bf16[64,3584]{1,0:T(8,128)(2,1)} %param.6), channel_id=1, source_target_pairs={{0,1},{1,0},{2,3},{3,2},{4,5},{5,4},{6,7},{7,6},{8,9},{9,8},{10,11... | collective-permute-start | bytes 1376264 | tf_op jit(solution)/shard_map/ppermute | solution.py:12
  3.1 9.1 %copy-start.3 = (bf16[1,160,3584]{2,1,0:T(8,128)(2,1)S(1)}, bf16[1,160,3584]{2,1,0:T(8,128)(2,1)}, u32[]{:S(2)}) copy-start(bf16[1,160,3584]{2,1,0:T(8,128)(2,1)} %param.9) | copy-start | bytes 3440644
  3.1 19.0 %copy-start.4 = (bf16[1,160,3584]{2,1,0:T(8,128)(2,1)S(1)}, bf16[1,160,3584]{2,1,0:T(8,128)(2,1)}, u32[]{:S(2)}) copy-start(bf16[1,160,3584]{2,1,0:T(8,128)(2,1)} %param.10) | copy-start | bytes 3440644
  4.7 17.4 %collective-permute-start.11 = (bf16[1,40,3584]{2,1,0:T(8,128)(2,1)S(1)}, bf16[1,40,3584]{2,1,0:T(8,128)(2,1)S(1)}, u32[]{:S(2)}, u32[]{:S(2)}) collective-permute-start(bf16[1,40,3584]{2,1,0:T(8,128)(2,1)S(1)} %get-tuple-element.13), channel_id=1, source_target_pairs={{0,8},{8,0},{1,9},{9,1},{2,10},{10,2},{3,11},{11,3},{4,12},{12,4},... | collective-permute-start | bytes 860168 | tf_op jit(solution)/shard_map/ppermute | solution.py:12
  8.7 15.7 %collective-permute-start.4 = (bf16[1,40,3584]{2,1,0:T(8,128)(2,1)S(1)}, bf16[1,40,3584]{2,1,0:T(8,128)(2,1)S(1)}, u32[]{:S(2)}, u32[]{:S(2)}) collective-permute-start(bf16[1,40,3584]{2,1,0:T(8,128)(2,1)S(1)} %get-tuple-element.12), channel_id=1, source_target_pairs={{0,6},{2,4},{4,2},{6,0},{1,7},{3,5},{5,3},{7,1},{8,14},{10,12},{12... | collective-permute-start | bytes 860168 | tf_op jit(solution)/shard_map/ppermute | solution.py:16
  11.2 19.3 %collective-permute-start.3 = (bf16[1,40,3584]{2,1,0:T(8,128)(2,1)S(1)}, bf16[1,40,3584]{2,1,0:T(8,128)(2,1)S(1)}, u32[]{:S(2)}, u32[]{:S(2)}) collective-permute-start(bf16[1,40,3584]{2,1,0:T(8,128)(2,1)S(1)} %get-tuple-element.12), channel_id=1, source_target_pairs={{0,4},{2,6},{4,0},{6,2},{1,5},{3,7},{5,1},{7,3},{8,12},{10,14},{12... | collective-permute-start | bytes 860168 | tf_op jit(solution)/shard_map/ppermute | solution.py:16
  11.6 19.1 %collective-permute-start.2 = (bf16[1,40,3584]{2,1,0:T(8,128)(2,1)S(1)}, bf16[1,40,3584]{2,1,0:T(8,128)(2,1)S(1)}, u32[]{:S(2)}, u32[]{:S(2)}) collective-permute-start(bf16[1,40,3584]{2,1,0:T(8,128)(2,1)S(1)} %get-tuple-element.12), channel_id=1, source_target_pairs={{0,2},{2,0},{4,6},{6,4},{1,3},{3,1},{5,7},{7,5},{8,10},{10,8},{12,... | collective-permute-start | bytes 860168 | tf_op jit(solution)/shard_map/ppermute | solution.py:16
  12.2 29.7 %collective-permute-start.5 = (bf16[160,3584]{1,0:T(8,128)(2,1)S(1)}, bf16[160,3584]{1,0:T(8,128)(2,1)S(1)}, u32[]{:S(2)}, u32[]{:S(2)}) collective-permute-start(bf16[160,3584]{1,0:T(8,128)(2,1)S(1)} %bitcast.73), channel_id=1, source_target_pairs={{0,1},{1,0},{2,3},{3,2},{4,5},{5,4},{6,7},{7,6},{8,9},{9,8},{10,11... | collective-permute-start | bytes 3440648 | tf_op jit(solution)/shard_map/ppermute | solution.py:12
  22.1 20.8 %collective-permute-start.6 = (bf16[160,3584]{1,0:T(8,128)(2,1)S(1)}, bf16[160,3584]{1,0:T(8,128)(2,1)S(1)}, u32[]{:S(2)}, u32[]{:S(2)}) collective-permute-start(bf16[160,3584]{1,0:T(8,128)(2,1)S(1)} %bitcast.76), channel_id=1, source_target_pairs={{0,1},{1,0},{2,3},{3,2},{4,5},{5,4},{6,7},{7,6},{8,9},{9,8},{10,11... | collective-permute-start | bytes 3440648 | tf_op jit(solution)/shard_map/ppermute | solution.py:12
  24.4 12.3 %collective-permute-start.14 = (bf16[1,40,3584]{2,1,0:T(8,128)(2,1)S(1)}, bf16[1,40,3584]{2,1,0:T(8,128)(2,1)S(1)}, u32[]{:S(2)}, u32[]{:S(2)}) collective-permute-start(bf16[1,40,3584]{2,1,0:T(8,128)(2,1)S(1)} %collective-permute-done.11), channel_id=1, source_target_pairs={{0,6},{2,4},{4,2},{6,0},{1,7},{3,5},{5,3},{7,1},{8,14},{10,12},{12... | collective-permute-start | bytes 860168 | tf_op jit(solution)/shard_map/ppermute | solution.py:16
  30.5 11.2 %collective-permute-start.13 = (bf16[1,40,3584]{2,1,0:T(8,128)(2,1)S(1)}, bf16[1,40,3584]{2,1,0:T(8,128)(2,1)S(1)}, u32[]{:S(2)}, u32[]{:S(2)}) collective-permute-start(bf16[1,40,3584]{2,1,0:T(8,128)(2,1)S(1)} %collective-permute-done.11), channel_id=1, source_target_pairs={{0,4},{2,6},{4,0},{6,2},{1,5},{3,7},{5,1},{7,3},{8,12},{10,14},{12... | collective-permute-start | bytes 860168 | tf_op jit(solution)/shard_map/ppermute | solution.py:16
  30.8 11.0 %collective-permute-start.12 = (bf16[1,40,3584]{2,1,0:T(8,128)(2,1)S(1)}, bf16[1,40,3584]{2,1,0:T(8,128)(2,1)S(1)}, u32[]{:S(2)}, u32[]{:S(2)}) collective-permute-start(bf16[1,40,3584]{2,1,0:T(8,128)(2,1)S(1)} %collective-permute-done.11), channel_id=1, source_target_pairs={{0,2},{2,0},{4,6},{6,4},{1,3},{3,1},{5,7},{7,5},{8,10},{10,8},{12,... | collective-permute-start | bytes 860168 | tf_op jit(solution)/shard_map/ppermute | solution.py:16
  32.2 4.5 %copy-start = (bf16[1,160,3584]{2,1,0:T(8,128)(2,1)S(1)}, bf16[1,160,3584]{2,1,0:T(8,128)(2,1)}, u32[]{:S(2)}) copy-start(bf16[1,160,3584]{2,1,0:T(8,128)(2,1)} %param.11) | copy-start | bytes 3440644
  36.7 10.1 %collective-permute-start.7 = (bf16[160,3584]{1,0:T(8,128)(2,1)S(1)}, bf16[160,3584]{1,0:T(8,128)(2,1)S(1)}, u32[]{:S(2)}, u32[]{:S(2)}) collective-permute-start(bf16[160,3584]{1,0:T(8,128)(2,1)S(1)} %bitcast.61), channel_id=1, source_target_pairs={{0,1},{1,0},{2,3},{3,2},{4,5},{5,4},{6,7},{7,6},{8,9},{9,8},{10,11... | collective-permute-start | bytes 3440648 | tf_op jit(solution)/shard_map/ppermute | solution.py:12
  47.5 10.7 %collective-permute-start.15 = (bf16[1,40,3584]{2,1,0:T(8,128)(2,1)S(1)}, bf16[1,40,3584]{2,1,0:T(8,128)(2,1)S(1)}, u32[]{:S(2)}, u32[]{:S(2)}) collective-permute-start(bf16[1,40,3584]{2,1,0:T(8,128)(2,1)S(1)} %get-tuple-element.8), channel_id=1, source_target_pairs={{0,6},{2,4},{4,2},{6,0},{1,7},{3,5},{5,3},{7,1},{8,14},{10,12},{12... | collective-permute-start | bytes 860168 | tf_op jit(solution)/shard_map/ppermute | solution.py:16
  49.0 15.4 %collective-permute-start.17 = (bf16[1,40,3584]{2,1,0:T(8,128)(2,1)S(1)}, bf16[1,40,3584]{2,1,0:T(8,128)(2,1)S(1)}, u32[]{:S(2)}, u32[]{:S(2)}) collective-permute-start(bf16[1,40,3584]{2,1,0:T(8,128)(2,1)S(1)} %get-tuple-element.9), channel_id=1, source_target_pairs={{0,2},{2,0},{4,6},{6,4},{1,3},{3,1},{5,7},{7,5},{8,10},{10,8},{12,... | collective-permute-start | bytes 860168 | tf_op jit(solution)/shard_map/ppermute | solution.py:16
  50.4 13.9 %collective-permute-start.16 = (bf16[1,40,3584]{2,1,0:T(8,128)(2,1)S(1)}, bf16[1,40,3584]{2,1,0:T(8,128)(2,1)S(1)}, u32[]{:S(2)}, u32[]{:S(2)}) collective-permute-start(bf16[1,40,3584]{2,1,0:T(8,128)(2,1)S(1)} %get-tuple-element.10), channel_id=1, source_target_pairs={{0,4},{2,6},{4,0},{6,2},{1,5},{3,7},{5,1},{7,3},{8,12},{10,14},{12... | collective-permute-start | bytes 860168 | tf_op jit(solution)/shard_map/ppermute | solution.py:16
  51.6 23.2 %collective-permute-start.8 = (bf16[1,40,3584]{2,1,0:T(8,128)(2,1)S(1)}, bf16[1,40,3584]{2,1,0:T(8,128)(2,1)S(1)}, u32[]{:S(2)}, u32[]{:S(2)}) collective-permute-start(bf16[1,40,3584]{2,1,0:T(8,128)(2,1)S(1)} %get-tuple-element.5), channel_id=1, source_target_pairs={{0,2},{2,0},{4,6},{6,4},{1,3},{3,1},{5,7},{7,5},{8,10},{10,8},{12,... | collective-permute-start | bytes 860168 | tf_op jit(solution)/shard_map/ppermute | solution.py:16
  53.1 23.6 %collective-permute-start.10 = (bf16[1,40,3584]{2,1,0:T(8,128)(2,1)S(1)}, bf16[1,40,3584]{2,1,0:T(8,128)(2,1)S(1)}, u32[]{:S(2)}, u32[]{:S(2)}) collective-permute-start(bf16[1,40,3584]{2,1,0:T(8,128)(2,1)S(1)} %get-tuple-element.6), channel_id=1, source_target_pairs={{0,6},{2,4},{4,2},{6,0},{1,7},{3,5},{5,3},{7,1},{8,14},{10,12},{12... | collective-permute-start | bytes 860168 | tf_op jit(solution)/shard_map/ppermute | solution.py:16
  58.2 23.6 %collective-permute-start.9 = (bf16[1,40,3584]{2,1,0:T(8,128)(2,1)S(1)}, bf16[1,40,3584]{2,1,0:T(8,128)(2,1)S(1)}, u32[]{:S(2)}, u32[]{:S(2)}) collective-permute-start(bf16[1,40,3584]{2,1,0:T(8,128)(2,1)S(1)} %get-tuple-element.7), channel_id=1, source_target_pairs={{0,4},{2,6},{4,0},{6,2},{1,5},{3,7},{5,1},{7,3},{8,12},{10,14},{12... | collective-permute-start | bytes 860168 | tf_op jit(solution)/shard_map/ppermute | solution.py:16
  64.5 17.4 %collective-permute-start.18 = (bf16[1,40,3584]{2,1,0:T(8,128)(2,1)S(1)}, bf16[1,40,3584]{2,1,0:T(8,128)(2,1)S(1)}, u32[]{:S(2)}, u32[]{:S(2)}) collective-permute-start(bf16[1,40,3584]{2,1,0:T(8,128)(2,1)S(1)} %fusion.17), channel_id=1, source_target_pairs={{0,8},{8,0},{1,9},{9,1},{2,10},{10,2},{3,11},{11,3},{4,12},{12,4},... | collective-permute-start | bytes 860168 | tf_op jit(solution)/shard_map/ppermute | solution.py:12
  82.0 0.7 copy-start.1
  82.0 0.7 copy-start.2
  82.1 2.9 %collective-permute-start.19 = (f32[2,40,3584]{2,1,0:T(8,128)S(1)}, f32[2,40,3584]{2,1,0:T(8,128)S(1)}, u32[]{:S(2)}, u32[]{:S(2)}) collective-permute-start(f32[2,40,3584]{2,1,0:T(8,128)S(1)} %pad_maximum_fusion.9), channel_id=1, source_target_pairs={{0,1},{1,0},{2,3},{3,2},{4,5},{5,4},{6,7},{7,6},{8,9},{9,8},{10,11... | collective-permute-start | bytes 3440648 | tf_op jit(solution)/shard_map/ppermute | solution.py:12

commit v19 on v18

--- a/solution.py
+++ b/solution.py
@@ -100,7 +100,8 @@
 
     def group_sum(partial, far_first=True):
         total = partial[0].astype(jnp.float32)
-        for k in range(sharers - 1, 0, -1) if far_first else range(1, sharers):
+        order = list(range(sharers - 1, 0, -1)) if far_first else sorted(range(1, sharers), key=lambda k: k == 2)
+        for k in order:
             total = total + back_exchange(partial[k], k).astype(jnp.float32)
         return total
 

time: 87 us -> 87 us (level)
  starting transfers between devices: 20.3 us -> 18.7 us
  waiting for transfers between devices: 53.7 us -> 55.3 us
    ppermute x12, waiting for transfers between devices: 40.8 us -> 42.4 us  [swap(): return lax.ppermute(x, axis, [(i, i ^ k) for i in range(size)])]
  transfers between devices with their start and end apart: 20 -> 20, of which waited for: 12 -> 13; matrix products, arithmetic and copies ran while one was open for 9% -> 9% of each run, Pallas kernels for 0% -> 0%
where the time goes in v19:
time: 87 us; the launch traced here: 86.8 us
  waiting for transfers between devices  55.3 us (64%)
  starting transfers between devices  18.7 us (21%)
  matrix products  9.06 us (10%)
  other arithmetic  2.48 us (3%)
  local copies, waits for them, and re-layouts  0.99 us (1%)
    ppermute x12, waiting for transfers between devices, swap(): return lax.ppermute(x, axis, [(i, i ^ k) for i in range(size)])  42.4 us
    ppermute x12, starting transfers between devices, swap(): return lax.ppermute(x, axis, [(i, i ^ k) for i in range(size)])  13.5 us
    ppermute x8, waiting for transfers between devices, shift(): return lax.ppermute(x, axis, [(i, (i + k) % size) for i in range(size)])  12.9 us
    ppermute x8, starting transfers between devices, shift(): return lax.ppermute(x, axis, [(i, (i + k) % size) for i in range(size)])  5.21 us
    dot_general x2, matrix products, quarter_rows(): up = lax.dot_general(rows, w_up, dims, preferred_element_type=jnp.float32)  2.01 us
    dot_general x2, matrix products, quarter_rows(): lax.dot_general(rows, w_gate, dims, preferred_element_type=jnp.float32)  2.01 us
    dot_general x4, matrix products, quarter_rows(): jnp.dot(hidden[:, c * slab:(c + 1) * slab], w_down[c * slab:(c + 1) * sla...  1.92 us
  transfers between devices with their start and end apart: 20, of which 13 were waited for; matrix products, arithmetic and copies ran while one was open for 9% of the time, Pallas kernels for 0%

profile of v19, /device:TPU:0, one launch (start us, length us, event | category | flops | bytes accessed | tf_op | source)
XLA Modules:
  0.0 86.8 jit_solution(17383848609130491415)
XLA Ops:
  0.6 0.9 %collective-permute-done = s32[64,8]{0,1:T(8,128)S(1)} collective-permute-done((s32[64,8]{0,1:T(8,128)}, s32[64,8]{0,1:T(8,128)S(1)}, u32[]{:S(2)}, u32[]{:S(2)}) %collective-permute-start) | collective-permute-done | bytes 2080 | tf_op jit(solution)/shard_map/ppermute | solution.py:12
  1.5 0.8 add_select_fusion
  3.2 1.5 %convolution_convert_fusion.4 = bf16[80,3584]{1,0:T(8,128)(2,1)S(1)} fusion(pred[80,128]{1,0:T(8,128)(4,1)S(1)} %fusion.24, bf16[64,3584]{1,0:T(8,128)(2,1)S(1)} %collective-permute-done.1, bf16[64,3584]{1,0:T(8,128)(2,1)} %param.6), kind=kOutput, calls=%fused_computation.12 | convolution fusion | flops 75522048 | bytes 1501184 | tf_op jit(solution)/shard_map/dot_general | solution.py:80
  4.7 4.0 %collective-permute-start.11 = (bf16[1,40,3584]{2,1,0:T(8,128)(2,1)S(1)}, bf16[1,40,3584]{2,1,0:T(8,128)(2,1)S(1)}, u32[]{:S(2)}, u32[]{:S(2)}) collective-permute-start(bf16[1,40,3584]{2,1,0:T(8,128)(2,1)S(1)} %get-tuple-element.13), channel_id=1, source_target_pairs={{0,8},{8,0},{1,9},{9,1},{2,10},{10,2},{3,11},{11,3},{4,12},{12,4},... | collective-permute-start | bytes 860168 | tf_op jit(solution)/shard_map/ppermute | solution.py:12
  8.7 2.5 %collective-permute-start.4 = (bf16[1,40,3584]{2,1,0:T(8,128)(2,1)S(1)}, bf16[1,40,3584]{2,1,0:T(8,128)(2,1)S(1)}, u32[]{:S(2)}, u32[]{:S(2)}) collective-permute-start(bf16[1,40,3584]{2,1,0:T(8,128)(2,1)S(1)} %get-tuple-element.12), channel_id=1, source_target_pairs={{0,6},{2,4},{4,2},{6,0},{1,7},{3,5},{5,3},{7,1},{8,14},{10,12},{12... | collective-permute-start | bytes 860168 | tf_op jit(solution)/shard_map/ppermute | solution.py:16
  11.6 0.5 collective-permute-start.2
  12.2 9.9 %collective-permute-done.11 = bf16[1,40,3584]{2,1,0:T(8,128)(2,1)S(1)} collective-permute-done((bf16[1,40,3584]{2,1,0:T(8,128)(2,1)S(1)}, bf16[1,40,3584]{2,1,0:T(8,128)(2,1)S(1)}, u32[]{:S(2)}, u32[]{:S(2)}) %collective-permute-start.11) | collective-permute-done | bytes 286752 | tf_op jit(solution)/shard_map/ppermute | solution.py:12
  22.1 2.3 %collective-permute-done.4 = bf16[1,40,3584]{2,1,0:T(8,128)(2,1)S(1)} collective-permute-done((bf16[1,40,3584]{2,1,0:T(8,128)(2,1)S(1)}, bf16[1,40,3584]{2,1,0:T(8,128)(2,1)S(1)}, u32[]{:S(2)}, u32[]{:S(2)}) %collective-permute-start.4) | collective-permute-done | bytes 286752 | tf_op jit(solution)/shard_map/ppermute | solution.py:16
  24.4 1.1 %collective-permute-start.14 = (bf16[1,40,3584]{2,1,0:T(8,128)(2,1)S(1)}, bf16[1,40,3584]{2,1,0:T(8,128)(2,1)S(1)}, u32[]{:S(2)}, u32[]{:S(2)}) collective-permute-start(bf16[1,40,3584]{2,1,0:T(8,128)(2,1)S(1)} %collective-permute-done.11), channel_id=1, source_target_pairs={{0,6},{2,4},{4,2},{6,0},{1,7},{3,5},{5,3},{7,1},{8,14},{10,12},{12... | collective-permute-start | bytes 860168 | tf_op jit(solution)/shard_map/ppermute | solution.py:16
  25.5 5.0 %collective-permute-done.3 = bf16[1,40,3584]{2,1,0:T(8,128)(2,1)S(1)} collective-permute-done((bf16[1,40,3584]{2,1,0:T(8,128)(2,1)S(1)}, bf16[1,40,3584]{2,1,0:T(8,128)(2,1)S(1)}, u32[]{:S(2)}, u32[]{:S(2)}) %collective-permute-start.3) | collective-permute-done | bytes 286752 | tf_op jit(solution)/shard_map/ppermute | solution.py:16
  30.8 1.5 %collective-permute-start.12 = (bf16[1,40,3584]{2,1,0:T(8,128)(2,1)S(1)}, bf16[1,40,3584]{2,1,0:T(8,128)(2,1)S(1)}, u32[]{:S(2)}, u32[]{:S(2)}) collective-permute-start(bf16[1,40,3584]{2,1,0:T(8,128)(2,1)S(1)} %collective-permute-done.11), channel_id=1, source_target_pairs={{0,2},{2,0},{4,6},{6,4},{1,3},{3,1},{5,7},{7,5},{8,10},{10,8},{12,... | collective-permute-start | bytes 860168 | tf_op jit(solution)/shard_map/ppermute | solution.py:16
  32.4 4.3 %collective-permute-done.14 = bf16[1,40,3584]{2,1,0:T(8,128)(2,1)S(1)} collective-permute-done((bf16[1,40,3584]{2,1,0:T(8,128)(2,1)S(1)}, bf16[1,40,3584]{2,1,0:T(8,128)(2,1)S(1)}, u32[]{:S(2)}, u32[]{:S(2)}) %collective-permute-start.14) | collective-permute-done | bytes 286752 | tf_op jit(solution)/shard_map/ppermute | solution.py:16
  36.7 5.0 %collective-permute-done.13 = bf16[1,40,3584]{2,1,0:T(8,128)(2,1)S(1)} collective-permute-done((bf16[1,40,3584]{2,1,0:T(8,128)(2,1)S(1)}, bf16[1,40,3584]{2,1,0:T(8,128)(2,1)S(1)}, u32[]{:S(2)}, u32[]{:S(2)}) %collective-permute-start.13) | collective-permute-done | bytes 286752 | tf_op jit(solution)/shard_map/ppermute | solution.py:16
  41.9 1.0 %fusion.11 = f32[160,320]{1,0:T(8,128)S(1)} fusion(bf16[160,3584]{1,0:T(8,128)(2,1)S(1)} %bitcast.62, bf16[160,3584]{1,0:T(8,128)(2,1)S(1)} %collective-permute-done.5, bf16[160,3584]{1,0:T(8,128)(2,1)S(1)} %bitcast.74), kind=kOutput, calls=%fused_computation.20 | convolution fusion | flops 371589120 | bytes 3645440 | tf_op jit(solution)/shard_map/dot_general | solution.py:21
  42.9 1.0 %multiply_convert_fusion.1 = bf16[160,320]{1,0:T(8,128)(2,1)S(1)} fusion(f32[160,320]{1,0:T(8,128)S(1)} %fusion.11, bf16[160,3584]{1,0:T(8,128)(2,1)S(1)} %bitcast.63, bf16[160,3584]{1,0:T(8,128)(2,1)S(1)} %collective-permute-done.6, bf16[160,3584]{1,0:T(8,128)(2,1)S(1)} %bitcast.77), kind=kOutput, calls=%fused_computation.46 | convolution fusion | flops 371896320 | bytes 3747840 | tf_op jit(solution)/shard_map/dot_general | solution.py:22
  43.9 1.0 %fusion.10 = f32[160,320]{1,0:T(8,128)S(1)} fusion(bf16[160,3584]{1,0:T(8,128)(2,1)S(1)} %bitcast.64, bf16[160,3584]{1,0:T(8,128)(2,1)S(1)} %collective-permute-done.5, bf16[160,3584]{1,0:T(8,128)(2,1)S(1)} %bitcast.75), kind=kOutput, calls=%fused_computation.19 | convolution fusion | flops 371589120 | bytes 3645440 | tf_op jit(solution)/shard_map/dot_general | solution.py:21
  45.4 1.0 %multiply_convert_fusion = bf16[160,320]{1,0:T(8,128)(2,1)S(1)} fusion(f32[160,320]{1,0:T(8,128)S(1)} %fusion.10, bf16[160,3584]{1,0:T(8,128)(2,1)S(1)} %bitcast.65, bf16[160,3584]{1,0:T(8,128)(2,1)S(1)} %collective-permute-done.6, bf16[160,3584]{1,0:T(8,128)(2,1)S(1)} %bitcast.78), kind=kOutput, calls=%fused_computation.45 | convolution fusion | flops 371896320 | bytes 3747840 | tf_op jit(solution)/shard_map/dot_general | solution.py:22
  47.5 1.6 %collective-permute-start.15 = (bf16[1,40,3584]{2,1,0:T(8,128)(2,1)S(1)}, bf16[1,40,3584]{2,1,0:T(8,128)(2,1)S(1)}, u32[]{:S(2)}, u32[]{:S(2)}) collective-permute-start(bf16[1,40,3584]{2,1,0:T(8,128)(2,1)S(1)} %get-tuple-element.8), channel_id=1, source_target_pairs={{0,6},{2,4},{4,2},{6,0},{1,7},{3,5},{5,3},{7,1},{8,14},{10,12},{12... | collective-permute-start | bytes 860168 | tf_op jit(solution)/shard_map/ppermute | solution.py:16
  49.0 1.4 %collective-permute-start.17 = (bf16[1,40,3584]{2,1,0:T(8,128)(2,1)S(1)}, bf16[1,40,3584]{2,1,0:T(8,128)(2,1)S(1)}, u32[]{:S(2)}, u32[]{:S(2)}) collective-permute-start(bf16[1,40,3584]{2,1,0:T(8,128)(2,1)S(1)} %get-tuple-element.9), channel_id=1, source_target_pairs={{0,2},{2,0},{4,6},{6,4},{1,3},{3,1},{5,7},{7,5},{8,10},{10,8},{12,... | collective-permute-start | bytes 860168 | tf_op jit(solution)/shard_map/ppermute | solution.py:16
  50.4 0.6 collective-permute-start.16
  51.6 1.5 %collective-permute-start.8 = (bf16[1,40,3584]{2,1,0:T(8,128)(2,1)S(1)}, bf16[1,40,3584]{2,1,0:T(8,128)(2,1)S(1)}, u32[]{:S(2)}, u32[]{:S(2)}) collective-permute-start(bf16[1,40,3584]{2,1,0:T(8,128)(2,1)S(1)} %get-tuple-element.5), channel_id=1, source_target_pairs={{0,2},{2,0},{4,6},{6,4},{1,3},{3,1},{5,7},{7,5},{8,10},{10,8},{12,... | collective-permute-start | bytes 860168 | tf_op jit(solution)/shard_map/ppermute | solution.py:16
  53.1 0.6 collective-permute-start.10
  53.7 4.5 %collective-permute-done.15 = bf16[1,40,3584]{2,1,0:T(8,128)(2,1)S(1)} collective-permute-done((bf16[1,40,3584]{2,1,0:T(8,128)(2,1)S(1)}, bf16[1,40,3584]{2,1,0:T(8,128)(2,1)S(1)}, u32[]{:S(2)}, u32[]{:S(2)}) %collective-permute-start.15) | collective-permute-done | bytes 286752 | tf_op jit(solution)/shard_map/ppermute | solution.py:16
  58.2 1.5 %collective-permute-start.9 = (bf16[1,40,3584]{2,1,0:T(8,128)(2,1)S(1)}, bf16[1,40,3584]{2,1,0:T(8,128)(2,1)S(1)}, u32[]{:S(2)}, u32[]{:S(2)}) collective-permute-start(bf16[1,40,3584]{2,1,0:T(8,128)(2,1)S(1)} %get-tuple-element.7), channel_id=1, source_target_pairs={{0,6},{2,4},{4,2},{6,0},{1,7},{3,5},{5,3},{7,1},{8,14},{10,12},{12... | collective-permute-start | bytes 860168 | tf_op jit(solution)/shard_map/ppermute | solution.py:16
  59.7 3.7 %collective-permute-done.17 = bf16[1,40,3584]{2,1,0:T(8,128)(2,1)S(1)} collective-permute-done((bf16[1,40,3584]{2,1,0:T(8,128)(2,1)S(1)}, bf16[1,40,3584]{2,1,0:T(8,128)(2,1)S(1)}, u32[]{:S(2)}, u32[]{:S(2)}) %collective-permute-start.17) | collective-permute-done | bytes 286752 | tf_op jit(solution)/shard_map/ppermute | solution.py:16
  63.4 0.9 %collective-permute-done.16 = bf16[1,40,3584]{2,1,0:T(8,128)(2,1)S(1)} collective-permute-done((bf16[1,40,3584]{2,1,0:T(8,128)(2,1)S(1)}, bf16[1,40,3584]{2,1,0:T(8,128)(2,1)S(1)}, u32[]{:S(2)}, u32[]{:S(2)}) %collective-permute-start.16) | collective-permute-done | bytes 286752 | tf_op jit(solution)/shard_map/ppermute | solution.py:16
  64.4 0.6 collective-permute-start.18
  65.1 4.4 %collective-permute-done.8 = bf16[1,40,3584]{2,1,0:T(8,128)(2,1)S(1)} collective-permute-done((bf16[1,40,3584]{2,1,0:T(8,128)(2,1)S(1)}, bf16[1,40,3584]{2,1,0:T(8,128)(2,1)S(1)}, u32[]{:S(2)}, u32[]{:S(2)}) %collective-permute-start.8) | collective-permute-done | bytes 286752 | tf_op jit(solution)/shard_map/ppermute | solution.py:16
  69.4 7.1 %collective-permute-done.10 = bf16[1,40,3584]{2,1,0:T(8,128)(2,1)S(1)} collective-permute-done((bf16[1,40,3584]{2,1,0:T(8,128)(2,1)S(1)}, bf16[1,40,3584]{2,1,0:T(8,128)(2,1)S(1)}, u32[]{:S(2)}, u32[]{:S(2)}) %collective-permute-start.10) | collective-permute-done | bytes 286752 | tf_op jit(solution)/shard_map/ppermute | solution.py:16
  76.6 5.2 %collective-permute-done.9 = bf16[1,40,3584]{2,1,0:T(8,128)(2,1)S(1)} collective-permute-done((bf16[1,40,3584]{2,1,0:T(8,128)(2,1)S(1)}, bf16[1,40,3584]{2,1,0:T(8,128)(2,1)S(1)}, u32[]{:S(2)}, u32[]{:S(2)}) %collective-permute-start.9) | collective-permute-done | bytes 286752 | tf_op jit(solution)/shard_map/ppermute | solution.py:16
  82.9 2.1 %collective-permute-done.19 = f32[2,40,3584]{2,1,0:T(8,128)S(1)} collective-permute-done((f32[2,40,3584]{2,1,0:T(8,128)S(1)}, f32[2,40,3584]{2,1,0:T(8,128)S(1)}, u32[]{:S(2)}, u32[]{:S(2)}) %collective-permute-start.19) | collective-permute-done | bytes 1146912 | tf_op jit(solution)/shard_map/ppermute | solution.py:12
  85.1 1.6 %convolution_convert_fusion.5 = bf16[64,3584]{1,0:T(8,128)(2,1)} fusion(f32[64,160]{1,0:T(8,128)S(1)} %select_reduce_fusion, f32[160,3584]{1,0:T(8,128)S(1)} %bitcast.60), kind=kOutput, calls=%fused_computation.13 | convolution fusion | flops 220430336 | bytes 2793472 | tf_op jit(solution)/shard_map/dot_general | solution.py:135
  (58 shorter events, 5.9 us)
Async XLA Ops:
  0.0 1.5 %collective-permute-start = (s32[64,8]{0,1:T(8,128)}, s32[64,8]{0,1:T(8,128)S(1)}, u32[]{:S(2)}, u32[]{:S(2)}) collective-permute-start(s32[64,8]{0,1:T(8,128)} %param.7), channel_id=1, source_target_pairs={{0,1},{1,0},{2,3},{3,2},{4,5},{5,4},{6,7},{7,6},{8,9},{9,8},{10,11... | collective-permute-start | bytes 6152 | tf_op jit(solution)/shard_map/ppermute | solution.py:12
  0.5 2.7 %collective-permute-start.1 = (bf16[64,3584]{1,0:T(8,128)(2,1)}, bf16[64,3584]{1,0:T(8,128)(2,1)S(1)}, u32[]{:S(2)}, u32[]{:S(2)}) collective-permute-start(bf16[64,3584]{1,0:T(8,128)(2,1)} %param.6), channel_id=1, source_target_pairs={{0,1},{1,0},{2,3},{3,2},{4,5},{5,4},{6,7},{7,6},{8,9},{9,8},{10,11... | collective-permute-start | bytes 1376264 | tf_op jit(solution)/shard_map/ppermute | solution.py:12
  3.1 9.1 %copy-start.3 = (bf16[1,160,3584]{2,1,0:T(8,128)(2,1)S(1)}, bf16[1,160,3584]{2,1,0:T(8,128)(2,1)}, u32[]{:S(2)}) copy-start(bf16[1,160,3584]{2,1,0:T(8,128)(2,1)} %param.9) | copy-start | bytes 3440644
  3.1 19.0 %copy-start.4 = (bf16[1,160,3584]{2,1,0:T(8,128)(2,1)S(1)}, bf16[1,160,3584]{2,1,0:T(8,128)(2,1)}, u32[]{:S(2)}) copy-start(bf16[1,160,3584]{2,1,0:T(8,128)(2,1)} %param.10) | copy-start | bytes 3440644
  4.7 17.4 %collective-permute-start.11 = (bf16[1,40,3584]{2,1,0:T(8,128)(2,1)S(1)}, bf16[1,40,3584]{2,1,0:T(8,128)(2,1)S(1)}, u32[]{:S(2)}, u32[]{:S(2)}) collective-permute-start(bf16[1,40,3584]{2,1,0:T(8,128)(2,1)S(1)} %get-tuple-element.13), channel_id=1, source_target_pairs={{0,8},{8,0},{1,9},{9,1},{2,10},{10,2},{3,11},{11,3},{4,12},{12,4},... | collective-permute-start | bytes 860168 | tf_op jit(solution)/shard_map/ppermute | solution.py:12
  8.7 15.7 %collective-permute-start.4 = (bf16[1,40,3584]{2,1,0:T(8,128)(2,1)S(1)}, bf16[1,40,3584]{2,1,0:T(8,128)(2,1)S(1)}, u32[]{:S(2)}, u32[]{:S(2)}) collective-permute-start(bf16[1,40,3584]{2,1,0:T(8,128)(2,1)S(1)} %get-tuple-element.12), channel_id=1, source_target_pairs={{0,6},{2,4},{4,2},{6,0},{1,7},{3,5},{5,3},{7,1},{8,14},{10,12},{12... | collective-permute-start | bytes 860168 | tf_op jit(solution)/shard_map/ppermute | solution.py:16
  11.2 19.3 %collective-permute-start.3 = (bf16[1,40,3584]{2,1,0:T(8,128)(2,1)S(1)}, bf16[1,40,3584]{2,1,0:T(8,128)(2,1)S(1)}, u32[]{:S(2)}, u32[]{:S(2)}) collective-permute-start(bf16[1,40,3584]{2,1,0:T(8,128)(2,1)S(1)} %get-tuple-element.12), channel_id=1, source_target_pairs={{0,4},{2,6},{4,0},{6,2},{1,5},{3,7},{5,1},{7,3},{8,12},{10,14},{12... | collective-permute-start | bytes 860168 | tf_op jit(solution)/shard_map/ppermute | solution.py:16
  11.6 19.1 %collective-permute-start.2 = (bf16[1,40,3584]{2,1,0:T(8,128)(2,1)S(1)}, bf16[1,40,3584]{2,1,0:T(8,128)(2,1)S(1)}, u32[]{:S(2)}, u32[]{:S(2)}) collective-permute-start(bf16[1,40,3584]{2,1,0:T(8,128)(2,1)S(1)} %get-tuple-element.12), channel_id=1, source_target_pairs={{0,2},{2,0},{4,6},{6,4},{1,3},{3,1},{5,7},{7,5},{8,10},{10,8},{12,... | collective-permute-start | bytes 860168 | tf_op jit(solution)/shard_map/ppermute | solution.py:16
  12.2 29.7 %collective-permute-start.5 = (bf16[160,3584]{1,0:T(8,128)(2,1)S(1)}, bf16[160,3584]{1,0:T(8,128)(2,1)S(1)}, u32[]{:S(2)}, u32[]{:S(2)}) collective-permute-start(bf16[160,3584]{1,0:T(8,128)(2,1)S(1)} %bitcast.73), channel_id=1, source_target_pairs={{0,1},{1,0},{2,3},{3,2},{4,5},{5,4},{6,7},{7,6},{8,9},{9,8},{10,11... | collective-permute-start | bytes 3440648 | tf_op jit(solution)/shard_map/ppermute | solution.py:12
  22.1 20.8 %collective-permute-start.6 = (bf16[160,3584]{1,0:T(8,128)(2,1)S(1)}, bf16[160,3584]{1,0:T(8,128)(2,1)S(1)}, u32[]{:S(2)}, u32[]{:S(2)}) collective-permute-start(bf16[160,3584]{1,0:T(8,128)(2,1)S(1)} %bitcast.76), channel_id=1, source_target_pairs={{0,1},{1,0},{2,3},{3,2},{4,5},{5,4},{6,7},{7,6},{8,9},{9,8},{10,11... | collective-permute-start | bytes 3440648 | tf_op jit(solution)/shard_map/ppermute | solution.py:12
  24.4 12.3 %collective-permute-start.14 = (bf16[1,40,3584]{2,1,0:T(8,128)(2,1)S(1)}, bf16[1,40,3584]{2,1,0:T(8,128)(2,1)S(1)}, u32[]{:S(2)}, u32[]{:S(2)}) collective-permute-start(bf16[1,40,3584]{2,1,0:T(8,128)(2,1)S(1)} %collective-permute-done.11), channel_id=1, source_target_pairs={{0,6},{2,4},{4,2},{6,0},{1,7},{3,5},{5,3},{7,1},{8,14},{10,12},{12... | collective-permute-start | bytes 860168 | tf_op jit(solution)/shard_map/ppermute | solution.py:16
  30.5 11.2 %collective-permute-start.13 = (bf16[1,40,3584]{2,1,0:T(8,128)(2,1)S(1)}, bf16[1,40,3584]{2,1,0:T(8,128)(2,1)S(1)}, u32[]{:S(2)}, u32[]{:S(2)}) collective-permute-start(bf16[1,40,3584]{2,1,0:T(8,128)(2,1)S(1)} %collective-permute-done.11), channel_id=1, source_target_pairs={{0,4},{2,6},{4,0},{6,2},{1,5},{3,7},{5,1},{7,3},{8,12},{10,14},{12... | collective-permute-start | bytes 860168 | tf_op jit(solution)/shard_map/ppermute | solution.py:16
  30.8 11.0 %collective-permute-start.12 = (bf16[1,40,3584]{2,1,0:T(8,128)(2,1)S(1)}, bf16[1,40,3584]{2,1,0:T(8,128)(2,1)S(1)}, u32[]{:S(2)}, u32[]{:S(2)}) collective-permute-start(bf16[1,40,3584]{2,1,0:T(8,128)(2,1)S(1)} %collective-permute-done.11), channel_id=1, source_target_pairs={{0,2},{2,0},{4,6},{6,4},{1,3},{3,1},{5,7},{7,5},{8,10},{10,8},{12,... | collective-permute-start | bytes 860168 | tf_op jit(solution)/shard_map/ppermute | solution.py:16
  32.2 4.5 %copy-start = (bf16[1,160,3584]{2,1,0:T(8,128)(2,1)S(1)}, bf16[1,160,3584]{2,1,0:T(8,128)(2,1)}, u32[]{:S(2)}) copy-start(bf16[1,160,3584]{2,1,0:T(8,128)(2,1)} %param.11) | copy-start | bytes 3440644
  36.7 10.1 %collective-permute-start.7 = (bf16[160,3584]{1,0:T(8,128)(2,1)S(1)}, bf16[160,3584]{1,0:T(8,128)(2,1)S(1)}, u32[]{:S(2)}, u32[]{:S(2)}) collective-permute-start(bf16[160,3584]{1,0:T(8,128)(2,1)S(1)} %bitcast.61), channel_id=1, source_target_pairs={{0,1},{1,0},{2,3},{3,2},{4,5},{5,4},{6,7},{7,6},{8,9},{9,8},{10,11... | collective-permute-start | bytes 3440648 | tf_op jit(solution)/shard_map/ppermute | solution.py:12
  47.5 10.7 %collective-permute-start.15 = (bf16[1,40,3584]{2,1,0:T(8,128)(2,1)S(1)}, bf16[1,40,3584]{2,1,0:T(8,128)(2,1)S(1)}, u32[]{:S(2)}, u32[]{:S(2)}) collective-permute-start(bf16[1,40,3584]{2,1,0:T(8,128)(2,1)S(1)} %get-tuple-element.8), channel_id=1, source_target_pairs={{0,6},{2,4},{4,2},{6,0},{1,7},{3,5},{5,3},{7,1},{8,14},{10,12},{12... | collective-permute-start | bytes 860168 | tf_op jit(solution)/shard_map/ppermute | solution.py:16
  49.0 14.4 %collective-permute-start.17 = (bf16[1,40,3584]{2,1,0:T(8,128)(2,1)S(1)}, bf16[1,40,3584]{2,1,0:T(8,128)(2,1)S(1)}, u32[]{:S(2)}, u32[]{:S(2)}) collective-permute-start(bf16[1,40,3584]{2,1,0:T(8,128)(2,1)S(1)} %get-tuple-element.9), channel_id=1, source_target_pairs={{0,2},{2,0},{4,6},{6,4},{1,3},{3,1},{5,7},{7,5},{8,10},{10,8},{12,... | collective-permute-start | bytes 860168 | tf_op jit(solution)/shard_map/ppermute | solution.py:16
  50.4 13.8 %collective-permute-start.16 = (bf16[1,40,3584]{2,1,0:T(8,128)(2,1)S(1)}, bf16[1,40,3584]{2,1,0:T(8,128)(2,1)S(1)}, u32[]{:S(2)}, u32[]{:S(2)}) collective-permute-start(bf16[1,40,3584]{2,1,0:T(8,128)(2,1)S(1)} %get-tuple-element.10), channel_id=1, source_target_pairs={{0,4},{2,6},{4,0},{6,2},{1,5},{3,7},{5,1},{7,3},{8,12},{10,14},{12... | collective-permute-start | bytes 860168 | tf_op jit(solution)/shard_map/ppermute | solution.py:16
  51.6 17.8 %collective-permute-start.8 = (bf16[1,40,3584]{2,1,0:T(8,128)(2,1)S(1)}, bf16[1,40,3584]{2,1,0:T(8,128)(2,1)S(1)}, u32[]{:S(2)}, u32[]{:S(2)}) collective-permute-start(bf16[1,40,3584]{2,1,0:T(8,128)(2,1)S(1)} %get-tuple-element.5), channel_id=1, source_target_pairs={{0,2},{2,0},{4,6},{6,4},{1,3},{3,1},{5,7},{7,5},{8,10},{10,8},{12,... | collective-permute-start | bytes 860168 | tf_op jit(solution)/shard_map/ppermute | solution.py:16
  53.1 23.5 %collective-permute-start.10 = (bf16[1,40,3584]{2,1,0:T(8,128)(2,1)S(1)}, bf16[1,40,3584]{2,1,0:T(8,128)(2,1)S(1)}, u32[]{:S(2)}, u32[]{:S(2)}) collective-permute-start(bf16[1,40,3584]{2,1,0:T(8,128)(2,1)S(1)} %get-tuple-element.6), channel_id=1, source_target_pairs={{0,4},{2,6},{4,0},{6,2},{1,5},{3,7},{5,1},{7,3},{8,12},{10,14},{12... | collective-permute-start | bytes 860168 | tf_op jit(solution)/shard_map/ppermute | solution.py:16
  58.2 23.6 %collective-permute-start.9 = (bf16[1,40,3584]{2,1,0:T(8,128)(2,1)S(1)}, bf16[1,40,3584]{2,1,0:T(8,128)(2,1)S(1)}, u32[]{:S(2)}, u32[]{:S(2)}) collective-permute-start(bf16[1,40,3584]{2,1,0:T(8,128)(2,1)S(1)} %get-tuple-element.7), channel_id=1, source_target_pairs={{0,6},{2,4},{4,2},{6,0},{1,7},{3,5},{5,3},{7,1},{8,14},{10,12},{12... | collective-permute-start | bytes 860168 | tf_op jit(solution)/shard_map/ppermute | solution.py:16
  64.4 17.5 %collective-permute-start.18 = (bf16[1,40,3584]{2,1,0:T(8,128)(2,1)S(1)}, bf16[1,40,3584]{2,1,0:T(8,128)(2,1)S(1)}, u32[]{:S(2)}, u32[]{:S(2)}) collective-permute-start(bf16[1,40,3584]{2,1,0:T(8,128)(2,1)S(1)} %fusion.17), channel_id=1, source_target_pairs={{0,8},{8,0},{1,9},{9,1},{2,10},{10,2},{3,11},{11,3},{4,12},{12,4},... | collective-permute-start | bytes 860168 | tf_op jit(solution)/shard_map/ppermute | solution.py:12
  82.0 0.7 copy-start.1
  82.0 0.7 copy-start.2
  82.1 2.9 %collective-permute-start.19 = (f32[2,40,3584]{2,1,0:T(8,128)S(1)}, f32[2,40,3584]{2,1,0:T(8,128)S(1)}, u32[]{:S(2)}, u32[]{:S(2)}) collective-permute-start(f32[2,40,3584]{2,1,0:T(8,128)S(1)} %pad_maximum_fusion.9), channel_id=1, source_target_pairs={{0,1},{1,0},{2,3},{3,2},{4,5},{5,4},{6,7},{7,6},{8,9},{9,8},{10,11... | collective-permute-start | bytes 3440648 | tf_op jit(solution)/shard_map/ppermute | solution.py:12

commit v20 on v18

--- a/solution.py
+++ b/solution.py
@@ -100,7 +100,7 @@
 
     def group_sum(partial, far_first=True):
         total = partial[0].astype(jnp.float32)
-        for k in range(sharers - 1, 0, -1) if far_first else range(1, sharers):
+        for k in sorted(range(1, sharers), key=lambda k: (k == 2, -k)) if far_first else range(1, sharers):
             total = total + back_exchange(partial[k], k).astype(jnp.float32)
         return total
 

time: 87 us -> 87 us (level)
  transfers between devices with their start and end apart: 20 -> 20, of which waited for: 12 -> 13; matrix products, arithmetic and copies ran while one was open for 9% -> 9% of each run, Pallas kernels for 0% -> 0%
where the time goes in v20:
time: 87 us; the launch traced here: 86.8 us
  waiting for transfers between devices  53.7 us (62%)
  starting transfers between devices  20.3 us (23%)
  matrix products  9.06 us (10%)
  other arithmetic  2.48 us (3%)
  local copies, waits for them, and re-layouts  0.99 us (1%)
    ppermute x12, waiting for transfers between devices, swap(): return lax.ppermute(x, axis, [(i, i ^ k) for i in range(size)])  40.9 us
    ppermute x12, starting transfers between devices, swap(): return lax.ppermute(x, axis, [(i, i ^ k) for i in range(size)])  14.3 us
    ppermute x8, waiting for transfers between devices, shift(): return lax.ppermute(x, axis, [(i, (i + k) % size) for i in range(size)])  12.9 us
    ppermute x8, starting transfers between devices, shift(): return lax.ppermute(x, axis, [(i, (i + k) % size) for i in range(size)])  5.98 us
    dot_general x2, matrix products, quarter_rows(): up = lax.dot_general(rows, w_up, dims, preferred_element_type=jnp.float32)  2.01 us
    dot_general x2, matrix products, quarter_rows(): lax.dot_general(rows, w_gate, dims, preferred_element_type=jnp.float32)  2.01 us
    dot_general x4, matrix products, quarter_rows(): jnp.dot(hidden[:, c * slab:(c + 1) * slab], w_down[c * slab:(c + 1) * sla...  1.92 us
  transfers between devices with their start and end apart: 20, of which 13 were waited for; matrix products, arithmetic and copies ran while one was open for 9% of the time, Pallas kernels for 0%

profile of v20, /device:TPU:0, one launch (start us, length us, event | category | flops | bytes accessed | tf_op | source)
XLA Modules:
  0.0 86.8 jit_solution(17784993100832172958)
XLA Ops:
  0.6 0.9 %collective-permute-done = s32[64,8]{0,1:T(8,128)S(1)} collective-permute-done((s32[64,8]{0,1:T(8,128)}, s32[64,8]{0,1:T(8,128)S(1)}, u32[]{:S(2)}, u32[]{:S(2)}) %collective-permute-start) | collective-permute-done | bytes 2080 | tf_op jit(solution)/shard_map/ppermute | solution.py:12
  1.5 0.8 add_select_fusion
  3.2 1.5 %convolution_convert_fusion.4 = bf16[80,3584]{1,0:T(8,128)(2,1)S(1)} fusion(pred[80,128]{1,0:T(8,128)(4,1)S(1)} %fusion.24, bf16[64,3584]{1,0:T(8,128)(2,1)S(1)} %collective-permute-done.1, bf16[64,3584]{1,0:T(8,128)(2,1)} %param.6), kind=kOutput, calls=%fused_computation.12 | convolution fusion | flops 75522048 | bytes 1501184 | tf_op jit(solution)/shard_map/dot_general | solution.py:80
  4.7 4.0 %collective-permute-start.11 = (bf16[1,40,3584]{2,1,0:T(8,128)(2,1)S(1)}, bf16[1,40,3584]{2,1,0:T(8,128)(2,1)S(1)}, u32[]{:S(2)}, u32[]{:S(2)}) collective-permute-start(bf16[1,40,3584]{2,1,0:T(8,128)(2,1)S(1)} %get-tuple-element.13), channel_id=1, source_target_pairs={{0,8},{8,0},{1,9},{9,1},{2,10},{10,2},{3,11},{11,3},{4,12},{12,4},... | collective-permute-start | bytes 860168 | tf_op jit(solution)/shard_map/ppermute | solution.py:12
  8.7 2.5 %collective-permute-start.4 = (bf16[1,40,3584]{2,1,0:T(8,128)(2,1)S(1)}, bf16[1,40,3584]{2,1,0:T(8,128)(2,1)S(1)}, u32[]{:S(2)}, u32[]{:S(2)}) collective-permute-start(bf16[1,40,3584]{2,1,0:T(8,128)(2,1)S(1)} %get-tuple-element.12), channel_id=1, source_target_pairs={{0,6},{2,4},{4,2},{6,0},{1,7},{3,5},{5,3},{7,1},{8,14},{10,12},{12... | collective-permute-start | bytes 860168 | tf_op jit(solution)/shard_map/ppermute | solution.py:16
  11.6 0.5 collective-permute-start.2
  12.2 9.9 %collective-permute-done.11 = bf16[1,40,3584]{2,1,0:T(8,128)(2,1)S(1)} collective-permute-done((bf16[1,40,3584]{2,1,0:T(8,128)(2,1)S(1)}, bf16[1,40,3584]{2,1,0:T(8,128)(2,1)S(1)}, u32[]{:S(2)}, u32[]{:S(2)}) %collective-permute-start.11) | collective-permute-done | bytes 286752 | tf_op jit(solution)/shard_map/ppermute | solution.py:12
  22.1 2.3 %collective-permute-done.4 = bf16[1,40,3584]{2,1,0:T(8,128)(2,1)S(1)} collective-permute-done((bf16[1,40,3584]{2,1,0:T(8,128)(2,1)S(1)}, bf16[1,40,3584]{2,1,0:T(8,128)(2,1)S(1)}, u32[]{:S(2)}, u32[]{:S(2)}) %collective-permute-start.4) | collective-permute-done | bytes 286752 | tf_op jit(solution)/shard_map/ppermute | solution.py:16
  24.4 1.1 %collective-permute-start.14 = (bf16[1,40,3584]{2,1,0:T(8,128)(2,1)S(1)}, bf16[1,40,3584]{2,1,0:T(8,128)(2,1)S(1)}, u32[]{:S(2)}, u32[]{:S(2)}) collective-permute-start(bf16[1,40,3584]{2,1,0:T(8,128)(2,1)S(1)} %collective-permute-done.11), channel_id=1, source_target_pairs={{0,6},{2,4},{4,2},{6,0},{1,7},{3,5},{5,3},{7,1},{8,14},{10,12},{12... | collective-permute-start | bytes 860168 | tf_op jit(solution)/shard_map/ppermute | solution.py:16
  25.5 5.0 %collective-permute-done.3 = bf16[1,40,3584]{2,1,0:T(8,128)(2,1)S(1)} collective-permute-done((bf16[1,40,3584]{2,1,0:T(8,128)(2,1)S(1)}, bf16[1,40,3584]{2,1,0:T(8,128)(2,1)S(1)}, u32[]{:S(2)}, u32[]{:S(2)}) %collective-permute-start.3) | collective-permute-done | bytes 286752 | tf_op jit(solution)/shard_map/ppermute | solution.py:16
  30.8 1.5 %collective-permute-start.12 = (bf16[1,40,3584]{2,1,0:T(8,128)(2,1)S(1)}, bf16[1,40,3584]{2,1,0:T(8,128)(2,1)S(1)}, u32[]{:S(2)}, u32[]{:S(2)}) collective-permute-start(bf16[1,40,3584]{2,1,0:T(8,128)(2,1)S(1)} %collective-permute-done.11), channel_id=1, source_target_pairs={{0,2},{2,0},{4,6},{6,4},{1,3},{3,1},{5,7},{7,5},{8,10},{10,8},{12,... | collective-permute-start | bytes 860168 | tf_op jit(solution)/shard_map/ppermute | solution.py:16
  32.4 4.3 %collective-permute-done.14 = bf16[1,40,3584]{2,1,0:T(8,128)(2,1)S(1)} collective-permute-done((bf16[1,40,3584]{2,1,0:T(8,128)(2,1)S(1)}, bf16[1,40,3584]{2,1,0:T(8,128)(2,1)S(1)}, u32[]{:S(2)}, u32[]{:S(2)}) %collective-permute-start.14) | collective-permute-done | bytes 286752 | tf_op jit(solution)/shard_map/ppermute | solution.py:16
  36.7 5.0 %collective-permute-done.13 = bf16[1,40,3584]{2,1,0:T(8,128)(2,1)S(1)} collective-permute-done((bf16[1,40,3584]{2,1,0:T(8,128)(2,1)S(1)}, bf16[1,40,3584]{2,1,0:T(8,128)(2,1)S(1)}, u32[]{:S(2)}, u32[]{:S(2)}) %collective-permute-start.13) | collective-permute-done | bytes 286752 | tf_op jit(solution)/shard_map/ppermute | solution.py:16
  41.9 1.0 %fusion.11 = f32[160,320]{1,0:T(8,128)S(1)} fusion(bf16[160,3584]{1,0:T(8,128)(2,1)S(1)} %bitcast.62, bf16[160,3584]{1,0:T(8,128)(2,1)S(1)} %collective-permute-done.5, bf16[160,3584]{1,0:T(8,128)(2,1)S(1)} %bitcast.74), kind=kOutput, calls=%fused_computation.20 | convolution fusion | flops 371589120 | bytes 3645440 | tf_op jit(solution)/shard_map/dot_general | solution.py:21
  42.9 1.0 %multiply_convert_fusion.1 = bf16[160,320]{1,0:T(8,128)(2,1)S(1)} fusion(f32[160,320]{1,0:T(8,128)S(1)} %fusion.11, bf16[160,3584]{1,0:T(8,128)(2,1)S(1)} %bitcast.63, bf16[160,3584]{1,0:T(8,128)(2,1)S(1)} %collective-permute-done.6, bf16[160,3584]{1,0:T(8,128)(2,1)S(1)} %bitcast.77), kind=kOutput, calls=%fused_computation.46 | convolution fusion | flops 371896320 | bytes 3747840 | tf_op jit(solution)/shard_map/dot_general | solution.py:22
  43.9 1.0 %fusion.10 = f32[160,320]{1,0:T(8,128)S(1)} fusion(bf16[160,3584]{1,0:T(8,128)(2,1)S(1)} %bitcast.64, bf16[160,3584]{1,0:T(8,128)(2,1)S(1)} %collective-permute-done.5, bf16[160,3584]{1,0:T(8,128)(2,1)S(1)} %bitcast.75), kind=kOutput, calls=%fused_computation.19 | convolution fusion | flops 371589120 | bytes 3645440 | tf_op jit(solution)/shard_map/dot_general | solution.py:21
  45.4 1.0 %multiply_convert_fusion = bf16[160,320]{1,0:T(8,128)(2,1)S(1)} fusion(f32[160,320]{1,0:T(8,128)S(1)} %fusion.10, bf16[160,3584]{1,0:T(8,128)(2,1)S(1)} %bitcast.65, bf16[160,3584]{1,0:T(8,128)(2,1)S(1)} %collective-permute-done.6, bf16[160,3584]{1,0:T(8,128)(2,1)S(1)} %bitcast.78), kind=kOutput, calls=%fused_computation.45 | convolution fusion | flops 371896320 | bytes 3747840 | tf_op jit(solution)/shard_map/dot_general | solution.py:22
  46.9 0.5 fusion.2
  47.5 1.6 %collective-permute-start.15 = (bf16[1,40,3584]{2,1,0:T(8,128)(2,1)S(1)}, bf16[1,40,3584]{2,1,0:T(8,128)(2,1)S(1)}, u32[]{:S(2)}, u32[]{:S(2)}) collective-permute-start(bf16[1,40,3584]{2,1,0:T(8,128)(2,1)S(1)} %get-tuple-element.8), channel_id=1, source_target_pairs={{0,6},{2,4},{4,2},{6,0},{1,7},{3,5},{5,3},{7,1},{8,14},{10,12},{12... | collective-permute-start | bytes 860168 | tf_op jit(solution)/shard_map/ppermute | solution.py:16
  49.0 1.4 %collective-permute-start.17 = (bf16[1,40,3584]{2,1,0:T(8,128)(2,1)S(1)}, bf16[1,40,3584]{2,1,0:T(8,128)(2,1)S(1)}, u32[]{:S(2)}, u32[]{:S(2)}) collective-permute-start(bf16[1,40,3584]{2,1,0:T(8,128)(2,1)S(1)} %get-tuple-element.9), channel_id=1, source_target_pairs={{0,4},{2,6},{4,0},{6,2},{1,5},{3,7},{5,1},{7,3},{8,12},{10,14},{12... | collective-permute-start | bytes 860168 | tf_op jit(solution)/shard_map/ppermute | solution.py:16
  50.4 0.6 collective-permute-start.16
  51.6 1.5 %collective-permute-start.8 = (bf16[1,40,3584]{2,1,0:T(8,128)(2,1)S(1)}, bf16[1,40,3584]{2,1,0:T(8,128)(2,1)S(1)}, u32[]{:S(2)}, u32[]{:S(2)}) collective-permute-start(bf16[1,40,3584]{2,1,0:T(8,128)(2,1)S(1)} %get-tuple-element.5), channel_id=1, source_target_pairs={{0,2},{2,0},{4,6},{6,4},{1,3},{3,1},{5,7},{7,5},{8,10},{10,8},{12,... | collective-permute-start | bytes 860168 | tf_op jit(solution)/shard_map/ppermute | solution.py:16
  53.1 1.5 %collective-permute-start.10 = (bf16[1,40,3584]{2,1,0:T(8,128)(2,1)S(1)}, bf16[1,40,3584]{2,1,0:T(8,128)(2,1)S(1)}, u32[]{:S(2)}, u32[]{:S(2)}) collective-permute-start(bf16[1,40,3584]{2,1,0:T(8,128)(2,1)S(1)} %get-tuple-element.6), channel_id=1, source_target_pairs={{0,6},{2,4},{4,2},{6,0},{1,7},{3,5},{5,3},{7,1},{8,14},{10,12},{12... | collective-permute-start | bytes 860168 | tf_op jit(solution)/shard_map/ppermute | solution.py:16
  54.6 3.6 %collective-permute-done.15 = bf16[1,40,3584]{2,1,0:T(8,128)(2,1)S(1)} collective-permute-done((bf16[1,40,3584]{2,1,0:T(8,128)(2,1)S(1)}, bf16[1,40,3584]{2,1,0:T(8,128)(2,1)S(1)}, u32[]{:S(2)}, u32[]{:S(2)}) %collective-permute-start.15) | collective-permute-done | bytes 286752 | tf_op jit(solution)/shard_map/ppermute | solution.py:16
  58.2 1.4 %collective-permute-start.9 = (bf16[1,40,3584]{2,1,0:T(8,128)(2,1)S(1)}, bf16[1,40,3584]{2,1,0:T(8,128)(2,1)S(1)}, u32[]{:S(2)}, u32[]{:S(2)}) collective-permute-start(bf16[1,40,3584]{2,1,0:T(8,128)(2,1)S(1)} %get-tuple-element.7), channel_id=1, source_target_pairs={{0,4},{2,6},{4,0},{6,2},{1,5},{3,7},{5,1},{7,3},{8,12},{10,14},{12... | collective-permute-start | bytes 860168 | tf_op jit(solution)/shard_map/ppermute | solution.py:16
  59.6 4.7 %collective-permute-done.17 = bf16[1,40,3584]{2,1,0:T(8,128)(2,1)S(1)} collective-permute-done((bf16[1,40,3584]{2,1,0:T(8,128)(2,1)S(1)}, bf16[1,40,3584]{2,1,0:T(8,128)(2,1)S(1)}, u32[]{:S(2)}, u32[]{:S(2)}) %collective-permute-start.17) | collective-permute-done | bytes 286752 | tf_op jit(solution)/shard_map/ppermute | solution.py:16
  64.5 1.4 %collective-permute-start.18 = (bf16[1,40,3584]{2,1,0:T(8,128)(2,1)S(1)}, bf16[1,40,3584]{2,1,0:T(8,128)(2,1)S(1)}, u32[]{:S(2)}, u32[]{:S(2)}) collective-permute-start(bf16[1,40,3584]{2,1,0:T(8,128)(2,1)S(1)} %fusion.17), channel_id=1, source_target_pairs={{0,8},{8,0},{1,9},{9,1},{2,10},{10,2},{3,11},{11,3},{4,12},{12,4},... | collective-permute-start | bytes 860168 | tf_op jit(solution)/shard_map/ppermute | solution.py:12
  65.9 8.8 %collective-permute-done.8 = bf16[1,40,3584]{2,1,0:T(8,128)(2,1)S(1)} collective-permute-done((bf16[1,40,3584]{2,1,0:T(8,128)(2,1)S(1)}, bf16[1,40,3584]{2,1,0:T(8,128)(2,1)S(1)}, u32[]{:S(2)}, u32[]{:S(2)}) %collective-permute-start.8) | collective-permute-done | bytes 286752 | tf_op jit(solution)/shard_map/ppermute | solution.py:16
  74.7 1.9 %collective-permute-done.10 = bf16[1,40,3584]{2,1,0:T(8,128)(2,1)S(1)} collective-permute-done((bf16[1,40,3584]{2,1,0:T(8,128)(2,1)S(1)}, bf16[1,40,3584]{2,1,0:T(8,128)(2,1)S(1)}, u32[]{:S(2)}, u32[]{:S(2)}) %collective-permute-start.10) | collective-permute-done | bytes 286752 | tf_op jit(solution)/shard_map/ppermute | solution.py:16
  76.6 5.1 %collective-permute-done.9 = bf16[1,40,3584]{2,1,0:T(8,128)(2,1)S(1)} collective-permute-done((bf16[1,40,3584]{2,1,0:T(8,128)(2,1)S(1)}, bf16[1,40,3584]{2,1,0:T(8,128)(2,1)S(1)}, u32[]{:S(2)}, u32[]{:S(2)}) %collective-permute-start.9) | collective-permute-done | bytes 286752 | tf_op jit(solution)/shard_map/ppermute | solution.py:16
  82.9 2.1 %collective-permute-done.19 = f32[2,40,3584]{2,1,0:T(8,128)S(1)} collective-permute-done((f32[2,40,3584]{2,1,0:T(8,128)S(1)}, f32[2,40,3584]{2,1,0:T(8,128)S(1)}, u32[]{:S(2)}, u32[]{:S(2)}) %collective-permute-start.19) | collective-permute-done | bytes 1146912 | tf_op jit(solution)/shard_map/ppermute | solution.py:12
  85.1 1.6 %convolution_convert_fusion.5 = bf16[64,3584]{1,0:T(8,128)(2,1)} fusion(f32[64,160]{1,0:T(8,128)S(1)} %select_reduce_fusion, f32[160,3584]{1,0:T(8,128)S(1)} %bitcast.60), kind=kOutput, calls=%fused_computation.13 | convolution fusion | flops 220430336 | bytes 2793472 | tf_op jit(solution)/shard_map/dot_general | solution.py:134
  (58 shorter events, 5.4 us)
Async XLA Ops:
  0.0 1.5 %collective-permute-start = (s32[64,8]{0,1:T(8,128)}, s32[64,8]{0,1:T(8,128)S(1)}, u32[]{:S(2)}, u32[]{:S(2)}) collective-permute-start(s32[64,8]{0,1:T(8,128)} %param.7), channel_id=1, source_target_pairs={{0,1},{1,0},{2,3},{3,2},{4,5},{5,4},{6,7},{7,6},{8,9},{9,8},{10,11... | collective-permute-start | bytes 6152 | tf_op jit(solution)/shard_map/ppermute | solution.py:12
  0.5 2.7 %collective-permute-start.1 = (bf16[64,3584]{1,0:T(8,128)(2,1)}, bf16[64,3584]{1,0:T(8,128)(2,1)S(1)}, u32[]{:S(2)}, u32[]{:S(2)}) collective-permute-start(bf16[64,3584]{1,0:T(8,128)(2,1)} %param.6), channel_id=1, source_target_pairs={{0,1},{1,0},{2,3},{3,2},{4,5},{5,4},{6,7},{7,6},{8,9},{9,8},{10,11... | collective-permute-start | bytes 1376264 | tf_op jit(solution)/shard_map/ppermute | solution.py:12
  3.1 9.1 %copy-start.3 = (bf16[1,160,3584]{2,1,0:T(8,128)(2,1)S(1)}, bf16[1,160,3584]{2,1,0:T(8,128)(2,1)}, u32[]{:S(2)}) copy-start(bf16[1,160,3584]{2,1,0:T(8,128)(2,1)} %param.9) | copy-start | bytes 3440644
  3.1 19.0 %copy-start.4 = (bf16[1,160,3584]{2,1,0:T(8,128)(2,1)S(1)}, bf16[1,160,3584]{2,1,0:T(8,128)(2,1)}, u32[]{:S(2)}) copy-start(bf16[1,160,3584]{2,1,0:T(8,128)(2,1)} %param.10) | copy-start | bytes 3440644
  4.7 17.4 %collective-permute-start.11 = (bf16[1,40,3584]{2,1,0:T(8,128)(2,1)S(1)}, bf16[1,40,3584]{2,1,0:T(8,128)(2,1)S(1)}, u32[]{:S(2)}, u32[]{:S(2)}) collective-permute-start(bf16[1,40,3584]{2,1,0:T(8,128)(2,1)S(1)} %get-tuple-element.13), channel_id=1, source_target_pairs={{0,8},{8,0},{1,9},{9,1},{2,10},{10,2},{3,11},{11,3},{4,12},{12,4},... | collective-permute-start | bytes 860168 | tf_op jit(solution)/shard_map/ppermute | solution.py:12
  8.7 15.7 %collective-permute-start.4 = (bf16[1,40,3584]{2,1,0:T(8,128)(2,1)S(1)}, bf16[1,40,3584]{2,1,0:T(8,128)(2,1)S(1)}, u32[]{:S(2)}, u32[]{:S(2)}) collective-permute-start(bf16[1,40,3584]{2,1,0:T(8,128)(2,1)S(1)} %get-tuple-element.12), channel_id=1, source_target_pairs={{0,6},{2,4},{4,2},{6,0},{1,7},{3,5},{5,3},{7,1},{8,14},{10,12},{12... | collective-permute-start | bytes 860168 | tf_op jit(solution)/shard_map/ppermute | solution.py:16
  11.2 19.3 %collective-permute-start.3 = (bf16[1,40,3584]{2,1,0:T(8,128)(2,1)S(1)}, bf16[1,40,3584]{2,1,0:T(8,128)(2,1)S(1)}, u32[]{:S(2)}, u32[]{:S(2)}) collective-permute-start(bf16[1,40,3584]{2,1,0:T(8,128)(2,1)S(1)} %get-tuple-element.12), channel_id=1, source_target_pairs={{0,4},{2,6},{4,0},{6,2},{1,5},{3,7},{5,1},{7,3},{8,12},{10,14},{12... | collective-permute-start | bytes 860168 | tf_op jit(solution)/shard_map/ppermute | solution.py:16
  11.6 19.1 %collective-permute-start.2 = (bf16[1,40,3584]{2,1,0:T(8,128)(2,1)S(1)}, bf16[1,40,3584]{2,1,0:T(8,128)(2,1)S(1)}, u32[]{:S(2)}, u32[]{:S(2)}) collective-permute-start(bf16[1,40,3584]{2,1,0:T(8,128)(2,1)S(1)} %get-tuple-element.12), channel_id=1, source_target_pairs={{0,2},{2,0},{4,6},{6,4},{1,3},{3,1},{5,7},{7,5},{8,10},{10,8},{12,... | collective-permute-start | bytes 860168 | tf_op jit(solution)/shard_map/ppermute | solution.py:16
  12.2 29.7 %collective-permute-start.5 = (bf16[160,3584]{1,0:T(8,128)(2,1)S(1)}, bf16[160,3584]{1,0:T(8,128)(2,1)S(1)}, u32[]{:S(2)}, u32[]{:S(2)}) collective-permute-start(bf16[160,3584]{1,0:T(8,128)(2,1)S(1)} %bitcast.73), channel_id=1, source_target_pairs={{0,1},{1,0},{2,3},{3,2},{4,5},{5,4},{6,7},{7,6},{8,9},{9,8},{10,11... | collective-permute-start | bytes 3440648 | tf_op jit(solution)/shard_map/ppermute | solution.py:12
  22.1 20.8 %collective-permute-start.6 = (bf16[160,3584]{1,0:T(8,128)(2,1)S(1)}, bf16[160,3584]{1,0:T(8,128)(2,1)S(1)}, u32[]{:S(2)}, u32[]{:S(2)}) collective-permute-start(bf16[160,3584]{1,0:T(8,128)(2,1)S(1)} %bitcast.76), channel_id=1, source_target_pairs={{0,1},{1,0},{2,3},{3,2},{4,5},{5,4},{6,7},{7,6},{8,9},{9,8},{10,11... | collective-permute-start | bytes 3440648 | tf_op jit(solution)/shard_map/ppermute | solution.py:12
  24.4 12.3 %collective-permute-start.14 = (bf16[1,40,3584]{2,1,0:T(8,128)(2,1)S(1)}, bf16[1,40,3584]{2,1,0:T(8,128)(2,1)S(1)}, u32[]{:S(2)}, u32[]{:S(2)}) collective-permute-start(bf16[1,40,3584]{2,1,0:T(8,128)(2,1)S(1)} %collective-permute-done.11), channel_id=1, source_target_pairs={{0,6},{2,4},{4,2},{6,0},{1,7},{3,5},{5,3},{7,1},{8,14},{10,12},{12... | collective-permute-start | bytes 860168 | tf_op jit(solution)/shard_map/ppermute | solution.py:16
  30.5 11.2 %collective-permute-start.13 = (bf16[1,40,3584]{2,1,0:T(8,128)(2,1)S(1)}, bf16[1,40,3584]{2,1,0:T(8,128)(2,1)S(1)}, u32[]{:S(2)}, u32[]{:S(2)}) collective-permute-start(bf16[1,40,3584]{2,1,0:T(8,128)(2,1)S(1)} %collective-permute-done.11), channel_id=1, source_target_pairs={{0,4},{2,6},{4,0},{6,2},{1,5},{3,7},{5,1},{7,3},{8,12},{10,14},{12... | collective-permute-start | bytes 860168 | tf_op jit(solution)/shard_map/ppermute | solution.py:16
  30.8 11.0 %collective-permute-start.12 = (bf16[1,40,3584]{2,1,0:T(8,128)(2,1)S(1)}, bf16[1,40,3584]{2,1,0:T(8,128)(2,1)S(1)}, u32[]{:S(2)}, u32[]{:S(2)}) collective-permute-start(bf16[1,40,3584]{2,1,0:T(8,128)(2,1)S(1)} %collective-permute-done.11), channel_id=1, source_target_pairs={{0,2},{2,0},{4,6},{6,4},{1,3},{3,1},{5,7},{7,5},{8,10},{10,8},{12,... | collective-permute-start | bytes 860168 | tf_op jit(solution)/shard_map/ppermute | solution.py:16
  32.2 4.5 %copy-start = (bf16[1,160,3584]{2,1,0:T(8,128)(2,1)S(1)}, bf16[1,160,3584]{2,1,0:T(8,128)(2,1)}, u32[]{:S(2)}) copy-start(bf16[1,160,3584]{2,1,0:T(8,128)(2,1)} %param.11) | copy-start | bytes 3440644
  36.7 10.1 %collective-permute-start.7 = (bf16[160,3584]{1,0:T(8,128)(2,1)S(1)}, bf16[160,3584]{1,0:T(8,128)(2,1)S(1)}, u32[]{:S(2)}, u32[]{:S(2)}) collective-permute-start(bf16[160,3584]{1,0:T(8,128)(2,1)S(1)} %bitcast.61), channel_id=1, source_target_pairs={{0,1},{1,0},{2,3},{3,2},{4,5},{5,4},{6,7},{7,6},{8,9},{9,8},{10,11... | collective-permute-start | bytes 3440648 | tf_op jit(solution)/shard_map/ppermute | solution.py:12
  47.5 10.7 %collective-permute-start.15 = (bf16[1,40,3584]{2,1,0:T(8,128)(2,1)S(1)}, bf16[1,40,3584]{2,1,0:T(8,128)(2,1)S(1)}, u32[]{:S(2)}, u32[]{:S(2)}) collective-permute-start(bf16[1,40,3584]{2,1,0:T(8,128)(2,1)S(1)} %get-tuple-element.8), channel_id=1, source_target_pairs={{0,6},{2,4},{4,2},{6,0},{1,7},{3,5},{5,3},{7,1},{8,14},{10,12},{12... | collective-permute-start | bytes 860168 | tf_op jit(solution)/shard_map/ppermute | solution.py:16
  49.0 15.2 %collective-permute-start.17 = (bf16[1,40,3584]{2,1,0:T(8,128)(2,1)S(1)}, bf16[1,40,3584]{2,1,0:T(8,128)(2,1)S(1)}, u32[]{:S(2)}, u32[]{:S(2)}) collective-permute-start(bf16[1,40,3584]{2,1,0:T(8,128)(2,1)S(1)} %get-tuple-element.9), channel_id=1, source_target_pairs={{0,4},{2,6},{4,0},{6,2},{1,5},{3,7},{5,1},{7,3},{8,12},{10,14},{12... | collective-permute-start | bytes 860168 | tf_op jit(solution)/shard_map/ppermute | solution.py:16
  50.4 14.0 %collective-permute-start.16 = (bf16[1,40,3584]{2,1,0:T(8,128)(2,1)S(1)}, bf16[1,40,3584]{2,1,0:T(8,128)(2,1)S(1)}, u32[]{:S(2)}, u32[]{:S(2)}) collective-permute-start(bf16[1,40,3584]{2,1,0:T(8,128)(2,1)S(1)} %get-tuple-element.10), channel_id=1, source_target_pairs={{0,2},{2,0},{4,6},{6,4},{1,3},{3,1},{5,7},{7,5},{8,10},{10,8},{12,... | collective-permute-start | bytes 860168 | tf_op jit(solution)/shard_map/ppermute | solution.py:16
  51.6 23.2 %collective-permute-start.8 = (bf16[1,40,3584]{2,1,0:T(8,128)(2,1)S(1)}, bf16[1,40,3584]{2,1,0:T(8,128)(2,1)S(1)}, u32[]{:S(2)}, u32[]{:S(2)}) collective-permute-start(bf16[1,40,3584]{2,1,0:T(8,128)(2,1)S(1)} %get-tuple-element.5), channel_id=1, source_target_pairs={{0,2},{2,0},{4,6},{6,4},{1,3},{3,1},{5,7},{7,5},{8,10},{10,8},{12,... | collective-permute-start | bytes 860168 | tf_op jit(solution)/shard_map/ppermute | solution.py:16
  53.1 23.5 %collective-permute-start.10 = (bf16[1,40,3584]{2,1,0:T(8,128)(2,1)S(1)}, bf16[1,40,3584]{2,1,0:T(8,128)(2,1)S(1)}, u32[]{:S(2)}, u32[]{:S(2)}) collective-permute-start(bf16[1,40,3584]{2,1,0:T(8,128)(2,1)S(1)} %get-tuple-element.6), channel_id=1, source_target_pairs={{0,6},{2,4},{4,2},{6,0},{1,7},{3,5},{5,3},{7,1},{8,14},{10,12},{12... | collective-permute-start | bytes 860168 | tf_op jit(solution)/shard_map/ppermute | solution.py:16
  58.2 23.6 %collective-permute-start.9 = (bf16[1,40,3584]{2,1,0:T(8,128)(2,1)S(1)}, bf16[1,40,3584]{2,1,0:T(8,128)(2,1)S(1)}, u32[]{:S(2)}, u32[]{:S(2)}) collective-permute-start(bf16[1,40,3584]{2,1,0:T(8,128)(2,1)S(1)} %get-tuple-element.7), channel_id=1, source_target_pairs={{0,4},{2,6},{4,0},{6,2},{1,5},{3,7},{5,1},{7,3},{8,12},{10,14},{12... | collective-permute-start | bytes 860168 | tf_op jit(solution)/shard_map/ppermute | solution.py:16
  64.5 17.4 %collective-permute-start.18 = (bf16[1,40,3584]{2,1,0:T(8,128)(2,1)S(1)}, bf16[1,40,3584]{2,1,0:T(8,128)(2,1)S(1)}, u32[]{:S(2)}, u32[]{:S(2)}) collective-permute-start(bf16[1,40,3584]{2,1,0:T(8,128)(2,1)S(1)} %fusion.17), channel_id=1, source_target_pairs={{0,8},{8,0},{1,9},{9,1},{2,10},{10,2},{3,11},{11,3},{4,12},{12,4},... | collective-permute-start | bytes 860168 | tf_op jit(solution)/shard_map/ppermute | solution.py:12
  82.0 0.7 copy-start.1
  82.0 0.7 copy-start.2
  82.1 2.9 %collective-permute-start.19 = (f32[2,40,3584]{2,1,0:T(8,128)S(1)}, f32[2,40,3584]{2,1,0:T(8,128)S(1)}, u32[]{:S(2)}, u32[]{:S(2)}) collective-permute-start(f32[2,40,3584]{2,1,0:T(8,128)S(1)} %pad_maximum_fusion.9), channel_id=1, source_target_pairs={{0,1},{1,0},{2,3},{3,2},{4,5},{5,4},{6,7},{7,6},{8,9},{9,8},{10,11... | collective-permute-start | bytes 3440648 | tf_op jit(solution)/shard_map/ppermute | solution.py:12
